TPU v7x, 32 devices: a whole 2x2x4 slice. The times are simulated.
32 devices in a mesh: groups: 2 (over y), gx: 4 (over z), gy: 4 (over x, core).
Axes of the slice: x: 2, y: 2, z: 4, core: 2. Of those that a mesh axis runs over, the one named last changes fastest.
Arguments:
- tokens: bfloat16 [40, 8192], P(('groups', 'gx'), 'gy'), parts along dimension 0, may hold values from -180 to 180, as said below
- norm_gain: float32 [8192], P('gy'), may hold values from 0.1 to 1.9
- w_gate: bfloat16 [8192, 24576], P('gy', 'gx'), may hold values from -0.0625 to 0.0625
- w_up: bfloat16 [8192, 24576], P('gy', 'gx'), may hold values from -0.0625 to 0.0625
- w_down: bfloat16 [24576, 8192], P('gx', 'gy'), may hold values from -0.0390625 to 0.0390625
Outputs:
- mixed: bfloat16 [40, 8192], P(('groups', 'gx'), 'gy'), parts along dimension 0
There are 2 independent parts, one for each index of `groups`. A program takes and returns all parts, laid end to end along the dimension named above; an argument that names none is the same for every part. Nothing has to cross between parts.
Inputs may be any that keep to these rules, and one draw needn't show every extreme that they name: tokens are real-valued activations of order one to some tens.
All inputs are finite; a program needn't handle non-finite values.
Results may differ from a plain program's by a relative error of at most 0.0064.
Values may be sent and summed in bfloat16 or wider, within the bound.
No kernel may reach another device: no remote copies, remote signals or barrier semaphores. Data moves between devices by JAX's collectives and lax.ppermute only.
A program may use at most 192 MiB of HBM per device.

v0:
```python
import jax
import jax.numpy as jnp
from jax import lax
from jax.sharding import PartitionSpec as P

D = 8192


epsilon = 1e-06


def activate(both, width):
    gate = both[:, :width]
    up_part = both[:, width:]
    return (jax.nn.silu(gate) * up_part).astype(jnp.bfloat16)


def local(tokens, norm_gain, w_gate, w_up, w_down):
    values = tokens.astype(jnp.float32)
    local_sq = jnp.sum(values * values, axis=1)
    total_sq = lax.psum(local_sq, "gy")
    inverse = lax.rsqrt(total_sq / D + epsilon)
    normed = (values * inverse[:, None] * norm_gain[None, :]).astype(jnp.bfloat16)
    width = w_gate.shape[1]
    piece = lax.all_gather(normed, "gx", axis=0, tiled=True)
    gate_part = jnp.dot(piece, w_gate, preferred_element_type=jnp.float32)
    up_part = jnp.dot(piece, w_up, preferred_element_type=jnp.float32)
    partial_value = jnp.concatenate([gate_part, up_part], axis=1)
    summed = lax.psum(partial_value, "gy")
    hidden = activate(summed, width)
    result = lax.psum_scatter(
        jnp.dot(hidden, w_down, preferred_element_type=jnp.float32),
        "gx",
        scatter_dimension=0,
        tiled=True,
    )
    return result.astype(jnp.bfloat16)


def solution(mesh):
    in_specs = (P(("groups", "gx"), "gy"), P("gy"), P("gy", "gx"), P("gy", "gx"), P("gx", "gy"))
    out_specs = P(("groups", "gx"), "gy")
    return jax.shard_map(local, mesh=mesh, in_specs=in_specs, out_specs=out_specs, check_vma=False)
```

profile of v0, /device:TPU:0, one launch (start us, length us, event | category | flops | bytes accessed | tf_op | source)
XLA Modules:
  0.0 128.5 jit_solution(15527987693795817400)
XLA Ops:
  6.5 0.0 all-reduce.4.cloned.1.call-start
  6.5 0.9 fusion.5
  7.4 8.3 %psum.14 = f32[5]{0:T(128)S(1)} all-reduce(f32[5]{0:T(128)S(1)} %fusion.5), channel_id=1, replica_groups=mesh['groups'=2,'gx'=4,'gy'=4] {'gy'}, use_global_device_ids=true, to_apply=%region_1.0 | all-reduce | flops 5 | bytes 40 | tf_op jit(solution)/shard_map/psum | solution.py:21
  15.8 0.8 fusion.8
  16.6 13.6 %all-gather = bf16[4,5,2048]{2,1,0:T(8,128)(2,1)S(1)} all-gather(bf16[1,5,2048]{2,1,0:T(8,128)(2,1)S(1)} %fusion.8), channel_id=1, replica_groups=mesh['groups'=2,'gx'=4,'gy'=4] {'gx'}, dimensions={0}, use_global_device_ids=true | all-gather | bytes 102400 | tf_op jit(solution)/shard_map/all_gather | solution.py:25
  30.3 9.9 %fusion.10 = f32[20,6144]{1,0:T(8,128)S(1)} fusion(bf16[20,2048]{1,0:T(8,128)(2,1)S(1)} %reshape.3, bf16[2048,6144]{1,0:T(8,128)(2,1)} %param.7), kind=kOutput, calls=%fused_computation.14 | convolution fusion | flops 503316480 | bytes 25739264 | tf_op jit(solution)/shard_map/dot_general | solution.py:26
  40.2 9.9 %fusion.11 = f32[20,6144]{1,0:T(8,128)S(1)} fusion(bf16[20,2048]{1,0:T(8,128)(2,1)S(1)} %reshape.3, bf16[2048,6144]{1,0:T(8,128)(2,1)} %param.8), kind=kOutput, calls=%fused_computation.15 | convolution fusion | flops 503316480 | bytes 25739264 | tf_op jit(solution)/shard_map/dot_general | solution.py:27
  50.1 0.0 copy-start
  50.1 1.1 pad_maximum_fusion
  51.2 0.0 all-reduce.4.cloned.1.call-update
  51.2 37.8 %all-reduce.4.cloned.1.call-done = f32[20,12288]{1,0:T(8,128)} async-done(((f32[20,12288]{1,0:T(8,128)}), f32[20,12288]{1,0:T(8,128)}) %all-reduce.4.cloned.1.call-update) | async-done | bytes 983056 | tf_op jit(solution)/shard_map/psum | solution.py:29
  89.0 10.2 %fusion.2 = f32[20,2048]{1,0:T(8,128)S(1)} fusion(bf16[6144,2048]{1,0:T(8,128)(2,1)} %param.9, f32[20,12288]{1,0:T(8,128)} %all-reduce.4.cloned.1.call-done), kind=kOutput, calls=%fused_computation.3 | convolution fusion | flops 504053760 | bytes 26312704 | tf_op jit(solution)/shard_map/dot_general | solution.py:32
  99.3 14.6 %fusion = f32[8,2048]{1,0:T(8,128)S(1)} fusion(f32[20,2048]{1,0:T(8,128)S(1)} %fusion.2), kind=kCustom, calls=%all-reduce-scatter | all-reduce-scatter fusion | flops 65537 | bytes 229888
  113.9 2.2 %collective-permute-start = (bf16[8,2048]{1,0:T(8,128)(2,1)S(1)}, bf16[8,2048]{1,0:T(8,128)(2,1)S(1)}, u32[]{:S(2)}, u32[]{:S(2)}) collective-permute-start(bf16[8,2048]{1,0:T(8,128)(2,1)S(1)} %convert), channel_id=1, source_target_pairs={{0,4},{4,8},{8,12},{1,5},{5,9},{9,13},{2,6},{6,10},{10,14},{3,7},{... | collective-permute-start | bytes 98312
  116.2 3.2 %collective-permute-start.1 = (bf16[1,2048]{1,0:T(2,128)(2,1)S(1)}, bf16[1,2048]{1,0:T(2,128)(2,1)S(1)}, u32[]{:S(2)}, u32[]{:S(2)}) collective-permute-start(bf16[1,2048]{1,0:T(2,128)(2,1)S(1)} %slice.10), channel_id=1, source_target_pairs={{0,8},{4,12},{1,9},{5,13},{2,10},{6,14},{3,11},{7,15},{16,24},{20,... | collective-permute-start | bytes 12296
  119.4 0.0 copy-done
  119.4 0.6 dynamic-slice.4
  120.6 0.1 collective-permute-done.1
  120.7 0.0 collective-permute-done
  120.7 0.3 concatenate.4
  121.0 0.6 dynamic-slice_convert_fusion
  (4 shorter events, 0.1 us)
Async XLA Ops:
  6.5 82.5 %all-reduce.4.cloned.1.call-start = ((), (), s32[]{:S(2)}) async-start(), calls=%async_computation | async-start | bytes 2359296 | tf_op jit(solution)/shard_map/psum | solution.py:29
  50.1 69.3 %copy-start = (u32[32]{0:T(128)S(1)}, u32[32]{0:T(128)}, u32[]{:S(2)}) copy-start(u32[32]{0:T(128)} %constant.13) | copy-start | bytes 388
  113.9 6.8 %collective-permute-start = (bf16[8,2048]{1,0:T(8,128)(2,1)S(1)}, bf16[8,2048]{1,0:T(8,128)(2,1)S(1)}, u32[]{:S(2)}, u32[]{:S(2)}) collective-permute-start(bf16[8,2048]{1,0:T(8,128)(2,1)S(1)} %convert), channel_id=1, source_target_pairs={{0,4},{4,8},{8,12},{1,5},{5,9},{9,13},{2,6},{6,10},{10,14},{3,7},{... | collective-permute-start | bytes 98312
  116.2 4.5 %collective-permute-start.1 = (bf16[1,2048]{1,0:T(2,128)(2,1)S(1)}, bf16[1,2048]{1,0:T(2,128)(2,1)S(1)}, u32[]{:S(2)}, u32[]{:S(2)}) collective-permute-start(bf16[1,2048]{1,0:T(2,128)(2,1)S(1)} %slice.10), channel_id=1, source_target_pairs={{0,8},{4,12},{1,9},{5,13},{2,10},{6,14},{3,11},{7,15},{16,24},{20,... | collective-permute-start | bytes 12296
Sparse Core Ops, SparseCore 0:
  51.4 37.6 all-reduce.3
where the time goes:
time: 129 us
  waiting for transfers between devices  37.9 us (29%)
  blocking collectives  36.6 us (28%)
  matrix products  30 us (23%)
  between operations  14.1 us (11%)
  starting transfers between devices  5.42 us (4%)
  other arithmetic  2.87 us (2%)
  local copies, waits for them, and re-layouts  1.57 us (1%)
    psum x1, waiting for transfers between devices, local(): summed = lax.psum(partial_value, 'gy')  37.8 us
    unnamed x1, blocking collectives  14.6 us
    all_gather x1, blocking collectives, local(): piece = lax.all_gather(normed, 'gx', axis=0, tiled=True)  13.6 us
    dot_general x1, matrix products, local(): jnp.dot(hidden, w_down, preferred_element_type=jnp.float32)  10.2 us
    dot_general x1, matrix products, local(): up_part = jnp.dot(piece, w_up, preferred_element_type=jnp.float32)  9.91 us
    dot_general x1, matrix products, local(): gate_part = jnp.dot(piece, w_gate, preferred_element_type=jnp.float32)  9.91 us
    psum x1, blocking collectives, local(): total_sq = lax.psum(local_sq, 'gy')  8.34 us
    unnamed x2, starting transfers between devices  5.41 us
  transfers between devices with their start and end apart: 3, of which 2 were waited for; matrix products, arithmetic and copies ran while one was open for 0% of the time, Pallas kernels for 0%

commit v1 on v0

v1 whole, which is shorter than its diff:
```python
import jax
import jax.numpy as jnp
from jax import lax
from jax.sharding import PartitionSpec as P


epsilon = 1e-06

FANOUT_MAX = 8
CHUNKS = 4


def fanout(x, axis, n):
    outs = [x]
    for k in range(1, n):
        outs.append(lax.ppermute(x, axis, [(a, (a + k) % n) for a in range(n)]))
    return outs


def gather_rows(normed, ngx):
    if ngx <= FANOUT_MAX:
        return jnp.concatenate(fanout(normed, "gx", ngx), axis=0)
    return lax.all_gather(normed, "gx", axis=0, tiled=True)


def scatter_rows(total, ngx):
    if ngx <= FANOUT_MAX:
        rows = total.shape[0] // ngx
        own = total[:rows]
        for m in range(1, ngx):
            k = (ngx - m) % ngx
            block = total[k * rows:(k + 1) * rows]
            own = own + lax.ppermute(block, "gx", [(a, (a + m) % ngx) for a in range(ngx)])
        return own
    return lax.psum_scatter(total, "gx", scatter_dimension=0, tiled=True)


def reduce_columns(both, ngy):
    if ngy <= FANOUT_MAX:
        me = lax.axis_index("gy")
        own = lax.dynamic_index_in_dim(both, me, axis=2, keepdims=False)
        for k in range(1, ngy):
            part = lax.dynamic_index_in_dim(both, (me + k) % ngy, axis=2, keepdims=False)
            own = own + lax.ppermute(part, "gy", [(a, (a + k) % ngy) for a in range(ngy)])
        return own
    return lax.psum_scatter(both, "gy", scatter_dimension=2, tiled=True)[:, :, 0]


def gather_columns(hidden, ngy):
    if ngy <= FANOUT_MAX:
        me = lax.axis_index("gy")
        stacked = jnp.stack(fanout(hidden, "gy", ngy), axis=0)
        order = (me - jnp.arange(ngy)) % ngy
        ordered = jnp.take(stacked, order, axis=0)
        return jnp.transpose(ordered, (1, 0, 2)).reshape(hidden.shape[0], -1)
    return lax.all_gather(hidden, "gy", axis=1, tiled=True)


def local(tokens, norm_gain, w_gate, w_up, w_down):
    ngx = lax.axis_size("gx")
    ngy = lax.axis_size("gy")
    features = tokens.shape[1] * ngy
    values = tokens.astype(jnp.float32)
    local_sq = jnp.sum(values * values, axis=1)
    if ngy <= FANOUT_MAX:
        total_sq = sum(fanout(local_sq, "gy", ngy))
    else:
        total_sq = lax.psum(local_sq, "gy")
    inverse = lax.rsqrt(total_sq / features + epsilon)
    normed = (values * inverse[:, None] * norm_gain[None, :]).astype(jnp.bfloat16)
    piece = gather_rows(normed, ngx)
    rows = piece.shape[0]

    width = w_gate.shape[1]
    chunks = CHUNKS if width % (CHUNKS * ngy * 128) == 0 else 1
    step = width // chunks
    total = None
    for c in range(chunks):
        cols = slice(c * step, (c + 1) * step)
        gate_part = jnp.dot(piece, w_gate[:, cols], preferred_element_type=jnp.float32)
        up_part = jnp.dot(piece, w_up[:, cols], preferred_element_type=jnp.float32)
        both = jnp.stack([gate_part, up_part]).reshape(2, rows, ngy, step // ngy)
        summed = reduce_columns(both, ngy)
        hidden = (jax.nn.silu(summed[0]) * summed[1]).astype(jnp.bfloat16)
        hidden_all = gather_columns(hidden, ngy)
        term = jnp.dot(hidden_all, w_down[cols, :], preferred_element_type=jnp.float32)
        total = term if total is None else total + term
    result = scatter_rows(total, ngx)
    return result.astype(jnp.bfloat16)


def solution(mesh):
    in_specs = (P(("groups", "gx"), "gy"), P("gy"), P("gy", "gx"), P("gy", "gx"), P("gx", "gy"))
    out_specs = P(("groups", "gx"), "gy")
    return jax.shard_map(local, mesh=mesh, in_specs=in_specs, out_specs=out_specs, check_vma=False)
```

time: 129 us -> 97.5 us (0.76)
  blocking collectives: 36.6 us -> 0 us
  starting transfers between devices: 5.42 us -> 28.3 us
  waiting for transfers between devices: 37.9 us -> 20.2 us
  between operations: 14.1 us -> 0.66 us
  matrix products: 30 us -> 39.8 us
  local copies, waits for them, and re-layouts: 1.57 us -> 4.08 us
    psum x1 -> x0, waiting for transfers between devices: 37.8 us -> none  [local(): summed = lax.psum(partial_value, 'gy')]
    ppermute x0 -> x33, starting transfers between devices: none -> 28.3 us  [the longest x18 16.5 us: fanout(): outs.append(lax.ppermute(x, axis, [(a, (a + k) % n) for a in range(n)]))]
    ppermute x0 -> x33, waiting for transfers between devices: none -> 20.2 us  [the longest x18 8.84 us: fanout(): outs.append(lax.ppermute(x, axis, [(a, (a + k) % n) for a in range(n)]))]
    unnamed x1 -> x0, blocking collectives: 14.6 us -> none
    all_gather x1 -> x0, blocking collectives: 13.6 us -> none  [local(): piece = lax.all_gather(normed, 'gx', axis=0, tiled=True)]
    dot_general x3 -> x12, matrix products: 30 us -> 39.8 us  [the longest x4 14.9 us: local(): jnp.dot(hidden_all, w_down[cols, :], preferred_element_type=jnp.float32)]
    psum x1 -> x0, blocking collectives: 8.34 us -> none  [local(): total_sq = lax.psum(local_sq, 'gy')]
    unnamed x2 -> x0, starting transfers between devices: 5.41 us -> none
  transfers between devices with their start and end apart: 3 -> 33, of which waited for: 2 -> 17; matrix products, arithmetic and copies ran while one was open for 0% -> 4% of each run, Pallas kernels for 0% -> 0%
where the time goes in v1:
time: 97.5 us; the launch traced here: 96.9 us
  matrix products  39.8 us (41%)
  starting transfers between devices  28.3 us (29%)
  waiting for transfers between devices  20.2 us (21%)
  local copies, waits for them, and re-layouts  4.08 us (4%)
  other arithmetic  3.87 us (4%)
    ppermute x18, starting transfers between devices, fanout(): outs.append(lax.ppermute(x, axis, [(a, (a + k) % n) for a in range(n)]))  16.5 us
    dot_general x4, matrix products, local(): jnp.dot(hidden_all, w_down[cols, :], preferred_element_type=jnp.float32)  14.9 us
    dot_general x4, matrix products, local(): jnp.dot(piece, w_gate[:, cols], preferred_element_type=jnp.float32)  14.9 us
    dot_general x4, matrix products, local(): up_part = jnp.dot(piece, w_up[:, cols], preferred_element_type=jnp.float32)  10.1 us
    ppermute x18, waiting for transfers between devices, fanout(): outs.append(lax.ppermute(x, axis, [(a, (a + k) % n) for a in range(n)]))  8.84 us
    ppermute x12, starting transfers between devices, reduce_columns(): lax.ppermute(part, 'gy', [(a, (a + k) % ngy) for a in range(ngy)])  7.97 us
    ppermute x3, waiting for transfers between devices, scatter_rows(): lax.ppermute(block, 'gx', [(a, (a + m) % ngx) for a in range(ngx)])  5.75 us
    ppermute x12, waiting for transfers between devices, reduce_columns(): lax.ppermute(part, 'gy', [(a, (a + k) % ngy) for a in range(ngy)])  5.57 us
  transfers between devices with their start and end apart: 33, of which 17 were waited for; matrix products, arithmetic and copies ran while one was open for 4% of the time, Pallas kernels for 0%

profile of v1, /device:TPU:0, one launch (start us, length us, event | category | flops | bytes accessed | tf_op | source)
XLA Modules:
  0.0 96.9 jit_solution(15878127815166595712)
XLA Ops:
  0.9 2.4 %collective-permute-start.2 = (f32[5]{0:T(128)S(1)}, f32[5]{0:T(128)S(1)}, u32[]{:S(2)}, u32[]{:S(2)}) collective-permute-start(f32[5]{0:T(128)S(1)} %fusion.39), channel_id=1, source_target_pairs={{0,3},{1,0},{2,1},{3,2},{4,7},{5,4},{6,5},{7,6},{8,11},{9,8},{10,9... | collective-permute-start | bytes 68 | tf_op jit(solution)/shard_map/ppermute | solution.py:16
  4.6 2.2 %collective-permute-done.1 = f32[5]{0:T(128)S(1)} collective-permute-done((f32[5]{0:T(128)S(1)}, f32[5]{0:T(128)S(1)}, u32[]{:S(2)}, u32[]{:S(2)}) %collective-permute-start.1) | collective-permute-done | bytes 52 | tf_op jit(solution)/shard_map/ppermute | solution.py:16
  7.8 3.7 %collective-permute-start.5 = (bf16[5,2048]{1,0:T(8,128)(2,1)S(1)}, bf16[5,2048]{1,0:T(8,128)(2,1)S(1)}, u32[]{:S(2)}, u32[]{:S(2)}) collective-permute-start(bf16[5,2048]{1,0:T(8,128)(2,1)S(1)} %fusion.41), channel_id=1, source_target_pairs={{0,12},{4,0},{8,4},{12,8},{1,13},{5,1},{9,5},{13,9},{2,14},{6,2},{... | collective-permute-start | bytes 61448 | tf_op jit(solution)/shard_map/ppermute | solution.py:16
  13.0 3.2 %collective-permute-done.4 = bf16[5,2048]{1,0:T(8,128)(2,1)S(1)} collective-permute-done((bf16[5,2048]{1,0:T(8,128)(2,1)S(1)}, bf16[5,2048]{1,0:T(8,128)(2,1)S(1)}, u32[]{:S(2)}, u32[]{:S(2)}) %collective-permute-start.4) | collective-permute-done | bytes 20512 | tf_op jit(solution)/shard_map/ppermute | solution.py:16
  17.2 4.5 %fusion.2 = f32[20,1536]{1,0:T(8,128)S(1)} fusion(bf16[20,2048]{1,0:T(8,128)(2,1)S(1)} %pad_maximum_fusion, bf16[2048,6144]{1,0:T(8,128)(2,1)} %param.10), kind=kOutput, calls=%fused_computation.6 | convolution fusion | flops 125829120 | bytes 6496256 | tf_op jit(solution)/shard_map/dot_general | solution.py:81
  21.6 3.7 %fusion.8 = f32[20,1536]{1,0:T(8,128)S(1)} fusion(bf16[20,2048]{1,0:T(8,128)(2,1)S(1)} %pad_maximum_fusion, bf16[2048,6144]{1,0:T(8,128)(2,1)} %param.10), kind=kOutput, calls=%fused_computation.12 | convolution fusion | flops 125829120 | bytes 6496256 | tf_op jit(solution)/shard_map/dot_general | solution.py:81
  25.4 3.7 %fusion.4 = f32[20,1536]{1,0:T(8,128)S(1)} fusion(bf16[20,2048]{1,0:T(8,128)(2,1)S(1)} %pad_maximum_fusion, bf16[2048,6144]{1,0:T(8,128)(2,1)} %param.9), kind=kOutput, calls=%fused_computation.8 | convolution fusion | flops 125829120 | bytes 6496256 | tf_op jit(solution)/shard_map/dot_general | solution.py:80
  29.1 3.7 %fusion.10 = f32[20,1536]{1,0:T(8,128)S(1)} fusion(bf16[20,2048]{1,0:T(8,128)(2,1)S(1)} %pad_maximum_fusion, bf16[2048,6144]{1,0:T(8,128)(2,1)} %param.9), kind=kOutput, calls=%fused_computation.14 | convolution fusion | flops 125829120 | bytes 6496256 | tf_op jit(solution)/shard_map/dot_general | solution.py:80
  33.8 3.7 %fusion.16 = f32[20,1536]{1,0:T(8,128)S(1)} fusion(bf16[20,2048]{1,0:T(8,128)(2,1)S(1)} %pad_maximum_fusion, bf16[2048,6144]{1,0:T(8,128)(2,1)} %param.9), kind=kOutput, calls=%fused_computation.20 | convolution fusion | flops 125829120 | bytes 6496256 | tf_op jit(solution)/shard_map/dot_general | solution.py:80
  38.4 3.7 %fusion.22 = f32[20,1536]{1,0:T(8,128)S(1)} fusion(bf16[20,2048]{1,0:T(8,128)(2,1)S(1)} %pad_maximum_fusion, bf16[2048,6144]{1,0:T(8,128)(2,1)} %param.9), kind=kOutput, calls=%fused_computation.26 | convolution fusion | flops 125829120 | bytes 6496256 | tf_op jit(solution)/shard_map/dot_general | solution.py:80
  42.9 1.5 %collective-permute-start.25 = (f32[2,20,384]{2,1,0:T(8,128)S(1)}, f32[2,20,384]{2,1,0:T(8,128)S(1)}, u32[]{:S(2)}, u32[]{:S(2)}) collective-permute-start(f32[2,20,384]{2,1,0:T(8,128)S(1)} %copy.29), channel_id=1, source_target_pairs={{0,2},{1,3},{2,0},{3,1},{4,6},{5,7},{6,4},{7,5},{8,10},{9,11},{10,... | collective-permute-start | bytes 184328 | tf_op jit(solution)/shard_map/ppermute | solution.py:44
  49.6 1.3 %collective-permute-done.7 = f32[2,20,384]{2,0,1:T(2,128)S(1)} collective-permute-done((f32[2,20,384]{2,0,1:T(2,128)S(1)}, f32[2,20,384]{2,0,1:T(2,128)S(1)}, u32[]{:S(2)}, u32[]{:S(2)}) %collective-permute-start.7) | collective-permute-done | bytes 61472 | tf_op jit(solution)/shard_map/ppermute | solution.py:44
  52.9 1.7 %collective-permute-start.14 = (f32[2,20,384]{2,1,0:T(8,128)S(1)}, f32[2,20,384]{2,1,0:T(8,128)S(1)}, u32[]{:S(2)}, u32[]{:S(2)}) collective-permute-start(f32[2,20,384]{2,1,0:T(8,128)S(1)} %copy.16), channel_id=1, source_target_pairs={{0,3},{1,0},{2,1},{3,2},{4,7},{5,4},{6,5},{7,6},{8,11},{9,8},{10,9... | collective-permute-start | bytes 184328 | tf_op jit(solution)/shard_map/ppermute | solution.py:44
  55.6 1.3 %collective-permute-done.19 = f32[2,20,384]{2,1,0:T(8,128)S(1)} collective-permute-done((f32[2,20,384]{2,1,0:T(8,128)S(1)}, f32[2,20,384]{2,1,0:T(8,128)S(1)}, u32[]{:S(2)}, u32[]{:S(2)}) %collective-permute-start.19) | collective-permute-done | bytes 61472 | tf_op jit(solution)/shard_map/ppermute | solution.py:44
  58.8 1.4 %collective-permute-done.13 = f32[2,20,384]{2,1,0:T(8,128)S(1)} collective-permute-done((f32[2,20,384]{2,1,0:T(8,128)S(1)}, f32[2,20,384]{2,1,0:T(8,128)S(1)}, u32[]{:S(2)}, u32[]{:S(2)}) %collective-permute-start.13) | collective-permute-done | bytes 61472 | tf_op jit(solution)/shard_map/ppermute | solution.py:44
  61.6 1.7 %collective-permute-start.17 = (bf16[20,384]{1,0:T(8,128)(2,1)S(1)}, bf16[20,384]{1,0:T(8,128)(2,1)S(1)}, u32[]{:S(2)}, u32[]{:S(2)}) collective-permute-start(bf16[20,384]{1,0:T(8,128)(2,1)S(1)} %fusion.97), channel_id=1, source_target_pairs={{0,3},{1,0},{2,1},{3,2},{4,7},{5,4},{6,5},{7,6},{8,11},{9,8},{10,9... | collective-permute-start | bytes 46088 | tf_op jit(solution)/shard_map/ppermute | solution.py:16
  64.6 1.7 %collective-permute-start.11 = (bf16[20,384]{1,0:T(8,128)(2,1)S(1)}, bf16[20,384]{1,0:T(8,128)(2,1)S(1)}, u32[]{:S(2)}, u32[]{:S(2)}) collective-permute-start(bf16[20,384]{1,0:T(8,128)(2,1)S(1)} %fusion.82), channel_id=1, source_target_pairs={{0,3},{1,0},{2,1},{3,2},{4,7},{5,4},{6,5},{7,6},{8,11},{9,8},{10,9... | collective-permute-start | bytes 46088 | tf_op jit(solution)/shard_map/ppermute | solution.py:16
  71.7 3.7 %fusion.12 = f32[20,2048]{1,0:T(8,128)S(1)} fusion(bf16[20,1536]{1,0:T(8,128)(2,1)S(1)} %bitcast.158, bf16[6144,2048]{1,0:T(8,128)(2,1)} %param.11), kind=kOutput, calls=%fused_computation.16 | convolution fusion | flops 125829120 | bytes 6516736 | tf_op jit(solution)/shard_map/dot_general | solution.py:86
  75.4 3.7 %fusion.24 = f32[20,2048]{1,0:T(8,128)S(1)} fusion(f32[20,2048]{1,0:T(8,128)S(1)} %fusion.12, bf16[20,1536]{1,0:T(8,128)(2,1)S(1)} %bitcast.160, bf16[6144,2048]{1,0:T(8,128)(2,1)} %param.11), kind=kOutput, calls=%fused_computation.28 | convolution fusion | flops 125870080 | bytes 6680576 | tf_op jit(solution)/shard_map/dot_general | solution.py:86
  79.2 3.7 %fusion.27 = f32[20,2048]{1,0:T(8,128)S(1)} fusion(f32[20,2048]{1,0:T(8,128)S(1)} %fusion.24, bf16[20,1536]{1,0:T(8,128)(2,1)S(1)} %bitcast.159, bf16[6144,2048]{1,0:T(8,128)(2,1)} %param.11), kind=kOutput, calls=%fused_computation.29 | convolution fusion | flops 125870080 | bytes 6680576 | tf_op jit(solution)/shard_map/dot_general | solution.py:86
  82.9 3.7 %fusion.30 = f32[20,2048]{1,0:T(8,128)S(1)} fusion(f32[20,2048]{1,0:T(8,128)S(1)} %fusion.27, bf16[20,1536]{1,0:T(8,128)(2,1)S(1)} %bitcast.157, bf16[6144,2048]{1,0:T(8,128)(2,1)} %param.11), kind=kOutput, calls=%fused_computation.30 | convolution fusion | flops 125870080 | bytes 6680576 | tf_op jit(solution)/shard_map/dot_general | solution.py:86
  87.1 3.4 %collective-permute-start.32 = (f32[5,2048]{1,0:T(8,128)S(1)}, f32[5,2048]{1,0:T(8,128)S(1)}, u32[]{:S(2)}, u32[]{:S(2)}) collective-permute-start(f32[5,2048]{1,0:T(8,128)S(1)} %get-tuple-element.22), channel_id=1, source_target_pairs={{0,12},{4,0},{8,4},{12,8},{1,13},{5,1},{9,5},{13,9},{2,14},{6,2},{... | collective-permute-start | bytes 122888 | tf_op jit(solution)/shard_map/ppermute | solution.py:33
  90.5 3.0 %collective-permute-done.30 = f32[5,2048]{1,0:T(8,128)S(1)} collective-permute-done((f32[5,2048]{1,0:T(8,128)S(1)}, f32[5,2048]{1,0:T(8,128)S(1)}, u32[]{:S(2)}, u32[]{:S(2)}) %collective-permute-start.30) | collective-permute-done | bytes 40992 | tf_op jit(solution)/shard_map/ppermute | solution.py:33
  93.5 2.8 %collective-permute-done.31 = f32[5,2048]{1,0:T(8,128)S(1)} collective-permute-done((f32[5,2048]{1,0:T(8,128)S(1)}, f32[5,2048]{1,0:T(8,128)S(1)}, u32[]{:S(2)}, u32[]{:S(2)}) %collective-permute-start.31) | collective-permute-done | bytes 40992 | tf_op jit(solution)/shard_map/ppermute | solution.py:33
  (128 shorter events, 27.0 us)
Async XLA Ops:
  7.8 5.2 %collective-permute-start.5 = (bf16[5,2048]{1,0:T(8,128)(2,1)S(1)}, bf16[5,2048]{1,0:T(8,128)(2,1)S(1)}, u32[]{:S(2)}, u32[]{:S(2)}) collective-permute-start(bf16[5,2048]{1,0:T(8,128)(2,1)S(1)} %fusion.41), channel_id=1, source_target_pairs={{0,12},{4,0},{8,4},{12,8},{1,13},{5,1},{9,5},{13,9},{2,14},{6,2},{... | collective-permute-start | bytes 61448 | tf_op jit(solution)/shard_map/ppermute | solution.py:16
  11.4 4.8 %collective-permute-start.4 = (bf16[5,2048]{1,0:T(8,128)(2,1)S(1)}, bf16[5,2048]{1,0:T(8,128)(2,1)S(1)}, u32[]{:S(2)}, u32[]{:S(2)}) collective-permute-start(bf16[5,2048]{1,0:T(8,128)(2,1)S(1)} %fusion.41), channel_id=1, source_target_pairs={{0,8},{4,12},{8,0},{12,4},{1,9},{5,13},{9,1},{13,5},{2,10},{6,14},... | collective-permute-start | bytes 61448 | tf_op jit(solution)/shard_map/ppermute | solution.py:16
  11.4 5.7 %collective-permute-start.3 = (bf16[5,2048]{1,0:T(8,128)(2,1)S(1)}, bf16[5,2048]{1,0:T(8,128)(2,1)S(1)}, u32[]{:S(2)}, u32[]{:S(2)}) collective-permute-start(bf16[5,2048]{1,0:T(8,128)(2,1)S(1)} %fusion.41), channel_id=1, source_target_pairs={{0,4},{4,8},{8,12},{12,0},{1,5},{5,9},{9,13},{13,1},{2,6},{6,10},{... | collective-permute-start | bytes 61448 | tf_op jit(solution)/shard_map/ppermute | solution.py:16
  42.8 10.1 %collective-permute-start.26 = (f32[2,20,384]{2,1,0:T(8,128)S(1)}, f32[2,20,384]{2,1,0:T(8,128)S(1)}, u32[]{:S(2)}, u32[]{:S(2)}) collective-permute-start(f32[2,20,384]{2,1,0:T(8,128)S(1)} %copy.30), channel_id=1, source_target_pairs={{0,3},{1,0},{2,1},{3,2},{4,7},{5,4},{6,5},{7,6},{8,11},{9,8},{10,9... | collective-permute-start | bytes 184328 | tf_op jit(solution)/shard_map/ppermute | solution.py:44
  42.9 10.1 %collective-permute-start.25 = (f32[2,20,384]{2,1,0:T(8,128)S(1)}, f32[2,20,384]{2,1,0:T(8,128)S(1)}, u32[]{:S(2)}, u32[]{:S(2)}) collective-permute-start(f32[2,20,384]{2,1,0:T(8,128)S(1)} %copy.29), channel_id=1, source_target_pairs={{0,2},{1,3},{2,0},{3,1},{4,6},{5,7},{6,4},{7,5},{8,10},{9,11},{10,... | collective-permute-start | bytes 184328 | tf_op jit(solution)/shard_map/ppermute | solution.py:44
  46.1 4.8 %collective-permute-start.7 = (f32[2,20,384]{2,0,1:T(2,128)S(1)}, f32[2,20,384]{2,0,1:T(2,128)S(1)}, u32[]{:S(2)}, u32[]{:S(2)}) collective-permute-start(f32[2,20,384]{2,0,1:T(2,128)S(1)} %get-tuple-element.15), channel_id=1, source_target_pairs={{0,2},{1,3},{2,0},{3,1},{4,6},{5,7},{6,4},{7,5},{8,10},{9,11},{10,... | collective-permute-start | bytes 184328 | tf_op jit(solution)/shard_map/ppermute | solution.py:44
  46.8 4.6 %collective-permute-start.8 = (f32[2,20,384]{2,0,1:T(2,128)S(1)}, f32[2,20,384]{2,0,1:T(2,128)S(1)}, u32[]{:S(2)}, u32[]{:S(2)}) collective-permute-start(f32[2,20,384]{2,0,1:T(2,128)S(1)} %get-tuple-element.16), channel_id=1, source_target_pairs={{0,3},{1,0},{2,1},{3,2},{4,7},{5,4},{6,5},{7,6},{8,11},{9,8},{10,9... | collective-permute-start | bytes 184328 | tf_op jit(solution)/shard_map/ppermute | solution.py:44
  49.6 5.1 %collective-permute-start.24 = (f32[2,20,384]{2,1,0:T(8,128)S(1)}, f32[2,20,384]{2,1,0:T(8,128)S(1)}, u32[]{:S(2)}, u32[]{:S(2)}) collective-permute-start(f32[2,20,384]{2,1,0:T(8,128)S(1)} %copy.27), channel_id=1, source_target_pairs={{0,1},{1,2},{2,3},{3,0},{4,5},{5,6},{6,7},{7,4},{8,9},{9,10},{10,1... | collective-permute-start | bytes 184328 | tf_op jit(solution)/shard_map/ppermute | solution.py:44
  50.9 4.6 %collective-permute-start.20 = (f32[2,20,384]{2,1,0:T(8,128)S(1)}, f32[2,20,384]{2,1,0:T(8,128)S(1)}, u32[]{:S(2)}, u32[]{:S(2)}) collective-permute-start(f32[2,20,384]{2,1,0:T(8,128)S(1)} %copy.23), channel_id=1, source_target_pairs={{0,3},{1,0},{2,1},{3,2},{4,7},{5,4},{6,5},{7,6},{8,11},{9,8},{10,9... | collective-permute-start | bytes 184328 | tf_op jit(solution)/shard_map/ppermute | solution.py:44
  51.4 5.5 %collective-permute-start.19 = (f32[2,20,384]{2,1,0:T(8,128)S(1)}, f32[2,20,384]{2,1,0:T(8,128)S(1)}, u32[]{:S(2)}, u32[]{:S(2)}) collective-permute-start(f32[2,20,384]{2,1,0:T(8,128)S(1)} %copy.22), channel_id=1, source_target_pairs={{0,2},{1,3},{2,0},{3,1},{4,6},{5,7},{6,4},{7,5},{8,10},{9,11},{10,... | collective-permute-start | bytes 184328 | tf_op jit(solution)/shard_map/ppermute | solution.py:44
  52.9 4.6 %collective-permute-start.18 = (f32[2,20,384]{2,1,0:T(8,128)S(1)}, f32[2,20,384]{2,1,0:T(8,128)S(1)}, u32[]{:S(2)}, u32[]{:S(2)}) collective-permute-start(f32[2,20,384]{2,1,0:T(8,128)S(1)} %copy.20), channel_id=1, source_target_pairs={{0,1},{1,2},{2,3},{3,0},{4,5},{5,6},{6,7},{7,4},{8,9},{9,10},{10,1... | collective-permute-start | bytes 184328 | tf_op jit(solution)/shard_map/ppermute | solution.py:44
  52.9 5.7 %collective-permute-start.14 = (f32[2,20,384]{2,1,0:T(8,128)S(1)}, f32[2,20,384]{2,1,0:T(8,128)S(1)}, u32[]{:S(2)}, u32[]{:S(2)}) collective-permute-start(f32[2,20,384]{2,1,0:T(8,128)S(1)} %copy.16), channel_id=1, source_target_pairs={{0,3},{1,0},{2,1},{3,2},{4,7},{5,4},{6,5},{7,6},{8,11},{9,8},{10,9... | collective-permute-start | bytes 184328 | tf_op jit(solution)/shard_map/ppermute | solution.py:44
  54.7 5.5 %collective-permute-start.13 = (f32[2,20,384]{2,1,0:T(8,128)S(1)}, f32[2,20,384]{2,1,0:T(8,128)S(1)}, u32[]{:S(2)}, u32[]{:S(2)}) collective-permute-start(f32[2,20,384]{2,1,0:T(8,128)S(1)} %copy.15), channel_id=1, source_target_pairs={{0,2},{1,3},{2,0},{3,1},{4,6},{5,7},{6,4},{7,5},{8,10},{9,11},{10,... | collective-permute-start | bytes 184328 | tf_op jit(solution)/shard_map/ppermute | solution.py:44
  55.5 5.1 %collective-permute-start.12 = (f32[2,20,384]{2,1,0:T(8,128)S(1)}, f32[2,20,384]{2,1,0:T(8,128)S(1)}, u32[]{:S(2)}, u32[]{:S(2)}) collective-permute-start(f32[2,20,384]{2,1,0:T(8,128)S(1)} %copy.13), channel_id=1, source_target_pairs={{0,1},{1,2},{2,3},{3,0},{4,5},{5,6},{6,7},{7,4},{8,9},{9,10},{10,1... | collective-permute-start | bytes 184328 | tf_op jit(solution)/shard_map/ppermute | solution.py:44
  56.9 4.6 %collective-permute-start.29 = (bf16[20,384]{1,0:T(8,128)(2,1)S(1)}, bf16[20,384]{1,0:T(8,128)(2,1)S(1)}, u32[]{:S(2)}, u32[]{:S(2)}) collective-permute-start(bf16[20,384]{1,0:T(8,128)(2,1)S(1)} %fusion.89), channel_id=1, source_target_pairs={{0,3},{1,0},{2,1},{3,2},{4,7},{5,4},{6,5},{7,6},{8,11},{9,8},{10,9... | collective-permute-start | bytes 46088 | tf_op jit(solution)/shard_map/ppermute | solution.py:16
  58.7 4.6 %collective-permute-start.27 = (bf16[20,384]{1,0:T(8,128)(2,1)S(1)}, bf16[20,384]{1,0:T(8,128)(2,1)S(1)}, u32[]{:S(2)}, u32[]{:S(2)}) collective-permute-start(bf16[20,384]{1,0:T(8,128)(2,1)S(1)} %fusion.89), channel_id=1, source_target_pairs={{0,1},{1,2},{2,3},{3,0},{4,5},{5,6},{6,7},{7,4},{8,9},{9,10},{10,1... | collective-permute-start | bytes 46088 | tf_op jit(solution)/shard_map/ppermute | solution.py:16
  60.1 4.4 %collective-permute-start.23 = (bf16[20,384]{1,0:T(8,128)(2,1)S(1)}, bf16[20,384]{1,0:T(8,128)(2,1)S(1)}, u32[]{:S(2)}, u32[]{:S(2)}) collective-permute-start(bf16[20,384]{1,0:T(8,128)(2,1)S(1)} %fusion.93), channel_id=1, source_target_pairs={{0,3},{1,0},{2,1},{3,2},{4,7},{5,4},{6,5},{7,6},{8,11},{9,8},{10,9... | collective-permute-start | bytes 46088 | tf_op jit(solution)/shard_map/ppermute | solution.py:16
  61.5 4.8 %collective-permute-start.21 = (bf16[20,384]{1,0:T(8,128)(2,1)S(1)}, bf16[20,384]{1,0:T(8,128)(2,1)S(1)}, u32[]{:S(2)}, u32[]{:S(2)}) collective-permute-start(bf16[20,384]{1,0:T(8,128)(2,1)S(1)} %fusion.93), channel_id=1, source_target_pairs={{0,1},{1,2},{2,3},{3,0},{4,5},{5,6},{6,7},{7,4},{8,9},{9,10},{10,1... | collective-permute-start | bytes 46088 | tf_op jit(solution)/shard_map/ppermute | solution.py:16
  61.6 5.6 %collective-permute-start.17 = (bf16[20,384]{1,0:T(8,128)(2,1)S(1)}, bf16[20,384]{1,0:T(8,128)(2,1)S(1)}, u32[]{:S(2)}, u32[]{:S(2)}) collective-permute-start(bf16[20,384]{1,0:T(8,128)(2,1)S(1)} %fusion.97), channel_id=1, source_target_pairs={{0,3},{1,0},{2,1},{3,2},{4,7},{5,4},{6,5},{7,6},{8,11},{9,8},{10,9... | collective-permute-start | bytes 46088 | tf_op jit(solution)/shard_map/ppermute | solution.py:16
  63.3 4.1 %collective-permute-start.16 = (bf16[20,384]{1,0:T(8,128)(2,1)S(1)}, bf16[20,384]{1,0:T(8,128)(2,1)S(1)}, u32[]{:S(2)}, u32[]{:S(2)}) collective-permute-start(bf16[20,384]{1,0:T(8,128)(2,1)S(1)} %fusion.97), channel_id=1, source_target_pairs={{0,2},{1,3},{2,0},{3,1},{4,6},{5,7},{6,4},{7,5},{8,10},{9,11},{10,... | collective-permute-start | bytes 46088 | tf_op jit(solution)/shard_map/ppermute | solution.py:16
  64.6 4.9 %collective-permute-start.11 = (bf16[20,384]{1,0:T(8,128)(2,1)S(1)}, bf16[20,384]{1,0:T(8,128)(2,1)S(1)}, u32[]{:S(2)}, u32[]{:S(2)}) collective-permute-start(bf16[20,384]{1,0:T(8,128)(2,1)S(1)} %fusion.82), channel_id=1, source_target_pairs={{0,3},{1,0},{2,1},{3,2},{4,7},{5,4},{6,5},{7,6},{8,11},{9,8},{10,9... | collective-permute-start | bytes 46088 | tf_op jit(solution)/shard_map/ppermute | solution.py:16
  86.6 6.9 %collective-permute-start.30 = (f32[5,2048]{1,0:T(8,128)S(1)}, f32[5,2048]{1,0:T(8,128)S(1)}, u32[]{:S(2)}, u32[]{:S(2)}) collective-permute-start(f32[5,2048]{1,0:T(8,128)S(1)} %get-tuple-element.21), channel_id=1, source_target_pairs={{0,4},{4,8},{8,12},{12,0},{1,5},{5,9},{9,13},{13,1},{2,6},{6,10},{... | collective-permute-start | bytes 122888 | tf_op jit(solution)/shard_map/ppermute | solution.py:33
  87.1 6.4 %collective-permute-start.32 = (f32[5,2048]{1,0:T(8,128)S(1)}, f32[5,2048]{1,0:T(8,128)S(1)}, u32[]{:S(2)}, u32[]{:S(2)}) collective-permute-start(f32[5,2048]{1,0:T(8,128)S(1)} %get-tuple-element.22), channel_id=1, source_target_pairs={{0,12},{4,0},{8,4},{12,8},{1,13},{5,1},{9,5},{13,9},{2,14},{6,2},{... | collective-permute-start | bytes 122888 | tf_op jit(solution)/shard_map/ppermute | solution.py:33
  90.5 5.8 %collective-permute-start.31 = (f32[5,2048]{1,0:T(8,128)S(1)}, f32[5,2048]{1,0:T(8,128)S(1)}, u32[]{:S(2)}, u32[]{:S(2)}) collective-permute-start(f32[5,2048]{1,0:T(8,128)S(1)} %get-tuple-element.23), channel_id=1, source_target_pairs={{0,8},{4,12},{8,0},{12,4},{1,9},{5,13},{9,1},{13,5},{2,10},{6,14},... | collective-permute-start | bytes 122888 | tf_op jit(solution)/shard_map/ppermute | solution.py:33
  (10 other events, 52.8 us)

commit v2 on v0

v2 whole, which is shorter than its diff:
```python
import jax
import jax.numpy as jnp
from jax import lax
from jax.sharding import PartitionSpec as P


epsilon = 1e-06

EXCHANGE_MAX = 8


def pairwise(n):
    return n <= EXCHANGE_MAX and n & (n - 1) == 0


def exchange(x, axis, n, s):
    return lax.ppermute(x, axis, [(a, a ^ (1 << s)) for a in range(n)])


def xor_reduce_scatter(x, axis, n, pos, bits):
    levels = n.bit_length() - 1
    me = lax.axis_index(axis)
    shape = x.shape
    x = x.reshape(shape[:pos] + (2,) * levels + (shape[pos] // n,) + shape[pos + 1:])
    remaining = list(range(levels - 1, -1, -1))
    for s in bits:
        at = pos + remaining.index(s)
        bit = (me >> s) & 1
        keep = lax.dynamic_index_in_dim(x, bit, axis=at, keepdims=False)
        send = lax.dynamic_index_in_dim(x, 1 - bit, axis=at, keepdims=False)
        x = keep + exchange(send, axis, n, s)
        remaining.remove(s)
    return x


def xor_all_gather(x, axis, n, pos, bits):
    levels = n.bit_length() - 1
    me = lax.axis_index(axis)
    have = []
    for s in bits:
        other = exchange(x, axis, n, s)
        at = pos + sum(1 for b in have if b > s)
        low = jnp.stack([x, other], axis=at)
        high = jnp.stack([other, x], axis=at)
        x = jnp.where(((me >> s) & 1) == 0, low, high)
        have.append(s)
    shape = x.shape
    return x.reshape(shape[:pos] + (-1,) + shape[pos + levels + 1:])


def xor_all_reduce(x, axis, n):
    for s in range(n.bit_length() - 1):
        x = x + exchange(x, axis, n, s)
    return x


def local(tokens, norm_gain, w_gate, w_up, w_down):
    ngx = lax.axis_size("gx")
    ngy = lax.axis_size("gy")
    features = tokens.shape[1] * ngy
    values = tokens.astype(jnp.float32)
    local_sq = jnp.sum(values * values, axis=1)
    if pairwise(ngy):
        total_sq = xor_all_reduce(local_sq, "gy", ngy)
    else:
        total_sq = lax.psum(local_sq, "gy")
    inverse = lax.rsqrt(total_sq / features + epsilon)
    normed = (values * inverse[:, None] * norm_gain[None, :]).astype(jnp.bfloat16)
    gx_levels = list(range(ngx.bit_length() - 1))
    if pairwise(ngx):
        piece = xor_all_gather(normed, "gx", ngx, 0, gx_levels[::-1])
    else:
        piece = lax.all_gather(normed, "gx", axis=0, tiled=True)

    gate_part = jnp.dot(piece, w_gate, preferred_element_type=jnp.float32)
    up_part = jnp.dot(piece, w_up, preferred_element_type=jnp.float32)
    both = jnp.stack([gate_part, up_part])
    gy_levels = list(range(ngy.bit_length() - 1))
    if pairwise(ngy):
        summed = xor_reduce_scatter(both, "gy", ngy, 2, gy_levels)
    else:
        summed = lax.psum_scatter(both, "gy", scatter_dimension=2, tiled=True)
    hidden = (jax.nn.silu(summed[0]) * summed[1]).astype(jnp.bfloat16)
    if pairwise(ngy):
        hidden_all = xor_all_gather(hidden, "gy", ngy, 1, gy_levels[::-1])
    else:
        hidden_all = lax.all_gather(hidden, "gy", axis=1, tiled=True)

    total = jnp.dot(hidden_all, w_down, preferred_element_type=jnp.float32)
    if pairwise(ngx):
        result = xor_reduce_scatter(total, "gx", ngx, 0, gx_levels)
    else:
        result = lax.psum_scatter(total, "gx", scatter_dimension=0, tiled=True)
    return result.astype(jnp.bfloat16)


def solution(mesh):
    in_specs = (P(("groups", "gx"), "gy"), P("gy"), P("gy", "gx"), P("gy", "gx"), P("gx", "gy"))
    out_specs = P(("groups", "gx"), "gy")
    return jax.shard_map(local, mesh=mesh, in_specs=in_specs, out_specs=out_specs, check_vma=False)
```

time: 129 us -> 144 us (1.12); the launches traced: 129 us -> 142 us
  local copies, waits for them, and re-layouts: 1.57 us -> 64.4 us
  blocking collectives: 36.6 us -> 0 us
  between operations: 14.1 us -> 0.2 us
  waiting for transfers between devices: 37.9 us -> 24.3 us
  starting transfers between devices: 5.42 us -> 16.7 us
  matrix products: 30 us -> 33.3 us
    dot_general x0 -> x2, local copies, waits for them, and re-layouts: none -> 62.6 us  [the longest x1 32.3 us: local(): up_part = jnp.dot(piece, w_up, preferred_element_type=jnp.float32)]
    psum x1 -> x0, waiting for transfers between devices: 37.8 us -> none  [local(): summed = lax.psum(partial_value, 'gy')]
    ppermute x0 -> x10, waiting for transfers between devices: none -> 24.3 us  [exchange(): return lax.ppermute(x, axis, [(a, a ^ 1 << s) for a in range(n)])]
    ppermute x0 -> x10, starting transfers between devices: none -> 16.7 us  [exchange(): return lax.ppermute(x, axis, [(a, a ^ 1 << s) for a in range(n)])]
    unnamed x1 -> x0, blocking collectives: 14.6 us -> none
    all_gather x1 -> x0, blocking collectives: 13.6 us -> none  [local(): piece = lax.all_gather(normed, 'gx', axis=0, tiled=True)]
    psum x1 -> x0, blocking collectives: 8.34 us -> none  [local(): total_sq = lax.psum(local_sq, 'gy')]
    unnamed x2 -> x0, starting transfers between devices: 5.41 us -> none
  transfers between devices with their start and end apart: 3 -> 10, of which waited for: 2 -> 9; matrix products, arithmetic and copies ran while one was open for 0% -> 44% of each run, Pallas kernels for 0% -> 0%
where the time goes in v2:
time: 144 us; the launch traced here: 142 us
  local copies, waits for them, and re-layouts  64.4 us (45%)
  matrix products  33.3 us (23%)
  waiting for transfers between devices  24.3 us (17%)
  starting transfers between devices  16.7 us (12%)
  other arithmetic  2.86 us (2%)
    dot_general x1, local copies, waits for them, and re-layouts, local(): up_part = jnp.dot(piece, w_up, preferred_element_type=jnp.float32)  32.3 us
    dot_general x1, local copies, waits for them, and re-layouts, local(): gate_part = jnp.dot(piece, w_gate, preferred_element_type=jnp.float32)  30.3 us
    ppermute x10, waiting for transfers between devices, exchange(): return lax.ppermute(x, axis, [(a, a ^ 1 << s) for a in range(n)])  24.3 us
    ppermute x10, starting transfers between devices, exchange(): return lax.ppermute(x, axis, [(a, a ^ 1 << s) for a in range(n)])  16.7 us
    dot_general x1, matrix products, local(): up_part = jnp.dot(piece, w_up, preferred_element_type=jnp.float32)  11.5 us
    dot_general x1, matrix products, local(): gate_part = jnp.dot(piece, w_gate, preferred_element_type=jnp.float32)  11.5 us
    dot_general x1, matrix products, local(): total = jnp.dot(hidden_all, w_down, preferred_element_type=jnp.float32)  10.3 us
  transfers between devices with their start and end apart: 10, of which 9 were waited for; matrix products, arithmetic and copies ran while one was open for 44% of the time, Pallas kernels for 0%

profile of v2, /device:TPU:0, one launch (start us, length us, event | category | flops | bytes accessed | tf_op | source)
XLA Modules:
  0.0 141.8 jit_solution(8396767124220830263)
XLA Ops:
  0.0 0.9 fusion.20
  0.9 0.5 collective-permute-start
  1.4 32.3 %copy.53 = bf16[6144,2048]{1,0:T(8,128)(2,1)} copy(bf16[6144,2048]{0,1:T(8,128)(2,1)} %bitcast.98) | data formatting | bytes 50331648 | tf_op jit(solution)/shard_map/dot_general | solution.py:76
  33.7 30.3 %copy.52 = bf16[6144,2048]{1,0:T(8,128)(2,1)} copy(bf16[6144,2048]{0,1:T(8,128)(2,1)} %bitcast.99) | data formatting | bytes 50331648 | tf_op jit(solution)/shard_map/dot_general | solution.py:75
  64.1 2.6 %collective-permute-start.1 = (f32[5]{0:T(128)S(1)}, f32[5]{0:T(128)S(1)}, u32[]{:S(2)}, u32[]{:S(2)}) collective-permute-start(f32[5]{0:T(128)S(1)} %add.75), channel_id=1, source_target_pairs={{0,2},{1,3},{2,0},{3,1},{4,6},{5,7},{6,4},{7,5},{8,10},{9,11},{10,... | collective-permute-start | bytes 68 | tf_op jit(solution)/shard_map/ppermute | solution.py:17
  66.6 1.5 %collective-permute-done.1 = f32[5]{0:T(128)S(1)} collective-permute-done((f32[5]{0:T(128)S(1)}, f32[5]{0:T(128)S(1)}, u32[]{:S(2)}, u32[]{:S(2)}) %collective-permute-start.1) | collective-permute-done | bytes 52 | tf_op jit(solution)/shard_map/ppermute | solution.py:17
  68.3 3.2 %collective-permute-start.2 = (bf16[5,2048]{1,0:T(8,128)(2,1)S(1)}, bf16[5,2048]{1,0:T(8,128)(2,1)S(1)}, u32[]{:S(2)}, u32[]{:S(2)}) collective-permute-start(bf16[5,2048]{1,0:T(8,128)(2,1)S(1)} %fusion.22), channel_id=1, source_target_pairs={{0,8},{4,12},{8,0},{12,4},{1,9},{5,13},{9,1},{13,5},{2,10},{6,14},... | collective-permute-start | bytes 61448 | tf_op jit(solution)/shard_map/ppermute | solution.py:17
  71.6 1.9 %collective-permute-done.2 = bf16[5,2048]{1,0:T(8,128)(2,1)S(1)} collective-permute-done((bf16[5,2048]{1,0:T(8,128)(2,1)S(1)}, bf16[5,2048]{1,0:T(8,128)(2,1)S(1)}, u32[]{:S(2)}, u32[]{:S(2)}) %collective-permute-start.2) | collective-permute-done | bytes 20512 | tf_op jit(solution)/shard_map/ppermute | solution.py:17
  73.5 1.9 %collective-permute-start.3 = (bf16[2,5,2048]{2,1,0:T(8,128)(2,1)S(1)}, bf16[2,5,2048]{2,1,0:T(8,128)(2,1)S(1)}, u32[]{:S(2)}, u32[]{:S(2)}) collective-permute-start(bf16[2,5,2048]{2,1,0:T(8,128)(2,1)S(1)} %maximum_select_fusion.5), channel_id=1, source_target_pairs={{0,4},{4,0},{8,12},{12,8},{1,5},{5,1},{9,13},{13,9},{2,6},{6,2},{1... | collective-permute-start | bytes 122888 | tf_op jit(solution)/shard_map/ppermute | solution.py:17
  75.4 2.4 %collective-permute-done.3 = bf16[2,5,2048]{2,1,0:T(8,128)(2,1)S(1)} collective-permute-done((bf16[2,5,2048]{2,1,0:T(8,128)(2,1)S(1)}, bf16[2,5,2048]{2,1,0:T(8,128)(2,1)S(1)}, u32[]{:S(2)}, u32[]{:S(2)}) %collective-permute-start.3) | collective-permute-done | bytes 40992 | tf_op jit(solution)/shard_map/ppermute | solution.py:17
  77.9 11.5 %convolution_bitcast_fusion = f32[1,20,2,2,1536]{4,1,3,2,0:T(8,128)S(1)} fusion(bf16[2,2,1536,2048]{3,2,1,0:T(8,128)(2,1)} %bitcast.97, bf16[20,2048,1,1]{1,0,2,3:T(8,128)(2,1)S(1)} %reshape.215), kind=kOutput, calls=%fused_computation.2 | convolution fusion | flops 503316480 | bytes 25739264 | tf_op jit(solution)/shard_map/dot_general | solution.py:76
  89.4 11.5 %convolution_bitcast_fusion.1 = f32[1,20,2,2,1536]{4,1,3,2,0:T(8,128)S(1)} fusion(bf16[2,2,1536,2048]{3,2,1,0:T(8,128)(2,1)} %bitcast.96, bf16[20,2048,1,1]{1,0,2,3:T(8,128)(2,1)S(1)} %reshape.215), kind=kOutput, calls=%fused_computation.3 | convolution fusion | flops 503316480 | bytes 25739264 | tf_op jit(solution)/shard_map/dot_general | solution.py:75
  101.6 1.8 %collective-permute-done.4 = f32[2,20,2,1536]{3,2,1,0:T(2,128)S(1)} collective-permute-done((f32[2,20,2,1536]{3,2,1,0:T(2,128)S(1)}, f32[2,20,2,1536]{3,2,1,0:T(2,128)S(1)}, u32[]{:S(2)}, u32[]{:S(2)}) %collective-permute-start.4) | collective-permute-done | bytes 491552 | tf_op jit(solution)/shard_map/ppermute | solution.py:17
  104.5 1.8 %collective-permute-start.5 = (f32[2,20,1536]{2,0,1:T(2,128)S(1)}, f32[2,20,1536]{2,0,1:T(2,128)S(1)}, u32[]{:S(2)}, u32[]{:S(2)}) collective-permute-start(f32[2,20,1536]{2,0,1:T(2,128)S(1)} %bitcast.105), channel_id=1, source_target_pairs={{0,2},{1,3},{2,0},{3,1},{4,6},{5,7},{6,4},{7,5},{8,10},{9,11},{10,... | collective-permute-start | bytes 737288 | tf_op jit(solution)/shard_map/ppermute | solution.py:17
  106.3 6.3 %collective-permute-done.5 = f32[2,20,1536]{2,0,1:T(2,128)S(1)} collective-permute-done((f32[2,20,1536]{2,0,1:T(2,128)S(1)}, f32[2,20,1536]{2,0,1:T(2,128)S(1)}, u32[]{:S(2)}, u32[]{:S(2)}) %collective-permute-start.5) | collective-permute-done | bytes 245792 | tf_op jit(solution)/shard_map/ppermute | solution.py:17
  113.0 1.8 %collective-permute-start.6 = (bf16[20,1536]{1,0:T(8,128)(2,1)S(1)}, bf16[20,1536]{1,0:T(8,128)(2,1)S(1)}, u32[]{:S(2)}, u32[]{:S(2)}) collective-permute-start(bf16[20,1536]{1,0:T(8,128)(2,1)S(1)} %fusion.17), channel_id=1, source_target_pairs={{0,2},{1,3},{2,0},{3,1},{4,6},{5,7},{6,4},{7,5},{8,10},{9,11},{10,... | collective-permute-start | bytes 184328 | tf_op jit(solution)/shard_map/ppermute | solution.py:17
  114.9 2.6 %collective-permute-done.6 = bf16[20,1536]{1,0:T(8,128)(2,1)S(1)} collective-permute-done((bf16[20,1536]{1,0:T(8,128)(2,1)S(1)}, bf16[20,1536]{1,0:T(8,128)(2,1)S(1)}, u32[]{:S(2)}, u32[]{:S(2)}) %collective-permute-start.6) | collective-permute-done | bytes 61472 | tf_op jit(solution)/shard_map/ppermute | solution.py:17
  117.6 1.3 collective-permute-done.7
  119.5 10.3 %fusion = f32[2,2,5,2048]{3,2,1,0:T(8,128)S(1)} fusion(bf16[2,2,5,6144]{3,2,1,0:T(8,128)(2,1)S(1)} %select_n.117, bf16[6144,2048]{1,0:T(8,128)(2,1)} %param.9), kind=kOutput, calls=%fused_computation | convolution fusion | flops 503316480 | bytes 25575424 | tf_op jit(solution)/shard_map/dot_general | solution.py:89
  129.8 1.9 %collective-permute-start.8 = (f32[2,5,2048]{2,1,0:T(8,128)S(1)}, f32[2,5,2048]{2,1,0:T(8,128)S(1)}, u32[]{:S(2)}, u32[]{:S(2)}) collective-permute-start(f32[2,5,2048]{2,1,0:T(8,128)S(1)} %dynamic-slice_bitcast_fusion), channel_id=1, source_target_pairs={{0,4},{4,0},{8,12},{12,8},{1,5},{5,1},{9,13},{13,9},{2,6},{6,2},{1... | collective-permute-start | bytes 245768 | tf_op jit(solution)/shard_map/ppermute | solution.py:17
  131.7 3.8 %collective-permute-done.8 = f32[2,5,2048]{2,1,0:T(8,128)S(1)} collective-permute-done((f32[2,5,2048]{2,1,0:T(8,128)S(1)}, f32[2,5,2048]{2,1,0:T(8,128)S(1)}, u32[]{:S(2)}, u32[]{:S(2)}) %collective-permute-start.8) | collective-permute-done | bytes 81952 | tf_op jit(solution)/shard_map/ppermute | solution.py:17
  135.5 2.9 %collective-permute-start.9 = (f32[5,2048]{1,0:T(8,128)S(1)}, f32[5,2048]{1,0:T(8,128)S(1)}, u32[]{:S(2)}, u32[]{:S(2)}) collective-permute-start(f32[5,2048]{1,0:T(8,128)S(1)} %dynamic-slice_bitcast_fusion.1), channel_id=1, source_target_pairs={{0,8},{4,12},{8,0},{12,4},{1,9},{5,13},{9,1},{13,5},{2,10},{6,14},... | collective-permute-start | bytes 122888 | tf_op jit(solution)/shard_map/ppermute | solution.py:17
  138.4 2.7 %collective-permute-done.9 = f32[5,2048]{1,0:T(8,128)S(1)} collective-permute-done((f32[5,2048]{1,0:T(8,128)S(1)}, f32[5,2048]{1,0:T(8,128)S(1)}, u32[]{:S(2)}, u32[]{:S(2)}) %collective-permute-start.9) | collective-permute-done | bytes 40992 | tf_op jit(solution)/shard_map/ppermute | solution.py:17
  141.2 0.6 fusion.23
  (36 shorter events, 3.2 us)
Async XLA Ops:
  0.9 63.2 %collective-permute-start = (f32[5]{0:T(128)S(1)}, f32[5]{0:T(128)S(1)}, u32[]{:S(2)}, u32[]{:S(2)}) collective-permute-start(f32[5]{0:T(128)S(1)} %fusion.20), channel_id=1, source_target_pairs={{0,1},{1,0},{2,3},{3,2},{4,5},{5,4},{6,7},{7,6},{8,9},{9,8},{10,11... | collective-permute-start | bytes 68 | tf_op jit(solution)/shard_map/ppermute | solution.py:17
  33.7 34.4 %copy-start = (bf16[5,2048]{1,0:T(8,128)(2,1)S(1)}, bf16[5,2048]{1,0:T(8,128)(2,1)}, u32[]{:S(2)}) copy-start(bf16[5,2048]{1,0:T(8,128)(2,1)} %param.5) | copy-start | bytes 61444
  33.7 34.4 %copy-start.1 = (f32[2048]{0:T(1024)S(1)}, f32[2048]{0:T(1024)}, u32[]{:S(2)}) copy-start(f32[2048]{0:T(1024)} %param.6) | copy-start | bytes 24580
  64.1 4.1 %collective-permute-start.1 = (f32[5]{0:T(128)S(1)}, f32[5]{0:T(128)S(1)}, u32[]{:S(2)}, u32[]{:S(2)}) collective-permute-start(f32[5]{0:T(128)S(1)} %add.75), channel_id=1, source_target_pairs={{0,2},{1,3},{2,0},{3,1},{4,6},{5,7},{6,4},{7,5},{8,10},{9,11},{10,... | collective-permute-start | bytes 68 | tf_op jit(solution)/shard_map/ppermute | solution.py:17
  68.3 5.1 %collective-permute-start.2 = (bf16[5,2048]{1,0:T(8,128)(2,1)S(1)}, bf16[5,2048]{1,0:T(8,128)(2,1)S(1)}, u32[]{:S(2)}, u32[]{:S(2)}) collective-permute-start(bf16[5,2048]{1,0:T(8,128)(2,1)S(1)} %fusion.22), channel_id=1, source_target_pairs={{0,8},{4,12},{8,0},{12,4},{1,9},{5,13},{9,1},{13,5},{2,10},{6,14},... | collective-permute-start | bytes 61448 | tf_op jit(solution)/shard_map/ppermute | solution.py:17
  73.5 4.3 %collective-permute-start.3 = (bf16[2,5,2048]{2,1,0:T(8,128)(2,1)S(1)}, bf16[2,5,2048]{2,1,0:T(8,128)(2,1)S(1)}, u32[]{:S(2)}, u32[]{:S(2)}) collective-permute-start(bf16[2,5,2048]{2,1,0:T(8,128)(2,1)S(1)} %maximum_select_fusion.5), channel_id=1, source_target_pairs={{0,4},{4,0},{8,12},{12,8},{1,5},{5,1},{9,13},{13,9},{2,6},{6,2},{1... | collective-permute-start | bytes 122888 | tf_op jit(solution)/shard_map/ppermute | solution.py:17
  101.5 1.9 %collective-permute-start.4 = (f32[2,20,2,1536]{3,2,1,0:T(2,128)S(1)}, f32[2,20,2,1536]{3,2,1,0:T(2,128)S(1)}, u32[]{:S(2)}, u32[]{:S(2)}) collective-permute-start(f32[2,20,2,1536]{3,2,1,0:T(2,128)S(1)} %bitcast.101), channel_id=1, source_target_pairs={{0,1},{1,0},{2,3},{3,2},{4,5},{5,4},{6,7},{7,6},{8,9},{9,8},{10,11... | collective-permute-start | bytes 1474568 | tf_op jit(solution)/shard_map/ppermute | solution.py:17
  104.5 8.1 %collective-permute-start.5 = (f32[2,20,1536]{2,0,1:T(2,128)S(1)}, f32[2,20,1536]{2,0,1:T(2,128)S(1)}, u32[]{:S(2)}, u32[]{:S(2)}) collective-permute-start(f32[2,20,1536]{2,0,1:T(2,128)S(1)} %bitcast.105), channel_id=1, source_target_pairs={{0,2},{1,3},{2,0},{3,1},{4,6},{5,7},{6,4},{7,5},{8,10},{9,11},{10,... | collective-permute-start | bytes 737288 | tf_op jit(solution)/shard_map/ppermute | solution.py:17
  113.0 4.4 %collective-permute-start.6 = (bf16[20,1536]{1,0:T(8,128)(2,1)S(1)}, bf16[20,1536]{1,0:T(8,128)(2,1)S(1)}, u32[]{:S(2)}, u32[]{:S(2)}) collective-permute-start(bf16[20,1536]{1,0:T(8,128)(2,1)S(1)} %fusion.17), channel_id=1, source_target_pairs={{0,2},{1,3},{2,0},{3,1},{4,6},{5,7},{6,4},{7,5},{8,10},{9,11},{10,... | collective-permute-start | bytes 184328 | tf_op jit(solution)/shard_map/ppermute | solution.py:17
  117.5 1.4 %collective-permute-start.7 = (bf16[20,2,1536]{2,0,1:T(8,128)(2,1)S(1)}, bf16[20,2,1536]{2,0,1:T(8,128)(2,1)S(1)}, u32[]{:S(2)}, u32[]{:S(2)}) collective-permute-start(bf16[20,2,1536]{2,0,1:T(8,128)(2,1)S(1)} %maximum_select_fusion.2), channel_id=1, source_target_pairs={{0,1},{1,0},{2,3},{3,2},{4,5},{5,4},{6,7},{7,6},{8,9},{9,8},{10,11... | collective-permute-start | bytes 368648 | tf_op jit(solution)/shard_map/ppermute | solution.py:17
  129.8 5.7 %collective-permute-start.8 = (f32[2,5,2048]{2,1,0:T(8,128)S(1)}, f32[2,5,2048]{2,1,0:T(8,128)S(1)}, u32[]{:S(2)}, u32[]{:S(2)}) collective-permute-start(f32[2,5,2048]{2,1,0:T(8,128)S(1)} %dynamic-slice_bitcast_fusion), channel_id=1, source_target_pairs={{0,4},{4,0},{8,12},{12,8},{1,5},{5,1},{9,13},{13,9},{2,6},{6,2},{1... | collective-permute-start | bytes 245768 | tf_op jit(solution)/shard_map/ppermute | solution.py:17
  135.5 5.6 %collective-permute-start.9 = (f32[5,2048]{1,0:T(8,128)S(1)}, f32[5,2048]{1,0:T(8,128)S(1)}, u32[]{:S(2)}, u32[]{:S(2)}) collective-permute-start(f32[5,2048]{1,0:T(8,128)S(1)} %dynamic-slice_bitcast_fusion.1), channel_id=1, source_target_pairs={{0,8},{4,12},{8,0},{12,4},{1,9},{5,13},{9,1},{13,5},{2,10},{6,14},... | collective-permute-start | bytes 122888 | tf_op jit(solution)/shard_map/ppermute | solution.py:17

commit v3 on v2

--- a/solution.py
+++ b/solution.py
@@ -17,35 +17,26 @@
     return lax.ppermute(x, axis, [(a, a ^ (1 << s)) for a in range(n)])
 
 
-def xor_reduce_scatter(x, axis, n, pos, bits):
-    levels = n.bit_length() - 1
+def xor_reduce_scatter(parts, axis, n, dim, bits):
     me = lax.axis_index(axis)
-    shape = x.shape
-    x = x.reshape(shape[:pos] + (2,) * levels + (shape[pos] // n,) + shape[pos + 1:])
-    remaining = list(range(levels - 1, -1, -1))
     for s in bits:
-        at = pos + remaining.index(s)
         bit = (me >> s) & 1
-        keep = lax.dynamic_index_in_dim(x, bit, axis=at, keepdims=False)
-        send = lax.dynamic_index_in_dim(x, 1 - bit, axis=at, keepdims=False)
-        x = keep + exchange(send, axis, n, s)
-        remaining.remove(s)
-    return x
+        half = parts[0].shape[dim] // 2
+        keep = [lax.dynamic_slice_in_dim(p, bit * half, half, axis=dim) for p in parts]
+        send = [lax.dynamic_slice_in_dim(p, (1 - bit) * half, half, axis=dim) for p in parts]
+        got = exchange(jnp.stack(send), axis, n, s)
+        parts = [k + got[i] for i, k in enumerate(keep)]
+    return parts
 
 
-def xor_all_gather(x, axis, n, pos, bits):
-    levels = n.bit_length() - 1
+def xor_all_gather(x, axis, n, dim, bits):
     me = lax.axis_index(axis)
-    have = []
     for s in bits:
         other = exchange(x, axis, n, s)
-        at = pos + sum(1 for b in have if b > s)
-        low = jnp.stack([x, other], axis=at)
-        high = jnp.stack([other, x], axis=at)
+        low = jnp.concatenate([x, other], axis=dim)
+        high = jnp.concatenate([other, x], axis=dim)
         x = jnp.where(((me >> s) & 1) == 0, low, high)
-        have.append(s)
-    shape = x.shape
-    return x.reshape(shape[:pos] + (-1,) + shape[pos + levels + 1:])
+    return x
 
 
 def xor_all_reduce(x, axis, n):
@@ -74,13 +65,13 @@
 
     gate_part = jnp.dot(piece, w_gate, preferred_element_type=jnp.float32)
     up_part = jnp.dot(piece, w_up, preferred_element_type=jnp.float32)
-    both = jnp.stack([gate_part, up_part])
     gy_levels = list(range(ngy.bit_length() - 1))
     if pairwise(ngy):
-        summed = xor_reduce_scatter(both, "gy", ngy, 2, gy_levels)
+        gate, up = xor_reduce_scatter([gate_part, up_part], "gy", ngy, 1, gy_levels)
     else:
-        summed = lax.psum_scatter(both, "gy", scatter_dimension=2, tiled=True)
-    hidden = (jax.nn.silu(summed[0]) * summed[1]).astype(jnp.bfloat16)
+        gate = lax.psum_scatter(gate_part, "gy", scatter_dimension=1, tiled=True)
+        up = lax.psum_scatter(up_part, "gy", scatter_dimension=1, tiled=True)
+    hidden = (jax.nn.silu(gate) * up).astype(jnp.bfloat16)
     if pairwise(ngy):
         hidden_all = xor_all_gather(hidden, "gy", ngy, 1, gy_levels[::-1])
     else:
@@ -88,7 +79,7 @@
 
     total = jnp.dot(hidden_all, w_down, preferred_element_type=jnp.float32)
     if pairwise(ngx):
-        result = xor_reduce_scatter(total, "gx", ngx, 0, gx_levels)
+        (result,) = xor_reduce_scatter([total], "gx", ngx, 0, gx_levels)
     else:
         result = lax.psum_scatter(total, "gx", scatter_dimension=0, tiled=True)
     return result.astype(jnp.bfloat16)

time: 144 us -> 77.4 us (0.54); the launches traced: 142 us -> 77.1 us
  local copies, waits for them, and re-layouts: 64.4 us -> 0.85 us
  matrix products: 33.3 us -> 29.7 us
  waiting for transfers between devices: 24.3 us -> 26.3 us
    dot_general x2 -> x0, local copies, waits for them, and re-layouts: 62.6 us -> none  [the longest x1 32.3 us: local(): up_part = jnp.dot(piece, w_up, preferred_element_type=jnp.float32)]
    ppermute x10, waiting for transfers between devices: 24.3 us -> 26.3 us  [exchange(): return lax.ppermute(x, axis, [(a, a ^ 1 << s) for a in range(n)])]
    dot_general x1, matrix products: 11.5 us -> 9.89 us  [local(): gate_part = jnp.dot(piece, w_gate, preferred_element_type=jnp.float32)]
    dot_general x1, matrix products: 11.5 us -> 9.9 us  [local(): up_part = jnp.dot(piece, w_up, preferred_element_type=jnp.float32)]
  transfers between devices with their start and end apart: 10 -> 10, of which waited for: 9 -> 10; matrix products, arithmetic and copies ran while one was open for 44% -> 0% of each run, Pallas kernels for 0% -> 0%
where the time goes in v3:
time: 77.4 us; the launch traced here: 77.1 us
  matrix products  29.7 us (38%)
  waiting for transfers between devices  26.3 us (34%)
  starting transfers between devices  17.1 us (22%)
  other arithmetic  3.13 us (4%)
  local copies, waits for them, and re-layouts  0.85 us (1%)
    ppermute x10, waiting for transfers between devices, exchange(): return lax.ppermute(x, axis, [(a, a ^ 1 << s) for a in range(n)])  26.3 us
    ppermute x10, starting transfers between devices, exchange(): return lax.ppermute(x, axis, [(a, a ^ 1 << s) for a in range(n)])  17.1 us
    dot_general x1, matrix products, local(): up_part = jnp.dot(piece, w_up, preferred_element_type=jnp.float32)  9.9 us
    dot_general x1, matrix products, local(): gate_part = jnp.dot(piece, w_gate, preferred_element_type=jnp.float32)  9.89 us
    dot_general x1, matrix products, local(): total = jnp.dot(hidden_all, w_down, preferred_element_type=jnp.float32)  9.89 us
  transfers between devices with their start and end apart: 10, of which 10 were waited for; matrix products, arithmetic and copies ran while one was open for 0% of the time, Pallas kernels for 0%

profile of v3, /device:TPU:0, one launch (start us, length us, event | category | flops | bytes accessed | tf_op | source)
XLA Modules:
  0.0 77.1 jit_solution(14445693663936447160)
XLA Ops:
  0.0 0.9 %fusion.13 = f32[5]{0:T(128)S(1)} fusion(bf16[5,2048]{1,0:T(8,128)(2,1)} %param.5), kind=kLoop, calls=%fused_computation.28 | loop fusion | flops 30715 | bytes 20500 | tf_op jit(solution)/shard_map/reduce_sum | solution.py:53
  0.9 0.5 collective-permute-start
  1.4 0.8 %collective-permute-done = f32[5]{0:T(128)S(1)} collective-permute-done((f32[5]{0:T(128)S(1)}, f32[5]{0:T(128)S(1)}, u32[]{:S(2)}, u32[]{:S(2)}) %collective-permute-start) | collective-permute-done | bytes 52 | tf_op jit(solution)/shard_map/ppermute | solution.py:17
  2.2 2.8 %collective-permute-start.1 = (f32[5]{0:T(128)S(1)}, f32[5]{0:T(128)S(1)}, u32[]{:S(2)}, u32[]{:S(2)}) collective-permute-start(f32[5]{0:T(128)S(1)} %add.59), channel_id=1, source_target_pairs={{0,2},{1,3},{2,0},{3,1},{4,6},{5,7},{6,4},{7,5},{8,10},{9,11},{10,... | collective-permute-start | bytes 68 | tf_op jit(solution)/shard_map/ppermute | solution.py:17
  5.0 1.5 %collective-permute-done.1 = f32[5]{0:T(128)S(1)} collective-permute-done((f32[5]{0:T(128)S(1)}, f32[5]{0:T(128)S(1)}, u32[]{:S(2)}, u32[]{:S(2)}) %collective-permute-start.1) | collective-permute-done | bytes 52 | tf_op jit(solution)/shard_map/ppermute | solution.py:17
  6.5 0.8 %fusion.15 = bf16[5,2048]{1,0:T(8,128)(2,1)S(1)} fusion(bf16[5,2048]{1,0:T(8,128)(2,1)} %param.5, f32[2048]{0:T(1024)} %param.6, f32[5]{0:T(128)S(1)} %add_rsqrt_fusion), kind=kLoop, calls=%fused_computation.30 | loop fusion | flops 40960 | bytes 49172 | tf_op jit(solution)/shard_map/convert_element_type | solution.py:59
  7.4 3.2 %collective-permute-start.2 = (bf16[5,2048]{1,0:T(8,128)(2,1)S(1)}, bf16[5,2048]{1,0:T(8,128)(2,1)S(1)}, u32[]{:S(2)}, u32[]{:S(2)}) collective-permute-start(bf16[5,2048]{1,0:T(8,128)(2,1)S(1)} %fusion.15), channel_id=1, source_target_pairs={{0,8},{4,12},{8,0},{12,4},{1,9},{5,13},{9,1},{13,5},{2,10},{6,14},... | collective-permute-start | bytes 61448 | tf_op jit(solution)/shard_map/ppermute | solution.py:17
  10.6 1.9 %collective-permute-done.2 = bf16[5,2048]{1,0:T(8,128)(2,1)S(1)} collective-permute-done((bf16[5,2048]{1,0:T(8,128)(2,1)S(1)}, bf16[5,2048]{1,0:T(8,128)(2,1)S(1)}, u32[]{:S(2)}, u32[]{:S(2)}) %collective-permute-start.2) | collective-permute-done | bytes 20512 | tf_op jit(solution)/shard_map/ppermute | solution.py:17
  12.5 2.0 %collective-permute-start.3 = (bf16[10,2048]{1,0:T(8,128)(2,1)S(1)}, bf16[10,2048]{1,0:T(8,128)(2,1)S(1)}, u32[]{:S(2)}, u32[]{:S(2)}) collective-permute-start(bf16[10,2048]{1,0:T(8,128)(2,1)S(1)} %maximum_select_fusion.4), channel_id=1, source_target_pairs={{0,4},{4,0},{8,12},{12,8},{1,5},{5,1},{9,13},{13,9},{2,6},{6,2},{1... | collective-permute-start | bytes 122888 | tf_op jit(solution)/shard_map/ppermute | solution.py:17
  14.5 2.4 %collective-permute-done.3 = bf16[10,2048]{1,0:T(8,128)(2,1)S(1)} collective-permute-done((bf16[10,2048]{1,0:T(8,128)(2,1)S(1)}, bf16[10,2048]{1,0:T(8,128)(2,1)S(1)}, u32[]{:S(2)}, u32[]{:S(2)}) %collective-permute-start.3) | collective-permute-done | bytes 40992 | tf_op jit(solution)/shard_map/ppermute | solution.py:17
  16.8 9.9 %fusion.18 = f32[20,6144]{1,0:T(8,128)S(1)} fusion(bf16[2048,6144]{1,0:T(8,128)(2,1)} %param.7, bf16[10,2048]{1,0:T(8,128)(2,1)S(1)} %collective-permute-done.3, bf16[10,2048]{1,0:T(8,128)(2,1)S(1)} %maximum_select_fusion.4, pred[]{:T(512)S(6)} %eq.14), kind=kOutput, calls=%fused_computation.39 | convolution fusion | flops 503685120 | bytes 25739264 | tf_op jit(solution)/shard_map/dot_general | solution.py:66
  26.7 9.9 %fusion.17 = f32[20,6144]{1,0:T(8,128)S(1)} fusion(bf16[2048,6144]{1,0:T(8,128)(2,1)} %param.8, bf16[10,2048]{1,0:T(8,128)(2,1)S(1)} %collective-permute-done.3, bf16[10,2048]{1,0:T(8,128)(2,1)S(1)} %maximum_select_fusion.4, pred[]{:T(512)S(6)} %eq.14), kind=kOutput, calls=%fused_computation.38 | convolution fusion | flops 503685120 | bytes 25739264 | tf_op jit(solution)/shard_map/dot_general | solution.py:67
  37.6 1.8 %collective-permute-done.4 = f32[2,20,3072]{2,0,1:T(2,128)S(1)} collective-permute-done((f32[2,20,3072]{2,0,1:T(2,128)S(1)}, f32[2,20,3072]{2,0,1:T(2,128)S(1)}, u32[]{:S(2)}, u32[]{:S(2)}) %collective-permute-start.4) | collective-permute-done | bytes 491552 | tf_op jit(solution)/shard_map/ppermute | solution.py:17
  40.0 1.9 %collective-permute-start.5 = (f32[2,20,1536]{2,1,0:T(8,128)S(1)}, f32[2,20,1536]{2,1,0:T(8,128)S(1)}, u32[]{:S(2)}, u32[]{:S(2)}) collective-permute-start(f32[2,20,1536]{2,1,0:T(8,128)S(1)} %pad_maximum_fusion.1), channel_id=1, source_target_pairs={{0,2},{1,3},{2,0},{3,1},{4,6},{5,7},{6,4},{7,5},{8,10},{9,11},{10,... | collective-permute-start | bytes 737288 | tf_op jit(solution)/shard_map/ppermute | solution.py:17
  41.9 7.3 %collective-permute-done.5 = f32[2,20,1536]{2,1,0:T(8,128)S(1)} collective-permute-done((f32[2,20,1536]{2,1,0:T(8,128)S(1)}, f32[2,20,1536]{2,1,0:T(8,128)S(1)}, u32[]{:S(2)}, u32[]{:S(2)}) %collective-permute-start.5) | collective-permute-done | bytes 245792 | tf_op jit(solution)/shard_map/ppermute | solution.py:17
  49.3 1.8 %collective-permute-start.6 = (bf16[20,1536]{1,0:T(8,128)(2,1)S(1)}, bf16[20,1536]{1,0:T(8,128)(2,1)S(1)}, u32[]{:S(2)}, u32[]{:S(2)}) collective-permute-start(bf16[20,1536]{1,0:T(8,128)(2,1)S(1)} %fusion.11), channel_id=1, source_target_pairs={{0,2},{1,3},{2,0},{3,1},{4,6},{5,7},{6,4},{7,5},{8,10},{9,11},{10,... | collective-permute-start | bytes 184328 | tf_op jit(solution)/shard_map/ppermute | solution.py:17
  51.1 2.6 %collective-permute-done.6 = bf16[20,1536]{1,0:T(8,128)(2,1)S(1)} collective-permute-done((bf16[20,1536]{1,0:T(8,128)(2,1)S(1)}, bf16[20,1536]{1,0:T(8,128)(2,1)S(1)}, u32[]{:S(2)}, u32[]{:S(2)}) %collective-permute-start.6) | collective-permute-done | bytes 61472 | tf_op jit(solution)/shard_map/ppermute | solution.py:17
  53.8 1.3 %collective-permute-done.7 = bf16[20,3072]{1,0:T(8,128)(2,1)S(1)} collective-permute-done((bf16[20,3072]{1,0:T(8,128)(2,1)S(1)}, bf16[20,3072]{1,0:T(8,128)(2,1)S(1)}, u32[]{:S(2)}, u32[]{:S(2)}) %collective-permute-start.7) | collective-permute-done | bytes 122912 | tf_op jit(solution)/shard_map/ppermute | solution.py:17
  55.2 9.9 %fusion = f32[20,2048]{1,0:T(8,128)S(1)} fusion(bf16[6144,2048]{1,0:T(8,128)(2,1)} %param.9, bf16[20,3072]{1,0:T(8,128)(2,1)S(1)} %collective-permute-done.7, bf16[20,3072]{1,0:T(8,128)(2,1)S(1)} %maximum_select_fusion.2, pred[]{:T(512)S(6)} %eq.12), kind=kOutput, calls=%fused_computation.3 | convolution fusion | flops 504422400 | bytes 25575424 | tf_op jit(solution)/shard_map/dot_general | solution.py:80
  65.1 1.9 %collective-permute-start.8 = (f32[1,10,2048]{2,1,0:T(8,128)S(1)}, f32[1,10,2048]{2,1,0:T(8,128)S(1)}, u32[]{:S(2)}, u32[]{:S(2)}) collective-permute-start(f32[1,10,2048]{2,1,0:T(8,128)S(1)} %dynamic-slice_bitcast_fusion.2), channel_id=1, source_target_pairs={{0,4},{4,0},{8,12},{12,8},{1,5},{5,1},{9,13},{13,9},{2,6},{6,2},{1... | collective-permute-start | bytes 245768 | tf_op jit(solution)/shard_map/ppermute | solution.py:17
  67.0 3.8 %collective-permute-done.8 = f32[1,10,2048]{2,1,0:T(8,128)S(1)} collective-permute-done((f32[1,10,2048]{2,1,0:T(8,128)S(1)}, f32[1,10,2048]{2,1,0:T(8,128)S(1)}, u32[]{:S(2)}, u32[]{:S(2)}) %collective-permute-start.8) | collective-permute-done | bytes 81952 | tf_op jit(solution)/shard_map/ppermute | solution.py:17
  70.9 2.9 %collective-permute-start.9 = (f32[1,5,2048]{2,1,0:T(8,128)S(1)}, f32[1,5,2048]{2,1,0:T(8,128)S(1)}, u32[]{:S(2)}, u32[]{:S(2)}) collective-permute-start(f32[1,5,2048]{2,1,0:T(8,128)S(1)} %dynamic-slice_bitcast_fusion.3), channel_id=1, source_target_pairs={{0,8},{4,12},{8,0},{12,4},{1,9},{5,13},{9,1},{13,5},{2,10},{6,14},... | collective-permute-start | bytes 122888 | tf_op jit(solution)/shard_map/ppermute | solution.py:17
  73.8 2.7 %collective-permute-done.9 = f32[1,5,2048]{2,1,0:T(8,128)S(1)} collective-permute-done((f32[1,5,2048]{2,1,0:T(8,128)S(1)}, f32[1,5,2048]{2,1,0:T(8,128)S(1)}, u32[]{:S(2)}, u32[]{:S(2)}) %collective-permute-start.9) | collective-permute-done | bytes 40992 | tf_op jit(solution)/shard_map/ppermute | solution.py:17
  76.5 0.6 fusion.16
  (20 shorter events, 1.8 us)
Async XLA Ops:
  0.9 1.3 %collective-permute-start = (f32[5]{0:T(128)S(1)}, f32[5]{0:T(128)S(1)}, u32[]{:S(2)}, u32[]{:S(2)}) collective-permute-start(f32[5]{0:T(128)S(1)} %fusion.13), channel_id=1, source_target_pairs={{0,1},{1,0},{2,3},{3,2},{4,5},{5,4},{6,7},{7,6},{8,9},{9,8},{10,11... | collective-permute-start | bytes 68 | tf_op jit(solution)/shard_map/ppermute | solution.py:17
  2.2 4.3 %collective-permute-start.1 = (f32[5]{0:T(128)S(1)}, f32[5]{0:T(128)S(1)}, u32[]{:S(2)}, u32[]{:S(2)}) collective-permute-start(f32[5]{0:T(128)S(1)} %add.59), channel_id=1, source_target_pairs={{0,2},{1,3},{2,0},{3,1},{4,6},{5,7},{6,4},{7,5},{8,10},{9,11},{10,... | collective-permute-start | bytes 68 | tf_op jit(solution)/shard_map/ppermute | solution.py:17
  7.4 5.1 %collective-permute-start.2 = (bf16[5,2048]{1,0:T(8,128)(2,1)S(1)}, bf16[5,2048]{1,0:T(8,128)(2,1)S(1)}, u32[]{:S(2)}, u32[]{:S(2)}) collective-permute-start(bf16[5,2048]{1,0:T(8,128)(2,1)S(1)} %fusion.15), channel_id=1, source_target_pairs={{0,8},{4,12},{8,0},{12,4},{1,9},{5,13},{9,1},{13,5},{2,10},{6,14},... | collective-permute-start | bytes 61448 | tf_op jit(solution)/shard_map/ppermute | solution.py:17
  12.5 4.3 %collective-permute-start.3 = (bf16[10,2048]{1,0:T(8,128)(2,1)S(1)}, bf16[10,2048]{1,0:T(8,128)(2,1)S(1)}, u32[]{:S(2)}, u32[]{:S(2)}) collective-permute-start(bf16[10,2048]{1,0:T(8,128)(2,1)S(1)} %maximum_select_fusion.4), channel_id=1, source_target_pairs={{0,4},{4,0},{8,12},{12,8},{1,5},{5,1},{9,13},{13,9},{2,6},{6,2},{1... | collective-permute-start | bytes 122888 | tf_op jit(solution)/shard_map/ppermute | solution.py:17
  37.5 1.9 %collective-permute-start.4 = (f32[2,20,3072]{2,0,1:T(2,128)S(1)}, f32[2,20,3072]{2,0,1:T(2,128)S(1)}, u32[]{:S(2)}, u32[]{:S(2)}) collective-permute-start(f32[2,20,3072]{2,0,1:T(2,128)S(1)} %pad_maximum_fusion), channel_id=1, source_target_pairs={{0,1},{1,0},{2,3},{3,2},{4,5},{5,4},{6,7},{7,6},{8,9},{9,8},{10,11... | collective-permute-start | bytes 1474568 | tf_op jit(solution)/shard_map/ppermute | solution.py:17
  40.0 9.2 %collective-permute-start.5 = (f32[2,20,1536]{2,1,0:T(8,128)S(1)}, f32[2,20,1536]{2,1,0:T(8,128)S(1)}, u32[]{:S(2)}, u32[]{:S(2)}) collective-permute-start(f32[2,20,1536]{2,1,0:T(8,128)S(1)} %pad_maximum_fusion.1), channel_id=1, source_target_pairs={{0,2},{1,3},{2,0},{3,1},{4,6},{5,7},{6,4},{7,5},{8,10},{9,11},{10,... | collective-permute-start | bytes 737288 | tf_op jit(solution)/shard_map/ppermute | solution.py:17
  49.3 4.4 %collective-permute-start.6 = (bf16[20,1536]{1,0:T(8,128)(2,1)S(1)}, bf16[20,1536]{1,0:T(8,128)(2,1)S(1)}, u32[]{:S(2)}, u32[]{:S(2)}) collective-permute-start(bf16[20,1536]{1,0:T(8,128)(2,1)S(1)} %fusion.11), channel_id=1, source_target_pairs={{0,2},{1,3},{2,0},{3,1},{4,6},{5,7},{6,4},{7,5},{8,10},{9,11},{10,... | collective-permute-start | bytes 184328 | tf_op jit(solution)/shard_map/ppermute | solution.py:17
  53.8 1.4 %collective-permute-start.7 = (bf16[20,3072]{1,0:T(8,128)(2,1)S(1)}, bf16[20,3072]{1,0:T(8,128)(2,1)S(1)}, u32[]{:S(2)}, u32[]{:S(2)}) collective-permute-start(bf16[20,3072]{1,0:T(8,128)(2,1)S(1)} %maximum_select_fusion.2), channel_id=1, source_target_pairs={{0,1},{1,0},{2,3},{3,2},{4,5},{5,4},{6,7},{7,6},{8,9},{9,8},{10,11... | collective-permute-start | bytes 368648 | tf_op jit(solution)/shard_map/ppermute | solution.py:17
  65.1 5.7 %collective-permute-start.8 = (f32[1,10,2048]{2,1,0:T(8,128)S(1)}, f32[1,10,2048]{2,1,0:T(8,128)S(1)}, u32[]{:S(2)}, u32[]{:S(2)}) collective-permute-start(f32[1,10,2048]{2,1,0:T(8,128)S(1)} %dynamic-slice_bitcast_fusion.2), channel_id=1, source_target_pairs={{0,4},{4,0},{8,12},{12,8},{1,5},{5,1},{9,13},{13,9},{2,6},{6,2},{1... | collective-permute-start | bytes 245768 | tf_op jit(solution)/shard_map/ppermute | solution.py:17
  70.9 5.6 %collective-permute-start.9 = (f32[1,5,2048]{2,1,0:T(8,128)S(1)}, f32[1,5,2048]{2,1,0:T(8,128)S(1)}, u32[]{:S(2)}, u32[]{:S(2)}) collective-permute-start(f32[1,5,2048]{2,1,0:T(8,128)S(1)} %dynamic-slice_bitcast_fusion.3), channel_id=1, source_target_pairs={{0,8},{4,12},{8,0},{12,4},{1,9},{5,13},{9,1},{13,5},{2,10},{6,14},... | collective-permute-start | bytes 122888 | tf_op jit(solution)/shard_map/ppermute | solution.py:17

commit v4 on v3

--- a/solution.py
+++ b/solution.py
@@ -45,41 +45,53 @@
     return x
 
 
+def spread(x, axis, n):
+    return lax.all_to_all(x, axis, 0, 0, tiled=True)
+
+
 def local(tokens, norm_gain, w_gate, w_up, w_down):
     ngx = lax.axis_size("gx")
     ngy = lax.axis_size("gy")
-    features = tokens.shape[1] * ngy
-    values = tokens.astype(jnp.float32)
-    local_sq = jnp.sum(values * values, axis=1)
-    if pairwise(ngy):
-        total_sq = xor_all_reduce(local_sq, "gy", ngy)
+    rows_here, width_here = tokens.shape
+    features = width_here * ngy
+    if ngx * ngy <= 4 * EXCHANGE_MAX:
+        copies = jnp.broadcast_to(tokens[None], (ngx * ngy,) + tokens.shape)
+        every = spread(copies, ("gx", "gy"), ngx * ngy).reshape(ngx, ngy, rows_here, width_here)
+        values_all = every.astype(jnp.float32)
+        total_sq = jnp.sum(values_all * values_all, axis=(1, 3)).reshape(-1)
+        mine = lax.dynamic_index_in_dim(every, lax.axis_index("gy"), axis=1, keepdims=False)
+        values = mine.reshape(ngx * rows_here, width_here).astype(jnp.float32)
+        inverse = lax.rsqrt(total_sq / features + epsilon)
+        piece = (values * inverse[:, None] * norm_gain[None, :]).astype(jnp.bfloat16)
     else:
-        total_sq = lax.psum(local_sq, "gy")
-    inverse = lax.rsqrt(total_sq / features + epsilon)
-    normed = (values * inverse[:, None] * norm_gain[None, :]).astype(jnp.bfloat16)
-    gx_levels = list(range(ngx.bit_length() - 1))
-    if pairwise(ngx):
-        piece = xor_all_gather(normed, "gx", ngx, 0, gx_levels[::-1])
-    else:
+        values = tokens.astype(jnp.float32)
+        total_sq = lax.psum(jnp.sum(values * values, axis=1), "gy")
+        inverse = lax.rsqrt(total_sq / features + epsilon)
+        normed = (values * inverse[:, None] * norm_gain[None, :]).astype(jnp.bfloat16)
         piece = lax.all_gather(normed, "gx", axis=0, tiled=True)
+    rows = piece.shape[0]
 
     gate_part = jnp.dot(piece, w_gate, preferred_element_type=jnp.float32)
     up_part = jnp.dot(piece, w_up, preferred_element_type=jnp.float32)
-    gy_levels = list(range(ngy.bit_length() - 1))
-    if pairwise(ngy):
-        gate, up = xor_reduce_scatter([gate_part, up_part], "gy", ngy, 1, gy_levels)
+    width = w_gate.shape[1]
+    block = width // ngy
+    if ngy <= EXCHANGE_MAX:
+        both = jnp.stack([gate_part, up_part])
+        blocks = jnp.stack([both[:, :, k * block:(k + 1) * block] for k in range(ngy)])
+        summed = jnp.sum(spread(blocks, "gy", ngy), axis=0)
+        hidden = (jax.nn.silu(summed[0]) * summed[1]).astype(jnp.bfloat16)
+        copies = jnp.broadcast_to(hidden[None], (ngy,) + hidden.shape)
+        hidden_all = jnp.transpose(spread(copies, "gy", ngy), (1, 0, 2)).reshape(rows, width)
     else:
         gate = lax.psum_scatter(gate_part, "gy", scatter_dimension=1, tiled=True)
         up = lax.psum_scatter(up_part, "gy", scatter_dimension=1, tiled=True)
-    hidden = (jax.nn.silu(gate) * up).astype(jnp.bfloat16)
-    if pairwise(ngy):
-        hidden_all = xor_all_gather(hidden, "gy", ngy, 1, gy_levels[::-1])
-    else:
+        hidden = (jax.nn.silu(gate) * up).astype(jnp.bfloat16)
         hidden_all = lax.all_gather(hidden, "gy", axis=1, tiled=True)
 
     total = jnp.dot(hidden_all, w_down, preferred_element_type=jnp.float32)
-    if pairwise(ngx):
-        (result,) = xor_reduce_scatter([total], "gx", ngx, 0, gx_levels)
+    if ngx <= EXCHANGE_MAX:
+        parts = spread(total.reshape(ngx, rows // ngx, -1), "gx", ngx)
+        result = jnp.sum(parts, axis=0)
     else:
         result = lax.psum_scatter(total, "gx", scatter_dimension=0, tiled=True)
     return result.astype(jnp.bfloat16)

time: 77.4 us -> 94.9 us (1.23)
  blocking collectives: 0 us -> 37.2 us
  waiting for transfers between devices: 26.3 us -> 14.5 us
  starting transfers between devices: 17.1 us -> 7.49 us
  local copies, waits for them, and re-layouts: 0.85 us -> 3.02 us
  other arithmetic: 3.13 us -> 1.93 us
    all_to_all x0 -> x3, blocking collectives: none -> 37.2 us  [spread(): return lax.all_to_all(x, axis, 0, 0, tiled=True)]
    ppermute x10 -> x0, waiting for transfers between devices: 26.3 us -> none  [exchange(): return lax.ppermute(x, axis, [(a, a ^ 1 << s) for a in range(n)])]
    ppermute x10 -> x0, starting transfers between devices: 17.1 us -> none  [exchange(): return lax.ppermute(x, axis, [(a, a ^ 1 << s) for a in range(n)])]
    all_to_all x0 -> x1, waiting for transfers between devices: none -> 14.5 us  [spread(): return lax.all_to_all(x, axis, 0, 0, tiled=True)]
    all_to_all x0 -> x1, starting transfers between devices: none -> 7.49 us  [spread(): return lax.all_to_all(x, axis, 0, 0, tiled=True)]
    broadcast_in_dim x0 -> x2, local copies, waits for them, and re-layouts: none -> 1.62 us  [the longest x1 1.6 us: local(): copies = jnp.broadcast_to(tokens[None], (ngx * ngy,) + tokens.shape)]
    convert_element_type x3 -> x2, other arithmetic: 1.53 us -> 0.32 us  [the longest x1 0.3 us: local(): hidden = (jax.nn.silu(summed[0]) * summed[1]).astype(jnp.bfloat16)]
  transfers between devices with their start and end apart: 10 -> 1, of which waited for: 10 -> 1; matrix products, arithmetic and copies ran while one was open for 0% -> 0% of each run, Pallas kernels for 0% -> 0%
where the time goes in v4:
time: 94.9 us; the launch traced here: 94.5 us
  blocking collectives  37.2 us (39%)
  matrix products  30.2 us (32%)
  waiting for transfers between devices  14.5 us (15%)
  starting transfers between devices  7.49 us (8%)
  local copies, waits for them, and re-layouts  3.02 us (3%)
  other arithmetic  1.93 us (2%)
    all_to_all x3, blocking collectives, spread(): return lax.all_to_all(x, axis, 0, 0, tiled=True)  37.2 us
    all_to_all x1, waiting for transfers between devices, spread(): return lax.all_to_all(x, axis, 0, 0, tiled=True)  14.5 us
    dot_general x1, matrix products, local(): total = jnp.dot(hidden_all, w_down, preferred_element_type=jnp.float32)  10.3 us
    dot_general x1, matrix products, local(): up_part = jnp.dot(piece, w_up, preferred_element_type=jnp.float32)  9.98 us
    dot_general x1, matrix products, local(): gate_part = jnp.dot(piece, w_gate, preferred_element_type=jnp.float32)  9.97 us
    all_to_all x1, starting transfers between devices, spread(): return lax.all_to_all(x, axis, 0, 0, tiled=True)  7.49 us
  transfers between devices with their start and end apart: 1, of which 1 were waited for; matrix products, arithmetic and copies ran while one was open for 0% of the time, Pallas kernels for 0%

profile of v4, /device:TPU:0, one launch (start us, length us, event | category | flops | bytes accessed | tf_op | source)
XLA Modules:
  0.0 94.5 jit_solution(10999854343700923923)
XLA Ops:
  0.0 1.6 %broadcast_in_dim.6 = bf16[16,5,2048]{2,1,0:T(8,128)(2,1)} broadcast(bf16[5,2048]{1,0:T(8,128)(2,1)} %param.5), dimensions={1,2} | broadcast | bytes 348160 | tf_op jit(solution)/shard_map/broadcast_in_dim | solution.py:58
  1.6 0.0 copy-start
  1.6 7.5 %all-to-all-start = ((bf16[16,5,2048]{2,1,0:T(8,128)(2,1)}), bf16[16,5,2048]{2,1,0:T(8,128)(2,1)S(1)}, u32[]{:S(2)}, u32[]{:S(2)}) async-start(bf16[16,5,2048]{2,1,0:T(8,128)(2,1)} %broadcast_in_dim.6), calls=%async_computation | async-start | bytes 1048576 | tf_op jit(solution)/shard_map/all_to_all | solution.py:49
  9.1 14.5 %all-to-all-done = bf16[16,5,2048]{2,1,0:T(8,128)(2,1)S(1)} async-done(((bf16[16,5,2048]{2,1,0:T(8,128)(2,1)}), bf16[16,5,2048]{2,1,0:T(8,128)(2,1)S(1)}, u32[]{:S(2)}, u32[]{:S(2)}) %all-to-all-start) | async-done | bytes 327712 | tf_op jit(solution)/shard_map/all_to_all | solution.py:49
  23.6 0.2 multiply_reduce_fusion
  23.8 0.1 copy.35
  23.9 0.1 copy.28
  24.0 0.1 rsqrt.11
  24.2 0.0 copy-done
  24.2 10.0 %convolution_bitcast_fusion = f32[1,20,6144]{2,1,0:T(8,128)S(1)} fusion(bf16[2048,6144]{1,0:T(8,128)(2,1)} %param.8, f32[20,2048]{1,0:T(8,128)S(1)} %reshape.28, f32[2048]{0:T(1024)S(1)} %copy-done, f32[20]{0:T(128)S(1)} %rsqrt.11), kind=kOutput, calls=%fused_computation.2 | convolution fusion | flops 503439360 | bytes 25829456 | tf_op jit(solution)/shard_map/dot_general | solution.py:75
  34.2 10.0 %convolution_bitcast_fusion.1 = f32[1,20,6144]{2,1,0:T(8,128)S(1)} fusion(bf16[2048,6144]{1,0:T(8,128)(2,1)} %param.7, f32[20,2048]{1,0:T(8,128)S(1)} %reshape.28, f32[2048]{0:T(1024)S(1)} %copy-done, f32[20]{0:T(128)S(1)} %rsqrt.11), kind=kOutput, calls=%fused_computation.3 | convolution fusion | flops 503439360 | bytes 25829456 | tf_op jit(solution)/shard_map/dot_general | solution.py:74
  44.1 0.1 fusion.5
  44.2 0.1 pad_maximum_fusion
  44.3 0.8 copy.29
  45.1 16.2 %all_to_all.20 = f32[4,2,20,1536]{3,1,2,0:T(2,128)S(1)} all-to-all(f32[4,2,20,1536]{3,1,2,0:T(2,128)S(1)} %copy.29), channel_id=1, replica_groups=mesh['groups'=2,'gx'=4,'gy'=4] {'gy'}, dimensions={0} | all-to-all | bytes 1966080 | tf_op jit(solution)/shard_map/all_to_all | solution.py:49
  61.3 0.5 reduce_sum.37
  61.8 0.3 fusion.10
  62.2 8.8 %all_to_all.21 = bf16[4,20,1536]{2,1,0:T(8,128)(2,1)S(1)} all-to-all(bf16[4,20,1536]{2,1,0:T(8,128)(2,1)S(1)} %broadcast_in_dim.8), channel_id=1, replica_groups=mesh['groups'=2,'gx'=4,'gy'=4] {'gy'}, dimensions={0} | all-to-all | bytes 491520 | tf_op jit(solution)/shard_map/all_to_all | solution.py:49
  70.9 0.1 copy.30
  71.0 0.2 dot_general.13
  71.2 10.3 %fusion = f32[4,5,2048]{2,1,0:T(8,128)S(1)} fusion(bf16[4,5,6144]{2,1,0:T(8,128)(2,1)S(1)} %dot_general.13, bf16[6144,2048]{1,0:T(8,128)(2,1)} %param.9), kind=kOutput, calls=%fused_computation | convolution fusion | flops 503316480 | bytes 25575424 | tf_op jit(solution)/shard_map/dot_general | solution.py:91
  81.5 12.3 %all_to_all.22 = f32[4,5,2048]{2,1,0:T(8,128)S(1)} all-to-all(f32[4,5,2048]{2,1,0:T(8,128)S(1)} %fusion), channel_id=1, replica_groups=mesh['groups'=2,'gx'=4,'gy'=4] {'gx'}, dimensions={0} | all-to-all | bytes 327680 | tf_op jit(solution)/shard_map/all_to_all | solution.py:49
  93.8 0.6 reduce_sum.38
  (6 shorter events, 0.1 us)
Async XLA Ops:
  1.6 22.6 %copy-start = (f32[2048]{0:T(1024)S(1)}, f32[2048]{0:T(1024)}, u32[]{:S(2)}) copy-start(f32[2048]{0:T(1024)} %param.6) | copy-start | bytes 24580
  1.6 22.0 %all-to-all-start = ((bf16[16,5,2048]{2,1,0:T(8,128)(2,1)}), bf16[16,5,2048]{2,1,0:T(8,128)(2,1)S(1)}, u32[]{:S(2)}, u32[]{:S(2)}) async-start(bf16[16,5,2048]{2,1,0:T(8,128)(2,1)} %broadcast_in_dim.6), calls=%async_computation | async-start | bytes 1048576 | tf_op jit(solution)/shard_map/all_to_all | solution.py:49

commit v5 on v3

--- a/solution.py
+++ b/solution.py
@@ -7,6 +7,7 @@
 epsilon = 1e-06
 
 EXCHANGE_MAX = 8
+CHUNKS = 2
 
 
 def pairwise(n):
@@ -63,21 +64,27 @@
     else:
         piece = lax.all_gather(normed, "gx", axis=0, tiled=True)
 
-    gate_part = jnp.dot(piece, w_gate, preferred_element_type=jnp.float32)
-    up_part = jnp.dot(piece, w_up, preferred_element_type=jnp.float32)
+    width = w_gate.shape[1]
+    chunks = CHUNKS if width % (CHUNKS * ngy * 128) == 0 else 1
+    step = width // chunks
     gy_levels = list(range(ngy.bit_length() - 1))
-    if pairwise(ngy):
-        gate, up = xor_reduce_scatter([gate_part, up_part], "gy", ngy, 1, gy_levels)
-    else:
-        gate = lax.psum_scatter(gate_part, "gy", scatter_dimension=1, tiled=True)
-        up = lax.psum_scatter(up_part, "gy", scatter_dimension=1, tiled=True)
-    hidden = (jax.nn.silu(gate) * up).astype(jnp.bfloat16)
-    if pairwise(ngy):
-        hidden_all = xor_all_gather(hidden, "gy", ngy, 1, gy_levels[::-1])
-    else:
-        hidden_all = lax.all_gather(hidden, "gy", axis=1, tiled=True)
-
-    total = jnp.dot(hidden_all, w_down, preferred_element_type=jnp.float32)
+    total = None
+    for c in range(chunks):
+        cols = slice(c * step, (c + 1) * step)
+        gate_part = jnp.dot(piece, w_gate[:, cols], preferred_element_type=jnp.float32)
+        up_part = jnp.dot(piece, w_up[:, cols], preferred_element_type=jnp.float32)
+        if pairwise(ngy):
+            gate, up = xor_reduce_scatter([gate_part, up_part], "gy", ngy, 1, gy_levels)
+        else:
+            gate = lax.psum_scatter(gate_part, "gy", scatter_dimension=1, tiled=True)
+            up = lax.psum_scatter(up_part, "gy", scatter_dimension=1, tiled=True)
+        hidden = (jax.nn.silu(gate) * up).astype(jnp.bfloat16)
+        if pairwise(ngy):
+            hidden_all = xor_all_gather(hidden, "gy", ngy, 1, gy_levels[::-1])
+        else:
+            hidden_all = lax.all_gather(hidden, "gy", axis=1, tiled=True)
+        term = jnp.dot(hidden_all, w_down[cols, :], preferred_element_type=jnp.float32)
+        total = term if total is None else total + term
     if pairwise(ngx):
         (result,) = xor_reduce_scatter([total], "gx", ngx, 0, gx_levels)
     else:

time: 77.4 us -> 77.4 us (level)
  waiting for transfers between devices: 26.3 us -> 23.7 us
  starting transfers between devices: 17.1 us -> 19 us
  matrix products: 29.7 us -> 31 us
    ppermute x10 -> x14, waiting for transfers between devices: 26.3 us -> 23.7 us  [exchange(): return lax.ppermute(x, axis, [(a, a ^ 1 << s) for a in range(n)])]
    ppermute x10 -> x14, starting transfers between devices: 17.1 us -> 19 us  [exchange(): return lax.ppermute(x, axis, [(a, a ^ 1 << s) for a in range(n)])]
    dot_general x3 -> x6, matrix products: 29.7 us -> 31 us  [the longest x2 11.8 us: local(): up_part = jnp.dot(piece, w_up[:, cols], preferred_element_type=jnp.float32)]
  transfers between devices with their start and end apart: 10 -> 14, of which waited for: 10 -> 10; matrix products, arithmetic and copies ran while one was open for 0% -> 17% of each run, Pallas kernels for 0% -> 0%
where the time goes in v5:
time: 77.4 us; the launch traced here: 77.1 us
  matrix products  31 us (40%)
  waiting for transfers between devices  23.7 us (31%)
  starting transfers between devices  19 us (25%)
  other arithmetic  2.7 us (3%)
    ppermute x14, waiting for transfers between devices, exchange(): return lax.ppermute(x, axis, [(a, a ^ 1 << s) for a in range(n)])  23.7 us
    ppermute x14, starting transfers between devices, exchange(): return lax.ppermute(x, axis, [(a, a ^ 1 << s) for a in range(n)])  19 us
    dot_general x2, matrix products, local(): up_part = jnp.dot(piece, w_up[:, cols], preferred_element_type=jnp.float32)  11.8 us
    dot_general x2, matrix products, local(): jnp.dot(hidden_all, w_down[cols, :], preferred_element_type=jnp.float32)  11.1 us
    dot_general x2, matrix products, local(): jnp.dot(piece, w_gate[:, cols], preferred_element_type=jnp.float32)  8.03 us
  transfers between devices with their start and end apart: 14, of which 10 were waited for; matrix products, arithmetic and copies ran while one was open for 17% of the time, Pallas kernels for 0%

profile of v5, /device:TPU:0, one launch (start us, length us, event | category | flops | bytes accessed | tf_op | source)
XLA Modules:
  0.0 77.1 jit_solution(16893959104433460776)
XLA Ops:
  0.0 0.9 %fusion.39 = f32[5]{0:T(128)S(1)} fusion(bf16[5,2048]{1,0:T(8,128)(2,1)} %param.5), kind=kLoop, calls=%fused_computation.66 | loop fusion | flops 30715 | bytes 20500 | tf_op jit(solution)/shard_map/reduce_sum | solution.py:54
  2.2 2.8 %collective-permute-start.1 = (f32[5]{0:T(128)S(1)}, f32[5]{0:T(128)S(1)}, u32[]{:S(2)}, u32[]{:S(2)}) collective-permute-start(f32[5]{0:T(128)S(1)} %add.85), channel_id=1, source_target_pairs={{0,2},{1,3},{2,0},{3,1},{4,6},{5,7},{6,4},{7,5},{8,10},{9,11},{10,... | collective-permute-start | bytes 68 | tf_op jit(solution)/shard_map/ppermute | solution.py:18
  5.0 1.5 %collective-permute-done.1 = f32[5]{0:T(128)S(1)} collective-permute-done((f32[5]{0:T(128)S(1)}, f32[5]{0:T(128)S(1)}, u32[]{:S(2)}, u32[]{:S(2)}) %collective-permute-start.1) | collective-permute-done | bytes 52 | tf_op jit(solution)/shard_map/ppermute | solution.py:18
  7.4 3.2 %collective-permute-start.2 = (bf16[5,2048]{1,0:T(8,128)(2,1)S(1)}, bf16[5,2048]{1,0:T(8,128)(2,1)S(1)}, u32[]{:S(2)}, u32[]{:S(2)}) collective-permute-start(bf16[5,2048]{1,0:T(8,128)(2,1)S(1)} %fusion.41), channel_id=1, source_target_pairs={{0,8},{4,12},{8,0},{12,4},{1,9},{5,13},{9,1},{13,5},{2,10},{6,14},... | collective-permute-start | bytes 61448 | tf_op jit(solution)/shard_map/ppermute | solution.py:18
  10.6 1.9 %collective-permute-done.2 = bf16[5,2048]{1,0:T(8,128)(2,1)S(1)} collective-permute-done((bf16[5,2048]{1,0:T(8,128)(2,1)S(1)}, bf16[5,2048]{1,0:T(8,128)(2,1)S(1)}, u32[]{:S(2)}, u32[]{:S(2)}) %collective-permute-start.2) | collective-permute-done | bytes 20512 | tf_op jit(solution)/shard_map/ppermute | solution.py:18
  12.5 2.0 %collective-permute-start.3 = (bf16[10,2048]{1,0:T(8,128)(2,1)S(1)}, bf16[10,2048]{1,0:T(8,128)(2,1)S(1)}, u32[]{:S(2)}, u32[]{:S(2)}) collective-permute-start(bf16[10,2048]{1,0:T(8,128)(2,1)S(1)} %maximum_select_fusion.7), channel_id=1, source_target_pairs={{0,4},{4,0},{8,12},{12,8},{1,5},{5,1},{9,13},{13,9},{2,6},{6,2},{1... | collective-permute-start | bytes 122888 | tf_op jit(solution)/shard_map/ppermute | solution.py:18
  14.5 2.4 %collective-permute-done.3 = bf16[10,2048]{1,0:T(8,128)(2,1)S(1)} collective-permute-done((bf16[10,2048]{1,0:T(8,128)(2,1)S(1)}, bf16[10,2048]{1,0:T(8,128)(2,1)S(1)}, u32[]{:S(2)}, u32[]{:S(2)}) %collective-permute-start.3) | collective-permute-done | bytes 40992 | tf_op jit(solution)/shard_map/ppermute | solution.py:18
  16.8 6.3 %fusion.10 = f32[20,3072]{1,0:T(8,128)S(1)} fusion(bf16[2048,6144]{1,0:T(8,128)(2,1)} %param.7, bf16[10,2048]{1,0:T(8,128)(2,1)S(1)} %collective-permute-done.3, bf16[10,2048]{1,0:T(8,128)(2,1)S(1)} %maximum_select_fusion.7, pred[]{:T(512)S(6)} %eq.16), kind=kOutput, calls=%fused_computation.10 | convolution fusion | flops 252026880 | bytes 12910593 | tf_op jit(solution)/shard_map/dot_general | solution.py:74
  23.1 6.3 %fusion.8 = f32[20,3072]{1,0:T(8,128)S(1)} fusion(bf16[2048,6144]{1,0:T(8,128)(2,1)} %param.8, bf16[10,2048]{1,0:T(8,128)(2,1)S(1)} %collective-permute-done.3, bf16[10,2048]{1,0:T(8,128)(2,1)S(1)} %maximum_select_fusion.7, pred[]{:T(512)S(6)} %eq.16), kind=kOutput, calls=%fused_computation.8 | convolution fusion | flops 252026880 | bytes 12910593 | tf_op jit(solution)/shard_map/dot_general | solution.py:75
  29.9 1.7 %fusion.4 = f32[20,3072]{1,0:T(8,128)S(1)} fusion(bf16[2048,6144]{1,0:T(8,128)(2,1)S(1)} %copy-done, bf16[10,2048]{1,0:T(8,128)(2,1)S(1)} %collective-permute-done.3, bf16[10,2048]{1,0:T(8,128)(2,1)S(1)} %maximum_select_fusion.7, pred[]{:T(512)S(6)} %eq.16), kind=kOutput, calls=%fused_computation.4 | convolution fusion | flops 252026880 | bytes 12959745 | tf_op jit(solution)/shard_map/dot_general | solution.py:74
  31.7 5.5 %fusion.2 = f32[20,3072]{1,0:T(8,128)S(1)} fusion(bf16[2048,6144]{1,0:T(8,128)(2,1)} %param.8, bf16[10,2048]{1,0:T(8,128)(2,1)S(1)} %collective-permute-done.3, bf16[10,2048]{1,0:T(8,128)(2,1)S(1)} %maximum_select_fusion.7, pred[]{:T(512)S(6)} %eq.16), kind=kOutput, calls=%fused_computation.2 | convolution fusion | flops 252026880 | bytes 12910593 | tf_op jit(solution)/shard_map/dot_general | solution.py:75
  37.6 1.4 %collective-permute-done.8 = f32[2,20,1536]{2,1,0:T(8,128)S(1)} collective-permute-done((f32[2,20,1536]{2,1,0:T(8,128)S(1)}, f32[2,20,1536]{2,1,0:T(8,128)S(1)}, u32[]{:S(2)}, u32[]{:S(2)}) %collective-permute-start.8) | collective-permute-done | bytes 245792 | tf_op jit(solution)/shard_map/ppermute | solution.py:18
  39.0 1.7 %collective-permute-start.9 = (f32[2,20,768]{2,1,0:T(8,128)S(1)}, f32[2,20,768]{2,1,0:T(8,128)S(1)}, u32[]{:S(2)}, u32[]{:S(2)}) collective-permute-start(f32[2,20,768]{2,1,0:T(8,128)S(1)} %pad_maximum_fusion.3), channel_id=1, source_target_pairs={{0,2},{1,3},{2,0},{3,1},{4,6},{5,7},{6,4},{7,5},{8,10},{9,11},{10,... | collective-permute-start | bytes 368648 | tf_op jit(solution)/shard_map/ppermute | solution.py:18
  41.2 4.6 %collective-permute-done.9 = f32[2,20,768]{2,1,0:T(8,128)S(1)} collective-permute-done((f32[2,20,768]{2,1,0:T(8,128)S(1)}, f32[2,20,768]{2,1,0:T(8,128)S(1)}, u32[]{:S(2)}, u32[]{:S(2)}) %collective-permute-start.9) | collective-permute-done | bytes 122912 | tf_op jit(solution)/shard_map/ppermute | solution.py:18
  45.8 1.7 %collective-permute-start.10 = (bf16[20,768]{1,0:T(8,128)(2,1)S(1)}, bf16[20,768]{1,0:T(8,128)(2,1)S(1)}, u32[]{:S(2)}, u32[]{:S(2)}) collective-permute-start(bf16[20,768]{1,0:T(8,128)(2,1)S(1)} %fusion.33), channel_id=1, source_target_pairs={{0,2},{1,3},{2,0},{3,1},{4,6},{5,7},{6,4},{7,5},{8,10},{9,11},{10,... | collective-permute-start | bytes 92168 | tf_op jit(solution)/shard_map/ppermute | solution.py:18
  47.5 1.1 %collective-permute-done.5 = f32[2,20,768]{2,1,0:T(8,128)S(1)} collective-permute-done((f32[2,20,768]{2,1,0:T(8,128)S(1)}, f32[2,20,768]{2,1,0:T(8,128)S(1)}, u32[]{:S(2)}, u32[]{:S(2)}) %collective-permute-start.5) | collective-permute-done | bytes 122912 | tf_op jit(solution)/shard_map/ppermute | solution.py:18
  48.7 1.8 %collective-permute-start.6 = (bf16[20,768]{1,0:T(8,128)(2,1)S(1)}, bf16[20,768]{1,0:T(8,128)(2,1)S(1)}, u32[]{:S(2)}, u32[]{:S(2)}) collective-permute-start(bf16[20,768]{1,0:T(8,128)(2,1)S(1)} %fusion.37), channel_id=1, source_target_pairs={{0,2},{1,3},{2,0},{3,1},{4,6},{5,7},{6,4},{7,5},{8,10},{9,11},{10,... | collective-permute-start | bytes 92168 | tf_op jit(solution)/shard_map/ppermute | solution.py:18
  50.6 2.1 %collective-permute-done.6 = bf16[20,768]{1,0:T(8,128)(2,1)S(1)} collective-permute-done((bf16[20,768]{1,0:T(8,128)(2,1)S(1)}, bf16[20,768]{1,0:T(8,128)(2,1)S(1)}, u32[]{:S(2)}, u32[]{:S(2)}) %collective-permute-start.6) | collective-permute-done | bytes 30752 | tf_op jit(solution)/shard_map/ppermute | solution.py:18
  52.8 5.6 %fusion = f32[20,2048]{1,0:T(8,128)S(1)} fusion(bf16[6144,2048]{1,0:T(8,128)(2,1)} %param.9, bf16[20,1536]{1,0:T(8,128)(2,1)S(1)} %collective-permute-done.11, bf16[20,1536]{1,0:T(8,128)(2,1)S(1)} %maximum_select_fusion.6, pred[]{:T(512)S(6)} %eq.14), kind=kOutput, calls=%fused_computation | convolution fusion | flops 252211200 | bytes 12869633 | tf_op jit(solution)/shard_map/dot_general | solution.py:86
  58.4 5.6 %fusion.12 = f32[20,2048]{1,0:T(8,128)S(1)} fusion(f32[20,2048]{1,0:T(8,128)S(1)} %fusion, bf16[6144,2048]{1,0:T(8,128)(2,1)} %param.9, bf16[20,1536]{1,0:T(8,128)(2,1)S(1)} %collective-permute-done.7, bf16[20,1536]{1,0:T(8,128)(2,1)S(1)} %maximum_select_fusion.5, pred[]{:T(512)S(6)} %eq.14), kind=kOutput, calls=%fused_computation.12 | convolution fusion | flops 252252160 | bytes 13033473 | tf_op jit(solution)/shard_map/dot_general | solution.py:86
  64.0 1.6 %collective-permute-start.12 = (f32[1,10,2048]{2,1,0:T(8,128)S(1)}, f32[1,10,2048]{2,1,0:T(8,128)S(1)}, u32[]{:S(2)}, u32[]{:S(2)}) collective-permute-start(f32[1,10,2048]{2,1,0:T(8,128)S(1)} %dynamic-slice_bitcast_fusion.4), channel_id=1, source_target_pairs={{0,4},{4,0},{8,12},{12,8},{1,5},{5,1},{9,13},{13,9},{2,6},{6,2},{1... | collective-permute-start | bytes 245768 | tf_op jit(solution)/shard_map/ppermute | solution.py:18
  65.6 4.4 %collective-permute-done.12 = f32[1,10,2048]{2,1,0:T(8,128)S(1)} collective-permute-done((f32[1,10,2048]{2,1,0:T(8,128)S(1)}, f32[1,10,2048]{2,1,0:T(8,128)S(1)}, u32[]{:S(2)}, u32[]{:S(2)}) %collective-permute-start.12) | collective-permute-done | bytes 81952 | tf_op jit(solution)/shard_map/ppermute | solution.py:18
  70.0 2.9 %collective-permute-start.13 = (f32[1,5,2048]{2,1,0:T(8,128)S(1)}, f32[1,5,2048]{2,1,0:T(8,128)S(1)}, u32[]{:S(2)}, u32[]{:S(2)}) collective-permute-start(f32[1,5,2048]{2,1,0:T(8,128)S(1)} %dynamic-slice_bitcast_fusion.9), channel_id=1, source_target_pairs={{0,8},{4,12},{8,0},{12,4},{1,9},{5,13},{9,1},{13,5},{2,10},{6,14},... | collective-permute-start | bytes 122888 | tf_op jit(solution)/shard_map/ppermute | solution.py:18
  72.9 3.6 %collective-permute-done.13 = f32[1,5,2048]{2,1,0:T(8,128)S(1)} collective-permute-done((f32[1,5,2048]{2,1,0:T(8,128)S(1)}, f32[1,5,2048]{2,1,0:T(8,128)S(1)}, u32[]{:S(2)}, u32[]{:S(2)}) %collective-permute-start.13) | collective-permute-done | bytes 40992 | tf_op jit(solution)/shard_map/ppermute | solution.py:18
  (37 shorter events, 4.6 us)
Async XLA Ops:
  0.9 1.3 %collective-permute-start = (f32[5]{0:T(128)S(1)}, f32[5]{0:T(128)S(1)}, u32[]{:S(2)}, u32[]{:S(2)}) collective-permute-start(f32[5]{0:T(128)S(1)} %fusion.39), channel_id=1, source_target_pairs={{0,1},{1,0},{2,3},{3,2},{4,5},{5,4},{6,7},{7,6},{8,9},{9,8},{10,11... | collective-permute-start | bytes 68 | tf_op jit(solution)/shard_map/ppermute | solution.py:18
  2.2 4.3 %collective-permute-start.1 = (f32[5]{0:T(128)S(1)}, f32[5]{0:T(128)S(1)}, u32[]{:S(2)}, u32[]{:S(2)}) collective-permute-start(f32[5]{0:T(128)S(1)} %add.85), channel_id=1, source_target_pairs={{0,2},{1,3},{2,0},{3,1},{4,6},{5,7},{6,4},{7,5},{8,10},{9,11},{10,... | collective-permute-start | bytes 68 | tf_op jit(solution)/shard_map/ppermute | solution.py:18
  7.4 5.1 %collective-permute-start.2 = (bf16[5,2048]{1,0:T(8,128)(2,1)S(1)}, bf16[5,2048]{1,0:T(8,128)(2,1)S(1)}, u32[]{:S(2)}, u32[]{:S(2)}) collective-permute-start(bf16[5,2048]{1,0:T(8,128)(2,1)S(1)} %fusion.41), channel_id=1, source_target_pairs={{0,8},{4,12},{8,0},{12,4},{1,9},{5,13},{9,1},{13,5},{2,10},{6,14},... | collective-permute-start | bytes 61448 | tf_op jit(solution)/shard_map/ppermute | solution.py:18
  12.5 4.3 %collective-permute-start.3 = (bf16[10,2048]{1,0:T(8,128)(2,1)S(1)}, bf16[10,2048]{1,0:T(8,128)(2,1)S(1)}, u32[]{:S(2)}, u32[]{:S(2)}) collective-permute-start(bf16[10,2048]{1,0:T(8,128)(2,1)S(1)} %maximum_select_fusion.7), channel_id=1, source_target_pairs={{0,4},{4,0},{8,12},{12,8},{1,5},{5,1},{9,13},{13,9},{2,6},{6,2},{1... | collective-permute-start | bytes 122888 | tf_op jit(solution)/shard_map/ppermute | solution.py:18
  14.5 15.4 %copy-start = (bf16[2048,6144]{1,0:T(8,128)(2,1)S(1)}, bf16[2048,6144]{1,0:T(8,128)(2,1)}, u32[]{:S(2)}) copy-start(bf16[2048,6144]{1,0:T(8,128)(2,1)} %param.7) | copy-start | bytes 75497472
  29.5 8.0 %collective-permute-start.4 = (f32[2,20,1536]{2,1,0:T(8,128)S(1)}, f32[2,20,1536]{2,1,0:T(8,128)S(1)}, u32[]{:S(2)}, u32[]{:S(2)}) collective-permute-start(f32[2,20,1536]{2,1,0:T(8,128)S(1)} %pad_maximum_fusion), channel_id=1, source_target_pairs={{0,1},{1,0},{2,3},{3,2},{4,5},{5,4},{6,7},{7,6},{8,9},{9,8},{10,11... | collective-permute-start | bytes 737288 | tf_op jit(solution)/shard_map/ppermute | solution.py:18
  37.3 1.6 %collective-permute-start.8 = (f32[2,20,1536]{2,1,0:T(8,128)S(1)}, f32[2,20,1536]{2,1,0:T(8,128)S(1)}, u32[]{:S(2)}, u32[]{:S(2)}) collective-permute-start(f32[2,20,1536]{2,1,0:T(8,128)S(1)} %pad_maximum_fusion.1), channel_id=1, source_target_pairs={{0,1},{1,0},{2,3},{3,2},{4,5},{5,4},{6,7},{7,6},{8,9},{9,8},{10,11... | collective-permute-start | bytes 737288 | tf_op jit(solution)/shard_map/ppermute | solution.py:18
  39.0 6.7 %collective-permute-start.9 = (f32[2,20,768]{2,1,0:T(8,128)S(1)}, f32[2,20,768]{2,1,0:T(8,128)S(1)}, u32[]{:S(2)}, u32[]{:S(2)}) collective-permute-start(f32[2,20,768]{2,1,0:T(8,128)S(1)} %pad_maximum_fusion.3), channel_id=1, source_target_pairs={{0,2},{1,3},{2,0},{3,1},{4,6},{5,7},{6,4},{7,5},{8,10},{9,11},{10,... | collective-permute-start | bytes 368648 | tf_op jit(solution)/shard_map/ppermute | solution.py:18
  40.7 7.9 %collective-permute-start.5 = (f32[2,20,768]{2,1,0:T(8,128)S(1)}, f32[2,20,768]{2,1,0:T(8,128)S(1)}, u32[]{:S(2)}, u32[]{:S(2)}) collective-permute-start(f32[2,20,768]{2,1,0:T(8,128)S(1)} %pad_maximum_fusion.2), channel_id=1, source_target_pairs={{0,2},{1,3},{2,0},{3,1},{4,6},{5,7},{6,4},{7,5},{8,10},{9,11},{10,... | collective-permute-start | bytes 368648 | tf_op jit(solution)/shard_map/ppermute | solution.py:18
  45.8 4.7 %collective-permute-start.10 = (bf16[20,768]{1,0:T(8,128)(2,1)S(1)}, bf16[20,768]{1,0:T(8,128)(2,1)S(1)}, u32[]{:S(2)}, u32[]{:S(2)}) collective-permute-start(bf16[20,768]{1,0:T(8,128)(2,1)S(1)} %fusion.33), channel_id=1, source_target_pairs={{0,2},{1,3},{2,0},{3,1},{4,6},{5,7},{6,4},{7,5},{8,10},{9,11},{10,... | collective-permute-start | bytes 92168 | tf_op jit(solution)/shard_map/ppermute | solution.py:18
  48.7 4.0 %collective-permute-start.6 = (bf16[20,768]{1,0:T(8,128)(2,1)S(1)}, bf16[20,768]{1,0:T(8,128)(2,1)S(1)}, u32[]{:S(2)}, u32[]{:S(2)}) collective-permute-start(bf16[20,768]{1,0:T(8,128)(2,1)S(1)} %fusion.37), channel_id=1, source_target_pairs={{0,2},{1,3},{2,0},{3,1},{4,6},{5,7},{6,4},{7,5},{8,10},{9,11},{10,... | collective-permute-start | bytes 92168 | tf_op jit(solution)/shard_map/ppermute | solution.py:18
  50.5 2.3 %collective-permute-start.11 = (bf16[20,1536]{1,0:T(8,128)(2,1)S(1)}, bf16[20,1536]{1,0:T(8,128)(2,1)S(1)}, u32[]{:S(2)}, u32[]{:S(2)}) collective-permute-start(bf16[20,1536]{1,0:T(8,128)(2,1)S(1)} %maximum_select_fusion.6), channel_id=1, source_target_pairs={{0,1},{1,0},{2,3},{3,2},{4,5},{5,4},{6,7},{7,6},{8,9},{9,8},{10,11... | collective-permute-start | bytes 184328 | tf_op jit(solution)/shard_map/ppermute | solution.py:18
  52.7 5.7 %collective-permute-start.7 = (bf16[20,1536]{1,0:T(8,128)(2,1)S(1)}, bf16[20,1536]{1,0:T(8,128)(2,1)S(1)}, u32[]{:S(2)}, u32[]{:S(2)}) collective-permute-start(bf16[20,1536]{1,0:T(8,128)(2,1)S(1)} %maximum_select_fusion.5), channel_id=1, source_target_pairs={{0,1},{1,0},{2,3},{3,2},{4,5},{5,4},{6,7},{7,6},{8,9},{9,8},{10,11... | collective-permute-start | bytes 184328 | tf_op jit(solution)/shard_map/ppermute | solution.py:18
  64.0 5.9 %collective-permute-start.12 = (f32[1,10,2048]{2,1,0:T(8,128)S(1)}, f32[1,10,2048]{2,1,0:T(8,128)S(1)}, u32[]{:S(2)}, u32[]{:S(2)}) collective-permute-start(f32[1,10,2048]{2,1,0:T(8,128)S(1)} %dynamic-slice_bitcast_fusion.4), channel_id=1, source_target_pairs={{0,4},{4,0},{8,12},{12,8},{1,5},{5,1},{9,13},{13,9},{2,6},{6,2},{1... | collective-permute-start | bytes 245768 | tf_op jit(solution)/shard_map/ppermute | solution.py:18
  70.0 6.5 %collective-permute-start.13 = (f32[1,5,2048]{2,1,0:T(8,128)S(1)}, f32[1,5,2048]{2,1,0:T(8,128)S(1)}, u32[]{:S(2)}, u32[]{:S(2)}) collective-permute-start(f32[1,5,2048]{2,1,0:T(8,128)S(1)} %dynamic-slice_bitcast_fusion.9), channel_id=1, source_target_pairs={{0,8},{4,12},{8,0},{12,4},{1,9},{5,13},{9,1},{13,5},{2,10},{6,14},... | collective-permute-start | bytes 122888 | tf_op jit(solution)/shard_map/ppermute | solution.py:18

commit v6 on v5

--- a/solution.py
+++ b/solution.py
@@ -46,23 +46,38 @@
     return x
 
 
+def gathered_position(d, bits):
+    return sum(((d >> s) & 1) << t for t, s in enumerate(bits))
+
+
+def fanout_reduce_scatter(x, axis, n, bits):
+    me = lax.axis_index(axis)
+    rows = x.shape[0] // n
+    own = lax.dynamic_slice_in_dim(x, gathered_position(me, bits) * rows, rows, axis=0)
+    for k in range(1, n):
+        block = lax.dynamic_slice_in_dim(x, gathered_position(me ^ k, bits) * rows, rows, axis=0)
+        own = own + lax.ppermute(block, axis, [(a, a ^ k) for a in range(n)])
+    return own
+
+
 def local(tokens, norm_gain, w_gate, w_up, w_down):
     ngx = lax.axis_size("gx")
     ngy = lax.axis_size("gy")
     features = tokens.shape[1] * ngy
-    values = tokens.astype(jnp.float32)
+    gx_levels = list(range(ngx.bit_length() - 1))
+    if pairwise(ngx):
+        raw = xor_all_gather(tokens, "gx", ngx, 0, gx_levels[::-1])
+    else:
+        raw = lax.all_gather(tokens, "gx", axis=0, tiled=True)
+    values = raw.astype(jnp.float32)
+    piece = (values * norm_gain[None, :]).astype(jnp.bfloat16)
     local_sq = jnp.sum(values * values, axis=1)
     if pairwise(ngy):
         total_sq = xor_all_reduce(local_sq, "gy", ngy)
     else:
         total_sq = lax.psum(local_sq, "gy")
-    inverse = lax.rsqrt(total_sq / features + epsilon)
-    normed = (values * inverse[:, None] * norm_gain[None, :]).astype(jnp.bfloat16)
-    gx_levels = list(range(ngx.bit_length() - 1))
-    if pairwise(ngx):
-        piece = xor_all_gather(normed, "gx", ngx, 0, gx_levels[::-1])
-    else:
-        piece = lax.all_gather(normed, "gx", axis=0, tiled=True)
+    inverse = lax.rsqrt(total_sq / features + epsilon)[:, None]
+    rows = piece.shape[0]
 
     width = w_gate.shape[1]
     chunks = CHUNKS if width % (CHUNKS * ngy * 128) == 0 else 1
@@ -78,7 +93,7 @@
         else:
             gate = lax.psum_scatter(gate_part, "gy", scatter_dimension=1, tiled=True)
             up = lax.psum_scatter(up_part, "gy", scatter_dimension=1, tiled=True)
-        hidden = (jax.nn.silu(gate) * up).astype(jnp.bfloat16)
+        hidden = (jax.nn.silu(gate * inverse) * (up * inverse)).astype(jnp.bfloat16)
         if pairwise(ngy):
             hidden_all = xor_all_gather(hidden, "gy", ngy, 1, gy_levels[::-1])
         else:
@@ -86,7 +101,7 @@
         term = jnp.dot(hidden_all, w_down[cols, :], preferred_element_type=jnp.float32)
         total = term if total is None else total + term
     if pairwise(ngx):
-        (result,) = xor_reduce_scatter([total], "gx", ngx, 0, gx_levels)
+        result = fanout_reduce_scatter(total, "gx", ngx, gx_levels[::-1])
     else:
         result = lax.psum_scatter(total, "gx", scatter_dimension=0, tiled=True)
     return result.astype(jnp.bfloat16)

time: 77.4 us -> 67.8 us (0.88)
  matrix products: 31 us -> 27.2 us
  waiting for transfers between devices: 23.7 us -> 21 us
  starting transfers between devices: 19 us -> 17.1 us
    dot_general x2, matrix products: 11.8 us -> 3.5 us  [local(): up_part = jnp.dot(piece, w_up[:, cols], preferred_element_type=jnp.float32)]
    ppermute x14 -> x12, waiting for transfers between devices: 23.7 us -> 15.5 us  [exchange(): return lax.ppermute(x, axis, [(a, a ^ 1 << s) for a in range(n)])]
    ppermute x14 -> x12, starting transfers between devices: 19 us -> 12.7 us  [exchange(): return lax.ppermute(x, axis, [(a, a ^ 1 << s) for a in range(n)])]
    ppermute x0 -> x3, waiting for transfers between devices: none -> 5.48 us  [fanout_reduce_scatter(): own = own + lax.ppermute(block, axis, [(a, a ^ k) for a in range(n)])]
    dot_general x2, matrix products: 8.03 us -> 12.6 us  [local(): jnp.dot(piece, w_gate[:, cols], preferred_element_type=jnp.float32)]
    ppermute x0 -> x3, starting transfers between devices: none -> 4.45 us  [fanout_reduce_scatter(): own = own + lax.ppermute(block, axis, [(a, a ^ k) for a in range(n)])]
    select_n x3, other arithmetic: 0.08 us -> 0.92 us  [xor_all_gather(): x = jnp.where(me >> s & 1 == 0, low, high)]
    convert_element_type x3 -> x1, other arithmetic: 0.92 us -> 0.12 us  [local(): hidden = (jax.nn.silu(gate * inverse) * (up * inverse)).astype(jnp.bfloat16)]
  transfers between devices with their start and end apart: 14 -> 15, of which waited for: 10 -> 10; matrix products, arithmetic and copies ran while one was open for 17% -> 9% of each run, Pallas kernels for 0% -> 0%
where the time goes in v6:
time: 67.8 us; the launch traced here: 67.7 us
  matrix products  27.2 us (40%)
  waiting for transfers between devices  21 us (31%)
  starting transfers between devices  17.1 us (25%)
  other arithmetic  2.01 us (3%)
    ppermute x12, waiting for transfers between devices, exchange(): return lax.ppermute(x, axis, [(a, a ^ 1 << s) for a in range(n)])  15.5 us
    ppermute x12, starting transfers between devices, exchange(): return lax.ppermute(x, axis, [(a, a ^ 1 << s) for a in range(n)])  12.7 us
    dot_general x2, matrix products, local(): jnp.dot(piece, w_gate[:, cols], preferred_element_type=jnp.float32)  12.6 us
    dot_general x2, matrix products, local(): jnp.dot(hidden_all, w_down[cols, :], preferred_element_type=jnp.float32)  11.1 us
    ppermute x3, waiting for transfers between devices, fanout_reduce_scatter(): own = own + lax.ppermute(block, axis, [(a, a ^ k) for a in range(n)])  5.48 us
    ppermute x3, starting transfers between devices, fanout_reduce_scatter(): own = own + lax.ppermute(block, axis, [(a, a ^ k) for a in range(n)])  4.45 us
    dot_general x2, matrix products, local(): up_part = jnp.dot(piece, w_up[:, cols], preferred_element_type=jnp.float32)  3.5 us
  transfers between devices with their start and end apart: 15, of which 10 were waited for; matrix products, arithmetic and copies ran while one was open for 9% of the time, Pallas kernels for 0%

profile of v6, /device:TPU:0, one launch (start us, length us, event | category | flops | bytes accessed | tf_op | source)
XLA Modules:
  0.0 67.7 jit_solution(5132454772011829529)
XLA Ops:
  0.0 4.0 %collective-permute-start = (bf16[5,2048]{1,0:T(8,128)(2,1)}, bf16[5,2048]{1,0:T(8,128)(2,1)S(1)}, u32[]{:S(2)}, u32[]{:S(2)}) collective-permute-start(bf16[5,2048]{1,0:T(8,128)(2,1)} %param.5), channel_id=1, source_target_pairs={{0,8},{4,12},{8,0},{12,4},{1,9},{5,13},{9,1},{13,5},{2,10},{6,14},... | collective-permute-start | bytes 61448 | tf_op jit(solution)/shard_map/ppermute | solution.py:18
  4.0 2.5 %collective-permute-done = bf16[5,2048]{1,0:T(8,128)(2,1)S(1)} collective-permute-done((bf16[5,2048]{1,0:T(8,128)(2,1)}, bf16[5,2048]{1,0:T(8,128)(2,1)S(1)}, u32[]{:S(2)}, u32[]{:S(2)}) %collective-permute-start) | collective-permute-done | bytes 20512 | tf_op jit(solution)/shard_map/ppermute | solution.py:18
  6.5 0.9 %maximum_select_fusion.7 = bf16[10,2048]{1,0:T(8,128)(2,1)S(1)} fusion(bf16[5,2048]{1,0:T(8,128)(2,1)S(1)} %collective-permute-done, bf16[5,2048]{1,0:T(8,128)(2,1)} %param.5, pred[]{:T(512)S(6)} %eq.17), kind=kLoop, calls=%fused_computation.70 | loop fusion | flops 184320 | bytes 81921 | tf_op jit(solution)/shard_map/jit(_where)/select_n | solution.py:39
  7.4 1.6 %collective-permute-start.1 = (bf16[10,2048]{1,0:T(8,128)(2,1)S(1)}, bf16[10,2048]{1,0:T(8,128)(2,1)S(1)}, u32[]{:S(2)}, u32[]{:S(2)}) collective-permute-start(bf16[10,2048]{1,0:T(8,128)(2,1)S(1)} %maximum_select_fusion.7), channel_id=1, source_target_pairs={{0,4},{4,0},{8,12},{12,8},{1,5},{5,1},{9,13},{13,9},{2,6},{6,2},{1... | collective-permute-start | bytes 122888 | tf_op jit(solution)/shard_map/ppermute | solution.py:18
  9.0 2.7 %collective-permute-done.1 = bf16[10,2048]{1,0:T(8,128)(2,1)S(1)} collective-permute-done((bf16[10,2048]{1,0:T(8,128)(2,1)S(1)}, bf16[10,2048]{1,0:T(8,128)(2,1)S(1)}, u32[]{:S(2)}, u32[]{:S(2)}) %collective-permute-start.1) | collective-permute-done | bytes 40992 | tf_op jit(solution)/shard_map/ppermute | solution.py:18
  11.9 6.3 %fusion.4 = f32[20,3072]{1,0:T(8,128)S(1)} fusion(bf16[2048,6144]{1,0:T(8,128)(2,1)} %param.7, bf16[20,2048]{1,0:T(8,128)(2,1)S(1)} %get-tuple-element.6, f32[2048]{0:T(1024)} %param.6), kind=kOutput, calls=%fused_computation.4 | convolution fusion | flops 251781120 | bytes 12918784 | tf_op jit(solution)/shard_map/dot_general | solution.py:89
  18.2 6.3 %fusion.10 = f32[20,3072]{1,0:T(8,128)S(1)} fusion(bf16[2048,6144]{1,0:T(8,128)(2,1)} %param.7, bf16[20,2048]{1,0:T(8,128)(2,1)S(1)} %get-tuple-element.6, f32[2048]{0:T(1024)} %param.6), kind=kOutput, calls=%fused_computation.10 | convolution fusion | flops 251781120 | bytes 12918784 | tf_op jit(solution)/shard_map/dot_general | solution.py:89
  24.5 1.7 %fusion.2 = f32[20,3072]{1,0:T(8,128)S(1)} fusion(bf16[2048,6144]{1,0:T(8,128)(2,1)S(1)} %copy-done, bf16[20,2048]{1,0:T(8,128)(2,1)S(1)} %get-tuple-element.6, f32[2048]{0:T(1024)S(1)} %copy-done.1), kind=kOutput, calls=%fused_computation.2 | convolution fusion | flops 251781120 | bytes 12935168 | tf_op jit(solution)/shard_map/dot_general | solution.py:90
  26.3 1.8 %fusion.8 = f32[20,3072]{1,0:T(8,128)S(1)} fusion(bf16[2048,6144]{1,0:T(8,128)(2,1)S(1)} %copy-done, bf16[20,2048]{1,0:T(8,128)(2,1)S(1)} %get-tuple-element.6, f32[2048]{0:T(1024)S(1)} %copy-done.1), kind=kOutput, calls=%fused_computation.8 | convolution fusion | flops 251781120 | bytes 12935168 | tf_op jit(solution)/shard_map/dot_general | solution.py:90
  28.9 0.9 %collective-permute-done.4 = f32[20]{0:T(128)S(1)} collective-permute-done((f32[20]{0:T(128)S(1)}, f32[20]{0:T(128)S(1)}, u32[]{:S(2)}, u32[]{:S(2)}) %collective-permute-start.4) | collective-permute-done | bytes 112 | tf_op jit(solution)/shard_map/ppermute | solution.py:18
  29.8 1.7 %collective-permute-start.5 = (f32[20]{0:T(128)S(1)}, f32[20]{0:T(128)S(1)}, u32[]{:S(2)}, u32[]{:S(2)}) collective-permute-start(f32[20]{0:T(128)S(1)} %add.107), channel_id=1, source_target_pairs={{0,2},{1,3},{2,0},{3,1},{4,6},{5,7},{6,4},{7,5},{8,10},{9,11},{10,... | collective-permute-start | bytes 248 | tf_op jit(solution)/shard_map/ppermute | solution.py:18
  32.1 1.8 %collective-permute-start.3 = (f32[2,20,768]{2,1,0:T(8,128)S(1)}, f32[2,20,768]{2,1,0:T(8,128)S(1)}, u32[]{:S(2)}, u32[]{:S(2)}) collective-permute-start(f32[2,20,768]{2,1,0:T(8,128)S(1)} %pad_maximum_fusion.2), channel_id=1, source_target_pairs={{0,2},{1,3},{2,0},{3,1},{4,6},{5,7},{6,4},{7,5},{8,10},{9,11},{10,... | collective-permute-start | bytes 368648 | tf_op jit(solution)/shard_map/ppermute | solution.py:18
  33.8 4.5 %collective-permute-done.9 = f32[2,20,768]{2,1,0:T(8,128)S(1)} collective-permute-done((f32[2,20,768]{2,1,0:T(8,128)S(1)}, f32[2,20,768]{2,1,0:T(8,128)S(1)}, u32[]{:S(2)}, u32[]{:S(2)}) %collective-permute-start.9) | collective-permute-done | bytes 122912 | tf_op jit(solution)/shard_map/ppermute | solution.py:18
  38.4 2.0 %collective-permute-done.3 = f32[2,20,768]{2,1,0:T(8,128)S(1)} collective-permute-done((f32[2,20,768]{2,1,0:T(8,128)S(1)}, f32[2,20,768]{2,1,0:T(8,128)S(1)}, u32[]{:S(2)}, u32[]{:S(2)}) %collective-permute-start.3) | collective-permute-done | bytes 122912 | tf_op jit(solution)/shard_map/ppermute | solution.py:18
  40.9 1.7 %collective-permute-start.6 = (bf16[20,768]{1,0:T(8,128)(2,1)S(1)}, bf16[20,768]{1,0:T(8,128)(2,1)S(1)}, u32[]{:S(2)}, u32[]{:S(2)}) collective-permute-start(bf16[20,768]{1,0:T(8,128)(2,1)S(1)} %get-tuple-element.14), channel_id=1, source_target_pairs={{0,2},{1,3},{2,0},{3,1},{4,6},{5,7},{6,4},{7,5},{8,10},{9,11},{10,... | collective-permute-start | bytes 92168 | tf_op jit(solution)/shard_map/ppermute | solution.py:18
  42.6 1.9 %collective-permute-done.10 = bf16[20,768]{1,0:T(8,128)(2,1)S(1)} collective-permute-done((bf16[20,768]{1,0:T(8,128)(2,1)S(1)}, bf16[20,768]{1,0:T(8,128)(2,1)S(1)}, u32[]{:S(2)}, u32[]{:S(2)}) %collective-permute-start.10) | collective-permute-done | bytes 30752 | tf_op jit(solution)/shard_map/ppermute | solution.py:18
  45.2 0.7 collective-permute-done.11
  45.9 5.5 %fusion = f32[20,2048]{1,0:T(8,128)S(1)} fusion(bf16[6144,2048]{1,0:T(8,128)(2,1)} %param.9, bf16[20,1536]{1,0:T(8,128)(2,1)S(1)} %collective-permute-done.11, bf16[20,1536]{1,0:T(8,128)(2,1)S(1)} %maximum_select_fusion.6, pred[]{:T(512)S(6)} %eq.14), kind=kOutput, calls=%fused_computation | convolution fusion | flops 252211200 | bytes 12869633 | tf_op jit(solution)/shard_map/dot_general | solution.py:101
  51.5 5.6 %fusion.12 = f32[20,2048]{1,0:T(8,128)S(1)} fusion(f32[20,2048]{1,0:T(8,128)S(1)} %fusion, bf16[6144,2048]{1,0:T(8,128)(2,1)} %param.9, bf16[20,1536]{1,0:T(8,128)(2,1)S(1)} %collective-permute-done.7, bf16[20,1536]{1,0:T(8,128)(2,1)S(1)} %maximum_select_fusion.5, pred[]{:T(512)S(6)} %eq.14), kind=kOutput, calls=%fused_computation.12 | convolution fusion | flops 252252160 | bytes 13033473 | tf_op jit(solution)/shard_map/dot_general | solution.py:101
  57.1 1.4 %collective-permute-start.12 = (f32[5,2048]{1,0:T(8,128)S(1)}, f32[5,2048]{1,0:T(8,128)S(1)}, u32[]{:S(2)}, u32[]{:S(2)}) collective-permute-start(f32[5,2048]{1,0:T(8,128)S(1)} %get-tuple-element.11), channel_id=1, source_target_pairs={{0,4},{4,0},{8,12},{12,8},{1,5},{5,1},{9,13},{13,9},{2,6},{6,2},{1... | collective-permute-start | bytes 122888 | tf_op jit(solution)/shard_map/ppermute | solution.py:59
  58.5 2.4 %collective-permute-start.13 = (f32[5,2048]{1,0:T(8,128)S(1)}, f32[5,2048]{1,0:T(8,128)S(1)}, u32[]{:S(2)}, u32[]{:S(2)}) collective-permute-start(f32[5,2048]{1,0:T(8,128)S(1)} %get-tuple-element.13), channel_id=1, source_target_pairs={{0,8},{4,12},{8,0},{12,4},{1,9},{5,13},{9,1},{13,5},{2,10},{6,14},... | collective-permute-start | bytes 122888 | tf_op jit(solution)/shard_map/ppermute | solution.py:59
  60.8 0.7 %collective-permute-start.14 = (f32[5,2048]{1,0:T(8,128)S(1)}, f32[5,2048]{1,0:T(8,128)S(1)}, u32[]{:S(2)}, u32[]{:S(2)}) collective-permute-start(f32[5,2048]{1,0:T(8,128)S(1)} %get-tuple-element.12), channel_id=1, source_target_pairs={{0,12},{4,8},{8,4},{12,0},{1,13},{5,9},{9,5},{13,1},{2,14},{6,10},... | collective-permute-start | bytes 122888 | tf_op jit(solution)/shard_map/ppermute | solution.py:59
  61.5 4.5 %collective-permute-done.13 = f32[5,2048]{1,0:T(8,128)S(1)} collective-permute-done((f32[5,2048]{1,0:T(8,128)S(1)}, f32[5,2048]{1,0:T(8,128)S(1)}, u32[]{:S(2)}, u32[]{:S(2)}) %collective-permute-start.13) | collective-permute-done | bytes 40992 | tf_op jit(solution)/shard_map/ppermute | solution.py:59
  66.0 1.0 %collective-permute-done.14 = f32[5,2048]{1,0:T(8,128)S(1)} collective-permute-done((f32[5,2048]{1,0:T(8,128)S(1)}, f32[5,2048]{1,0:T(8,128)S(1)}, u32[]{:S(2)}, u32[]{:S(2)}) %collective-permute-start.14) | collective-permute-done | bytes 40992 | tf_op jit(solution)/shard_map/ppermute | solution.py:59
  (37 shorter events, 3.4 us)
Async XLA Ops:
  0.0 24.5 %copy-start.1 = (f32[2048]{0:T(1024)S(1)}, f32[2048]{0:T(1024)}, u32[]{:S(2)}) copy-start(f32[2048]{0:T(1024)} %param.6) | copy-start | bytes 24580
  0.0 6.5 %collective-permute-start = (bf16[5,2048]{1,0:T(8,128)(2,1)}, bf16[5,2048]{1,0:T(8,128)(2,1)S(1)}, u32[]{:S(2)}, u32[]{:S(2)}) collective-permute-start(bf16[5,2048]{1,0:T(8,128)(2,1)} %param.5), channel_id=1, source_target_pairs={{0,8},{4,12},{8,0},{12,4},{1,9},{5,13},{9,1},{13,5},{2,10},{6,14},... | collective-permute-start | bytes 61448 | tf_op jit(solution)/shard_map/ppermute | solution.py:18
  7.4 4.3 %collective-permute-start.1 = (bf16[10,2048]{1,0:T(8,128)(2,1)S(1)}, bf16[10,2048]{1,0:T(8,128)(2,1)S(1)}, u32[]{:S(2)}, u32[]{:S(2)}) collective-permute-start(bf16[10,2048]{1,0:T(8,128)(2,1)S(1)} %maximum_select_fusion.7), channel_id=1, source_target_pairs={{0,4},{4,0},{8,12},{12,8},{1,5},{5,1},{9,13},{13,9},{2,6},{6,2},{1... | collective-permute-start | bytes 122888 | tf_op jit(solution)/shard_map/ppermute | solution.py:18
  9.0 15.5 %copy-start = (bf16[2048,6144]{1,0:T(8,128)(2,1)S(1)}, bf16[2048,6144]{1,0:T(8,128)(2,1)}, u32[]{:S(2)}) copy-start(bf16[2048,6144]{1,0:T(8,128)(2,1)} %param.8) | copy-start | bytes 75497472
  28.1 3.4 %collective-permute-start.8 = (f32[2,20,1536]{2,1,0:T(8,128)S(1)}, f32[2,20,1536]{2,1,0:T(8,128)S(1)}, u32[]{:S(2)}, u32[]{:S(2)}) collective-permute-start(f32[2,20,1536]{2,1,0:T(8,128)S(1)} %pad_maximum_fusion.1), channel_id=1, source_target_pairs={{0,1},{1,0},{2,3},{3,2},{4,5},{5,4},{6,7},{7,6},{8,9},{9,8},{10,11... | collective-permute-start | bytes 737288 | tf_op jit(solution)/shard_map/ppermute | solution.py:18
  28.2 1.6 %collective-permute-start.4 = (f32[20]{0:T(128)S(1)}, f32[20]{0:T(128)S(1)}, u32[]{:S(2)}, u32[]{:S(2)}) collective-permute-start(f32[20]{0:T(128)S(1)} %get-tuple-element.5), channel_id=1, source_target_pairs={{0,1},{1,0},{2,3},{3,2},{4,5},{5,4},{6,7},{7,6},{8,9},{9,8},{10,11... | collective-permute-start | bytes 248 | tf_op jit(solution)/shard_map/ppermute | solution.py:18
  28.7 3.2 %collective-permute-start.2 = (f32[2,20,1536]{2,1,0:T(8,128)S(1)}, f32[2,20,1536]{2,1,0:T(8,128)S(1)}, u32[]{:S(2)}, u32[]{:S(2)}) collective-permute-start(f32[2,20,1536]{2,1,0:T(8,128)S(1)} %pad_maximum_fusion), channel_id=1, source_target_pairs={{0,1},{1,0},{2,3},{3,2},{4,5},{5,4},{6,7},{7,6},{8,9},{9,8},{10,11... | collective-permute-start | bytes 737288 | tf_op jit(solution)/shard_map/ppermute | solution.py:18
  29.8 4.1 %collective-permute-start.5 = (f32[20]{0:T(128)S(1)}, f32[20]{0:T(128)S(1)}, u32[]{:S(2)}, u32[]{:S(2)}) collective-permute-start(f32[20]{0:T(128)S(1)} %add.107), channel_id=1, source_target_pairs={{0,2},{1,3},{2,0},{3,1},{4,6},{5,7},{6,4},{7,5},{8,10},{9,11},{10,... | collective-permute-start | bytes 248 | tf_op jit(solution)/shard_map/ppermute | solution.py:18
  31.6 6.8 %collective-permute-start.9 = (f32[2,20,768]{2,1,0:T(8,128)S(1)}, f32[2,20,768]{2,1,0:T(8,128)S(1)}, u32[]{:S(2)}, u32[]{:S(2)}) collective-permute-start(f32[2,20,768]{2,1,0:T(8,128)S(1)} %pad_maximum_fusion.3), channel_id=1, source_target_pairs={{0,2},{1,3},{2,0},{3,1},{4,6},{5,7},{6,4},{7,5},{8,10},{9,11},{10,... | collective-permute-start | bytes 368648 | tf_op jit(solution)/shard_map/ppermute | solution.py:18
  32.1 8.3 %collective-permute-start.3 = (f32[2,20,768]{2,1,0:T(8,128)S(1)}, f32[2,20,768]{2,1,0:T(8,128)S(1)}, u32[]{:S(2)}, u32[]{:S(2)}) collective-permute-start(f32[2,20,768]{2,1,0:T(8,128)S(1)} %pad_maximum_fusion.2), channel_id=1, source_target_pairs={{0,2},{1,3},{2,0},{3,1},{4,6},{5,7},{6,4},{7,5},{8,10},{9,11},{10,... | collective-permute-start | bytes 368648 | tf_op jit(solution)/shard_map/ppermute | solution.py:18
  40.5 4.0 %collective-permute-start.10 = (bf16[20,768]{1,0:T(8,128)(2,1)S(1)}, bf16[20,768]{1,0:T(8,128)(2,1)S(1)}, u32[]{:S(2)}, u32[]{:S(2)}) collective-permute-start(bf16[20,768]{1,0:T(8,128)(2,1)S(1)} %get-tuple-element.15), channel_id=1, source_target_pairs={{0,2},{1,3},{2,0},{3,1},{4,6},{5,7},{6,4},{7,5},{8,10},{9,11},{10,... | collective-permute-start | bytes 92168 | tf_op jit(solution)/shard_map/ppermute | solution.py:18
  40.9 4.0 %collective-permute-start.6 = (bf16[20,768]{1,0:T(8,128)(2,1)S(1)}, bf16[20,768]{1,0:T(8,128)(2,1)S(1)}, u32[]{:S(2)}, u32[]{:S(2)}) collective-permute-start(bf16[20,768]{1,0:T(8,128)(2,1)S(1)} %get-tuple-element.14), channel_id=1, source_target_pairs={{0,2},{1,3},{2,0},{3,1},{4,6},{5,7},{6,4},{7,5},{8,10},{9,11},{10,... | collective-permute-start | bytes 92168 | tf_op jit(solution)/shard_map/ppermute | solution.py:18
  44.6 1.3 %collective-permute-start.11 = (bf16[20,1536]{1,0:T(8,128)(2,1)S(1)}, bf16[20,1536]{1,0:T(8,128)(2,1)S(1)}, u32[]{:S(2)}, u32[]{:S(2)}) collective-permute-start(bf16[20,1536]{1,0:T(8,128)(2,1)S(1)} %maximum_select_fusion.6), channel_id=1, source_target_pairs={{0,1},{1,0},{2,3},{3,2},{4,5},{5,4},{6,7},{7,6},{8,9},{9,8},{10,11... | collective-permute-start | bytes 184328 | tf_op jit(solution)/shard_map/ppermute | solution.py:18
  45.0 6.5 %collective-permute-start.7 = (bf16[20,1536]{1,0:T(8,128)(2,1)S(1)}, bf16[20,1536]{1,0:T(8,128)(2,1)S(1)}, u32[]{:S(2)}, u32[]{:S(2)}) collective-permute-start(bf16[20,1536]{1,0:T(8,128)(2,1)S(1)} %maximum_select_fusion.5), channel_id=1, source_target_pairs={{0,1},{1,0},{2,3},{3,2},{4,5},{5,4},{6,7},{7,6},{8,9},{9,8},{10,11... | collective-permute-start | bytes 184328 | tf_op jit(solution)/shard_map/ppermute | solution.py:18
  57.1 4.5 %collective-permute-start.12 = (f32[5,2048]{1,0:T(8,128)S(1)}, f32[5,2048]{1,0:T(8,128)S(1)}, u32[]{:S(2)}, u32[]{:S(2)}) collective-permute-start(f32[5,2048]{1,0:T(8,128)S(1)} %get-tuple-element.11), channel_id=1, source_target_pairs={{0,4},{4,0},{8,12},{12,8},{1,5},{5,1},{9,13},{13,9},{2,6},{6,2},{1... | collective-permute-start | bytes 122888 | tf_op jit(solution)/shard_map/ppermute | solution.py:59
  58.5 7.5 %collective-permute-start.13 = (f32[5,2048]{1,0:T(8,128)S(1)}, f32[5,2048]{1,0:T(8,128)S(1)}, u32[]{:S(2)}, u32[]{:S(2)}) collective-permute-start(f32[5,2048]{1,0:T(8,128)S(1)} %get-tuple-element.13), channel_id=1, source_target_pairs={{0,8},{4,12},{8,0},{12,4},{1,9},{5,13},{9,1},{13,5},{2,10},{6,14},... | collective-permute-start | bytes 122888 | tf_op jit(solution)/shard_map/ppermute | solution.py:59
  60.8 6.2 %collective-permute-start.14 = (f32[5,2048]{1,0:T(8,128)S(1)}, f32[5,2048]{1,0:T(8,128)S(1)}, u32[]{:S(2)}, u32[]{:S(2)}) collective-permute-start(f32[5,2048]{1,0:T(8,128)S(1)} %get-tuple-element.12), channel_id=1, source_target_pairs={{0,12},{4,8},{8,4},{12,0},{1,13},{5,9},{9,5},{13,1},{2,14},{6,10},... | collective-permute-start | bytes 122888 | tf_op jit(solution)/shard_map/ppermute | solution.py:59

commit v7 on v6

--- a/solution.py
+++ b/solution.py
@@ -70,13 +70,13 @@
     else:
         raw = lax.all_gather(tokens, "gx", axis=0, tiled=True)
     values = raw.astype(jnp.float32)
-    piece = (values * norm_gain[None, :]).astype(jnp.bfloat16)
     local_sq = jnp.sum(values * values, axis=1)
     if pairwise(ngy):
         total_sq = xor_all_reduce(local_sq, "gy", ngy)
     else:
         total_sq = lax.psum(local_sq, "gy")
-    inverse = lax.rsqrt(total_sq / features + epsilon)[:, None]
+    inverse = lax.rsqrt(total_sq / features + epsilon)
+    piece = (values * inverse[:, None] * norm_gain[None, :]).astype(jnp.bfloat16)
     rows = piece.shape[0]
 
     width = w_gate.shape[1]
@@ -93,7 +93,7 @@
         else:
             gate = lax.psum_scatter(gate_part, "gy", scatter_dimension=1, tiled=True)
             up = lax.psum_scatter(up_part, "gy", scatter_dimension=1, tiled=True)
-        hidden = (jax.nn.silu(gate * inverse) * (up * inverse)).astype(jnp.bfloat16)
+        hidden = (jax.nn.silu(gate) * up).astype(jnp.bfloat16)
         if pairwise(ngy):
             hidden_all = xor_all_gather(hidden, "gy", ngy, 1, gy_levels[::-1])
         else:

time: 67.8 us -> 75.6 us (1.12)
  matrix products: 27.2 us -> 31.3 us
  waiting for transfers between devices: 21 us -> 24.2 us
    dot_general x2, matrix products: 3.5 us -> 12 us  [local(): up_part = jnp.dot(piece, w_up[:, cols], preferred_element_type=jnp.float32)]
    dot_general x2, matrix products: 12.6 us -> 8.2 us  [local(): jnp.dot(piece, w_gate[:, cols], preferred_element_type=jnp.float32)]
    ppermute x12, waiting for transfers between devices: 15.5 us -> 18.3 us  [exchange(): return lax.ppermute(x, axis, [(a, a ^ 1 << s) for a in range(n)])]
  transfers between devices with their start and end apart: 15 -> 15, of which waited for: 10 -> 11; matrix products, arithmetic and copies ran while one was open for 9% -> 18% of each run, Pallas kernels for 0% -> 0%
where the time goes in v7:
time: 75.6 us; the launch traced here: 75.3 us
  matrix products  31.3 us (41%)
  waiting for transfers between devices  24.2 us (32%)
  starting transfers between devices  16.9 us (22%)
  other arithmetic  1.96 us (3%)
  local copies, waits for them, and re-layouts  0.87 us (1%)
    ppermute x12, waiting for transfers between devices, exchange(): return lax.ppermute(x, axis, [(a, a ^ 1 << s) for a in range(n)])  18.3 us
    ppermute x12, starting transfers between devices, exchange(): return lax.ppermute(x, axis, [(a, a ^ 1 << s) for a in range(n)])  12.4 us
    dot_general x2, matrix products, local(): up_part = jnp.dot(piece, w_up[:, cols], preferred_element_type=jnp.float32)  12 us
    dot_general x2, matrix products, local(): jnp.dot(hidden_all, w_down[cols, :], preferred_element_type=jnp.float32)  11.1 us
    dot_general x2, matrix products, local(): jnp.dot(piece, w_gate[:, cols], preferred_element_type=jnp.float32)  8.2 us
    ppermute x3, waiting for transfers between devices, fanout_reduce_scatter(): own = own + lax.ppermute(block, axis, [(a, a ^ k) for a in range(n)])  5.91 us
    ppermute x3, starting transfers between devices, fanout_reduce_scatter(): own = own + lax.ppermute(block, axis, [(a, a ^ k) for a in range(n)])  4.45 us
  transfers between devices with their start and end apart: 15, of which 11 were waited for; matrix products, arithmetic and copies ran while one was open for 18% of the time, Pallas kernels for 0%

profile of v7, /device:TPU:0, one launch (start us, length us, event | category | flops | bytes accessed | tf_op | source)
XLA Modules:
  0.0 75.3 jit_solution(8482931281536711769)
XLA Ops:
  0.0 4.0 %collective-permute-start = (bf16[5,2048]{1,0:T(8,128)(2,1)}, bf16[5,2048]{1,0:T(8,128)(2,1)S(1)}, u32[]{:S(2)}, u32[]{:S(2)}) collective-permute-start(bf16[5,2048]{1,0:T(8,128)(2,1)} %param.5), channel_id=1, source_target_pairs={{0,8},{4,12},{8,0},{12,4},{1,9},{5,13},{9,1},{13,5},{2,10},{6,14},... | collective-permute-start | bytes 61448 | tf_op jit(solution)/shard_map/ppermute | solution.py:18
  4.0 2.5 %collective-permute-done = bf16[5,2048]{1,0:T(8,128)(2,1)S(1)} collective-permute-done((bf16[5,2048]{1,0:T(8,128)(2,1)}, bf16[5,2048]{1,0:T(8,128)(2,1)S(1)}, u32[]{:S(2)}, u32[]{:S(2)}) %collective-permute-start) | collective-permute-done | bytes 20512 | tf_op jit(solution)/shard_map/ppermute | solution.py:18
  7.4 1.6 %collective-permute-start.1 = (bf16[10,2048]{1,0:T(8,128)(2,1)S(1)}, bf16[10,2048]{1,0:T(8,128)(2,1)S(1)}, u32[]{:S(2)}, u32[]{:S(2)}) collective-permute-start(bf16[10,2048]{1,0:T(8,128)(2,1)S(1)} %maximum_select_fusion.7), channel_id=1, source_target_pairs={{0,4},{4,0},{8,12},{12,8},{1,5},{5,1},{9,13},{13,9},{2,6},{6,2},{1... | collective-permute-start | bytes 122888 | tf_op jit(solution)/shard_map/ppermute | solution.py:18
  9.0 2.7 %collective-permute-done.1 = bf16[10,2048]{1,0:T(8,128)(2,1)S(1)} collective-permute-done((bf16[10,2048]{1,0:T(8,128)(2,1)S(1)}, bf16[10,2048]{1,0:T(8,128)(2,1)S(1)}, u32[]{:S(2)}, u32[]{:S(2)}) %collective-permute-start.1) | collective-permute-done | bytes 40992 | tf_op jit(solution)/shard_map/ppermute | solution.py:18
  12.0 1.1 %collective-permute-done.2 = f32[20]{0:T(128)S(1)} collective-permute-done((f32[20]{0:T(128)S(1)}, f32[20]{0:T(128)S(1)}, u32[]{:S(2)}, u32[]{:S(2)}) %collective-permute-start.2) | collective-permute-done | bytes 112 | tf_op jit(solution)/shard_map/ppermute | solution.py:18
  13.1 1.7 %collective-permute-start.3 = (f32[20]{0:T(128)S(1)}, f32[20]{0:T(128)S(1)}, u32[]{:S(2)}, u32[]{:S(2)}) collective-permute-start(f32[20]{0:T(128)S(1)} %add.100), channel_id=1, source_target_pairs={{0,2},{1,3},{2,0},{3,1},{4,6},{5,7},{6,4},{7,5},{8,10},{9,11},{10,... | collective-permute-start | bytes 248 | tf_op jit(solution)/shard_map/ppermute | solution.py:18
  14.8 1.8 %collective-permute-done.3 = f32[20]{0:T(128)S(1)} collective-permute-done((f32[20]{0:T(128)S(1)}, f32[20]{0:T(128)S(1)}, u32[]{:S(2)}, u32[]{:S(2)}) %collective-permute-start.3) | collective-permute-done | bytes 112 | tf_op jit(solution)/shard_map/ppermute | solution.py:18
  16.6 6.4 %fusion.10 = f32[20,3072]{1,0:T(8,128)S(1)} fusion(bf16[2048,6144]{1,0:T(8,128)(2,1)} %param.7, f32[2048]{0:T(1024)} %param.6, f32[20]{0:T(128)S(1)} %add_rsqrt_fusion, bf16[10,2048]{1,0:T(8,128)(2,1)S(1)} %maximum_select_fusion.7, bf16[10,2048]{1,0:T(8,128)(2,1)S(1)} %collective-permute-done.1, pred[]{:T(512)S(6)} %eq.16), kind=kOutput, calls=%fused_computation.10 | convolution fusion | flops 252190720 | bytes 12918865 | tf_op jit(solution)/shard_map/dot_general | solution.py:89
  23.0 6.4 %fusion.8 = f32[20,3072]{1,0:T(8,128)S(1)} fusion(bf16[2048,6144]{1,0:T(8,128)(2,1)} %param.8, f32[2048]{0:T(1024)} %param.6, f32[20]{0:T(128)S(1)} %add_rsqrt_fusion, bf16[10,2048]{1,0:T(8,128)(2,1)S(1)} %maximum_select_fusion.7, bf16[10,2048]{1,0:T(8,128)(2,1)S(1)} %collective-permute-done.1, pred[]{:T(512)S(6)} %eq.16), kind=kOutput, calls=%fused_computation.8 | convolution fusion | flops 252190720 | bytes 12918865 | tf_op jit(solution)/shard_map/dot_general | solution.py:90
  30.2 1.8 %fusion.4 = f32[20,3072]{1,0:T(8,128)S(1)} fusion(bf16[2048,6144]{1,0:T(8,128)(2,1)S(1)} %copy-done, f32[2048]{0:T(1024)S(1)} %copy-done.1, f32[20]{0:T(128)S(1)} %add_rsqrt_fusion, bf16[10,2048]{1,0:T(8,128)(2,1)S(1)} %maximum_select_fusion.7, bf16[10,2048]{1,0:T(8,128)(2,1)S(1)} %collective-permute-done.1, pred[]{:T(512)S(6)} %eq.16), kind=kOutput, calls=%fused_computation.4 | convolution fusion | flops 252190720 | bytes 12968449 | tf_op jit(solution)/shard_map/dot_general | solution.py:89
  32.1 5.6 %fusion.2 = f32[20,3072]{1,0:T(8,128)S(1)} fusion(bf16[2048,6144]{1,0:T(8,128)(2,1)} %param.8, f32[2048]{0:T(1024)S(1)} %copy-done.1, f32[20]{0:T(128)S(1)} %add_rsqrt_fusion, bf16[10,2048]{1,0:T(8,128)(2,1)S(1)} %maximum_select_fusion.7, bf16[10,2048]{1,0:T(8,128)(2,1)S(1)} %collective-permute-done.1, pred[]{:T(512)S(6)} %eq.16), kind=kOutput, calls=%fused_computation.2 | convolution fusion | flops 252190720 | bytes 12918865 | tf_op jit(solution)/shard_map/dot_general | solution.py:90
  37.9 1.5 %collective-permute-done.8 = f32[2,20,1536]{2,1,0:T(8,128)S(1)} collective-permute-done((f32[2,20,1536]{2,1,0:T(8,128)S(1)}, f32[2,20,1536]{2,1,0:T(8,128)S(1)}, u32[]{:S(2)}, u32[]{:S(2)}) %collective-permute-start.8) | collective-permute-done | bytes 245792 | tf_op jit(solution)/shard_map/ppermute | solution.py:18
  39.5 1.2 %collective-permute-start.9 = (f32[2,20,768]{2,1,0:T(8,128)S(1)}, f32[2,20,768]{2,1,0:T(8,128)S(1)}, u32[]{:S(2)}, u32[]{:S(2)}) collective-permute-start(f32[2,20,768]{2,1,0:T(8,128)S(1)} %pad_maximum_fusion.3), channel_id=1, source_target_pairs={{0,2},{1,3},{2,0},{3,1},{4,6},{5,7},{6,4},{7,5},{8,10},{9,11},{10,... | collective-permute-start | bytes 368648 | tf_op jit(solution)/shard_map/ppermute | solution.py:18
  41.7 4.6 %collective-permute-done.9 = f32[2,20,768]{2,1,0:T(8,128)S(1)} collective-permute-done((f32[2,20,768]{2,1,0:T(8,128)S(1)}, f32[2,20,768]{2,1,0:T(8,128)S(1)}, u32[]{:S(2)}, u32[]{:S(2)}) %collective-permute-start.9) | collective-permute-done | bytes 122912 | tf_op jit(solution)/shard_map/ppermute | solution.py:18
  46.3 1.2 %collective-permute-start.10 = (bf16[20,768]{1,0:T(8,128)(2,1)S(1)}, bf16[20,768]{1,0:T(8,128)(2,1)S(1)}, u32[]{:S(2)}, u32[]{:S(2)}) collective-permute-start(bf16[20,768]{1,0:T(8,128)(2,1)S(1)} %fusion.36), channel_id=1, source_target_pairs={{0,2},{1,3},{2,0},{3,1},{4,6},{5,7},{6,4},{7,5},{8,10},{9,11},{10,... | collective-permute-start | bytes 92168 | tf_op jit(solution)/shard_map/ppermute | solution.py:18
  47.4 1.6 %collective-permute-done.5 = f32[2,20,768]{2,1,0:T(8,128)S(1)} collective-permute-done((f32[2,20,768]{2,1,0:T(8,128)S(1)}, f32[2,20,768]{2,1,0:T(8,128)S(1)}, u32[]{:S(2)}, u32[]{:S(2)}) %collective-permute-start.5) | collective-permute-done | bytes 122912 | tf_op jit(solution)/shard_map/ppermute | solution.py:18
  49.0 1.4 %collective-permute-start.6 = (bf16[20,768]{1,0:T(8,128)(2,1)S(1)}, bf16[20,768]{1,0:T(8,128)(2,1)S(1)}, u32[]{:S(2)}, u32[]{:S(2)}) collective-permute-start(bf16[20,768]{1,0:T(8,128)(2,1)S(1)} %fusion.40), channel_id=1, source_target_pairs={{0,2},{1,3},{2,0},{3,1},{4,6},{5,7},{6,4},{7,5},{8,10},{9,11},{10,... | collective-permute-start | bytes 92168 | tf_op jit(solution)/shard_map/ppermute | solution.py:18
  50.5 2.5 %collective-permute-done.6 = bf16[20,768]{1,0:T(8,128)(2,1)S(1)} collective-permute-done((bf16[20,768]{1,0:T(8,128)(2,1)S(1)}, bf16[20,768]{1,0:T(8,128)(2,1)S(1)}, u32[]{:S(2)}, u32[]{:S(2)}) %collective-permute-start.6) | collective-permute-done | bytes 30752 | tf_op jit(solution)/shard_map/ppermute | solution.py:18
  53.2 5.6 %fusion = f32[20,2048]{1,0:T(8,128)S(1)} fusion(bf16[6144,2048]{1,0:T(8,128)(2,1)} %param.9, bf16[20,1536]{1,0:T(8,128)(2,1)S(1)} %collective-permute-done.11, bf16[20,1536]{1,0:T(8,128)(2,1)S(1)} %maximum_select_fusion.6, pred[]{:T(512)S(6)} %eq.14), kind=kOutput, calls=%fused_computation | convolution fusion | flops 252211200 | bytes 12869633 | tf_op jit(solution)/shard_map/dot_general | solution.py:101
  58.7 5.6 %fusion.12 = f32[20,2048]{1,0:T(8,128)S(1)} fusion(f32[20,2048]{1,0:T(8,128)S(1)} %fusion, bf16[6144,2048]{1,0:T(8,128)(2,1)} %param.9, bf16[20,1536]{1,0:T(8,128)(2,1)S(1)} %collective-permute-done.7, bf16[20,1536]{1,0:T(8,128)(2,1)S(1)} %maximum_select_fusion.5, pred[]{:T(512)S(6)} %eq.14), kind=kOutput, calls=%fused_computation.12 | convolution fusion | flops 252252160 | bytes 13033473 | tf_op jit(solution)/shard_map/dot_general | solution.py:101
  64.4 1.4 %collective-permute-start.12 = (f32[5,2048]{1,0:T(8,128)S(1)}, f32[5,2048]{1,0:T(8,128)S(1)}, u32[]{:S(2)}, u32[]{:S(2)}) collective-permute-start(f32[5,2048]{1,0:T(8,128)S(1)} %get-tuple-element.9), channel_id=1, source_target_pairs={{0,4},{4,0},{8,12},{12,8},{1,5},{5,1},{9,13},{13,9},{2,6},{6,2},{1... | collective-permute-start | bytes 122888 | tf_op jit(solution)/shard_map/ppermute | solution.py:59
  65.8 2.8 %collective-permute-start.13 = (f32[5,2048]{1,0:T(8,128)S(1)}, f32[5,2048]{1,0:T(8,128)S(1)}, u32[]{:S(2)}, u32[]{:S(2)}) collective-permute-start(f32[5,2048]{1,0:T(8,128)S(1)} %get-tuple-element.11), channel_id=1, source_target_pairs={{0,8},{4,12},{8,0},{12,4},{1,9},{5,13},{9,1},{13,5},{2,10},{6,14},... | collective-permute-start | bytes 122888 | tf_op jit(solution)/shard_map/ppermute | solution.py:59
  68.9 3.9 %collective-permute-done.13 = f32[5,2048]{1,0:T(8,128)S(1)} collective-permute-done((f32[5,2048]{1,0:T(8,128)S(1)}, f32[5,2048]{1,0:T(8,128)S(1)}, u32[]{:S(2)}, u32[]{:S(2)}) %collective-permute-start.13) | collective-permute-done | bytes 40992 | tf_op jit(solution)/shard_map/ppermute | solution.py:59
  72.8 1.9 %collective-permute-done.14 = f32[5,2048]{1,0:T(8,128)S(1)} collective-permute-done((f32[5,2048]{1,0:T(8,128)S(1)}, f32[5,2048]{1,0:T(8,128)S(1)}, u32[]{:S(2)}, u32[]{:S(2)}) %collective-permute-start.14) | collective-permute-done | bytes 40992 | tf_op jit(solution)/shard_map/ppermute | solution.py:59
  (38 shorter events, 4.5 us)
Async XLA Ops:
  0.0 29.5 %copy-start.1 = (f32[2048]{0:T(1024)S(1)}, f32[2048]{0:T(1024)}, u32[]{:S(2)}) copy-start(f32[2048]{0:T(1024)} %param.6) | copy-start | bytes 24580
  0.0 6.5 %collective-permute-start = (bf16[5,2048]{1,0:T(8,128)(2,1)}, bf16[5,2048]{1,0:T(8,128)(2,1)S(1)}, u32[]{:S(2)}, u32[]{:S(2)}) collective-permute-start(bf16[5,2048]{1,0:T(8,128)(2,1)} %param.5), channel_id=1, source_target_pairs={{0,8},{4,12},{8,0},{12,4},{1,9},{5,13},{9,1},{13,5},{2,10},{6,14},... | collective-permute-start | bytes 61448 | tf_op jit(solution)/shard_map/ppermute | solution.py:18
  7.4 4.3 %collective-permute-start.1 = (bf16[10,2048]{1,0:T(8,128)(2,1)S(1)}, bf16[10,2048]{1,0:T(8,128)(2,1)S(1)}, u32[]{:S(2)}, u32[]{:S(2)}) collective-permute-start(bf16[10,2048]{1,0:T(8,128)(2,1)S(1)} %maximum_select_fusion.7), channel_id=1, source_target_pairs={{0,4},{4,0},{8,12},{12,8},{1,5},{5,1},{9,13},{13,9},{2,6},{6,2},{1... | collective-permute-start | bytes 122888 | tf_op jit(solution)/shard_map/ppermute | solution.py:18
  11.9 1.2 %collective-permute-start.2 = (f32[20]{0:T(128)S(1)}, f32[20]{0:T(128)S(1)}, u32[]{:S(2)}, u32[]{:S(2)}) collective-permute-start(f32[20]{0:T(128)S(1)} %fusion.15), channel_id=1, source_target_pairs={{0,1},{1,0},{2,3},{3,2},{4,5},{5,4},{6,7},{7,6},{8,9},{9,8},{10,11... | collective-permute-start | bytes 248 | tf_op jit(solution)/shard_map/ppermute | solution.py:18
  13.1 3.5 %collective-permute-start.3 = (f32[20]{0:T(128)S(1)}, f32[20]{0:T(128)S(1)}, u32[]{:S(2)}, u32[]{:S(2)}) collective-permute-start(f32[20]{0:T(128)S(1)} %add.100), channel_id=1, source_target_pairs={{0,2},{1,3},{2,0},{3,1},{4,6},{5,7},{6,4},{7,5},{8,10},{9,11},{10,... | collective-permute-start | bytes 248 | tf_op jit(solution)/shard_map/ppermute | solution.py:18
  14.8 15.5 %copy-start = (bf16[2048,6144]{1,0:T(8,128)(2,1)S(1)}, bf16[2048,6144]{1,0:T(8,128)(2,1)}, u32[]{:S(2)}) copy-start(bf16[2048,6144]{1,0:T(8,128)(2,1)} %param.7) | copy-start | bytes 75497472
  29.4 8.4 %collective-permute-start.4 = (f32[2,20,1536]{2,1,0:T(8,128)S(1)}, f32[2,20,1536]{2,1,0:T(8,128)S(1)}, u32[]{:S(2)}, u32[]{:S(2)}) collective-permute-start(f32[2,20,1536]{2,1,0:T(8,128)S(1)} %pad_maximum_fusion), channel_id=1, source_target_pairs={{0,1},{1,0},{2,3},{3,2},{4,5},{5,4},{6,7},{7,6},{8,9},{9,8},{10,11... | collective-permute-start | bytes 737288 | tf_op jit(solution)/shard_map/ppermute | solution.py:18
  37.7 1.6 %collective-permute-start.8 = (f32[2,20,1536]{2,1,0:T(8,128)S(1)}, f32[2,20,1536]{2,1,0:T(8,128)S(1)}, u32[]{:S(2)}, u32[]{:S(2)}) collective-permute-start(f32[2,20,1536]{2,1,0:T(8,128)S(1)} %pad_maximum_fusion.1), channel_id=1, source_target_pairs={{0,1},{1,0},{2,3},{3,2},{4,5},{5,4},{6,7},{7,6},{8,9},{9,8},{10,11... | collective-permute-start | bytes 737288 | tf_op jit(solution)/shard_map/ppermute | solution.py:18
  39.5 6.8 %collective-permute-start.9 = (f32[2,20,768]{2,1,0:T(8,128)S(1)}, f32[2,20,768]{2,1,0:T(8,128)S(1)}, u32[]{:S(2)}, u32[]{:S(2)}) collective-permute-start(f32[2,20,768]{2,1,0:T(8,128)S(1)} %pad_maximum_fusion.3), channel_id=1, source_target_pairs={{0,2},{1,3},{2,0},{3,1},{4,6},{5,7},{6,4},{7,5},{8,10},{9,11},{10,... | collective-permute-start | bytes 368648 | tf_op jit(solution)/shard_map/ppermute | solution.py:18
  40.7 8.3 %collective-permute-start.5 = (f32[2,20,768]{2,1,0:T(8,128)S(1)}, f32[2,20,768]{2,1,0:T(8,128)S(1)}, u32[]{:S(2)}, u32[]{:S(2)}) collective-permute-start(f32[2,20,768]{2,1,0:T(8,128)S(1)} %pad_maximum_fusion.2), channel_id=1, source_target_pairs={{0,2},{1,3},{2,0},{3,1},{4,6},{5,7},{6,4},{7,5},{8,10},{9,11},{10,... | collective-permute-start | bytes 368648 | tf_op jit(solution)/shard_map/ppermute | solution.py:18
  46.3 4.2 %collective-permute-start.10 = (bf16[20,768]{1,0:T(8,128)(2,1)S(1)}, bf16[20,768]{1,0:T(8,128)(2,1)S(1)}, u32[]{:S(2)}, u32[]{:S(2)}) collective-permute-start(bf16[20,768]{1,0:T(8,128)(2,1)S(1)} %fusion.36), channel_id=1, source_target_pairs={{0,2},{1,3},{2,0},{3,1},{4,6},{5,7},{6,4},{7,5},{8,10},{9,11},{10,... | collective-permute-start | bytes 92168 | tf_op jit(solution)/shard_map/ppermute | solution.py:18
  49.0 4.0 %collective-permute-start.6 = (bf16[20,768]{1,0:T(8,128)(2,1)S(1)}, bf16[20,768]{1,0:T(8,128)(2,1)S(1)}, u32[]{:S(2)}, u32[]{:S(2)}) collective-permute-start(bf16[20,768]{1,0:T(8,128)(2,1)S(1)} %fusion.40), channel_id=1, source_target_pairs={{0,2},{1,3},{2,0},{3,1},{4,6},{5,7},{6,4},{7,5},{8,10},{9,11},{10,... | collective-permute-start | bytes 92168 | tf_op jit(solution)/shard_map/ppermute | solution.py:18
  50.5 2.7 %collective-permute-start.11 = (bf16[20,1536]{1,0:T(8,128)(2,1)S(1)}, bf16[20,1536]{1,0:T(8,128)(2,1)S(1)}, u32[]{:S(2)}, u32[]{:S(2)}) collective-permute-start(bf16[20,1536]{1,0:T(8,128)(2,1)S(1)} %maximum_select_fusion.6), channel_id=1, source_target_pairs={{0,1},{1,0},{2,3},{3,2},{4,5},{5,4},{6,7},{7,6},{8,9},{9,8},{10,11... | collective-permute-start | bytes 184328 | tf_op jit(solution)/shard_map/ppermute | solution.py:18
  53.1 5.6 %collective-permute-start.7 = (bf16[20,1536]{1,0:T(8,128)(2,1)S(1)}, bf16[20,1536]{1,0:T(8,128)(2,1)S(1)}, u32[]{:S(2)}, u32[]{:S(2)}) collective-permute-start(bf16[20,1536]{1,0:T(8,128)(2,1)S(1)} %maximum_select_fusion.5), channel_id=1, source_target_pairs={{0,1},{1,0},{2,3},{3,2},{4,5},{5,4},{6,7},{7,6},{8,9},{9,8},{10,11... | collective-permute-start | bytes 184328 | tf_op jit(solution)/shard_map/ppermute | solution.py:18
  64.4 4.5 %collective-permute-start.12 = (f32[5,2048]{1,0:T(8,128)S(1)}, f32[5,2048]{1,0:T(8,128)S(1)}, u32[]{:S(2)}, u32[]{:S(2)}) collective-permute-start(f32[5,2048]{1,0:T(8,128)S(1)} %get-tuple-element.9), channel_id=1, source_target_pairs={{0,4},{4,0},{8,12},{12,8},{1,5},{5,1},{9,13},{13,9},{2,6},{6,2},{1... | collective-permute-start | bytes 122888 | tf_op jit(solution)/shard_map/ppermute | solution.py:59
  65.8 7.1 %collective-permute-start.13 = (f32[5,2048]{1,0:T(8,128)S(1)}, f32[5,2048]{1,0:T(8,128)S(1)}, u32[]{:S(2)}, u32[]{:S(2)}) collective-permute-start(f32[5,2048]{1,0:T(8,128)S(1)} %get-tuple-element.11), channel_id=1, source_target_pairs={{0,8},{4,12},{8,0},{12,4},{1,9},{5,13},{9,1},{13,5},{2,10},{6,14},... | collective-permute-start | bytes 122888 | tf_op jit(solution)/shard_map/ppermute | solution.py:59
  68.6 6.1 %collective-permute-start.14 = (f32[5,2048]{1,0:T(8,128)S(1)}, f32[5,2048]{1,0:T(8,128)S(1)}, u32[]{:S(2)}, u32[]{:S(2)}) collective-permute-start(f32[5,2048]{1,0:T(8,128)S(1)} %get-tuple-element.10), channel_id=1, source_target_pairs={{0,12},{4,8},{8,4},{12,0},{1,13},{5,9},{9,5},{13,1},{2,14},{6,10},... | collective-permute-start | bytes 122888 | tf_op jit(solution)/shard_map/ppermute | solution.py:59

commit v8 on v7

--- a/solution.py
+++ b/solution.py
@@ -1,6 +1,8 @@
 import jax
 import jax.numpy as jnp
 from jax import lax
+from jax.experimental import pallas as pl
+from jax.experimental.pallas import tpu as pltpu
 from jax.sharding import PartitionSpec as P
 
 
@@ -8,6 +10,7 @@
 
 EXCHANGE_MAX = 8
 CHUNKS = 2
+TILE = 768
 
 
 def pairwise(n):
@@ -60,6 +63,31 @@
     return own
 
 
+def gate_up(piece, w_gate, w_up, first_block, blocks, tile):
+    rows, depth = piece.shape
+
+    def kernel(x_ref, g_ref, u_ref, gate_ref, up_ref):
+        x = x_ref[...]
+        gate_ref[...] = jnp.dot(x, g_ref[...], preferred_element_type=jnp.float32)
+        up_ref[...] = jnp.dot(x, u_ref[...], preferred_element_type=jnp.float32)
+
+    weight_spec = pl.BlockSpec((depth, tile), lambda j: (0, first_block + j))
+    out_spec = pl.BlockSpec((rows, tile), lambda j: (0, j))
+    out = jax.ShapeDtypeStruct((rows, blocks * tile), jnp.float32)
+    weight_bytes = 2 * depth * blocks * tile * w_gate.dtype.itemsize
+    return pl.pallas_call(
+        kernel,
+        grid=(blocks,),
+        in_specs=[pl.BlockSpec((rows, depth), lambda j: (0, 0)), weight_spec, weight_spec],
+        out_specs=[out_spec, out_spec],
+        out_shape=[out, out],
+        cost_estimate=pl.CostEstimate(
+            flops=4 * rows * depth * blocks * tile, transcendentals=0,
+            bytes_accessed=weight_bytes + 8 * rows * blocks * tile),
+        compiler_params=pltpu.CompilerParams(vmem_limit_bytes=8 * depth * tile * 2 + (4 << 20)),
+    )(piece, w_gate, w_up)
+
+
 def local(tokens, norm_gain, w_gate, w_up, w_down):
     ngx = lax.axis_size("gx")
     ngy = lax.axis_size("gy")
@@ -84,12 +112,21 @@
     step = width // chunks
     gy_levels = list(range(ngy.bit_length() - 1))
     total = None
+    anchor = None
     for c in range(chunks):
         cols = slice(c * step, (c + 1) * step)
-        gate_part = jnp.dot(piece, w_gate[:, cols], preferred_element_type=jnp.float32)
-        up_part = jnp.dot(piece, w_up[:, cols], preferred_element_type=jnp.float32)
+        rows_in = piece
+        if anchor is not None:
+            rows_in, _ = lax.optimization_barrier((piece, anchor))
+        if step % TILE == 0:
+            gate_part, up_part = gate_up(rows_in, w_gate, w_up, c * step // TILE, step // TILE, TILE)
+        else:
+            gate_part = jnp.dot(rows_in, w_gate[:, cols], preferred_element_type=jnp.float32)
+            up_part = jnp.dot(rows_in, w_up[:, cols], preferred_element_type=jnp.float32)
         if pairwise(ngy):
-            gate, up = xor_reduce_scatter([gate_part, up_part], "gy", ngy, 1, gy_levels)
+            first = xor_reduce_scatter([gate_part, up_part], "gy", ngy, 1, gy_levels[:1])
+            anchor = first[0]
+            gate, up = xor_reduce_scatter(first, "gy", ngy, 1, gy_levels[1:])
         else:
             gate = lax.psum_scatter(gate_part, "gy", scatter_dimension=1, tiled=True)
             up = lax.psum_scatter(up_part, "gy", scatter_dimension=1, tiled=True)

time: 75.6 us -> 90.1 us (1.19)
  matrix products: 31.3 us -> 11.1 us
  Pallas kernels: 0 us -> 16.2 us
  local copies, waits for them, and re-layouts: 0.87 us -> 16.5 us
  starting transfers between devices: 16.9 us -> 18 us
    dot_general x4 -> x0, matrix products: 20.2 us -> none  [the longest x2 12 us: local(): up_part = jnp.dot(piece, w_up[:, cols], preferred_element_type=jnp.float32)]
    pallas_call x0 -> x2, Pallas kernels: none -> 16.2 us  [gate_up(): pl.pallas_call(kernel, grid=(blocks,), in_specs=[pl.BlockSpec((rows, dept...]
    unnamed x4, local copies, waits for them, and re-layouts: 0.73 us -> 16.3 us
    ppermute x12, starting transfers between devices: 12.4 us -> 13.5 us  [exchange(): return lax.ppermute(x, axis, [(a, a ^ 1 << s) for a in range(n)])]
  transfers between devices with their start and end apart: 15 -> 15, of which waited for: 11 -> 12; matrix products, arithmetic and copies ran while one was open for 18% -> 6% of each run, Pallas kernels for 0% -> 0%
where the time goes in v8:
time: 90.1 us; the launch traced here: 89.6 us
  waiting for transfers between devices  24.9 us (28%)
  starting transfers between devices  18 us (20%)
  local copies, waits for them, and re-layouts  16.5 us (18%)
  Pallas kernels  16.2 us (18%)
  matrix products  11.1 us (12%)
  other arithmetic  2.75 us (3%)
    ppermute x12, waiting for transfers between devices, exchange(): return lax.ppermute(x, axis, [(a, a ^ 1 << s) for a in range(n)])  18.8 us
    unnamed x4, local copies, waits for them, and re-layouts  16.3 us
    pallas_call x2, Pallas kernels, gate_up(): pl.pallas_call(kernel, grid=(blocks,), in_specs=[pl.BlockSpec((rows, dept...  16.2 us
    ppermute x12, starting transfers between devices, exchange(): return lax.ppermute(x, axis, [(a, a ^ 1 << s) for a in range(n)])  13.5 us
    dot_general x2, matrix products, local(): jnp.dot(hidden_all, w_down[cols, :], preferred_element_type=jnp.float32)  11.1 us
    ppermute x3, waiting for transfers between devices, fanout_reduce_scatter(): own = own + lax.ppermute(block, axis, [(a, a ^ k) for a in range(n)])  6.12 us
    ppermute x3, starting transfers between devices, fanout_reduce_scatter(): own = own + lax.ppermute(block, axis, [(a, a ^ k) for a in range(n)])  4.45 us
  transfers between devices with their start and end apart: 15, of which 12 were waited for; matrix products, arithmetic and copies ran while one was open for 6% of the time, Pallas kernels for 0%

profile of v8, /device:TPU:0, one launch (start us, length us, event | category | flops | bytes accessed | tf_op | source)
XLA Modules:
  0.0 89.6 jit_solution(10769954096973741371)
XLA Ops:
  0.0 4.0 %collective-permute-start = (bf16[5,2048]{1,0:T(8,128)(2,1)}, bf16[5,2048]{1,0:T(8,128)(2,1)S(1)}, u32[]{:S(2)}, u32[]{:S(2)}) collective-permute-start(bf16[5,2048]{1,0:T(8,128)(2,1)} %param.5), channel_id=1, source_target_pairs={{0,8},{4,12},{8,0},{12,4},{1,9},{5,13},{9,1},{13,5},{2,10},{6,14},... | collective-permute-start | bytes 61448 | tf_op jit(solution)/shard_map/ppermute | solution.py:21
  4.0 2.5 %collective-permute-done = bf16[5,2048]{1,0:T(8,128)(2,1)S(1)} collective-permute-done((bf16[5,2048]{1,0:T(8,128)(2,1)}, bf16[5,2048]{1,0:T(8,128)(2,1)S(1)}, u32[]{:S(2)}, u32[]{:S(2)}) %collective-permute-start) | collective-permute-done | bytes 20512 | tf_op jit(solution)/shard_map/ppermute | solution.py:21
  7.4 1.6 %collective-permute-start.1 = (bf16[10,2048]{1,0:T(8,128)(2,1)S(1)}, bf16[10,2048]{1,0:T(8,128)(2,1)S(1)}, u32[]{:S(2)}, u32[]{:S(2)}) collective-permute-start(bf16[10,2048]{1,0:T(8,128)(2,1)S(1)} %maximum_select_fusion.7), channel_id=1, source_target_pairs={{0,4},{4,0},{8,12},{12,8},{1,5},{5,1},{9,13},{13,9},{2,6},{6,2},{1... | collective-permute-start | bytes 122888 | tf_op jit(solution)/shard_map/ppermute | solution.py:21
  9.0 2.7 %collective-permute-done.1 = bf16[10,2048]{1,0:T(8,128)(2,1)S(1)} collective-permute-done((bf16[10,2048]{1,0:T(8,128)(2,1)S(1)}, bf16[10,2048]{1,0:T(8,128)(2,1)S(1)}, u32[]{:S(2)}, u32[]{:S(2)}) %collective-permute-start.1) | collective-permute-done | bytes 40992 | tf_op jit(solution)/shard_map/ppermute | solution.py:21
  12.0 1.1 %collective-permute-done.2 = f32[20]{0:T(128)S(1)} collective-permute-done((f32[20]{0:T(128)S(1)}, f32[20]{0:T(128)S(1)}, u32[]{:S(2)}, u32[]{:S(2)}) %collective-permute-start.2) | collective-permute-done | bytes 112 | tf_op jit(solution)/shard_map/ppermute | solution.py:21
  13.1 1.7 %collective-permute-start.3 = (f32[20]{0:T(128)S(1)}, f32[20]{0:T(128)S(1)}, u32[]{:S(2)}, u32[]{:S(2)}) collective-permute-start(f32[20]{0:T(128)S(1)} %add.100), channel_id=1, source_target_pairs={{0,2},{1,3},{2,0},{3,1},{4,6},{5,7},{6,4},{7,5},{8,10},{9,11},{10,... | collective-permute-start | bytes 248 | tf_op jit(solution)/shard_map/ppermute | solution.py:21
  14.8 1.8 %collective-permute-done.3 = f32[20]{0:T(128)S(1)} collective-permute-done((f32[20]{0:T(128)S(1)}, f32[20]{0:T(128)S(1)}, u32[]{:S(2)}, u32[]{:S(2)}) %collective-permute-start.3) | collective-permute-done | bytes 112 | tf_op jit(solution)/shard_map/ppermute | solution.py:21
  17.4 8.1 %copy-done = bf16[2048,6144]{1,0:T(8,128)(2,1)S(1)} copy-done((bf16[2048,6144]{1,0:T(8,128)(2,1)S(1)}, bf16[2048,6144]{1,0:T(8,128)(2,1)}, u32[]{:S(2)}) %copy-start) | copy-done | bytes 25165848
  25.6 8.1 %shard_map.55 = (f32[20,3072]{1,0:T(8,128)S(1)}, f32[20,3072]{1,0:T(8,128)S(1)}) custom-call(bf16[20,2048]{1,0:T(8,128)(2,1)S(1)} %fusion.9.x_ref, bf16[2048,6144]{1,0:T(8,128)(2,1)S(1)} %copy-done, bf16[2048,6144]{1,0:T(8,128)(2,1)} %u_ref.3), custom_call_target="tpu_custom_call" | custom-call | flops 503316480 | bytes 25657344 | tf_op jit(solution)/shard_map/pallas_call | solution.py:78
  33.8 1.6 %collective-permute-done.4 = f32[2,20,1536]{2,1,0:T(8,128)S(1)} collective-permute-done((f32[2,20,1536]{2,1,0:T(8,128)S(1)}, f32[2,20,1536]{2,1,0:T(8,128)S(1)}, u32[]{:S(2)}, u32[]{:S(2)}) %collective-permute-start.4) | collective-permute-done | bytes 245792 | tf_op jit(solution)/shard_map/ppermute | solution.py:21
  35.4 8.1 %copy-done.1 = bf16[2048,6144]{1,0:T(8,128)(2,1)S(1)} copy-done((bf16[2048,6144]{1,0:T(8,128)(2,1)S(1)}, bf16[2048,6144]{1,0:T(8,128)(2,1)}, u32[]{:S(2)}) %copy-start.1) | copy-done | bytes 25165848
  43.6 8.1 %shard_map.56 = (f32[20,3072]{1,0:T(8,128)S(1)}, f32[20,3072]{1,0:T(8,128)S(1)}) custom-call(bf16[20,2048]{1,0:T(8,128)(2,1)S(1)} %fusion.9.x_ref, bf16[2048,6144]{1,0:T(8,128)(2,1)S(1)} %copy-done.1, bf16[2048,6144]{1,0:T(8,128)(2,1)} %u_ref.3), custom_call_target="tpu_custom_call" | custom-call | flops 503316480 | bytes 25657344 | tf_op jit(solution)/shard_map/pallas_call | solution.py:78
  52.0 1.4 %collective-permute-done.8 = f32[2,20,1536]{2,1,0:T(8,128)S(1)} collective-permute-done((f32[2,20,1536]{2,1,0:T(8,128)S(1)}, f32[2,20,1536]{2,1,0:T(8,128)S(1)}, u32[]{:S(2)}, u32[]{:S(2)}) %collective-permute-start.8) | collective-permute-done | bytes 245792 | tf_op jit(solution)/shard_map/ppermute | solution.py:21
  53.6 1.8 %collective-permute-start.9 = (f32[2,20,768]{2,1,0:T(8,128)S(1)}, f32[2,20,768]{2,1,0:T(8,128)S(1)}, u32[]{:S(2)}, u32[]{:S(2)}) collective-permute-start(f32[2,20,768]{2,1,0:T(8,128)S(1)} %pad_maximum_fusion.3), channel_id=1, source_target_pairs={{0,2},{1,3},{2,0},{3,1},{4,6},{5,7},{6,4},{7,5},{8,10},{9,11},{10,... | collective-permute-start | bytes 368648 | tf_op jit(solution)/shard_map/ppermute | solution.py:21
  55.7 4.6 %collective-permute-done.9 = f32[2,20,768]{2,1,0:T(8,128)S(1)} collective-permute-done((f32[2,20,768]{2,1,0:T(8,128)S(1)}, f32[2,20,768]{2,1,0:T(8,128)S(1)}, u32[]{:S(2)}, u32[]{:S(2)}) %collective-permute-start.9) | collective-permute-done | bytes 122912 | tf_op jit(solution)/shard_map/ppermute | solution.py:21
  60.4 1.8 %collective-permute-start.10 = (bf16[20,768]{1,0:T(8,128)(2,1)S(1)}, bf16[20,768]{1,0:T(8,128)(2,1)S(1)}, u32[]{:S(2)}, u32[]{:S(2)}) collective-permute-start(bf16[20,768]{1,0:T(8,128)(2,1)S(1)} %fusion.28), channel_id=1, source_target_pairs={{0,2},{1,3},{2,0},{3,1},{4,6},{5,7},{6,4},{7,5},{8,10},{9,11},{10,... | collective-permute-start | bytes 92168 | tf_op jit(solution)/shard_map/ppermute | solution.py:21
  63.1 1.8 %collective-permute-start.6 = (bf16[20,768]{1,0:T(8,128)(2,1)S(1)}, bf16[20,768]{1,0:T(8,128)(2,1)S(1)}, u32[]{:S(2)}, u32[]{:S(2)}) collective-permute-start(bf16[20,768]{1,0:T(8,128)(2,1)S(1)} %fusion.32), channel_id=1, source_target_pairs={{0,2},{1,3},{2,0},{3,1},{4,6},{5,7},{6,4},{7,5},{8,10},{9,11},{10,... | collective-permute-start | bytes 92168 | tf_op jit(solution)/shard_map/ppermute | solution.py:21
  65.0 2.2 %collective-permute-done.6 = bf16[20,768]{1,0:T(8,128)(2,1)S(1)} collective-permute-done((bf16[20,768]{1,0:T(8,128)(2,1)S(1)}, bf16[20,768]{1,0:T(8,128)(2,1)S(1)}, u32[]{:S(2)}, u32[]{:S(2)}) %collective-permute-start.6) | collective-permute-done | bytes 30752 | tf_op jit(solution)/shard_map/ppermute | solution.py:21
  67.2 5.6 %fusion = f32[20,2048]{1,0:T(8,128)S(1)} fusion(bf16[6144,2048]{1,0:T(8,128)(2,1)} %param.9, bf16[20,1536]{1,0:T(8,128)(2,1)S(1)} %collective-permute-done.11, bf16[20,1536]{1,0:T(8,128)(2,1)S(1)} %maximum_select_fusion.6, pred[]{:T(512)S(6)} %eq.14), kind=kOutput, calls=%fused_computation | convolution fusion | flops 252211200 | bytes 12869633 | tf_op jit(solution)/shard_map/dot_general | solution.py:138
  72.8 5.6 %fusion.4 = f32[20,2048]{1,0:T(8,128)S(1)} fusion(f32[20,2048]{1,0:T(8,128)S(1)} %fusion, bf16[6144,2048]{1,0:T(8,128)(2,1)} %param.9, bf16[20,1536]{1,0:T(8,128)(2,1)S(1)} %collective-permute-done.7, bf16[20,1536]{1,0:T(8,128)(2,1)S(1)} %maximum_select_fusion.5, pred[]{:T(512)S(6)} %eq.14), kind=kOutput, calls=%fused_computation.4 | convolution fusion | flops 252252160 | bytes 13033473 | tf_op jit(solution)/shard_map/dot_general | solution.py:138
  78.4 1.6 %collective-permute-start.12 = (f32[5,2048]{1,0:T(8,128)S(1)}, f32[5,2048]{1,0:T(8,128)S(1)}, u32[]{:S(2)}, u32[]{:S(2)}) collective-permute-start(f32[5,2048]{1,0:T(8,128)S(1)} %get-tuple-element.19), channel_id=1, source_target_pairs={{0,4},{4,0},{8,12},{12,8},{1,5},{5,1},{9,13},{13,9},{2,6},{6,2},{1... | collective-permute-start | bytes 122888 | tf_op jit(solution)/shard_map/ppermute | solution.py:62
  80.1 2.8 %collective-permute-start.13 = (f32[5,2048]{1,0:T(8,128)S(1)}, f32[5,2048]{1,0:T(8,128)S(1)}, u32[]{:S(2)}, u32[]{:S(2)}) collective-permute-start(f32[5,2048]{1,0:T(8,128)S(1)} %get-tuple-element.21), channel_id=1, source_target_pairs={{0,8},{4,12},{8,0},{12,4},{1,9},{5,13},{9,1},{13,5},{2,10},{6,14},... | collective-permute-start | bytes 122888 | tf_op jit(solution)/shard_map/ppermute | solution.py:62
  83.0 4.2 %collective-permute-done.13 = f32[5,2048]{1,0:T(8,128)S(1)} collective-permute-done((f32[5,2048]{1,0:T(8,128)S(1)}, f32[5,2048]{1,0:T(8,128)S(1)}, u32[]{:S(2)}, u32[]{:S(2)}) %collective-permute-start.13) | collective-permute-done | bytes 40992 | tf_op jit(solution)/shard_map/ppermute | solution.py:62
  87.1 1.9 %collective-permute-done.14 = f32[5,2048]{1,0:T(8,128)S(1)} collective-permute-done((f32[5,2048]{1,0:T(8,128)S(1)}, f32[5,2048]{1,0:T(8,128)S(1)}, u32[]{:S(2)}, u32[]{:S(2)}) %collective-permute-start.14) | collective-permute-done | bytes 40992 | tf_op jit(solution)/shard_map/ppermute | solution.py:62
  (38 shorter events, 4.8 us)
Async XLA Ops:
  0.0 6.5 %collective-permute-start = (bf16[5,2048]{1,0:T(8,128)(2,1)}, bf16[5,2048]{1,0:T(8,128)(2,1)S(1)}, u32[]{:S(2)}, u32[]{:S(2)}) collective-permute-start(bf16[5,2048]{1,0:T(8,128)(2,1)} %param.5), channel_id=1, source_target_pairs={{0,8},{4,12},{8,0},{12,4},{1,9},{5,13},{9,1},{13,5},{2,10},{6,14},... | collective-permute-start | bytes 61448 | tf_op jit(solution)/shard_map/ppermute | solution.py:21
  7.4 4.3 %collective-permute-start.1 = (bf16[10,2048]{1,0:T(8,128)(2,1)S(1)}, bf16[10,2048]{1,0:T(8,128)(2,1)S(1)}, u32[]{:S(2)}, u32[]{:S(2)}) collective-permute-start(bf16[10,2048]{1,0:T(8,128)(2,1)S(1)} %maximum_select_fusion.7), channel_id=1, source_target_pairs={{0,4},{4,0},{8,12},{12,8},{1,5},{5,1},{9,13},{13,9},{2,6},{6,2},{1... | collective-permute-start | bytes 122888 | tf_op jit(solution)/shard_map/ppermute | solution.py:21
  11.9 1.2 %collective-permute-start.2 = (f32[20]{0:T(128)S(1)}, f32[20]{0:T(128)S(1)}, u32[]{:S(2)}, u32[]{:S(2)}) collective-permute-start(f32[20]{0:T(128)S(1)} %fusion.7), channel_id=1, source_target_pairs={{0,1},{1,0},{2,3},{3,2},{4,5},{5,4},{6,7},{7,6},{8,9},{9,8},{10,11... | collective-permute-start | bytes 248 | tf_op jit(solution)/shard_map/ppermute | solution.py:21
  13.1 3.5 %collective-permute-start.3 = (f32[20]{0:T(128)S(1)}, f32[20]{0:T(128)S(1)}, u32[]{:S(2)}, u32[]{:S(2)}) collective-permute-start(f32[20]{0:T(128)S(1)} %add.100), channel_id=1, source_target_pairs={{0,2},{1,3},{2,0},{3,1},{4,6},{5,7},{6,4},{7,5},{8,10},{9,11},{10,... | collective-permute-start | bytes 248 | tf_op jit(solution)/shard_map/ppermute | solution.py:21
  17.4 8.2 %copy-start = (bf16[2048,6144]{1,0:T(8,128)(2,1)S(1)}, bf16[2048,6144]{1,0:T(8,128)(2,1)}, u32[]{:S(2)}) copy-start(bf16[2048,6144]{1,0:T(8,128)(2,1)} %g_ref.3) | copy-start | bytes 75497472
  33.7 1.6 %collective-permute-start.4 = (f32[2,20,1536]{2,1,0:T(8,128)S(1)}, f32[2,20,1536]{2,1,0:T(8,128)S(1)}, u32[]{:S(2)}, u32[]{:S(2)}) collective-permute-start(f32[2,20,1536]{2,1,0:T(8,128)S(1)} %pad_maximum_fusion), channel_id=1, source_target_pairs={{0,1},{1,0},{2,3},{3,2},{4,5},{5,4},{6,7},{7,6},{8,9},{9,8},{10,11... | collective-permute-start | bytes 737288 | tf_op jit(solution)/shard_map/ppermute | solution.py:21
  35.4 8.2 %copy-start.1 = (bf16[2048,6144]{1,0:T(8,128)(2,1)S(1)}, bf16[2048,6144]{1,0:T(8,128)(2,1)}, u32[]{:S(2)}) copy-start(bf16[2048,6144]{1,0:T(8,128)(2,1)} %g_ref.3) | copy-start | bytes 75497472
  51.8 1.6 %collective-permute-start.8 = (f32[2,20,1536]{2,1,0:T(8,128)S(1)}, f32[2,20,1536]{2,1,0:T(8,128)S(1)}, u32[]{:S(2)}, u32[]{:S(2)}) collective-permute-start(f32[2,20,1536]{2,1,0:T(8,128)S(1)} %pad_maximum_fusion.1), channel_id=1, source_target_pairs={{0,1},{1,0},{2,3},{3,2},{4,5},{5,4},{6,7},{7,6},{8,9},{9,8},{10,11... | collective-permute-start | bytes 737288 | tf_op jit(solution)/shard_map/ppermute | solution.py:21
  53.6 6.8 %collective-permute-start.9 = (f32[2,20,768]{2,1,0:T(8,128)S(1)}, f32[2,20,768]{2,1,0:T(8,128)S(1)}, u32[]{:S(2)}, u32[]{:S(2)}) collective-permute-start(f32[2,20,768]{2,1,0:T(8,128)S(1)} %pad_maximum_fusion.3), channel_id=1, source_target_pairs={{0,2},{1,3},{2,0},{3,1},{4,6},{5,7},{6,4},{7,5},{8,10},{9,11},{10,... | collective-permute-start | bytes 368648 | tf_op jit(solution)/shard_map/ppermute | solution.py:21
  55.3 7.7 %collective-permute-start.5 = (f32[2,20,768]{2,1,0:T(8,128)S(1)}, f32[2,20,768]{2,1,0:T(8,128)S(1)}, u32[]{:S(2)}, u32[]{:S(2)}) collective-permute-start(f32[2,20,768]{2,1,0:T(8,128)S(1)} %pad_maximum_fusion.2), channel_id=1, source_target_pairs={{0,2},{1,3},{2,0},{3,1},{4,6},{5,7},{6,4},{7,5},{8,10},{9,11},{10,... | collective-permute-start | bytes 368648 | tf_op jit(solution)/shard_map/ppermute | solution.py:21
  60.4 4.5 %collective-permute-start.10 = (bf16[20,768]{1,0:T(8,128)(2,1)S(1)}, bf16[20,768]{1,0:T(8,128)(2,1)S(1)}, u32[]{:S(2)}, u32[]{:S(2)}) collective-permute-start(bf16[20,768]{1,0:T(8,128)(2,1)S(1)} %fusion.28), channel_id=1, source_target_pairs={{0,2},{1,3},{2,0},{3,1},{4,6},{5,7},{6,4},{7,5},{8,10},{9,11},{10,... | collective-permute-start | bytes 92168 | tf_op jit(solution)/shard_map/ppermute | solution.py:21
  63.1 4.0 %collective-permute-start.6 = (bf16[20,768]{1,0:T(8,128)(2,1)S(1)}, bf16[20,768]{1,0:T(8,128)(2,1)S(1)}, u32[]{:S(2)}, u32[]{:S(2)}) collective-permute-start(bf16[20,768]{1,0:T(8,128)(2,1)S(1)} %fusion.32), channel_id=1, source_target_pairs={{0,2},{1,3},{2,0},{3,1},{4,6},{5,7},{6,4},{7,5},{8,10},{9,11},{10,... | collective-permute-start | bytes 92168 | tf_op jit(solution)/shard_map/ppermute | solution.py:21
  64.9 2.3 %collective-permute-start.11 = (bf16[20,1536]{1,0:T(8,128)(2,1)S(1)}, bf16[20,1536]{1,0:T(8,128)(2,1)S(1)}, u32[]{:S(2)}, u32[]{:S(2)}) collective-permute-start(bf16[20,1536]{1,0:T(8,128)(2,1)S(1)} %maximum_select_fusion.6), channel_id=1, source_target_pairs={{0,1},{1,0},{2,3},{3,2},{4,5},{5,4},{6,7},{7,6},{8,9},{9,8},{10,11... | collective-permute-start | bytes 184328 | tf_op jit(solution)/shard_map/ppermute | solution.py:21
  67.2 5.7 %collective-permute-start.7 = (bf16[20,1536]{1,0:T(8,128)(2,1)S(1)}, bf16[20,1536]{1,0:T(8,128)(2,1)S(1)}, u32[]{:S(2)}, u32[]{:S(2)}) collective-permute-start(bf16[20,1536]{1,0:T(8,128)(2,1)S(1)} %maximum_select_fusion.5), channel_id=1, source_target_pairs={{0,1},{1,0},{2,3},{3,2},{4,5},{5,4},{6,7},{7,6},{8,9},{9,8},{10,11... | collective-permute-start | bytes 184328 | tf_op jit(solution)/shard_map/ppermute | solution.py:21
  78.4 4.5 %collective-permute-start.12 = (f32[5,2048]{1,0:T(8,128)S(1)}, f32[5,2048]{1,0:T(8,128)S(1)}, u32[]{:S(2)}, u32[]{:S(2)}) collective-permute-start(f32[5,2048]{1,0:T(8,128)S(1)} %get-tuple-element.19), channel_id=1, source_target_pairs={{0,4},{4,0},{8,12},{12,8},{1,5},{5,1},{9,13},{13,9},{2,6},{6,2},{1... | collective-permute-start | bytes 122888 | tf_op jit(solution)/shard_map/ppermute | solution.py:62
  80.1 7.1 %collective-permute-start.13 = (f32[5,2048]{1,0:T(8,128)S(1)}, f32[5,2048]{1,0:T(8,128)S(1)}, u32[]{:S(2)}, u32[]{:S(2)}) collective-permute-start(f32[5,2048]{1,0:T(8,128)S(1)} %get-tuple-element.21), channel_id=1, source_target_pairs={{0,8},{4,12},{8,0},{12,4},{1,9},{5,13},{9,1},{13,5},{2,10},{6,14},... | collective-permute-start | bytes 122888 | tf_op jit(solution)/shard_map/ppermute | solution.py:62
  82.9 6.1 %collective-permute-start.14 = (f32[5,2048]{1,0:T(8,128)S(1)}, f32[5,2048]{1,0:T(8,128)S(1)}, u32[]{:S(2)}, u32[]{:S(2)}) collective-permute-start(f32[5,2048]{1,0:T(8,128)S(1)} %get-tuple-element.20), channel_id=1, source_target_pairs={{0,12},{4,8},{8,4},{12,0},{1,13},{5,9},{9,5},{13,1},{2,14},{6,10},... | collective-permute-start | bytes 122888 | tf_op jit(solution)/shard_map/ppermute | solution.py:62

commit v9 on v8

--- a/solution.py
+++ b/solution.py
@@ -85,7 +85,8 @@
             flops=4 * rows * depth * blocks * tile, transcendentals=0,
             bytes_accessed=weight_bytes + 8 * rows * blocks * tile),
         compiler_params=pltpu.CompilerParams(vmem_limit_bytes=8 * depth * tile * 2 + (4 << 20)),
-    )(piece, w_gate, w_up)
+    )(piece, pltpu.with_memory_space_constraint(w_gate, pltpu.HBM),
+      pltpu.with_memory_space_constraint(w_up, pltpu.HBM))
 
 
 def local(tokens, norm_gain, w_gate, w_up, w_down):

time: 90.1 us -> 77.6 us (0.86)
  local copies, waits for them, and re-layouts: 16.5 us -> 0.15 us
  Pallas kernels: 16.2 us -> 20.3 us
    unnamed x4 -> x0, local copies, waits for them, and re-layouts: 16.3 us -> none
    pallas_call x2, Pallas kernels: 16.2 us -> 20.3 us  [gate_up(): pl.pallas_call(kernel, grid=(blocks,), in_specs=[pl.BlockSpec((rows, dept...]
  transfers between devices with their start and end apart: 15 -> 15, of which waited for: 12 -> 12; matrix products, arithmetic and copies ran while one was open for 6% -> 7% of each run, Pallas kernels for 0% -> 0%
where the time goes in v9:
time: 77.6 us; the launch traced here: 77.4 us
  waiting for transfers between devices  24.9 us (32%)
  Pallas kernels  20.3 us (26%)
  starting transfers between devices  18 us (23%)
  matrix products  11.1 us (14%)
  other arithmetic  2.75 us (4%)
    pallas_call x2, Pallas kernels, gate_up(): pl.pallas_call(kernel, grid=(blocks,), in_specs=[pl.BlockSpec((rows, dept...  20.3 us
    ppermute x12, waiting for transfers between devices, exchange(): return lax.ppermute(x, axis, [(a, a ^ 1 << s) for a in range(n)])  18.8 us
    ppermute x12, starting transfers between devices, exchange(): return lax.ppermute(x, axis, [(a, a ^ 1 << s) for a in range(n)])  13.5 us
    dot_general x2, matrix products, local(): jnp.dot(hidden_all, w_down[cols, :], preferred_element_type=jnp.float32)  11.1 us
    ppermute x3, waiting for transfers between devices, fanout_reduce_scatter(): own = own + lax.ppermute(block, axis, [(a, a ^ k) for a in range(n)])  6.12 us
    ppermute x3, starting transfers between devices, fanout_reduce_scatter(): own = own + lax.ppermute(block, axis, [(a, a ^ k) for a in range(n)])  4.45 us
  transfers between devices with their start and end apart: 15, of which 12 were waited for; matrix products, arithmetic and copies ran while one was open for 7% of the time, Pallas kernels for 0%

profile of v9, /device:TPU:0, one launch (start us, length us, event | category | flops | bytes accessed | tf_op | source)
XLA Modules:
  0.0 77.4 jit_solution(13222143516555059378)
XLA Ops:
  0.0 4.0 %collective-permute-start = (bf16[5,2048]{1,0:T(8,128)(2,1)}, bf16[5,2048]{1,0:T(8,128)(2,1)S(1)}, u32[]{:S(2)}, u32[]{:S(2)}) collective-permute-start(bf16[5,2048]{1,0:T(8,128)(2,1)} %param.5), channel_id=1, source_target_pairs={{0,8},{4,12},{8,0},{12,4},{1,9},{5,13},{9,1},{13,5},{2,10},{6,14},... | collective-permute-start | bytes 61448 | tf_op jit(solution)/shard_map/ppermute | solution.py:21
  4.0 2.5 %collective-permute-done = bf16[5,2048]{1,0:T(8,128)(2,1)S(1)} collective-permute-done((bf16[5,2048]{1,0:T(8,128)(2,1)}, bf16[5,2048]{1,0:T(8,128)(2,1)S(1)}, u32[]{:S(2)}, u32[]{:S(2)}) %collective-permute-start) | collective-permute-done | bytes 20512 | tf_op jit(solution)/shard_map/ppermute | solution.py:21
  6.5 0.9 %maximum_select_fusion.7 = bf16[10,2048]{1,0:T(8,128)(2,1)S(1)} fusion(bf16[5,2048]{1,0:T(8,128)(2,1)S(1)} %collective-permute-done, bf16[5,2048]{1,0:T(8,128)(2,1)} %param.5, pred[]{:T(512)S(6)} %eq.17), kind=kLoop, calls=%fused_computation.59 | loop fusion | flops 184320 | bytes 81921 | tf_op jit(solution)/shard_map/jit(_where)/select_n | solution.py:42
  7.4 1.6 %collective-permute-start.1 = (bf16[10,2048]{1,0:T(8,128)(2,1)S(1)}, bf16[10,2048]{1,0:T(8,128)(2,1)S(1)}, u32[]{:S(2)}, u32[]{:S(2)}) collective-permute-start(bf16[10,2048]{1,0:T(8,128)(2,1)S(1)} %maximum_select_fusion.7), channel_id=1, source_target_pairs={{0,4},{4,0},{8,12},{12,8},{1,5},{5,1},{9,13},{13,9},{2,6},{6,2},{1... | collective-permute-start | bytes 122888 | tf_op jit(solution)/shard_map/ppermute | solution.py:21
  9.0 2.7 %collective-permute-done.1 = bf16[10,2048]{1,0:T(8,128)(2,1)S(1)} collective-permute-done((bf16[10,2048]{1,0:T(8,128)(2,1)S(1)}, bf16[10,2048]{1,0:T(8,128)(2,1)S(1)}, u32[]{:S(2)}, u32[]{:S(2)}) %collective-permute-start.1) | collective-permute-done | bytes 40992 | tf_op jit(solution)/shard_map/ppermute | solution.py:21
  12.0 1.1 %collective-permute-done.2 = f32[20]{0:T(128)S(1)} collective-permute-done((f32[20]{0:T(128)S(1)}, f32[20]{0:T(128)S(1)}, u32[]{:S(2)}, u32[]{:S(2)}) %collective-permute-start.2) | collective-permute-done | bytes 112 | tf_op jit(solution)/shard_map/ppermute | solution.py:21
  13.1 1.7 %collective-permute-start.3 = (f32[20]{0:T(128)S(1)}, f32[20]{0:T(128)S(1)}, u32[]{:S(2)}, u32[]{:S(2)}) collective-permute-start(f32[20]{0:T(128)S(1)} %add.100), channel_id=1, source_target_pairs={{0,2},{1,3},{2,0},{3,1},{4,6},{5,7},{6,4},{7,5},{8,10},{9,11},{10,... | collective-permute-start | bytes 248 | tf_op jit(solution)/shard_map/ppermute | solution.py:21
  14.8 1.8 %collective-permute-done.3 = f32[20]{0:T(128)S(1)} collective-permute-done((f32[20]{0:T(128)S(1)}, f32[20]{0:T(128)S(1)}, u32[]{:S(2)}, u32[]{:S(2)}) %collective-permute-start.3) | collective-permute-done | bytes 112 | tf_op jit(solution)/shard_map/ppermute | solution.py:21
  17.4 10.1 %shard_map.55 = (f32[20,3072]{1,0:T(8,128)S(1)}, f32[20,3072]{1,0:T(8,128)S(1)}) custom-call(bf16[20,2048]{1,0:T(8,128)(2,1)S(1)} %fusion.9.x_ref, bf16[2048,6144]{1,0:T(8,128)(2,1)} %g_ref.3, bf16[2048,6144]{1,0:T(8,128)(2,1)} %u_ref.3), custom_call_target="tpu_custom_call" | custom-call | flops 503316480 | bytes 25657344 | tf_op jit(solution)/shard_map/pallas_call | solution.py:78
  27.7 1.6 %collective-permute-done.4 = f32[2,20,1536]{2,1,0:T(8,128)S(1)} collective-permute-done((f32[2,20,1536]{2,1,0:T(8,128)S(1)}, f32[2,20,1536]{2,1,0:T(8,128)S(1)}, u32[]{:S(2)}, u32[]{:S(2)}) %collective-permute-start.4) | collective-permute-done | bytes 245792 | tf_op jit(solution)/shard_map/ppermute | solution.py:21
  29.3 10.2 %shard_map.56 = (f32[20,3072]{1,0:T(8,128)S(1)}, f32[20,3072]{1,0:T(8,128)S(1)}) custom-call(bf16[20,2048]{1,0:T(8,128)(2,1)S(1)} %fusion.9.x_ref, bf16[2048,6144]{1,0:T(8,128)(2,1)} %g_ref.3, bf16[2048,6144]{1,0:T(8,128)(2,1)} %u_ref.3), custom_call_target="tpu_custom_call" | custom-call | flops 503316480 | bytes 25657344 | tf_op jit(solution)/shard_map/pallas_call | solution.py:78
  39.8 1.4 %collective-permute-done.8 = f32[2,20,1536]{2,1,0:T(8,128)S(1)} collective-permute-done((f32[2,20,1536]{2,1,0:T(8,128)S(1)}, f32[2,20,1536]{2,1,0:T(8,128)S(1)}, u32[]{:S(2)}, u32[]{:S(2)}) %collective-permute-start.8) | collective-permute-done | bytes 245792 | tf_op jit(solution)/shard_map/ppermute | solution.py:21
  41.3 1.8 %collective-permute-start.9 = (f32[2,20,768]{2,1,0:T(8,128)S(1)}, f32[2,20,768]{2,1,0:T(8,128)S(1)}, u32[]{:S(2)}, u32[]{:S(2)}) collective-permute-start(f32[2,20,768]{2,1,0:T(8,128)S(1)} %pad_maximum_fusion.3), channel_id=1, source_target_pairs={{0,2},{1,3},{2,0},{3,1},{4,6},{5,7},{6,4},{7,5},{8,10},{9,11},{10,... | collective-permute-start | bytes 368648 | tf_op jit(solution)/shard_map/ppermute | solution.py:21
  43.5 4.6 %collective-permute-done.9 = f32[2,20,768]{2,1,0:T(8,128)S(1)} collective-permute-done((f32[2,20,768]{2,1,0:T(8,128)S(1)}, f32[2,20,768]{2,1,0:T(8,128)S(1)}, u32[]{:S(2)}, u32[]{:S(2)}) %collective-permute-start.9) | collective-permute-done | bytes 122912 | tf_op jit(solution)/shard_map/ppermute | solution.py:21
  48.1 1.8 %collective-permute-start.10 = (bf16[20,768]{1,0:T(8,128)(2,1)S(1)}, bf16[20,768]{1,0:T(8,128)(2,1)S(1)}, u32[]{:S(2)}, u32[]{:S(2)}) collective-permute-start(bf16[20,768]{1,0:T(8,128)(2,1)S(1)} %fusion.28), channel_id=1, source_target_pairs={{0,2},{1,3},{2,0},{3,1},{4,6},{5,7},{6,4},{7,5},{8,10},{9,11},{10,... | collective-permute-start | bytes 92168 | tf_op jit(solution)/shard_map/ppermute | solution.py:21
  49.9 0.9 %collective-permute-done.5 = f32[2,20,768]{2,1,0:T(8,128)S(1)} collective-permute-done((f32[2,20,768]{2,1,0:T(8,128)S(1)}, f32[2,20,768]{2,1,0:T(8,128)S(1)}, u32[]{:S(2)}, u32[]{:S(2)}) %collective-permute-start.5) | collective-permute-done | bytes 122912 | tf_op jit(solution)/shard_map/ppermute | solution.py:21
  50.9 1.8 %collective-permute-start.6 = (bf16[20,768]{1,0:T(8,128)(2,1)S(1)}, bf16[20,768]{1,0:T(8,128)(2,1)S(1)}, u32[]{:S(2)}, u32[]{:S(2)}) collective-permute-start(bf16[20,768]{1,0:T(8,128)(2,1)S(1)} %fusion.32), channel_id=1, source_target_pairs={{0,2},{1,3},{2,0},{3,1},{4,6},{5,7},{6,4},{7,5},{8,10},{9,11},{10,... | collective-permute-start | bytes 92168 | tf_op jit(solution)/shard_map/ppermute | solution.py:21
  52.7 2.2 %collective-permute-done.6 = bf16[20,768]{1,0:T(8,128)(2,1)S(1)} collective-permute-done((bf16[20,768]{1,0:T(8,128)(2,1)S(1)}, bf16[20,768]{1,0:T(8,128)(2,1)S(1)}, u32[]{:S(2)}, u32[]{:S(2)}) %collective-permute-start.6) | collective-permute-done | bytes 30752 | tf_op jit(solution)/shard_map/ppermute | solution.py:21
  55.0 5.6 %fusion = f32[20,2048]{1,0:T(8,128)S(1)} fusion(bf16[6144,2048]{1,0:T(8,128)(2,1)} %param.9, bf16[20,1536]{1,0:T(8,128)(2,1)S(1)} %collective-permute-done.11, bf16[20,1536]{1,0:T(8,128)(2,1)S(1)} %maximum_select_fusion.6, pred[]{:T(512)S(6)} %eq.14), kind=kOutput, calls=%fused_computation | convolution fusion | flops 252211200 | bytes 12869633 | tf_op jit(solution)/shard_map/dot_general | solution.py:139
  60.6 5.6 %fusion.4 = f32[20,2048]{1,0:T(8,128)S(1)} fusion(f32[20,2048]{1,0:T(8,128)S(1)} %fusion, bf16[6144,2048]{1,0:T(8,128)(2,1)} %param.9, bf16[20,1536]{1,0:T(8,128)(2,1)S(1)} %collective-permute-done.7, bf16[20,1536]{1,0:T(8,128)(2,1)S(1)} %maximum_select_fusion.5, pred[]{:T(512)S(6)} %eq.14), kind=kOutput, calls=%fused_computation.4 | convolution fusion | flops 252252160 | bytes 13033473 | tf_op jit(solution)/shard_map/dot_general | solution.py:139
  66.2 1.6 %collective-permute-start.12 = (f32[5,2048]{1,0:T(8,128)S(1)}, f32[5,2048]{1,0:T(8,128)S(1)}, u32[]{:S(2)}, u32[]{:S(2)}) collective-permute-start(f32[5,2048]{1,0:T(8,128)S(1)} %get-tuple-element.19), channel_id=1, source_target_pairs={{0,4},{4,0},{8,12},{12,8},{1,5},{5,1},{9,13},{13,9},{2,6},{6,2},{1... | collective-permute-start | bytes 122888 | tf_op jit(solution)/shard_map/ppermute | solution.py:62
  67.8 2.8 %collective-permute-start.13 = (f32[5,2048]{1,0:T(8,128)S(1)}, f32[5,2048]{1,0:T(8,128)S(1)}, u32[]{:S(2)}, u32[]{:S(2)}) collective-permute-start(f32[5,2048]{1,0:T(8,128)S(1)} %get-tuple-element.21), channel_id=1, source_target_pairs={{0,8},{4,12},{8,0},{12,4},{1,9},{5,13},{9,1},{13,5},{2,10},{6,14},... | collective-permute-start | bytes 122888 | tf_op jit(solution)/shard_map/ppermute | solution.py:62
  70.7 4.2 %collective-permute-done.13 = f32[5,2048]{1,0:T(8,128)S(1)} collective-permute-done((f32[5,2048]{1,0:T(8,128)S(1)}, f32[5,2048]{1,0:T(8,128)S(1)}, u32[]{:S(2)}, u32[]{:S(2)}) %collective-permute-start.13) | collective-permute-done | bytes 40992 | tf_op jit(solution)/shard_map/ppermute | solution.py:62
  74.9 1.9 %collective-permute-done.14 = f32[5,2048]{1,0:T(8,128)S(1)} collective-permute-done((f32[5,2048]{1,0:T(8,128)S(1)}, f32[5,2048]{1,0:T(8,128)S(1)}, u32[]{:S(2)}, u32[]{:S(2)}) %collective-permute-start.14) | collective-permute-done | bytes 40992 | tf_op jit(solution)/shard_map/ppermute | solution.py:62
  (34 shorter events, 3.0 us)
Async XLA Ops:
  0.0 6.5 %collective-permute-start = (bf16[5,2048]{1,0:T(8,128)(2,1)}, bf16[5,2048]{1,0:T(8,128)(2,1)S(1)}, u32[]{:S(2)}, u32[]{:S(2)}) collective-permute-start(bf16[5,2048]{1,0:T(8,128)(2,1)} %param.5), channel_id=1, source_target_pairs={{0,8},{4,12},{8,0},{12,4},{1,9},{5,13},{9,1},{13,5},{2,10},{6,14},... | collective-permute-start | bytes 61448 | tf_op jit(solution)/shard_map/ppermute | solution.py:21
  7.4 4.3 %collective-permute-start.1 = (bf16[10,2048]{1,0:T(8,128)(2,1)S(1)}, bf16[10,2048]{1,0:T(8,128)(2,1)S(1)}, u32[]{:S(2)}, u32[]{:S(2)}) collective-permute-start(bf16[10,2048]{1,0:T(8,128)(2,1)S(1)} %maximum_select_fusion.7), channel_id=1, source_target_pairs={{0,4},{4,0},{8,12},{12,8},{1,5},{5,1},{9,13},{13,9},{2,6},{6,2},{1... | collective-permute-start | bytes 122888 | tf_op jit(solution)/shard_map/ppermute | solution.py:21
  11.9 1.2 %collective-permute-start.2 = (f32[20]{0:T(128)S(1)}, f32[20]{0:T(128)S(1)}, u32[]{:S(2)}, u32[]{:S(2)}) collective-permute-start(f32[20]{0:T(128)S(1)} %fusion.7), channel_id=1, source_target_pairs={{0,1},{1,0},{2,3},{3,2},{4,5},{5,4},{6,7},{7,6},{8,9},{9,8},{10,11... | collective-permute-start | bytes 248 | tf_op jit(solution)/shard_map/ppermute | solution.py:21
  13.1 3.5 %collective-permute-start.3 = (f32[20]{0:T(128)S(1)}, f32[20]{0:T(128)S(1)}, u32[]{:S(2)}, u32[]{:S(2)}) collective-permute-start(f32[20]{0:T(128)S(1)} %add.100), channel_id=1, source_target_pairs={{0,2},{1,3},{2,0},{3,1},{4,6},{5,7},{6,4},{7,5},{8,10},{9,11},{10,... | collective-permute-start | bytes 248 | tf_op jit(solution)/shard_map/ppermute | solution.py:21
  27.6 1.6 %collective-permute-start.4 = (f32[2,20,1536]{2,1,0:T(8,128)S(1)}, f32[2,20,1536]{2,1,0:T(8,128)S(1)}, u32[]{:S(2)}, u32[]{:S(2)}) collective-permute-start(f32[2,20,1536]{2,1,0:T(8,128)S(1)} %pad_maximum_fusion), channel_id=1, source_target_pairs={{0,1},{1,0},{2,3},{3,2},{4,5},{5,4},{6,7},{7,6},{8,9},{9,8},{10,11... | collective-permute-start | bytes 737288 | tf_op jit(solution)/shard_map/ppermute | solution.py:21
  39.6 1.6 %collective-permute-start.8 = (f32[2,20,1536]{2,1,0:T(8,128)S(1)}, f32[2,20,1536]{2,1,0:T(8,128)S(1)}, u32[]{:S(2)}, u32[]{:S(2)}) collective-permute-start(f32[2,20,1536]{2,1,0:T(8,128)S(1)} %pad_maximum_fusion.1), channel_id=1, source_target_pairs={{0,1},{1,0},{2,3},{3,2},{4,5},{5,4},{6,7},{7,6},{8,9},{9,8},{10,11... | collective-permute-start | bytes 737288 | tf_op jit(solution)/shard_map/ppermute | solution.py:21
  41.3 6.8 %collective-permute-start.9 = (f32[2,20,768]{2,1,0:T(8,128)S(1)}, f32[2,20,768]{2,1,0:T(8,128)S(1)}, u32[]{:S(2)}, u32[]{:S(2)}) collective-permute-start(f32[2,20,768]{2,1,0:T(8,128)S(1)} %pad_maximum_fusion.3), channel_id=1, source_target_pairs={{0,2},{1,3},{2,0},{3,1},{4,6},{5,7},{6,4},{7,5},{8,10},{9,11},{10,... | collective-permute-start | bytes 368648 | tf_op jit(solution)/shard_map/ppermute | solution.py:21
  43.1 7.7 %collective-permute-start.5 = (f32[2,20,768]{2,1,0:T(8,128)S(1)}, f32[2,20,768]{2,1,0:T(8,128)S(1)}, u32[]{:S(2)}, u32[]{:S(2)}) collective-permute-start(f32[2,20,768]{2,1,0:T(8,128)S(1)} %pad_maximum_fusion.2), channel_id=1, source_target_pairs={{0,2},{1,3},{2,0},{3,1},{4,6},{5,7},{6,4},{7,5},{8,10},{9,11},{10,... | collective-permute-start | bytes 368648 | tf_op jit(solution)/shard_map/ppermute | solution.py:21
  48.1 4.5 %collective-permute-start.10 = (bf16[20,768]{1,0:T(8,128)(2,1)S(1)}, bf16[20,768]{1,0:T(8,128)(2,1)S(1)}, u32[]{:S(2)}, u32[]{:S(2)}) collective-permute-start(bf16[20,768]{1,0:T(8,128)(2,1)S(1)} %fusion.28), channel_id=1, source_target_pairs={{0,2},{1,3},{2,0},{3,1},{4,6},{5,7},{6,4},{7,5},{8,10},{9,11},{10,... | collective-permute-start | bytes 92168 | tf_op jit(solution)/shard_map/ppermute | solution.py:21
  50.9 4.0 %collective-permute-start.6 = (bf16[20,768]{1,0:T(8,128)(2,1)S(1)}, bf16[20,768]{1,0:T(8,128)(2,1)S(1)}, u32[]{:S(2)}, u32[]{:S(2)}) collective-permute-start(bf16[20,768]{1,0:T(8,128)(2,1)S(1)} %fusion.32), channel_id=1, source_target_pairs={{0,2},{1,3},{2,0},{3,1},{4,6},{5,7},{6,4},{7,5},{8,10},{9,11},{10,... | collective-permute-start | bytes 92168 | tf_op jit(solution)/shard_map/ppermute | solution.py:21
  52.7 2.3 %collective-permute-start.11 = (bf16[20,1536]{1,0:T(8,128)(2,1)S(1)}, bf16[20,1536]{1,0:T(8,128)(2,1)S(1)}, u32[]{:S(2)}, u32[]{:S(2)}) collective-permute-start(bf16[20,1536]{1,0:T(8,128)(2,1)S(1)} %maximum_select_fusion.6), channel_id=1, source_target_pairs={{0,1},{1,0},{2,3},{3,2},{4,5},{5,4},{6,7},{7,6},{8,9},{9,8},{10,11... | collective-permute-start | bytes 184328 | tf_op jit(solution)/shard_map/ppermute | solution.py:21
  54.9 5.7 %collective-permute-start.7 = (bf16[20,1536]{1,0:T(8,128)(2,1)S(1)}, bf16[20,1536]{1,0:T(8,128)(2,1)S(1)}, u32[]{:S(2)}, u32[]{:S(2)}) collective-permute-start(bf16[20,1536]{1,0:T(8,128)(2,1)S(1)} %maximum_select_fusion.5), channel_id=1, source_target_pairs={{0,1},{1,0},{2,3},{3,2},{4,5},{5,4},{6,7},{7,6},{8,9},{9,8},{10,11... | collective-permute-start | bytes 184328 | tf_op jit(solution)/shard_map/ppermute | solution.py:21
  66.2 4.5 %collective-permute-start.12 = (f32[5,2048]{1,0:T(8,128)S(1)}, f32[5,2048]{1,0:T(8,128)S(1)}, u32[]{:S(2)}, u32[]{:S(2)}) collective-permute-start(f32[5,2048]{1,0:T(8,128)S(1)} %get-tuple-element.19), channel_id=1, source_target_pairs={{0,4},{4,0},{8,12},{12,8},{1,5},{5,1},{9,13},{13,9},{2,6},{6,2},{1... | collective-permute-start | bytes 122888 | tf_op jit(solution)/shard_map/ppermute | solution.py:62
  67.8 7.1 %collective-permute-start.13 = (f32[5,2048]{1,0:T(8,128)S(1)}, f32[5,2048]{1,0:T(8,128)S(1)}, u32[]{:S(2)}, u32[]{:S(2)}) collective-permute-start(f32[5,2048]{1,0:T(8,128)S(1)} %get-tuple-element.21), channel_id=1, source_target_pairs={{0,8},{4,12},{8,0},{12,4},{1,9},{5,13},{9,1},{13,5},{2,10},{6,14},... | collective-permute-start | bytes 122888 | tf_op jit(solution)/shard_map/ppermute | solution.py:62
  70.6 6.1 %collective-permute-start.14 = (f32[5,2048]{1,0:T(8,128)S(1)}, f32[5,2048]{1,0:T(8,128)S(1)}, u32[]{:S(2)}, u32[]{:S(2)}) collective-permute-start(f32[5,2048]{1,0:T(8,128)S(1)} %get-tuple-element.20), channel_id=1, source_target_pairs={{0,12},{4,8},{8,4},{12,0},{1,13},{5,9},{9,5},{13,1},{2,14},{6,10},... | collective-permute-start | bytes 122888 | tf_op jit(solution)/shard_map/ppermute | solution.py:62

commit v10 on v7

--- a/solution.py
+++ b/solution.py
@@ -60,19 +60,36 @@
     return own
 
 
+def fanout_all_gather(x, axis, n, bits):
+    me = lax.axis_index(axis)
+    rows = x.shape[0]
+    out = jnp.zeros((n * rows,) + x.shape[1:], x.dtype)
+    for k in range(n):
+        block = x if k == 0 else lax.ppermute(x, axis, [(a, a ^ k) for a in range(n)])
+        out = lax.dynamic_update_slice_in_dim(out, block, gathered_position(me ^ k, bits) * rows, axis=0)
+    return out
+
+
+def fanout_all_reduce(x, axis, n):
+    me = lax.axis_index(axis)
+    got = jnp.stack([x] + [lax.ppermute(x, axis, [(a, a ^ k) for a in range(n)]) for k in range(1, n)])
+    ordered = jnp.take(got, jnp.arange(n) ^ me, axis=0)
+    return jnp.sum(ordered, axis=0)
+
+
 def local(tokens, norm_gain, w_gate, w_up, w_down):
     ngx = lax.axis_size("gx")
     ngy = lax.axis_size("gy")
     features = tokens.shape[1] * ngy
     gx_levels = list(range(ngx.bit_length() - 1))
     if pairwise(ngx):
-        raw = xor_all_gather(tokens, "gx", ngx, 0, gx_levels[::-1])
+        raw = fanout_all_gather(tokens, "gx", ngx, gx_levels[::-1])
     else:
         raw = lax.all_gather(tokens, "gx", axis=0, tiled=True)
     values = raw.astype(jnp.float32)
     local_sq = jnp.sum(values * values, axis=1)
     if pairwise(ngy):
-        total_sq = xor_all_reduce(local_sq, "gy", ngy)
+        total_sq = fanout_all_reduce(local_sq, "gy", ngy)
     else:
         total_sq = lax.psum(local_sq, "gy")
     inverse = lax.rsqrt(total_sq / features + epsilon)

time: 75.6 us -> 73 us (0.966)
  local copies, waits for them, and re-layouts: 0.87 us -> 5.81 us
  matrix products: 31.3 us -> 26.8 us
  waiting for transfers between devices: 24.2 us -> 22.6 us
  other arithmetic: 1.96 us -> 1.17 us
    dot_general x2, matrix products: 12 us -> 3.61 us  [local(): up_part = jnp.dot(piece, w_up[:, cols], preferred_element_type=jnp.float32)]
    ppermute x12 -> x8, starting transfers between devices: 12.4 us -> 4.23 us  [exchange(): return lax.ppermute(x, axis, [(a, a ^ 1 << s) for a in range(n)])]
    ppermute x0 -> x6, starting transfers between devices: none -> 7.54 us  [the longest x3 5.62 us: fanout_all_gather(): lax.ppermute(x, axis, [(a, a ^ k) for a in range(n)])]
    ppermute x12 -> x8, waiting for transfers between devices: 18.3 us -> 11.3 us  [exchange(): return lax.ppermute(x, axis, [(a, a ^ 1 << s) for a in range(n)])]
    ppermute x0 -> x6, waiting for transfers between devices: none -> 6.91 us  [the longest x3 4.25 us: fanout_all_gather(): lax.ppermute(x, axis, [(a, a ^ k) for a in range(n)])]
    dot_general x2, matrix products: 8.2 us -> 12.1 us  [local(): jnp.dot(piece, w_gate[:, cols], preferred_element_type=jnp.float32)]
    unnamed x4, local copies, waits for them, and re-layouts: 0.73 us -> 3.28 us
    dynamic_update_slice x0 -> x4, local copies, waits for them, and re-layouts: none -> 1.82 us  [fanout_all_gather(): lax.dynamic_update_slice_in_dim(out, block, gathered_position(me ^ k, bit...]
  transfers between devices with their start and end apart: 15 -> 17, of which waited for: 11 -> 12; matrix products, arithmetic and copies ran while one was open for 18% -> 10% of each run, Pallas kernels for 0% -> 0%
where the time goes in v10:
time: 73 us; the launch traced here: 72.8 us
  matrix products  26.8 us (37%)
  waiting for transfers between devices  22.6 us (31%)
  starting transfers between devices  16.2 us (22%)
  local copies, waits for them, and re-layouts  5.81 us (8%)
  other arithmetic  1.17 us (2%)
    dot_general x2, matrix products, local(): jnp.dot(piece, w_gate[:, cols], preferred_element_type=jnp.float32)  12.1 us
    ppermute x8, waiting for transfers between devices, exchange(): return lax.ppermute(x, axis, [(a, a ^ 1 << s) for a in range(n)])  11.3 us
    dot_general x2, matrix products, local(): jnp.dot(hidden_all, w_down[cols, :], preferred_element_type=jnp.float32)  11.1 us
    ppermute x3, starting transfers between devices, fanout_all_gather(): lax.ppermute(x, axis, [(a, a ^ k) for a in range(n)])  5.62 us
    ppermute x3, starting transfers between devices, fanout_reduce_scatter(): own = own + lax.ppermute(block, axis, [(a, a ^ k) for a in range(n)])  4.44 us
    ppermute x3, waiting for transfers between devices, fanout_reduce_scatter(): own = own + lax.ppermute(block, axis, [(a, a ^ k) for a in range(n)])  4.34 us
    ppermute x3, waiting for transfers between devices, fanout_all_gather(): lax.ppermute(x, axis, [(a, a ^ k) for a in range(n)])  4.25 us
    ppermute x8, starting transfers between devices, exchange(): return lax.ppermute(x, axis, [(a, a ^ 1 << s) for a in range(n)])  4.23 us
  transfers between devices with their start and end apart: 17, of which 12 were waited for; matrix products, arithmetic and copies ran while one was open for 10% of the time, Pallas kernels for 0%

profile of v10, /device:TPU:0, one launch (start us, length us, event | category | flops | bytes accessed | tf_op | source)
XLA Modules:
  0.0 72.8 jit_solution(937680046245588501)
XLA Ops:
  0.0 3.0 %collective-permute-start = (bf16[5,2048]{1,0:T(8,128)(2,1)}, bf16[5,2048]{1,0:T(8,128)(2,1)S(1)}, u32[]{:S(2)}, u32[]{:S(2)}) collective-permute-start(bf16[5,2048]{1,0:T(8,128)(2,1)} %param.5), channel_id=1, source_target_pairs={{0,4},{4,0},{8,12},{12,8},{1,5},{5,1},{9,13},{13,9},{2,6},{6,2},{1... | collective-permute-start | bytes 61448 | tf_op jit(solution)/shard_map/ppermute | solution.py:68
  3.0 2.6 %collective-permute-start.1 = (bf16[5,2048]{1,0:T(8,128)(2,1)}, bf16[5,2048]{1,0:T(8,128)(2,1)S(1)}, u32[]{:S(2)}, u32[]{:S(2)}) collective-permute-start(bf16[5,2048]{1,0:T(8,128)(2,1)} %param.5), channel_id=1, source_target_pairs={{0,8},{4,12},{8,0},{12,4},{1,9},{5,13},{9,1},{13,5},{2,10},{6,14},... | collective-permute-start | bytes 61448 | tf_op jit(solution)/shard_map/ppermute | solution.py:68
  5.7 1.0 %dynamic_update_slice.12 = bf16[20,2048]{1,0:T(8,128)(2,1)S(1)} dynamic-update-slice(bf16[20,2048]{1,0:T(8,128)(2,1)S(1)} %broadcast_in_dim.15, bf16[5,2048]{1,0:T(8,128)(2,1)} %param.5, s32[]{:T(128)S(6)} %select_n.86, s32[]{:T(128)} %constant.19.clone.1) | dynamic-update-slice | bytes 40964 | tf_op jit(solution)/shard_map/dynamic_update_slice | solution.py:69
  7.0 1.6 %collective-permute-done.1 = bf16[5,2048]{1,0:T(8,128)(2,1)S(1)} collective-permute-done((bf16[5,2048]{1,0:T(8,128)(2,1)}, bf16[5,2048]{1,0:T(8,128)(2,1)S(1)}, u32[]{:S(2)}, u32[]{:S(2)}) %collective-permute-start.1) | collective-permute-done | bytes 20512 | tf_op jit(solution)/shard_map/ppermute | solution.py:68
  8.9 2.6 %collective-permute-done.2 = bf16[5,2048]{1,0:T(8,128)(2,1)S(1)} collective-permute-done((bf16[5,2048]{1,0:T(8,128)(2,1)}, bf16[5,2048]{1,0:T(8,128)(2,1)S(1)}, u32[]{:S(2)}, u32[]{:S(2)}) %collective-permute-start.2) | collective-permute-done | bytes 20512 | tf_op jit(solution)/shard_map/ppermute | solution.py:68
  12.0 1.6 %collective-permute-start.4 = (f32[20]{0:T(128)S(1)}, f32[20]{0:T(128)S(1)}, u32[]{:S(2)}, u32[]{:S(2)}) collective-permute-start(f32[20]{0:T(128)S(1)} %fusion.15), channel_id=1, source_target_pairs={{0,2},{1,3},{2,0},{3,1},{4,6},{5,7},{6,4},{7,5},{8,10},{9,11},{10,... | collective-permute-start | bytes 248 | tf_op jit(solution)/shard_map/ppermute | solution.py:75
  13.9 1.7 %collective-permute-done.4 = f32[20]{0:T(128)S(1)} collective-permute-done((f32[20]{0:T(128)S(1)}, f32[20]{0:T(128)S(1)}, u32[]{:S(2)}, u32[]{:S(2)}) %collective-permute-start.4) | collective-permute-done | bytes 112 | tf_op jit(solution)/shard_map/ppermute | solution.py:75
  15.6 0.9 %collective-permute-done.5 = f32[20]{0:T(128)S(1)} collective-permute-done((f32[20]{0:T(128)S(1)}, f32[20]{0:T(128)S(1)}, u32[]{:S(2)}, u32[]{:S(2)}) %collective-permute-start.5) | collective-permute-done | bytes 112 | tf_op jit(solution)/shard_map/ppermute | solution.py:75
  17.2 5.8 %fusion.10 = f32[20,3072]{1,0:T(8,128)S(1)} fusion(bf16[2048,6144]{1,0:T(8,128)(2,1)} %param.7, bf16[20,2048]{1,0:T(8,128)(2,1)S(1)} %dynamic_update_slice.15, f32[2048]{0:T(1024)} %param.6, f32[20]{0:T(128)S(1)} %add_rsqrt_fusion), kind=kOutput, calls=%fused_computation.11 | convolution fusion | flops 251822080 | bytes 12918864 | tf_op jit(solution)/shard_map/dot_general | solution.py:106
  23.0 6.3 %fusion.4 = f32[20,3072]{1,0:T(8,128)S(1)} fusion(bf16[2048,6144]{1,0:T(8,128)(2,1)} %param.7, bf16[20,2048]{1,0:T(8,128)(2,1)S(1)} %dynamic_update_slice.15, f32[2048]{0:T(1024)} %param.6, f32[20]{0:T(128)S(1)} %add_rsqrt_fusion), kind=kOutput, calls=%fused_computation.5 | convolution fusion | flops 251822080 | bytes 12918864 | tf_op jit(solution)/shard_map/dot_general | solution.py:106
  29.3 3.3 %copy-done = bf16[2048,6144]{1,0:T(8,128)(2,1)S(1)} copy-done((bf16[2048,6144]{1,0:T(8,128)(2,1)S(1)}, bf16[2048,6144]{1,0:T(8,128)(2,1)}, u32[]{:S(2)}) %copy-start) | copy-done | bytes 25165848
  32.6 1.8 %fusion.8 = f32[20,3072]{1,0:T(8,128)S(1)} fusion(bf16[2048,6144]{1,0:T(8,128)(2,1)S(1)} %copy-done, bf16[20,2048]{1,0:T(8,128)(2,1)S(1)} %dynamic_update_slice.15, f32[2048]{0:T(1024)S(1)} %copy-done.1, f32[20]{0:T(128)S(1)} %add_rsqrt_fusion), kind=kOutput, calls=%fused_computation.9 | convolution fusion | flops 251822080 | bytes 12935680 | tf_op jit(solution)/shard_map/dot_general | solution.py:107
  34.4 1.8 %fusion.2 = f32[20,3072]{1,0:T(8,128)S(1)} fusion(bf16[2048,6144]{1,0:T(8,128)(2,1)S(1)} %copy-done, bf16[20,2048]{1,0:T(8,128)(2,1)S(1)} %dynamic_update_slice.15, f32[2048]{0:T(1024)S(1)} %copy-done.1, f32[20]{0:T(128)S(1)} %add_rsqrt_fusion), kind=kOutput, calls=%fused_computation.3 | convolution fusion | flops 251822080 | bytes 12935680 | tf_op jit(solution)/shard_map/dot_general | solution.py:107
  36.9 1.0 %collective-permute-done.6 = f32[2,20,1536]{2,1,0:T(8,128)S(1)} collective-permute-done((f32[2,20,1536]{2,1,0:T(8,128)S(1)}, f32[2,20,1536]{2,1,0:T(8,128)S(1)}, u32[]{:S(2)}, u32[]{:S(2)}) %collective-permute-start.6) | collective-permute-done | bytes 245792 | tf_op jit(solution)/shard_map/ppermute | solution.py:18
  39.1 1.5 %collective-permute-start.7 = (f32[2,20,768]{2,1,0:T(8,128)S(1)}, f32[2,20,768]{2,1,0:T(8,128)S(1)}, u32[]{:S(2)}, u32[]{:S(2)}) collective-permute-start(f32[2,20,768]{2,1,0:T(8,128)S(1)} %pad_maximum_fusion.2), channel_id=1, source_target_pairs={{0,2},{1,3},{2,0},{3,1},{4,6},{5,7},{6,4},{7,5},{8,10},{9,11},{10,... | collective-permute-start | bytes 368648 | tf_op jit(solution)/shard_map/ppermute | solution.py:18
  40.6 4.6 %collective-permute-done.11 = f32[2,20,768]{2,1,0:T(8,128)S(1)} collective-permute-done((f32[2,20,768]{2,1,0:T(8,128)S(1)}, f32[2,20,768]{2,1,0:T(8,128)S(1)}, u32[]{:S(2)}, u32[]{:S(2)}) %collective-permute-start.11) | collective-permute-done | bytes 122912 | tf_op jit(solution)/shard_map/ppermute | solution.py:18
  45.9 2.1 %collective-permute-done.7 = f32[2,20,768]{2,1,0:T(8,128)S(1)} collective-permute-done((f32[2,20,768]{2,1,0:T(8,128)S(1)}, f32[2,20,768]{2,1,0:T(8,128)S(1)}, u32[]{:S(2)}, u32[]{:S(2)}) %collective-permute-start.7) | collective-permute-done | bytes 122912 | tf_op jit(solution)/shard_map/ppermute | solution.py:18
  49.4 2.7 %collective-permute-done.8 = bf16[20,768]{1,0:T(8,128)(2,1)S(1)} collective-permute-done((bf16[20,768]{1,0:T(8,128)(2,1)S(1)}, bf16[20,768]{1,0:T(8,128)(2,1)S(1)}, u32[]{:S(2)}, u32[]{:S(2)}) %collective-permute-start.8) | collective-permute-done | bytes 30752 | tf_op jit(solution)/shard_map/ppermute | solution.py:18
  52.2 5.6 %fusion = f32[20,2048]{1,0:T(8,128)S(1)} fusion(bf16[6144,2048]{1,0:T(8,128)(2,1)} %param.9, bf16[20,1536]{1,0:T(8,128)(2,1)S(1)} %collective-permute-done.13, bf16[20,1536]{1,0:T(8,128)(2,1)S(1)} %maximum_select_fusion.5, pred[]{:T(512)S(6)} %eq.8), kind=kOutput, calls=%fused_computation.1 | convolution fusion | flops 252211200 | bytes 12869633 | tf_op jit(solution)/shard_map/dot_general | solution.py:118
  57.8 5.6 %fusion.12 = f32[20,2048]{1,0:T(8,128)S(1)} fusion(f32[20,2048]{1,0:T(8,128)S(1)} %fusion, bf16[6144,2048]{1,0:T(8,128)(2,1)} %param.9, bf16[20,1536]{1,0:T(8,128)(2,1)S(1)} %collective-permute-done.9, bf16[20,1536]{1,0:T(8,128)(2,1)S(1)} %maximum_select_fusion.4, pred[]{:T(512)S(6)} %eq.8), kind=kOutput, calls=%fused_computation.13 | convolution fusion | flops 252252160 | bytes 13033473 | tf_op jit(solution)/shard_map/dot_general | solution.py:118
  63.5 0.9 %collective-permute-start.15 = (f32[5,2048]{1,0:T(8,128)S(1)}, f32[5,2048]{1,0:T(8,128)S(1)}, u32[]{:S(2)}, u32[]{:S(2)}) collective-permute-start(f32[5,2048]{1,0:T(8,128)S(1)} %get-tuple-element.11), channel_id=1, source_target_pairs={{0,8},{4,12},{8,0},{12,4},{1,9},{5,13},{9,1},{13,5},{2,10},{6,14},... | collective-permute-start | bytes 122888 | tf_op jit(solution)/shard_map/ppermute | solution.py:59
  64.4 3.5 %collective-permute-start.16 = (f32[5,2048]{1,0:T(8,128)S(1)}, f32[5,2048]{1,0:T(8,128)S(1)}, u32[]{:S(2)}, u32[]{:S(2)}) collective-permute-start(f32[5,2048]{1,0:T(8,128)S(1)} %get-tuple-element.10), channel_id=1, source_target_pairs={{0,12},{4,8},{8,4},{12,0},{1,13},{5,9},{9,5},{13,1},{2,14},{6,10},... | collective-permute-start | bytes 122888 | tf_op jit(solution)/shard_map/ppermute | solution.py:59
  67.8 1.2 %collective-permute-done.14 = f32[5,2048]{1,0:T(8,128)S(1)} collective-permute-done((f32[5,2048]{1,0:T(8,128)S(1)}, f32[5,2048]{1,0:T(8,128)S(1)}, u32[]{:S(2)}, u32[]{:S(2)}) %collective-permute-start.14) | collective-permute-done | bytes 40992 | tf_op jit(solution)/shard_map/ppermute | solution.py:59
  69.0 3.2 %collective-permute-done.15 = f32[5,2048]{1,0:T(8,128)S(1)} collective-permute-done((f32[5,2048]{1,0:T(8,128)S(1)}, f32[5,2048]{1,0:T(8,128)S(1)}, u32[]{:S(2)}, u32[]{:S(2)}) %collective-permute-start.15) | collective-permute-done | bytes 40992 | tf_op jit(solution)/shard_map/ppermute | solution.py:59
  (51 shorter events, 6.8 us)
Async XLA Ops:
  0.0 29.3 %copy-start.1 = (f32[2048]{0:T(1024)S(1)}, f32[2048]{0:T(1024)}, u32[]{:S(2)}) copy-start(f32[2048]{0:T(1024)} %param.6) | copy-start | bytes 24580
  0.0 6.7 %collective-permute-start = (bf16[5,2048]{1,0:T(8,128)(2,1)}, bf16[5,2048]{1,0:T(8,128)(2,1)S(1)}, u32[]{:S(2)}, u32[]{:S(2)}) collective-permute-start(bf16[5,2048]{1,0:T(8,128)(2,1)} %param.5), channel_id=1, source_target_pairs={{0,4},{4,0},{8,12},{12,8},{1,5},{5,1},{9,13},{13,9},{2,6},{6,2},{1... | collective-permute-start | bytes 61448 | tf_op jit(solution)/shard_map/ppermute | solution.py:68
  3.0 5.6 %collective-permute-start.1 = (bf16[5,2048]{1,0:T(8,128)(2,1)}, bf16[5,2048]{1,0:T(8,128)(2,1)S(1)}, u32[]{:S(2)}, u32[]{:S(2)}) collective-permute-start(bf16[5,2048]{1,0:T(8,128)(2,1)} %param.5), channel_id=1, source_target_pairs={{0,8},{4,12},{8,0},{12,4},{1,9},{5,13},{9,1},{13,5},{2,10},{6,14},... | collective-permute-start | bytes 61448 | tf_op jit(solution)/shard_map/ppermute | solution.py:68
  5.6 5.9 %collective-permute-start.2 = (bf16[5,2048]{1,0:T(8,128)(2,1)}, bf16[5,2048]{1,0:T(8,128)(2,1)S(1)}, u32[]{:S(2)}, u32[]{:S(2)}) collective-permute-start(bf16[5,2048]{1,0:T(8,128)(2,1)} %param.5), channel_id=1, source_target_pairs={{0,12},{4,8},{8,4},{12,0},{1,13},{5,9},{9,5},{13,1},{2,14},{6,10},... | collective-permute-start | bytes 61448 | tf_op jit(solution)/shard_map/ppermute | solution.py:68
  11.9 1.9 %collective-permute-start.3 = (f32[20]{0:T(128)S(1)}, f32[20]{0:T(128)S(1)}, u32[]{:S(2)}, u32[]{:S(2)}) collective-permute-start(f32[20]{0:T(128)S(1)} %fusion.15), channel_id=1, source_target_pairs={{0,1},{1,0},{2,3},{3,2},{4,5},{5,4},{6,7},{7,6},{8,9},{9,8},{10,11... | collective-permute-start | bytes 248 | tf_op jit(solution)/shard_map/ppermute | solution.py:75
  12.0 3.6 %collective-permute-start.4 = (f32[20]{0:T(128)S(1)}, f32[20]{0:T(128)S(1)}, u32[]{:S(2)}, u32[]{:S(2)}) collective-permute-start(f32[20]{0:T(128)S(1)} %fusion.15), channel_id=1, source_target_pairs={{0,2},{1,3},{2,0},{3,1},{4,6},{5,7},{6,4},{7,5},{8,10},{9,11},{10,... | collective-permute-start | bytes 248 | tf_op jit(solution)/shard_map/ppermute | solution.py:75
  13.6 3.0 %collective-permute-start.5 = (f32[20]{0:T(128)S(1)}, f32[20]{0:T(128)S(1)}, u32[]{:S(2)}, u32[]{:S(2)}) collective-permute-start(f32[20]{0:T(128)S(1)} %fusion.15), channel_id=1, source_target_pairs={{0,3},{1,2},{2,1},{3,0},{4,7},{5,6},{6,5},{7,4},{8,11},{9,10},{10,... | collective-permute-start | bytes 248 | tf_op jit(solution)/shard_map/ppermute | solution.py:75
  17.1 15.5 %copy-start = (bf16[2048,6144]{1,0:T(8,128)(2,1)S(1)}, bf16[2048,6144]{1,0:T(8,128)(2,1)}, u32[]{:S(2)}) copy-start(bf16[2048,6144]{1,0:T(8,128)(2,1)} %param.8) | copy-start | bytes 75497472
  36.3 1.6 %collective-permute-start.6 = (f32[2,20,1536]{2,1,0:T(8,128)S(1)}, f32[2,20,1536]{2,1,0:T(8,128)S(1)}, u32[]{:S(2)}, u32[]{:S(2)}) collective-permute-start(f32[2,20,1536]{2,1,0:T(8,128)S(1)} %pad_maximum_fusion), channel_id=1, source_target_pairs={{0,1},{1,0},{2,3},{3,2},{4,5},{5,4},{6,7},{7,6},{8,9},{9,8},{10,11... | collective-permute-start | bytes 737288 | tf_op jit(solution)/shard_map/ppermute | solution.py:18
  36.5 1.8 %collective-permute-start.10 = (f32[2,20,1536]{2,1,0:T(8,128)S(1)}, f32[2,20,1536]{2,1,0:T(8,128)S(1)}, u32[]{:S(2)}, u32[]{:S(2)}) collective-permute-start(f32[2,20,1536]{2,1,0:T(8,128)S(1)} %pad_maximum_fusion.1), channel_id=1, source_target_pairs={{0,1},{1,0},{2,3},{3,2},{4,5},{5,4},{6,7},{7,6},{8,9},{9,8},{10,11... | collective-permute-start | bytes 737288 | tf_op jit(solution)/shard_map/ppermute | solution.py:18
  38.4 6.8 %collective-permute-start.11 = (f32[2,20,768]{2,1,0:T(8,128)S(1)}, f32[2,20,768]{2,1,0:T(8,128)S(1)}, u32[]{:S(2)}, u32[]{:S(2)}) collective-permute-start(f32[2,20,768]{2,1,0:T(8,128)S(1)} %pad_maximum_fusion.3), channel_id=1, source_target_pairs={{0,2},{1,3},{2,0},{3,1},{4,6},{5,7},{6,4},{7,5},{8,10},{9,11},{10,... | collective-permute-start | bytes 368648 | tf_op jit(solution)/shard_map/ppermute | solution.py:18
  39.1 8.9 %collective-permute-start.7 = (f32[2,20,768]{2,1,0:T(8,128)S(1)}, f32[2,20,768]{2,1,0:T(8,128)S(1)}, u32[]{:S(2)}, u32[]{:S(2)}) collective-permute-start(f32[2,20,768]{2,1,0:T(8,128)S(1)} %pad_maximum_fusion.2), channel_id=1, source_target_pairs={{0,2},{1,3},{2,0},{3,1},{4,6},{5,7},{6,4},{7,5},{8,10},{9,11},{10,... | collective-permute-start | bytes 368648 | tf_op jit(solution)/shard_map/ppermute | solution.py:18
  45.2 4.0 %collective-permute-start.12 = (bf16[20,768]{1,0:T(8,128)(2,1)S(1)}, bf16[20,768]{1,0:T(8,128)(2,1)S(1)}, u32[]{:S(2)}, u32[]{:S(2)}) collective-permute-start(bf16[20,768]{1,0:T(8,128)(2,1)S(1)} %fusion.36), channel_id=1, source_target_pairs={{0,2},{1,3},{2,0},{3,1},{4,6},{5,7},{6,4},{7,5},{8,10},{9,11},{10,... | collective-permute-start | bytes 92168 | tf_op jit(solution)/shard_map/ppermute | solution.py:18
  48.1 4.0 %collective-permute-start.8 = (bf16[20,768]{1,0:T(8,128)(2,1)S(1)}, bf16[20,768]{1,0:T(8,128)(2,1)S(1)}, u32[]{:S(2)}, u32[]{:S(2)}) collective-permute-start(bf16[20,768]{1,0:T(8,128)(2,1)S(1)} %fusion.40), channel_id=1, source_target_pairs={{0,2},{1,3},{2,0},{3,1},{4,6},{5,7},{6,4},{7,5},{8,10},{9,11},{10,... | collective-permute-start | bytes 92168 | tf_op jit(solution)/shard_map/ppermute | solution.py:18
  49.3 2.9 %collective-permute-start.13 = (bf16[20,1536]{1,0:T(8,128)(2,1)S(1)}, bf16[20,1536]{1,0:T(8,128)(2,1)S(1)}, u32[]{:S(2)}, u32[]{:S(2)}) collective-permute-start(bf16[20,1536]{1,0:T(8,128)(2,1)S(1)} %maximum_select_fusion.5), channel_id=1, source_target_pairs={{0,1},{1,0},{2,3},{3,2},{4,5},{5,4},{6,7},{7,6},{8,9},{9,8},{10,11... | collective-permute-start | bytes 184328 | tf_op jit(solution)/shard_map/ppermute | solution.py:18
  52.1 5.7 %collective-permute-start.9 = (bf16[20,1536]{1,0:T(8,128)(2,1)S(1)}, bf16[20,1536]{1,0:T(8,128)(2,1)S(1)}, u32[]{:S(2)}, u32[]{:S(2)}) collective-permute-start(bf16[20,1536]{1,0:T(8,128)(2,1)S(1)} %maximum_select_fusion.4), channel_id=1, source_target_pairs={{0,1},{1,0},{2,3},{3,2},{4,5},{5,4},{6,7},{7,6},{8,9},{9,8},{10,11... | collective-permute-start | bytes 184328 | tf_op jit(solution)/shard_map/ppermute | solution.py:18
  63.4 5.6 %collective-permute-start.14 = (f32[5,2048]{1,0:T(8,128)S(1)}, f32[5,2048]{1,0:T(8,128)S(1)}, u32[]{:S(2)}, u32[]{:S(2)}) collective-permute-start(f32[5,2048]{1,0:T(8,128)S(1)} %get-tuple-element.9), channel_id=1, source_target_pairs={{0,4},{4,0},{8,12},{12,8},{1,5},{5,1},{9,13},{13,9},{2,6},{6,2},{1... | collective-permute-start | bytes 122888 | tf_op jit(solution)/shard_map/ppermute | solution.py:59
  63.5 8.7 %collective-permute-start.15 = (f32[5,2048]{1,0:T(8,128)S(1)}, f32[5,2048]{1,0:T(8,128)S(1)}, u32[]{:S(2)}, u32[]{:S(2)}) collective-permute-start(f32[5,2048]{1,0:T(8,128)S(1)} %get-tuple-element.11), channel_id=1, source_target_pairs={{0,8},{4,12},{8,0},{12,4},{1,9},{5,13},{9,1},{13,5},{2,10},{6,14},... | collective-permute-start | bytes 122888 | tf_op jit(solution)/shard_map/ppermute | solution.py:59
  64.4 7.8 %collective-permute-start.16 = (f32[5,2048]{1,0:T(8,128)S(1)}, f32[5,2048]{1,0:T(8,128)S(1)}, u32[]{:S(2)}, u32[]{:S(2)}) collective-permute-start(f32[5,2048]{1,0:T(8,128)S(1)} %get-tuple-element.10), channel_id=1, source_target_pairs={{0,12},{4,8},{8,4},{12,0},{1,13},{5,9},{9,5},{13,1},{2,14},{6,10},... | collective-permute-start | bytes 122888 | tf_op jit(solution)/shard_map/ppermute | solution.py:59

commit v11 on v10

--- a/solution.py
+++ b/solution.py
@@ -1,6 +1,8 @@
 import jax
 import jax.numpy as jnp
 from jax import lax
+from jax.experimental import pallas as pl
+from jax.experimental.pallas import tpu as pltpu
 from jax.sharding import PartitionSpec as P
 
 
@@ -77,6 +79,25 @@
     return jnp.sum(ordered, axis=0)
 
 
+def rows_to_vmem(w, start, count):
+    size = count * w.shape[1] * w.dtype.itemsize
+
+    def kernel(src, dst, sem):
+        copy = pltpu.make_async_copy(src.at[pl.ds(start, count), :], dst, sem)
+        copy.start()
+        copy.wait()
+
+    return pl.pallas_call(
+        kernel,
+        out_shape=jax.ShapeDtypeStruct((count, w.shape[1]), w.dtype),
+        in_specs=[pl.BlockSpec(memory_space=pl.ANY)],
+        out_specs=pl.BlockSpec(memory_space=pltpu.VMEM),
+        scratch_shapes=[pltpu.SemaphoreType.DMA(())],
+        cost_estimate=pl.CostEstimate(flops=0, transcendentals=0, bytes_accessed=2 * size),
+        compiler_params=pltpu.CompilerParams(vmem_limit_bytes=size + (2 << 20)),
+    )(pltpu.with_memory_space_constraint(w, pltpu.HBM))
+
+
 def local(tokens, norm_gain, w_gate, w_up, w_down):
     ngx = lax.axis_size("gx")
     ngy = lax.axis_size("gy")
@@ -106,7 +127,11 @@
         gate_part = jnp.dot(piece, w_gate[:, cols], preferred_element_type=jnp.float32)
         up_part = jnp.dot(piece, w_up[:, cols], preferred_element_type=jnp.float32)
         if pairwise(ngy):
-            gate, up = xor_reduce_scatter([gate_part, up_part], "gy", ngy, 1, gy_levels)
+            first = xor_reduce_scatter([gate_part, up_part], "gy", ngy, 1, gy_levels[:1])
+            if c == 0:
+                source, _ = lax.optimization_barrier((w_down, first[0]))
+                staged = [rows_to_vmem(source, k * step, step) for k in range(chunks)]
+            gate, up = xor_reduce_scatter(first, "gy", ngy, 1, gy_levels[1:])
         else:
             gate = lax.psum_scatter(gate_part, "gy", scatter_dimension=1, tiled=True)
             up = lax.psum_scatter(up_part, "gy", scatter_dimension=1, tiled=True)
@@ -115,7 +140,8 @@
             hidden_all = xor_all_gather(hidden, "gy", ngy, 1, gy_levels[::-1])
         else:
             hidden_all = lax.all_gather(hidden, "gy", axis=1, tiled=True)
-        term = jnp.dot(hidden_all, w_down[cols, :], preferred_element_type=jnp.float32)
+        down = staged[c] if pairwise(ngy) else w_down[cols, :]
+        term = jnp.dot(hidden_all, down, preferred_element_type=jnp.float32)
         total = term if total is None else total + term
     if pairwise(ngx):
         result = fanout_reduce_scatter(total, "gx", ngx, gx_levels[::-1])

time: 73 us -> 72.4 us (level)
  Pallas kernels: 0 us -> 9.17 us
  matrix products: 26.8 us -> 19.2 us
  waiting for transfers between devices: 22.6 us -> 20 us
    pallas_call x0 -> x2, Pallas kernels: none -> 9.17 us  [rows_to_vmem(): pl.pallas_call(kernel, out_shape=jax.ShapeDtypeStruct((count, w.shape[1])...]
    dot_general x2, matrix products: 12.1 us -> 3.61 us  [local(): jnp.dot(piece, w_gate[:, cols], preferred_element_type=jnp.float32)]
    dot_general x2, matrix products: 3.61 us -> 12 us  [local(): up_part = jnp.dot(piece, w_up[:, cols], preferred_element_type=jnp.float32)]
    dot_general x2, matrix products: 11.1 us -> 3.53 us  [local(): term = jnp.dot(hidden_all, down, preferred_element_type=jnp.float32)]
    ppermute x8, waiting for transfers between devices: 11.3 us -> 7.91 us  [exchange(): return lax.ppermute(x, axis, [(a, a ^ 1 << s) for a in range(n)])]
    ppermute x3, waiting for transfers between devices: 4.34 us -> 6.45 us  [fanout_reduce_scatter(): own = own + lax.ppermute(block, axis, [(a, a ^ k) for a in range(n)])]
    ppermute x8, starting transfers between devices: 4.23 us -> 5.34 us  [exchange(): return lax.ppermute(x, axis, [(a, a ^ 1 << s) for a in range(n)])]
    ppermute x3, waiting for transfers between devices: 2.66 us -> 1.76 us  [fanout_all_reduce(): lax.ppermute(x, axis, [(a, a ^ k) for a in range(n)])]
  transfers between devices with their start and end apart: 17 -> 17, of which waited for: 12 -> 9; matrix products, arithmetic and copies ran while one was open for 10% -> 5% of each run, Pallas kernels for 0% -> 13%
where the time goes in v11:
time: 72.4 us; the launch traced here: 72.2 us
  waiting for transfers between devices  20 us (28%)
  matrix products  19.2 us (27%)
  starting transfers between devices  16.4 us (23%)
  Pallas kernels  9.17 us (13%)
  local copies, waits for them, and re-layouts  6 us (8%)
  other arithmetic  1.17 us (2%)
    dot_general x2, matrix products, local(): up_part = jnp.dot(piece, w_up[:, cols], preferred_element_type=jnp.float32)  12 us
    pallas_call x2, Pallas kernels, rows_to_vmem(): pl.pallas_call(kernel, out_shape=jax.ShapeDtypeStruct((count, w.shape[1])...  9.17 us
    ppermute x8, waiting for transfers between devices, exchange(): return lax.ppermute(x, axis, [(a, a ^ 1 << s) for a in range(n)])  7.91 us
    ppermute x3, waiting for transfers between devices, fanout_reduce_scatter(): own = own + lax.ppermute(block, axis, [(a, a ^ k) for a in range(n)])  6.45 us
    ppermute x3, starting transfers between devices, fanout_all_gather(): lax.ppermute(x, axis, [(a, a ^ k) for a in range(n)])  5.62 us
    ppermute x8, starting transfers between devices, exchange(): return lax.ppermute(x, axis, [(a, a ^ 1 << s) for a in range(n)])  5.34 us
    ppermute x3, waiting for transfers between devices, fanout_all_gather(): lax.ppermute(x, axis, [(a, a ^ k) for a in range(n)])  3.86 us
    dot_general x2, matrix products, local(): jnp.dot(piece, w_gate[:, cols], preferred_element_type=jnp.float32)  3.61 us
  transfers between devices with their start and end apart: 17, of which 9 were waited for; matrix products, arithmetic and copies ran while one was open for 5% of the time, Pallas kernels for 13%

profile of v11, /device:TPU:0, one launch (start us, length us, event | category | flops | bytes accessed | tf_op | source)
XLA Modules:
  0.0 72.2 jit_solution(13914068320729178893)
XLA Ops:
  0.0 3.0 %collective-permute-start = (bf16[5,2048]{1,0:T(8,128)(2,1)}, bf16[5,2048]{1,0:T(8,128)(2,1)S(1)}, u32[]{:S(2)}, u32[]{:S(2)}) collective-permute-start(bf16[5,2048]{1,0:T(8,128)(2,1)} %param.5), channel_id=1, source_target_pairs={{0,4},{4,0},{8,12},{12,8},{1,5},{5,1},{9,13},{13,9},{2,6},{6,2},{1... | collective-permute-start | bytes 61448 | tf_op jit(solution)/shard_map/ppermute | solution.py:70
  3.0 2.5 %collective-permute-start.2 = (bf16[5,2048]{1,0:T(8,128)(2,1)}, bf16[5,2048]{1,0:T(8,128)(2,1)S(1)}, u32[]{:S(2)}, u32[]{:S(2)}) collective-permute-start(bf16[5,2048]{1,0:T(8,128)(2,1)} %param.5), channel_id=1, source_target_pairs={{0,12},{4,8},{8,4},{12,0},{1,13},{5,9},{9,5},{13,1},{2,14},{6,10},... | collective-permute-start | bytes 61448 | tf_op jit(solution)/shard_map/ppermute | solution.py:70
  5.7 1.0 %dynamic_update_slice.12 = bf16[20,2048]{1,0:T(8,128)(2,1)S(1)} dynamic-update-slice(bf16[20,2048]{1,0:T(8,128)(2,1)S(1)} %broadcast_in_dim.15, bf16[5,2048]{1,0:T(8,128)(2,1)} %param.5, s32[]{:T(128)S(6)} %select_n.86, s32[]{:T(128)} %constant.19.clone.1) | dynamic-update-slice | bytes 40964 | tf_op jit(solution)/shard_map/dynamic_update_slice | solution.py:71
  7.0 3.9 %collective-permute-done.1 = bf16[5,2048]{1,0:T(8,128)(2,1)S(1)} collective-permute-done((bf16[5,2048]{1,0:T(8,128)(2,1)}, bf16[5,2048]{1,0:T(8,128)(2,1)S(1)}, u32[]{:S(2)}, u32[]{:S(2)}) %collective-permute-start.1) | collective-permute-done | bytes 20512 | tf_op jit(solution)/shard_map/ppermute | solution.py:70
  11.7 1.6 %collective-permute-start.4 = (f32[20]{0:T(128)S(1)}, f32[20]{0:T(128)S(1)}, u32[]{:S(2)}, u32[]{:S(2)}) collective-permute-start(f32[20]{0:T(128)S(1)} %fusion.8), channel_id=1, source_target_pairs={{0,2},{1,3},{2,0},{3,1},{4,6},{5,7},{6,4},{7,5},{8,10},{9,11},{10,... | collective-permute-start | bytes 248 | tf_op jit(solution)/shard_map/ppermute | solution.py:77
  13.5 1.1 %collective-permute-done.5 = f32[20]{0:T(128)S(1)} collective-permute-done((f32[20]{0:T(128)S(1)}, f32[20]{0:T(128)S(1)}, u32[]{:S(2)}, u32[]{:S(2)}) %collective-permute-start.5) | collective-permute-done | bytes 112 | tf_op jit(solution)/shard_map/ppermute | solution.py:77
  16.0 5.8 %fusion.4 = f32[20,3072]{1,0:T(8,128)S(1)} fusion(bf16[2048,6144]{1,0:T(8,128)(2,1)} %param.8, bf16[20,2048]{1,0:T(8,128)(2,1)S(1)} %dynamic_update_slice.15, f32[2048]{0:T(1024)} %param.6, f32[20]{0:T(128)S(1)} %add_rsqrt_fusion), kind=kOutput, calls=%fused_computation.5 | convolution fusion | flops 251822080 | bytes 12918864 | tf_op jit(solution)/shard_map/dot_general | solution.py:128
  21.7 6.3 %fusion = f32[20,3072]{1,0:T(8,128)S(1)} fusion(bf16[2048,6144]{1,0:T(8,128)(2,1)} %param.8, bf16[20,2048]{1,0:T(8,128)(2,1)S(1)} %dynamic_update_slice.15, f32[2048]{0:T(1024)S(1)} %copy-done.1, f32[20]{0:T(128)S(1)} %add_rsqrt_fusion), kind=kOutput, calls=%fused_computation.1 | convolution fusion | flops 251822080 | bytes 12918864 | tf_op jit(solution)/shard_map/dot_general | solution.py:128
  28.0 3.4 %copy-done = bf16[2048,6144]{1,0:T(8,128)(2,1)S(1)} copy-done((bf16[2048,6144]{1,0:T(8,128)(2,1)S(1)}, bf16[2048,6144]{1,0:T(8,128)(2,1)}, u32[]{:S(2)}) %copy-start) | copy-done | bytes 25165848
  31.4 1.8 %fusion.2 = f32[20,3072]{1,0:T(8,128)S(1)} fusion(bf16[2048,6144]{1,0:T(8,128)(2,1)S(1)} %copy-done, bf16[20,2048]{1,0:T(8,128)(2,1)S(1)} %dynamic_update_slice.15, f32[2048]{0:T(1024)S(1)} %copy-done.1, f32[20]{0:T(128)S(1)} %add_rsqrt_fusion), kind=kOutput, calls=%fused_computation.3 | convolution fusion | flops 251822080 | bytes 12935680 | tf_op jit(solution)/shard_map/dot_general | solution.py:127
  33.2 1.8 %fusion.6 = f32[20,3072]{1,0:T(8,128)S(1)} fusion(bf16[2048,6144]{1,0:T(8,128)(2,1)S(1)} %copy-done, bf16[20,2048]{1,0:T(8,128)(2,1)S(1)} %dynamic_update_slice.15, f32[2048]{0:T(1024)S(1)} %copy-done.1, f32[20]{0:T(128)S(1)} %add_rsqrt_fusion), kind=kOutput, calls=%fused_computation.7 | convolution fusion | flops 251822080 | bytes 12935680 | tf_op jit(solution)/shard_map/dot_general | solution.py:127
  36.8 1.6 %collective-permute-start.11 = (f32[2,20,768]{2,1,0:T(8,128)S(1)}, f32[2,20,768]{2,1,0:T(8,128)S(1)}, u32[]{:S(2)}, u32[]{:S(2)}) collective-permute-start(f32[2,20,768]{2,1,0:T(8,128)S(1)} %pad_maximum_fusion.3), channel_id=1, source_target_pairs={{0,2},{1,3},{2,0},{3,1},{4,6},{5,7},{6,4},{7,5},{8,10},{9,11},{10,... | collective-permute-start | bytes 368648 | tf_op jit(solution)/shard_map/ppermute | solution.py:20
  38.5 4.6 %shard_map.56 = bf16[3072,2048]{1,0:T(8,128)(2,1)S(1)} custom-call(bf16[6144,2048]{1,0:T(8,128)(2,1)} %src.1), custom_call_target="tpu_custom_call" | custom-call | bytes 25165824 | tf_op jit(solution)/shard_map/pallas_call | solution.py:90
  43.1 4.6 %shard_map.55 = bf16[3072,2048]{1,0:T(8,128)(2,1)S(1)} custom-call(bf16[6144,2048]{1,0:T(8,128)(2,1)} %src.1), custom_call_target="tpu_custom_call" | custom-call | bytes 25165824 | tf_op jit(solution)/shard_map/pallas_call | solution.py:90
  48.4 1.5 %collective-permute-start.12 = (bf16[20,768]{1,0:T(8,128)(2,1)S(1)}, bf16[20,768]{1,0:T(8,128)(2,1)S(1)}, u32[]{:S(2)}, u32[]{:S(2)}) collective-permute-start(bf16[20,768]{1,0:T(8,128)(2,1)S(1)} %fusion.30), channel_id=1, source_target_pairs={{0,2},{1,3},{2,0},{3,1},{4,6},{5,7},{6,4},{7,5},{8,10},{9,11},{10,... | collective-permute-start | bytes 92168 | tf_op jit(solution)/shard_map/ppermute | solution.py:20
  49.9 3.9 %collective-permute-done.7 = f32[2,20,768]{2,1,0:T(8,128)S(1)} collective-permute-done((f32[2,20,768]{2,1,0:T(8,128)S(1)}, f32[2,20,768]{2,1,0:T(8,128)S(1)}, u32[]{:S(2)}, u32[]{:S(2)}) %collective-permute-start.7) | collective-permute-done | bytes 122912 | tf_op jit(solution)/shard_map/ppermute | solution.py:20
  54.8 3.1 %collective-permute-done.8 = bf16[20,768]{1,0:T(8,128)(2,1)S(1)} collective-permute-done((bf16[20,768]{1,0:T(8,128)(2,1)S(1)}, bf16[20,768]{1,0:T(8,128)(2,1)S(1)}, u32[]{:S(2)}, u32[]{:S(2)}) %collective-permute-start.8) | collective-permute-done | bytes 30752 | tf_op jit(solution)/shard_map/ppermute | solution.py:20
  57.9 1.8 %fusion.20 = f32[20,2048]{1,0:T(8,128)S(1)} fusion(bf16[3072,2048]{1,0:T(8,128)(2,1)S(1)} %shard_map.56, bf16[20,1536]{1,0:T(8,128)(2,1)S(1)} %collective-permute-done.13, bf16[20,1536]{1,0:T(8,128)(2,1)S(1)} %maximum_select_fusion.5, pred[]{:T(512)S(6)} %eq.8), kind=kOutput, calls=%fused_computation.34 | convolution fusion | flops 252211200 | bytes 12869633 | tf_op jit(solution)/shard_map/dot_general | solution.py:144
  59.7 1.8 %convolution_add_fusion = f32[20,2048]{1,0:T(8,128)S(1)} fusion(f32[20,2048]{1,0:T(8,128)S(1)} %fusion.20, bf16[3072,2048]{1,0:T(8,128)(2,1)S(1)} %shard_map.55, bf16[20,1536]{1,0:T(8,128)(2,1)S(1)} %collective-permute-done.9, bf16[20,1536]{1,0:T(8,128)(2,1)S(1)} %maximum_select_fusion.4, pred[]{:T(512)S(6)} %eq.8), kind=kOutput, calls=%fused_computation.9 | convolution fusion | flops 252252160 | bytes 13033473 | tf_op jit(solution)/shard_map/dot_general | solution.py:144
  62.0 1.1 %collective-permute-start.16 = (f32[5,2048]{1,0:T(8,128)S(1)}, f32[5,2048]{1,0:T(8,128)S(1)}, u32[]{:S(2)}, u32[]{:S(2)}) collective-permute-start(f32[5,2048]{1,0:T(8,128)S(1)} %get-tuple-element.12), channel_id=1, source_target_pairs={{0,12},{4,8},{8,4},{12,0},{1,13},{5,9},{9,5},{13,1},{2,14},{6,10},... | collective-permute-start | bytes 122888 | tf_op jit(solution)/shard_map/ppermute | solution.py:61
  63.1 2.0 %collective-permute-start.15 = (f32[5,2048]{1,0:T(8,128)S(1)}, f32[5,2048]{1,0:T(8,128)S(1)}, u32[]{:S(2)}, u32[]{:S(2)}) collective-permute-start(f32[5,2048]{1,0:T(8,128)S(1)} %get-tuple-element.13), channel_id=1, source_target_pairs={{0,8},{4,12},{8,0},{12,4},{1,9},{5,13},{9,1},{13,5},{2,10},{6,14},... | collective-permute-start | bytes 122888 | tf_op jit(solution)/shard_map/ppermute | solution.py:61
  65.1 1.0 %collective-permute-done.14 = f32[5,2048]{1,0:T(8,128)S(1)} collective-permute-done((f32[5,2048]{1,0:T(8,128)S(1)}, f32[5,2048]{1,0:T(8,128)S(1)}, u32[]{:S(2)}, u32[]{:S(2)}) %collective-permute-start.14) | collective-permute-done | bytes 40992 | tf_op jit(solution)/shard_map/ppermute | solution.py:61
  66.1 2.7 %collective-permute-done.16 = f32[5,2048]{1,0:T(8,128)S(1)} collective-permute-done((f32[5,2048]{1,0:T(8,128)S(1)}, f32[5,2048]{1,0:T(8,128)S(1)}, u32[]{:S(2)}, u32[]{:S(2)}) %collective-permute-start.16) | collective-permute-done | bytes 40992 | tf_op jit(solution)/shard_map/ppermute | solution.py:61
  68.8 2.7 %collective-permute-done.15 = f32[5,2048]{1,0:T(8,128)S(1)} collective-permute-done((f32[5,2048]{1,0:T(8,128)S(1)}, f32[5,2048]{1,0:T(8,128)S(1)}, u32[]{:S(2)}, u32[]{:S(2)}) %collective-permute-start.15) | collective-permute-done | bytes 40992 | tf_op jit(solution)/shard_map/ppermute | solution.py:61
  (53 shorter events, 7.6 us)
Async XLA Ops:
  0.0 21.7 %copy-start.1 = (f32[2048]{0:T(1024)S(1)}, f32[2048]{0:T(1024)}, u32[]{:S(2)}) copy-start(f32[2048]{0:T(1024)} %param.6) | copy-start | bytes 24580
  0.0 6.7 %collective-permute-start = (bf16[5,2048]{1,0:T(8,128)(2,1)}, bf16[5,2048]{1,0:T(8,128)(2,1)S(1)}, u32[]{:S(2)}, u32[]{:S(2)}) collective-permute-start(bf16[5,2048]{1,0:T(8,128)(2,1)} %param.5), channel_id=1, source_target_pairs={{0,4},{4,0},{8,12},{12,8},{1,5},{5,1},{9,13},{13,9},{2,6},{6,2},{1... | collective-permute-start | bytes 61448 | tf_op jit(solution)/shard_map/ppermute | solution.py:70
  3.0 8.1 %collective-permute-start.2 = (bf16[5,2048]{1,0:T(8,128)(2,1)}, bf16[5,2048]{1,0:T(8,128)(2,1)S(1)}, u32[]{:S(2)}, u32[]{:S(2)}) collective-permute-start(bf16[5,2048]{1,0:T(8,128)(2,1)} %param.5), channel_id=1, source_target_pairs={{0,12},{4,8},{8,4},{12,0},{1,13},{5,9},{9,5},{13,1},{2,14},{6,10},... | collective-permute-start | bytes 61448 | tf_op jit(solution)/shard_map/ppermute | solution.py:70
  5.5 5.4 %collective-permute-start.1 = (bf16[5,2048]{1,0:T(8,128)(2,1)}, bf16[5,2048]{1,0:T(8,128)(2,1)S(1)}, u32[]{:S(2)}, u32[]{:S(2)}) collective-permute-start(bf16[5,2048]{1,0:T(8,128)(2,1)} %param.5), channel_id=1, source_target_pairs={{0,8},{4,12},{8,0},{12,4},{1,9},{5,13},{9,1},{13,5},{2,10},{6,14},... | collective-permute-start | bytes 61448 | tf_op jit(solution)/shard_map/ppermute | solution.py:70
  11.6 3.0 %collective-permute-start.5 = (f32[20]{0:T(128)S(1)}, f32[20]{0:T(128)S(1)}, u32[]{:S(2)}, u32[]{:S(2)}) collective-permute-start(f32[20]{0:T(128)S(1)} %fusion.8), channel_id=1, source_target_pairs={{0,3},{1,2},{2,1},{3,0},{4,7},{5,6},{6,5},{7,4},{8,11},{9,10},{10,... | collective-permute-start | bytes 248 | tf_op jit(solution)/shard_map/ppermute | solution.py:77
  11.7 3.6 %collective-permute-start.4 = (f32[20]{0:T(128)S(1)}, f32[20]{0:T(128)S(1)}, u32[]{:S(2)}, u32[]{:S(2)}) collective-permute-start(f32[20]{0:T(128)S(1)} %fusion.8), channel_id=1, source_target_pairs={{0,2},{1,3},{2,0},{3,1},{4,6},{5,7},{6,4},{7,5},{8,10},{9,11},{10,... | collective-permute-start | bytes 248 | tf_op jit(solution)/shard_map/ppermute | solution.py:77
  13.2 2.1 %collective-permute-start.3 = (f32[20]{0:T(128)S(1)}, f32[20]{0:T(128)S(1)}, u32[]{:S(2)}, u32[]{:S(2)}) collective-permute-start(f32[20]{0:T(128)S(1)} %fusion.8), channel_id=1, source_target_pairs={{0,1},{1,0},{2,3},{3,2},{4,5},{5,4},{6,7},{7,6},{8,9},{9,8},{10,11... | collective-permute-start | bytes 248 | tf_op jit(solution)/shard_map/ppermute | solution.py:77
  16.0 15.5 %copy-start = (bf16[2048,6144]{1,0:T(8,128)(2,1)S(1)}, bf16[2048,6144]{1,0:T(8,128)(2,1)}, u32[]{:S(2)}) copy-start(bf16[2048,6144]{1,0:T(8,128)(2,1)} %param.7) | copy-start | bytes 75497472
  35.1 1.7 %collective-permute-start.10 = (f32[2,20,1536]{2,1,0:T(8,128)S(1)}, f32[2,20,1536]{2,1,0:T(8,128)S(1)}, u32[]{:S(2)}, u32[]{:S(2)}) collective-permute-start(f32[2,20,1536]{2,1,0:T(8,128)S(1)} %pad_maximum_fusion.1), channel_id=1, source_target_pairs={{0,1},{1,0},{2,3},{3,2},{4,5},{5,4},{6,7},{7,6},{8,9},{9,8},{10,11... | collective-permute-start | bytes 737288 | tf_op jit(solution)/shard_map/ppermute | solution.py:20
  35.6 2.8 %collective-permute-start.6 = (f32[2,20,1536]{2,1,0:T(8,128)S(1)}, f32[2,20,1536]{2,1,0:T(8,128)S(1)}, u32[]{:S(2)}, u32[]{:S(2)}) collective-permute-start(f32[2,20,1536]{2,1,0:T(8,128)S(1)} %pad_maximum_fusion), channel_id=1, source_target_pairs={{0,1},{1,0},{2,3},{3,2},{4,5},{5,4},{6,7},{7,6},{8,9},{9,8},{10,11... | collective-permute-start | bytes 737288 | tf_op jit(solution)/shard_map/ppermute | solution.py:20
  36.8 11.5 %collective-permute-start.11 = (f32[2,20,768]{2,1,0:T(8,128)S(1)}, f32[2,20,768]{2,1,0:T(8,128)S(1)}, u32[]{:S(2)}, u32[]{:S(2)}) collective-permute-start(f32[2,20,768]{2,1,0:T(8,128)S(1)} %pad_maximum_fusion.3), channel_id=1, source_target_pairs={{0,2},{1,3},{2,0},{3,1},{4,6},{5,7},{6,4},{7,5},{8,10},{9,11},{10,... | collective-permute-start | bytes 368648 | tf_op jit(solution)/shard_map/ppermute | solution.py:20
  47.7 6.1 %collective-permute-start.7 = (f32[2,20,768]{2,1,0:T(8,128)S(1)}, f32[2,20,768]{2,1,0:T(8,128)S(1)}, u32[]{:S(2)}, u32[]{:S(2)}) collective-permute-start(f32[2,20,768]{2,1,0:T(8,128)S(1)} %pad_maximum_fusion.2), channel_id=1, source_target_pairs={{0,2},{1,3},{2,0},{3,1},{4,6},{5,7},{6,4},{7,5},{8,10},{9,11},{10,... | collective-permute-start | bytes 368648 | tf_op jit(solution)/shard_map/ppermute | solution.py:20
  48.4 6.3 %collective-permute-start.12 = (bf16[20,768]{1,0:T(8,128)(2,1)S(1)}, bf16[20,768]{1,0:T(8,128)(2,1)S(1)}, u32[]{:S(2)}, u32[]{:S(2)}) collective-permute-start(bf16[20,768]{1,0:T(8,128)(2,1)S(1)} %fusion.30), channel_id=1, source_target_pairs={{0,2},{1,3},{2,0},{3,1},{4,6},{5,7},{6,4},{7,5},{8,10},{9,11},{10,... | collective-permute-start | bytes 92168 | tf_op jit(solution)/shard_map/ppermute | solution.py:20
  53.8 4.0 %collective-permute-start.8 = (bf16[20,768]{1,0:T(8,128)(2,1)S(1)}, bf16[20,768]{1,0:T(8,128)(2,1)S(1)}, u32[]{:S(2)}, u32[]{:S(2)}) collective-permute-start(bf16[20,768]{1,0:T(8,128)(2,1)S(1)} %fusion.34), channel_id=1, source_target_pairs={{0,2},{1,3},{2,0},{3,1},{4,6},{5,7},{6,4},{7,5},{8,10},{9,11},{10,... | collective-permute-start | bytes 92168 | tf_op jit(solution)/shard_map/ppermute | solution.py:20
  54.7 3.3 %collective-permute-start.13 = (bf16[20,1536]{1,0:T(8,128)(2,1)S(1)}, bf16[20,1536]{1,0:T(8,128)(2,1)S(1)}, u32[]{:S(2)}, u32[]{:S(2)}) collective-permute-start(bf16[20,1536]{1,0:T(8,128)(2,1)S(1)} %maximum_select_fusion.5), channel_id=1, source_target_pairs={{0,1},{1,0},{2,3},{3,2},{4,5},{5,4},{6,7},{7,6},{8,9},{9,8},{10,11... | collective-permute-start | bytes 184328 | tf_op jit(solution)/shard_map/ppermute | solution.py:20
  57.9 1.8 %collective-permute-start.9 = (bf16[20,1536]{1,0:T(8,128)(2,1)S(1)}, bf16[20,1536]{1,0:T(8,128)(2,1)S(1)}, u32[]{:S(2)}, u32[]{:S(2)}) collective-permute-start(bf16[20,1536]{1,0:T(8,128)(2,1)S(1)} %maximum_select_fusion.4), channel_id=1, source_target_pairs={{0,1},{1,0},{2,3},{3,2},{4,5},{5,4},{6,7},{7,6},{8,9},{9,8},{10,11... | collective-permute-start | bytes 184328 | tf_op jit(solution)/shard_map/ppermute | solution.py:20
  61.5 4.6 %collective-permute-start.14 = (f32[5,2048]{1,0:T(8,128)S(1)}, f32[5,2048]{1,0:T(8,128)S(1)}, u32[]{:S(2)}, u32[]{:S(2)}) collective-permute-start(f32[5,2048]{1,0:T(8,128)S(1)} %get-tuple-element.11), channel_id=1, source_target_pairs={{0,4},{4,0},{8,12},{12,8},{1,5},{5,1},{9,13},{13,9},{2,6},{6,2},{1... | collective-permute-start | bytes 122888 | tf_op jit(solution)/shard_map/ppermute | solution.py:61
  62.0 6.8 %collective-permute-start.16 = (f32[5,2048]{1,0:T(8,128)S(1)}, f32[5,2048]{1,0:T(8,128)S(1)}, u32[]{:S(2)}, u32[]{:S(2)}) collective-permute-start(f32[5,2048]{1,0:T(8,128)S(1)} %get-tuple-element.12), channel_id=1, source_target_pairs={{0,12},{4,8},{8,4},{12,0},{1,13},{5,9},{9,5},{13,1},{2,14},{6,10},... | collective-permute-start | bytes 122888 | tf_op jit(solution)/shard_map/ppermute | solution.py:61
  63.1 8.5 %collective-permute-start.15 = (f32[5,2048]{1,0:T(8,128)S(1)}, f32[5,2048]{1,0:T(8,128)S(1)}, u32[]{:S(2)}, u32[]{:S(2)}) collective-permute-start(f32[5,2048]{1,0:T(8,128)S(1)} %get-tuple-element.13), channel_id=1, source_target_pairs={{0,8},{4,12},{8,0},{12,4},{1,9},{5,13},{9,1},{13,5},{2,10},{6,14},... | collective-permute-start | bytes 122888 | tf_op jit(solution)/shard_map/ppermute | solution.py:61

commit v12 on v11

--- a/solution.py
+++ b/solution.py
@@ -130,8 +130,12 @@
             first = xor_reduce_scatter([gate_part, up_part], "gy", ngy, 1, gy_levels[:1])
             if c == 0:
                 source, _ = lax.optimization_barrier((w_down, first[0]))
-                staged = [rows_to_vmem(source, k * step, step) for k in range(chunks)]
+                staged = [rows_to_vmem(source, 0, step)]
             gate, up = xor_reduce_scatter(first, "gy", ngy, 1, gy_levels[1:])
+            if c == 0:
+                for k in range(1, chunks):
+                    source, _ = lax.optimization_barrier((w_down, gate))
+                    staged.append(rows_to_vmem(source, k * step, step))
         else:
             gate = lax.psum_scatter(gate_part, "gy", scatter_dimension=1, tiled=True)
             up = lax.psum_scatter(up_part, "gy", scatter_dimension=1, tiled=True)

time: 72.4 us -> 67.7 us (0.935)
  waiting for transfers between devices: 20 us -> 14.3 us
  starting transfers between devices: 16.4 us -> 17.4 us
    ppermute x8, waiting for transfers between devices: 7.91 us -> 2.52 us  [exchange(): return lax.ppermute(x, axis, [(a, a ^ 1 << s) for a in range(n)])]
    ppermute x8, starting transfers between devices: 5.34 us -> 6.29 us  [exchange(): return lax.ppermute(x, axis, [(a, a ^ 1 << s) for a in range(n)])]
  transfers between devices with their start and end apart: 17 -> 17, of which waited for: 9 -> 9; matrix products, arithmetic and copies ran while one was open for 5% -> 5% of each run, Pallas kernels for 13% -> 14%
where the time goes in v12:
time: 67.7 us; the launch traced here: 67.4 us
  matrix products  19.2 us (28%)
  starting transfers between devices  17.4 us (26%)
  waiting for transfers between devices  14.3 us (21%)
  Pallas kernels  9.17 us (14%)
  local copies, waits for them, and re-layouts  6 us (9%)
  other arithmetic  1.18 us (2%)
    dot_general x2, matrix products, local(): up_part = jnp.dot(piece, w_up[:, cols], preferred_element_type=jnp.float32)  12 us
    pallas_call x2, Pallas kernels, rows_to_vmem(): pl.pallas_call(kernel, out_shape=jax.ShapeDtypeStruct((count, w.shape[1])...  9.17 us
    ppermute x8, starting transfers between devices, exchange(): return lax.ppermute(x, axis, [(a, a ^ 1 << s) for a in range(n)])  6.29 us
    ppermute x3, waiting for transfers between devices, fanout_reduce_scatter(): own = own + lax.ppermute(block, axis, [(a, a ^ k) for a in range(n)])  6.12 us
    ppermute x3, starting transfers between devices, fanout_all_gather(): lax.ppermute(x, axis, [(a, a ^ k) for a in range(n)])  5.62 us
    ppermute x3, waiting for transfers between devices, fanout_all_gather(): lax.ppermute(x, axis, [(a, a ^ k) for a in range(n)])  3.86 us
    dot_general x2, matrix products, local(): jnp.dot(piece, w_gate[:, cols], preferred_element_type=jnp.float32)  3.61 us
    ppermute x3, starting transfers between devices, fanout_reduce_scatter(): own = own + lax.ppermute(block, axis, [(a, a ^ k) for a in range(n)])  3.55 us
  transfers between devices with their start and end apart: 17, of which 9 were waited for; matrix products, arithmetic and copies ran while one was open for 5% of the time, Pallas kernels for 14%

profile of v12, /device:TPU:0, one launch (start us, length us, event | category | flops | bytes accessed | tf_op | source)
XLA Modules:
  0.0 67.4 jit_solution(9361006761742371320)
XLA Ops:
  0.0 3.0 %collective-permute-start = (bf16[5,2048]{1,0:T(8,128)(2,1)}, bf16[5,2048]{1,0:T(8,128)(2,1)S(1)}, u32[]{:S(2)}, u32[]{:S(2)}) collective-permute-start(bf16[5,2048]{1,0:T(8,128)(2,1)} %param.5), channel_id=1, source_target_pairs={{0,4},{4,0},{8,12},{12,8},{1,5},{5,1},{9,13},{13,9},{2,6},{6,2},{1... | collective-permute-start | bytes 61448 | tf_op jit(solution)/shard_map/ppermute | solution.py:70
  3.0 2.5 %collective-permute-start.2 = (bf16[5,2048]{1,0:T(8,128)(2,1)}, bf16[5,2048]{1,0:T(8,128)(2,1)S(1)}, u32[]{:S(2)}, u32[]{:S(2)}) collective-permute-start(bf16[5,2048]{1,0:T(8,128)(2,1)} %param.5), channel_id=1, source_target_pairs={{0,12},{4,8},{8,4},{12,0},{1,13},{5,9},{9,5},{13,1},{2,14},{6,10},... | collective-permute-start | bytes 61448 | tf_op jit(solution)/shard_map/ppermute | solution.py:70
  5.7 1.0 %dynamic_update_slice.12 = bf16[20,2048]{1,0:T(8,128)(2,1)S(1)} dynamic-update-slice(bf16[20,2048]{1,0:T(8,128)(2,1)S(1)} %broadcast_in_dim.15, bf16[5,2048]{1,0:T(8,128)(2,1)} %param.5, s32[]{:T(128)S(6)} %select_n.86, s32[]{:T(128)} %constant.19.clone.1) | dynamic-update-slice | bytes 40964 | tf_op jit(solution)/shard_map/dynamic_update_slice | solution.py:71
  7.0 3.9 %collective-permute-done.1 = bf16[5,2048]{1,0:T(8,128)(2,1)S(1)} collective-permute-done((bf16[5,2048]{1,0:T(8,128)(2,1)}, bf16[5,2048]{1,0:T(8,128)(2,1)S(1)}, u32[]{:S(2)}, u32[]{:S(2)}) %collective-permute-start.1) | collective-permute-done | bytes 20512 | tf_op jit(solution)/shard_map/ppermute | solution.py:70
  11.7 1.6 %collective-permute-start.4 = (f32[20]{0:T(128)S(1)}, f32[20]{0:T(128)S(1)}, u32[]{:S(2)}, u32[]{:S(2)}) collective-permute-start(f32[20]{0:T(128)S(1)} %fusion.8), channel_id=1, source_target_pairs={{0,2},{1,3},{2,0},{3,1},{4,6},{5,7},{6,4},{7,5},{8,10},{9,11},{10,... | collective-permute-start | bytes 248 | tf_op jit(solution)/shard_map/ppermute | solution.py:77
  13.5 1.1 %collective-permute-done.5 = f32[20]{0:T(128)S(1)} collective-permute-done((f32[20]{0:T(128)S(1)}, f32[20]{0:T(128)S(1)}, u32[]{:S(2)}, u32[]{:S(2)}) %collective-permute-start.5) | collective-permute-done | bytes 112 | tf_op jit(solution)/shard_map/ppermute | solution.py:77
  16.0 5.8 %fusion.4 = f32[20,3072]{1,0:T(8,128)S(1)} fusion(bf16[2048,6144]{1,0:T(8,128)(2,1)} %param.8, bf16[20,2048]{1,0:T(8,128)(2,1)S(1)} %dynamic_update_slice.15, f32[2048]{0:T(1024)} %param.6, f32[20]{0:T(128)S(1)} %add_rsqrt_fusion), kind=kOutput, calls=%fused_computation.5 | convolution fusion | flops 251822080 | bytes 12918864 | tf_op jit(solution)/shard_map/dot_general | solution.py:128
  21.7 6.3 %fusion = f32[20,3072]{1,0:T(8,128)S(1)} fusion(bf16[2048,6144]{1,0:T(8,128)(2,1)} %param.8, bf16[20,2048]{1,0:T(8,128)(2,1)S(1)} %dynamic_update_slice.15, f32[2048]{0:T(1024)S(1)} %copy-done.1, f32[20]{0:T(128)S(1)} %add_rsqrt_fusion), kind=kOutput, calls=%fused_computation.1 | convolution fusion | flops 251822080 | bytes 12918864 | tf_op jit(solution)/shard_map/dot_general | solution.py:128
  28.0 3.4 %copy-done = bf16[2048,6144]{1,0:T(8,128)(2,1)S(1)} copy-done((bf16[2048,6144]{1,0:T(8,128)(2,1)S(1)}, bf16[2048,6144]{1,0:T(8,128)(2,1)}, u32[]{:S(2)}) %copy-start) | copy-done | bytes 25165848
  31.4 1.8 %fusion.2 = f32[20,3072]{1,0:T(8,128)S(1)} fusion(bf16[2048,6144]{1,0:T(8,128)(2,1)S(1)} %copy-done, bf16[20,2048]{1,0:T(8,128)(2,1)S(1)} %dynamic_update_slice.15, f32[2048]{0:T(1024)S(1)} %copy-done.1, f32[20]{0:T(128)S(1)} %add_rsqrt_fusion), kind=kOutput, calls=%fused_computation.3 | convolution fusion | flops 251822080 | bytes 12935680 | tf_op jit(solution)/shard_map/dot_general | solution.py:127
  33.2 1.8 %fusion.6 = f32[20,3072]{1,0:T(8,128)S(1)} fusion(bf16[2048,6144]{1,0:T(8,128)(2,1)S(1)} %copy-done, bf16[20,2048]{1,0:T(8,128)(2,1)S(1)} %dynamic_update_slice.15, f32[2048]{0:T(1024)S(1)} %copy-done.1, f32[20]{0:T(128)S(1)} %add_rsqrt_fusion), kind=kOutput, calls=%fused_computation.7 | convolution fusion | flops 251822080 | bytes 12935680 | tf_op jit(solution)/shard_map/dot_general | solution.py:127
  35.8 1.0 %collective-permute-done.10 = f32[2,20,1536]{2,1,0:T(8,128)S(1)} collective-permute-done((f32[2,20,1536]{2,1,0:T(8,128)S(1)}, f32[2,20,1536]{2,1,0:T(8,128)S(1)}, u32[]{:S(2)}, u32[]{:S(2)}) %collective-permute-start.10) | collective-permute-done | bytes 245792 | tf_op jit(solution)/shard_map/ppermute | solution.py:20
  36.8 1.6 %collective-permute-start.11 = (f32[2,20,768]{2,1,0:T(8,128)S(1)}, f32[2,20,768]{2,1,0:T(8,128)S(1)}, u32[]{:S(2)}, u32[]{:S(2)}) collective-permute-start(f32[2,20,768]{2,1,0:T(8,128)S(1)} %pad_maximum_fusion.3), channel_id=1, source_target_pairs={{0,2},{1,3},{2,0},{3,1},{4,6},{5,7},{6,4},{7,5},{8,10},{9,11},{10,... | collective-permute-start | bytes 368648 | tf_op jit(solution)/shard_map/ppermute | solution.py:20
  39.1 4.6 %shard_map.55 = bf16[3072,2048]{1,0:T(8,128)(2,1)S(1)} custom-call(bf16[6144,2048]{1,0:T(8,128)(2,1)} %src.1), custom_call_target="tpu_custom_call" | custom-call | bytes 25165824 | tf_op jit(solution)/shard_map/pallas_call | solution.py:90
  43.8 1.5 %collective-permute-start.12 = (bf16[20,768]{1,0:T(8,128)(2,1)S(1)}, bf16[20,768]{1,0:T(8,128)(2,1)S(1)}, u32[]{:S(2)}, u32[]{:S(2)}) collective-permute-start(bf16[20,768]{1,0:T(8,128)(2,1)S(1)} %fusion.30), channel_id=1, source_target_pairs={{0,2},{1,3},{2,0},{3,1},{4,6},{5,7},{6,4},{7,5},{8,10},{9,11},{10,... | collective-permute-start | bytes 92168 | tf_op jit(solution)/shard_map/ppermute | solution.py:20
  45.3 0.9 %collective-permute-done.7 = f32[2,20,768]{2,1,0:T(8,128)S(1)} collective-permute-done((f32[2,20,768]{2,1,0:T(8,128)S(1)}, f32[2,20,768]{2,1,0:T(8,128)S(1)}, u32[]{:S(2)}, u32[]{:S(2)}) %collective-permute-start.7) | collective-permute-done | bytes 122912 | tf_op jit(solution)/shard_map/ppermute | solution.py:20
  46.2 1.3 %collective-permute-start.8 = (bf16[20,768]{1,0:T(8,128)(2,1)S(1)}, bf16[20,768]{1,0:T(8,128)(2,1)S(1)}, u32[]{:S(2)}, u32[]{:S(2)}) collective-permute-start(bf16[20,768]{1,0:T(8,128)(2,1)S(1)} %fusion.34), channel_id=1, source_target_pairs={{0,2},{1,3},{2,0},{3,1},{4,6},{5,7},{6,4},{7,5},{8,10},{9,11},{10,... | collective-permute-start | bytes 92168 | tf_op jit(solution)/shard_map/ppermute | solution.py:20
  47.6 4.6 %shard_map.56 = bf16[3072,2048]{1,0:T(8,128)(2,1)S(1)} custom-call(bf16[6144,2048]{1,0:T(8,128)(2,1)} %src.1), custom_call_target="tpu_custom_call" | custom-call | bytes 25165824 | tf_op jit(solution)/shard_map/pallas_call | solution.py:90
  53.5 1.8 %fusion.20 = f32[20,2048]{1,0:T(8,128)S(1)} fusion(bf16[3072,2048]{1,0:T(8,128)(2,1)S(1)} %shard_map.56, bf16[20,1536]{1,0:T(8,128)(2,1)S(1)} %collective-permute-done.13, bf16[20,1536]{1,0:T(8,128)(2,1)S(1)} %maximum_select_fusion.5, pred[]{:T(512)S(6)} %eq.8), kind=kOutput, calls=%fused_computation.34 | convolution fusion | flops 252211200 | bytes 12869633 | tf_op jit(solution)/shard_map/dot_general | solution.py:148
  55.3 1.8 %convolution_add_fusion = f32[20,2048]{1,0:T(8,128)S(1)} fusion(f32[20,2048]{1,0:T(8,128)S(1)} %fusion.20, bf16[3072,2048]{1,0:T(8,128)(2,1)S(1)} %shard_map.55, bf16[20,1536]{1,0:T(8,128)(2,1)S(1)} %collective-permute-done.9, bf16[20,1536]{1,0:T(8,128)(2,1)S(1)} %maximum_select_fusion.4, pred[]{:T(512)S(6)} %eq.8), kind=kOutput, calls=%fused_computation.9 | convolution fusion | flops 252252160 | bytes 13033473 | tf_op jit(solution)/shard_map/dot_general | solution.py:148
  57.6 1.1 %collective-permute-start.16 = (f32[5,2048]{1,0:T(8,128)S(1)}, f32[5,2048]{1,0:T(8,128)S(1)}, u32[]{:S(2)}, u32[]{:S(2)}) collective-permute-start(f32[5,2048]{1,0:T(8,128)S(1)} %get-tuple-element.16), channel_id=1, source_target_pairs={{0,12},{4,8},{8,4},{12,0},{1,13},{5,9},{9,5},{13,1},{2,14},{6,10},... | collective-permute-start | bytes 122888 | tf_op jit(solution)/shard_map/ppermute | solution.py:61
  58.7 2.0 %collective-permute-start.15 = (f32[5,2048]{1,0:T(8,128)S(1)}, f32[5,2048]{1,0:T(8,128)S(1)}, u32[]{:S(2)}, u32[]{:S(2)}) collective-permute-start(f32[5,2048]{1,0:T(8,128)S(1)} %get-tuple-element.17), channel_id=1, source_target_pairs={{0,8},{4,12},{8,0},{12,4},{1,9},{5,13},{9,1},{13,5},{2,10},{6,14},... | collective-permute-start | bytes 122888 | tf_op jit(solution)/shard_map/ppermute | solution.py:61
  61.4 2.6 %collective-permute-done.16 = f32[5,2048]{1,0:T(8,128)S(1)} collective-permute-done((f32[5,2048]{1,0:T(8,128)S(1)}, f32[5,2048]{1,0:T(8,128)S(1)}, u32[]{:S(2)}, u32[]{:S(2)}) %collective-permute-start.16) | collective-permute-done | bytes 40992 | tf_op jit(solution)/shard_map/ppermute | solution.py:61
  64.1 2.7 %collective-permute-done.15 = f32[5,2048]{1,0:T(8,128)S(1)} collective-permute-done((f32[5,2048]{1,0:T(8,128)S(1)}, f32[5,2048]{1,0:T(8,128)S(1)}, u32[]{:S(2)}, u32[]{:S(2)}) %collective-permute-start.15) | collective-permute-done | bytes 40992 | tf_op jit(solution)/shard_map/ppermute | solution.py:61
  (53 shorter events, 7.7 us)
Async XLA Ops:
  0.0 21.7 %copy-start.1 = (f32[2048]{0:T(1024)S(1)}, f32[2048]{0:T(1024)}, u32[]{:S(2)}) copy-start(f32[2048]{0:T(1024)} %param.6) | copy-start | bytes 24580
  0.0 6.7 %collective-permute-start = (bf16[5,2048]{1,0:T(8,128)(2,1)}, bf16[5,2048]{1,0:T(8,128)(2,1)S(1)}, u32[]{:S(2)}, u32[]{:S(2)}) collective-permute-start(bf16[5,2048]{1,0:T(8,128)(2,1)} %param.5), channel_id=1, source_target_pairs={{0,4},{4,0},{8,12},{12,8},{1,5},{5,1},{9,13},{13,9},{2,6},{6,2},{1... | collective-permute-start | bytes 61448 | tf_op jit(solution)/shard_map/ppermute | solution.py:70
  3.0 8.1 %collective-permute-start.2 = (bf16[5,2048]{1,0:T(8,128)(2,1)}, bf16[5,2048]{1,0:T(8,128)(2,1)S(1)}, u32[]{:S(2)}, u32[]{:S(2)}) collective-permute-start(bf16[5,2048]{1,0:T(8,128)(2,1)} %param.5), channel_id=1, source_target_pairs={{0,12},{4,8},{8,4},{12,0},{1,13},{5,9},{9,5},{13,1},{2,14},{6,10},... | collective-permute-start | bytes 61448 | tf_op jit(solution)/shard_map/ppermute | solution.py:70
  5.5 5.4 %collective-permute-start.1 = (bf16[5,2048]{1,0:T(8,128)(2,1)}, bf16[5,2048]{1,0:T(8,128)(2,1)S(1)}, u32[]{:S(2)}, u32[]{:S(2)}) collective-permute-start(bf16[5,2048]{1,0:T(8,128)(2,1)} %param.5), channel_id=1, source_target_pairs={{0,8},{4,12},{8,0},{12,4},{1,9},{5,13},{9,1},{13,5},{2,10},{6,14},... | collective-permute-start | bytes 61448 | tf_op jit(solution)/shard_map/ppermute | solution.py:70
  11.6 3.0 %collective-permute-start.5 = (f32[20]{0:T(128)S(1)}, f32[20]{0:T(128)S(1)}, u32[]{:S(2)}, u32[]{:S(2)}) collective-permute-start(f32[20]{0:T(128)S(1)} %fusion.8), channel_id=1, source_target_pairs={{0,3},{1,2},{2,1},{3,0},{4,7},{5,6},{6,5},{7,4},{8,11},{9,10},{10,... | collective-permute-start | bytes 248 | tf_op jit(solution)/shard_map/ppermute | solution.py:77
  11.7 3.6 %collective-permute-start.4 = (f32[20]{0:T(128)S(1)}, f32[20]{0:T(128)S(1)}, u32[]{:S(2)}, u32[]{:S(2)}) collective-permute-start(f32[20]{0:T(128)S(1)} %fusion.8), channel_id=1, source_target_pairs={{0,2},{1,3},{2,0},{3,1},{4,6},{5,7},{6,4},{7,5},{8,10},{9,11},{10,... | collective-permute-start | bytes 248 | tf_op jit(solution)/shard_map/ppermute | solution.py:77
  13.2 2.1 %collective-permute-start.3 = (f32[20]{0:T(128)S(1)}, f32[20]{0:T(128)S(1)}, u32[]{:S(2)}, u32[]{:S(2)}) collective-permute-start(f32[20]{0:T(128)S(1)} %fusion.8), channel_id=1, source_target_pairs={{0,1},{1,0},{2,3},{3,2},{4,5},{5,4},{6,7},{7,6},{8,9},{9,8},{10,11... | collective-permute-start | bytes 248 | tf_op jit(solution)/shard_map/ppermute | solution.py:77
  16.0 15.5 %copy-start = (bf16[2048,6144]{1,0:T(8,128)(2,1)S(1)}, bf16[2048,6144]{1,0:T(8,128)(2,1)}, u32[]{:S(2)}) copy-start(bf16[2048,6144]{1,0:T(8,128)(2,1)} %param.7) | copy-start | bytes 75497472
  35.1 1.7 %collective-permute-start.10 = (f32[2,20,1536]{2,1,0:T(8,128)S(1)}, f32[2,20,1536]{2,1,0:T(8,128)S(1)}, u32[]{:S(2)}, u32[]{:S(2)}) collective-permute-start(f32[2,20,1536]{2,1,0:T(8,128)S(1)} %pad_maximum_fusion.1), channel_id=1, source_target_pairs={{0,1},{1,0},{2,3},{3,2},{4,5},{5,4},{6,7},{7,6},{8,9},{9,8},{10,11... | collective-permute-start | bytes 737288 | tf_op jit(solution)/shard_map/ppermute | solution.py:20
  35.6 2.8 %collective-permute-start.6 = (f32[2,20,1536]{2,1,0:T(8,128)S(1)}, f32[2,20,1536]{2,1,0:T(8,128)S(1)}, u32[]{:S(2)}, u32[]{:S(2)}) collective-permute-start(f32[2,20,1536]{2,1,0:T(8,128)S(1)} %pad_maximum_fusion), channel_id=1, source_target_pairs={{0,1},{1,0},{2,3},{3,2},{4,5},{5,4},{6,7},{7,6},{8,9},{9,8},{10,11... | collective-permute-start | bytes 737288 | tf_op jit(solution)/shard_map/ppermute | solution.py:20
  36.8 6.9 %collective-permute-start.11 = (f32[2,20,768]{2,1,0:T(8,128)S(1)}, f32[2,20,768]{2,1,0:T(8,128)S(1)}, u32[]{:S(2)}, u32[]{:S(2)}) collective-permute-start(f32[2,20,768]{2,1,0:T(8,128)S(1)} %pad_maximum_fusion.3), channel_id=1, source_target_pairs={{0,2},{1,3},{2,0},{3,1},{4,6},{5,7},{6,4},{7,5},{8,10},{9,11},{10,... | collective-permute-start | bytes 368648 | tf_op jit(solution)/shard_map/ppermute | solution.py:20
  38.5 7.7 %collective-permute-start.7 = (f32[2,20,768]{2,1,0:T(8,128)S(1)}, f32[2,20,768]{2,1,0:T(8,128)S(1)}, u32[]{:S(2)}, u32[]{:S(2)}) collective-permute-start(f32[2,20,768]{2,1,0:T(8,128)S(1)} %pad_maximum_fusion.2), channel_id=1, source_target_pairs={{0,2},{1,3},{2,0},{3,1},{4,6},{5,7},{6,4},{7,5},{8,10},{9,11},{10,... | collective-permute-start | bytes 368648 | tf_op jit(solution)/shard_map/ppermute | solution.py:20
  43.8 8.4 %collective-permute-start.12 = (bf16[20,768]{1,0:T(8,128)(2,1)S(1)}, bf16[20,768]{1,0:T(8,128)(2,1)S(1)}, u32[]{:S(2)}, u32[]{:S(2)}) collective-permute-start(bf16[20,768]{1,0:T(8,128)(2,1)S(1)} %fusion.30), channel_id=1, source_target_pairs={{0,2},{1,3},{2,0},{3,1},{4,6},{5,7},{6,4},{7,5},{8,10},{9,11},{10,... | collective-permute-start | bytes 92168 | tf_op jit(solution)/shard_map/ppermute | solution.py:20
  46.2 6.0 %collective-permute-start.8 = (bf16[20,768]{1,0:T(8,128)(2,1)S(1)}, bf16[20,768]{1,0:T(8,128)(2,1)S(1)}, u32[]{:S(2)}, u32[]{:S(2)}) collective-permute-start(bf16[20,768]{1,0:T(8,128)(2,1)S(1)} %fusion.34), channel_id=1, source_target_pairs={{0,2},{1,3},{2,0},{3,1},{4,6},{5,7},{6,4},{7,5},{8,10},{9,11},{10,... | collective-permute-start | bytes 92168 | tf_op jit(solution)/shard_map/ppermute | solution.py:20
  52.2 1.3 %collective-permute-start.13 = (bf16[20,1536]{1,0:T(8,128)(2,1)S(1)}, bf16[20,1536]{1,0:T(8,128)(2,1)S(1)}, u32[]{:S(2)}, u32[]{:S(2)}) collective-permute-start(bf16[20,1536]{1,0:T(8,128)(2,1)S(1)} %maximum_select_fusion.5), channel_id=1, source_target_pairs={{0,1},{1,0},{2,3},{3,2},{4,5},{5,4},{6,7},{7,6},{8,9},{9,8},{10,11... | collective-permute-start | bytes 184328 | tf_op jit(solution)/shard_map/ppermute | solution.py:20
  52.3 3.0 %collective-permute-start.9 = (bf16[20,1536]{1,0:T(8,128)(2,1)S(1)}, bf16[20,1536]{1,0:T(8,128)(2,1)S(1)}, u32[]{:S(2)}, u32[]{:S(2)}) collective-permute-start(bf16[20,1536]{1,0:T(8,128)(2,1)S(1)} %maximum_select_fusion.4), channel_id=1, source_target_pairs={{0,1},{1,0},{2,3},{3,2},{4,5},{5,4},{6,7},{7,6},{8,9},{9,8},{10,11... | collective-permute-start | bytes 184328 | tf_op jit(solution)/shard_map/ppermute | solution.py:20
  57.1 4.3 %collective-permute-start.14 = (f32[5,2048]{1,0:T(8,128)S(1)}, f32[5,2048]{1,0:T(8,128)S(1)}, u32[]{:S(2)}, u32[]{:S(2)}) collective-permute-start(f32[5,2048]{1,0:T(8,128)S(1)} %get-tuple-element.15), channel_id=1, source_target_pairs={{0,4},{4,0},{8,12},{12,8},{1,5},{5,1},{9,13},{13,9},{2,6},{6,2},{1... | collective-permute-start | bytes 122888 | tf_op jit(solution)/shard_map/ppermute | solution.py:61
  57.6 6.5 %collective-permute-start.16 = (f32[5,2048]{1,0:T(8,128)S(1)}, f32[5,2048]{1,0:T(8,128)S(1)}, u32[]{:S(2)}, u32[]{:S(2)}) collective-permute-start(f32[5,2048]{1,0:T(8,128)S(1)} %get-tuple-element.16), channel_id=1, source_target_pairs={{0,12},{4,8},{8,4},{12,0},{1,13},{5,9},{9,5},{13,1},{2,14},{6,10},... | collective-permute-start | bytes 122888 | tf_op jit(solution)/shard_map/ppermute | solution.py:61
  58.7 8.1 %collective-permute-start.15 = (f32[5,2048]{1,0:T(8,128)S(1)}, f32[5,2048]{1,0:T(8,128)S(1)}, u32[]{:S(2)}, u32[]{:S(2)}) collective-permute-start(f32[5,2048]{1,0:T(8,128)S(1)} %get-tuple-element.17), channel_id=1, source_target_pairs={{0,8},{4,12},{8,0},{12,4},{1,9},{5,13},{9,1},{13,5},{2,10},{6,14},... | collective-permute-start | bytes 122888 | tf_op jit(solution)/shard_map/ppermute | solution.py:61

commit v13 on v12

--- a/solution.py
+++ b/solution.py
@@ -10,6 +10,7 @@
 
 EXCHANGE_MAX = 8
 CHUNKS = 2
+STREAMS = 4
 
 
 def pairwise(n):
@@ -83,16 +84,24 @@
     size = count * w.shape[1] * w.dtype.itemsize
 
     def kernel(src, dst, sem):
-        copy = pltpu.make_async_copy(src.at[pl.ds(start, count), :], dst, sem)
-        copy.start()
-        copy.wait()
+        streams = STREAMS if count % (STREAMS * 16) == 0 else 1
+        part = count // streams
+        copies = [
+            pltpu.make_async_copy(
+                src.at[pl.ds(start + i * part, part), :], dst.at[pl.ds(i * part, part), :], sem.at[i])
+            for i in range(streams)
+        ]
+        for copy in copies:
+            copy.start()
+        for copy in copies:
+            copy.wait()
 
     return pl.pallas_call(
         kernel,
         out_shape=jax.ShapeDtypeStruct((count, w.shape[1]), w.dtype),
         in_specs=[pl.BlockSpec(memory_space=pl.ANY)],
         out_specs=pl.BlockSpec(memory_space=pltpu.VMEM),
-        scratch_shapes=[pltpu.SemaphoreType.DMA(())],
+        scratch_shapes=[pltpu.SemaphoreType.DMA((STREAMS,))],
         cost_estimate=pl.CostEstimate(flops=0, transcendentals=0, bytes_accessed=2 * size),
         compiler_params=pltpu.CompilerParams(vmem_limit_bytes=size + (2 << 20)),
     )(pltpu.with_memory_space_constraint(w, pltpu.HBM))

time: 67.7 us -> 67.7 us (level)
  no operation moved by 1% of the time
where the time goes in v13:
time: 67.7 us; the launch traced here: 67.5 us
  matrix products  19.2 us (28%)
  starting transfers between devices  17.4 us (26%)
  waiting for transfers between devices  14.2 us (21%)
  Pallas kernels  9.37 us (14%)
  local copies, waits for them, and re-layouts  6 us (9%)
  other arithmetic  1.18 us (2%)
    dot_general x2, matrix products, local(): up_part = jnp.dot(piece, w_up[:, cols], preferred_element_type=jnp.float32)  12 us
    pallas_call x2, Pallas kernels, rows_to_vmem(): pl.pallas_call(kernel, out_shape=jax.ShapeDtypeStruct((count, w.shape[1])...  9.37 us
    ppermute x8, starting transfers between devices, exchange(): return lax.ppermute(x, axis, [(a, a ^ 1 << s) for a in range(n)])  6.29 us
    ppermute x3, waiting for transfers between devices, fanout_reduce_scatter(): own = own + lax.ppermute(block, axis, [(a, a ^ k) for a in range(n)])  6.12 us
    ppermute x3, starting transfers between devices, fanout_all_gather(): lax.ppermute(x, axis, [(a, a ^ k) for a in range(n)])  5.62 us
    ppermute x3, waiting for transfers between devices, fanout_all_gather(): lax.ppermute(x, axis, [(a, a ^ k) for a in range(n)])  3.86 us
    dot_general x2, matrix products, local(): jnp.dot(piece, w_gate[:, cols], preferred_element_type=jnp.float32)  3.61 us
    ppermute x3, starting transfers between devices, fanout_reduce_scatter(): own = own + lax.ppermute(block, axis, [(a, a ^ k) for a in range(n)])  3.55 us
  transfers between devices with their start and end apart: 17, of which 9 were waited for; matrix products, arithmetic and copies ran while one was open for 5% of the time, Pallas kernels for 14%

profile of v13, /device:TPU:0, one launch (start us, length us, event | category | flops | bytes accessed | tf_op | source)
XLA Modules:
  0.0 67.5 jit_solution(13582311315862886933)
XLA Ops:
  0.0 3.0 %collective-permute-start = (bf16[5,2048]{1,0:T(8,128)(2,1)}, bf16[5,2048]{1,0:T(8,128)(2,1)S(1)}, u32[]{:S(2)}, u32[]{:S(2)}) collective-permute-start(bf16[5,2048]{1,0:T(8,128)(2,1)} %param.5), channel_id=1, source_target_pairs={{0,4},{4,0},{8,12},{12,8},{1,5},{5,1},{9,13},{13,9},{2,6},{6,2},{1... | collective-permute-start | bytes 61448 | tf_op jit(solution)/shard_map/ppermute | solution.py:71
  3.0 2.5 %collective-permute-start.2 = (bf16[5,2048]{1,0:T(8,128)(2,1)}, bf16[5,2048]{1,0:T(8,128)(2,1)S(1)}, u32[]{:S(2)}, u32[]{:S(2)}) collective-permute-start(bf16[5,2048]{1,0:T(8,128)(2,1)} %param.5), channel_id=1, source_target_pairs={{0,12},{4,8},{8,4},{12,0},{1,13},{5,9},{9,5},{13,1},{2,14},{6,10},... | collective-permute-start | bytes 61448 | tf_op jit(solution)/shard_map/ppermute | solution.py:71
  5.7 1.0 %dynamic_update_slice.12 = bf16[20,2048]{1,0:T(8,128)(2,1)S(1)} dynamic-update-slice(bf16[20,2048]{1,0:T(8,128)(2,1)S(1)} %broadcast_in_dim.15, bf16[5,2048]{1,0:T(8,128)(2,1)} %param.5, s32[]{:T(128)S(6)} %select_n.86, s32[]{:T(128)} %constant.19.clone.1) | dynamic-update-slice | bytes 40964 | tf_op jit(solution)/shard_map/dynamic_update_slice | solution.py:72
  7.0 3.9 %collective-permute-done.1 = bf16[5,2048]{1,0:T(8,128)(2,1)S(1)} collective-permute-done((bf16[5,2048]{1,0:T(8,128)(2,1)}, bf16[5,2048]{1,0:T(8,128)(2,1)S(1)}, u32[]{:S(2)}, u32[]{:S(2)}) %collective-permute-start.1) | collective-permute-done | bytes 20512 | tf_op jit(solution)/shard_map/ppermute | solution.py:71
  11.7 1.6 %collective-permute-start.4 = (f32[20]{0:T(128)S(1)}, f32[20]{0:T(128)S(1)}, u32[]{:S(2)}, u32[]{:S(2)}) collective-permute-start(f32[20]{0:T(128)S(1)} %fusion.8), channel_id=1, source_target_pairs={{0,2},{1,3},{2,0},{3,1},{4,6},{5,7},{6,4},{7,5},{8,10},{9,11},{10,... | collective-permute-start | bytes 248 | tf_op jit(solution)/shard_map/ppermute | solution.py:78
  13.5 1.1 %collective-permute-done.5 = f32[20]{0:T(128)S(1)} collective-permute-done((f32[20]{0:T(128)S(1)}, f32[20]{0:T(128)S(1)}, u32[]{:S(2)}, u32[]{:S(2)}) %collective-permute-start.5) | collective-permute-done | bytes 112 | tf_op jit(solution)/shard_map/ppermute | solution.py:78
  16.0 5.8 %fusion.4 = f32[20,3072]{1,0:T(8,128)S(1)} fusion(bf16[2048,6144]{1,0:T(8,128)(2,1)} %param.8, bf16[20,2048]{1,0:T(8,128)(2,1)S(1)} %dynamic_update_slice.15, f32[2048]{0:T(1024)} %param.6, f32[20]{0:T(128)S(1)} %add_rsqrt_fusion), kind=kOutput, calls=%fused_computation.5 | convolution fusion | flops 251822080 | bytes 12918864 | tf_op jit(solution)/shard_map/dot_general | solution.py:137
  21.7 6.3 %fusion = f32[20,3072]{1,0:T(8,128)S(1)} fusion(bf16[2048,6144]{1,0:T(8,128)(2,1)} %param.8, bf16[20,2048]{1,0:T(8,128)(2,1)S(1)} %dynamic_update_slice.15, f32[2048]{0:T(1024)S(1)} %copy-done.1, f32[20]{0:T(128)S(1)} %add_rsqrt_fusion), kind=kOutput, calls=%fused_computation.1 | convolution fusion | flops 251822080 | bytes 12918864 | tf_op jit(solution)/shard_map/dot_general | solution.py:137
  28.0 3.4 %copy-done = bf16[2048,6144]{1,0:T(8,128)(2,1)S(1)} copy-done((bf16[2048,6144]{1,0:T(8,128)(2,1)S(1)}, bf16[2048,6144]{1,0:T(8,128)(2,1)}, u32[]{:S(2)}) %copy-start) | copy-done | bytes 25165848
  31.4 1.8 %fusion.2 = f32[20,3072]{1,0:T(8,128)S(1)} fusion(bf16[2048,6144]{1,0:T(8,128)(2,1)S(1)} %copy-done, bf16[20,2048]{1,0:T(8,128)(2,1)S(1)} %dynamic_update_slice.15, f32[2048]{0:T(1024)S(1)} %copy-done.1, f32[20]{0:T(128)S(1)} %add_rsqrt_fusion), kind=kOutput, calls=%fused_computation.3 | convolution fusion | flops 251822080 | bytes 12935680 | tf_op jit(solution)/shard_map/dot_general | solution.py:136
  33.2 1.8 %fusion.6 = f32[20,3072]{1,0:T(8,128)S(1)} fusion(bf16[2048,6144]{1,0:T(8,128)(2,1)S(1)} %copy-done, bf16[20,2048]{1,0:T(8,128)(2,1)S(1)} %dynamic_update_slice.15, f32[2048]{0:T(1024)S(1)} %copy-done.1, f32[20]{0:T(128)S(1)} %add_rsqrt_fusion), kind=kOutput, calls=%fused_computation.7 | convolution fusion | flops 251822080 | bytes 12935680 | tf_op jit(solution)/shard_map/dot_general | solution.py:136
  35.8 1.0 %collective-permute-done.10 = f32[2,20,1536]{2,1,0:T(8,128)S(1)} collective-permute-done((f32[2,20,1536]{2,1,0:T(8,128)S(1)}, f32[2,20,1536]{2,1,0:T(8,128)S(1)}, u32[]{:S(2)}, u32[]{:S(2)}) %collective-permute-start.10) | collective-permute-done | bytes 245792 | tf_op jit(solution)/shard_map/ppermute | solution.py:21
  36.8 1.6 %collective-permute-start.11 = (f32[2,20,768]{2,1,0:T(8,128)S(1)}, f32[2,20,768]{2,1,0:T(8,128)S(1)}, u32[]{:S(2)}, u32[]{:S(2)}) collective-permute-start(f32[2,20,768]{2,1,0:T(8,128)S(1)} %pad_maximum_fusion.3), channel_id=1, source_target_pairs={{0,2},{1,3},{2,0},{3,1},{4,6},{5,7},{6,4},{7,5},{8,10},{9,11},{10,... | collective-permute-start | bytes 368648 | tf_op jit(solution)/shard_map/ppermute | solution.py:21
  39.1 4.7 %shard_map.55 = bf16[3072,2048]{1,0:T(8,128)(2,1)S(1)} custom-call(bf16[6144,2048]{1,0:T(8,128)(2,1)} %src.1), custom_call_target="tpu_custom_call" | custom-call | bytes 25165824 | tf_op jit(solution)/shard_map/pallas_call | solution.py:99
  43.9 1.5 %collective-permute-start.12 = (bf16[20,768]{1,0:T(8,128)(2,1)S(1)}, bf16[20,768]{1,0:T(8,128)(2,1)S(1)}, u32[]{:S(2)}, u32[]{:S(2)}) collective-permute-start(bf16[20,768]{1,0:T(8,128)(2,1)S(1)} %fusion.30), channel_id=1, source_target_pairs={{0,2},{1,3},{2,0},{3,1},{4,6},{5,7},{6,4},{7,5},{8,10},{9,11},{10,... | collective-permute-start | bytes 92168 | tf_op jit(solution)/shard_map/ppermute | solution.py:21
  45.4 0.8 %collective-permute-done.7 = f32[2,20,768]{2,1,0:T(8,128)S(1)} collective-permute-done((f32[2,20,768]{2,1,0:T(8,128)S(1)}, f32[2,20,768]{2,1,0:T(8,128)S(1)}, u32[]{:S(2)}, u32[]{:S(2)}) %collective-permute-start.7) | collective-permute-done | bytes 122912 | tf_op jit(solution)/shard_map/ppermute | solution.py:21
  46.2 1.3 %collective-permute-start.8 = (bf16[20,768]{1,0:T(8,128)(2,1)S(1)}, bf16[20,768]{1,0:T(8,128)(2,1)S(1)}, u32[]{:S(2)}, u32[]{:S(2)}) collective-permute-start(bf16[20,768]{1,0:T(8,128)(2,1)S(1)} %fusion.34), channel_id=1, source_target_pairs={{0,2},{1,3},{2,0},{3,1},{4,6},{5,7},{6,4},{7,5},{8,10},{9,11},{10,... | collective-permute-start | bytes 92168 | tf_op jit(solution)/shard_map/ppermute | solution.py:21
  47.6 4.7 %shard_map.56 = bf16[3072,2048]{1,0:T(8,128)(2,1)S(1)} custom-call(bf16[6144,2048]{1,0:T(8,128)(2,1)} %src.1), custom_call_target="tpu_custom_call" | custom-call | bytes 25165824 | tf_op jit(solution)/shard_map/pallas_call | solution.py:99
  53.6 1.8 %fusion.20 = f32[20,2048]{1,0:T(8,128)S(1)} fusion(bf16[3072,2048]{1,0:T(8,128)(2,1)S(1)} %shard_map.56, bf16[20,1536]{1,0:T(8,128)(2,1)S(1)} %collective-permute-done.13, bf16[20,1536]{1,0:T(8,128)(2,1)S(1)} %maximum_select_fusion.5, pred[]{:T(512)S(6)} %eq.8), kind=kOutput, calls=%fused_computation.34 | convolution fusion | flops 252211200 | bytes 12869633 | tf_op jit(solution)/shard_map/dot_general | solution.py:157
  55.4 1.8 %convolution_add_fusion = f32[20,2048]{1,0:T(8,128)S(1)} fusion(f32[20,2048]{1,0:T(8,128)S(1)} %fusion.20, bf16[3072,2048]{1,0:T(8,128)(2,1)S(1)} %shard_map.55, bf16[20,1536]{1,0:T(8,128)(2,1)S(1)} %collective-permute-done.9, bf16[20,1536]{1,0:T(8,128)(2,1)S(1)} %maximum_select_fusion.4, pred[]{:T(512)S(6)} %eq.8), kind=kOutput, calls=%fused_computation.9 | convolution fusion | flops 252252160 | bytes 13033473 | tf_op jit(solution)/shard_map/dot_general | solution.py:157
  57.7 1.1 %collective-permute-start.16 = (f32[5,2048]{1,0:T(8,128)S(1)}, f32[5,2048]{1,0:T(8,128)S(1)}, u32[]{:S(2)}, u32[]{:S(2)}) collective-permute-start(f32[5,2048]{1,0:T(8,128)S(1)} %get-tuple-element.16), channel_id=1, source_target_pairs={{0,12},{4,8},{8,4},{12,0},{1,13},{5,9},{9,5},{13,1},{2,14},{6,10},... | collective-permute-start | bytes 122888 | tf_op jit(solution)/shard_map/ppermute | solution.py:62
  58.8 2.0 %collective-permute-start.15 = (f32[5,2048]{1,0:T(8,128)S(1)}, f32[5,2048]{1,0:T(8,128)S(1)}, u32[]{:S(2)}, u32[]{:S(2)}) collective-permute-start(f32[5,2048]{1,0:T(8,128)S(1)} %get-tuple-element.17), channel_id=1, source_target_pairs={{0,8},{4,12},{8,0},{12,4},{1,9},{5,13},{9,1},{13,5},{2,10},{6,14},... | collective-permute-start | bytes 122888 | tf_op jit(solution)/shard_map/ppermute | solution.py:62
  61.5 2.6 %collective-permute-done.16 = f32[5,2048]{1,0:T(8,128)S(1)} collective-permute-done((f32[5,2048]{1,0:T(8,128)S(1)}, f32[5,2048]{1,0:T(8,128)S(1)}, u32[]{:S(2)}, u32[]{:S(2)}) %collective-permute-start.16) | collective-permute-done | bytes 40992 | tf_op jit(solution)/shard_map/ppermute | solution.py:62
  64.2 2.7 %collective-permute-done.15 = f32[5,2048]{1,0:T(8,128)S(1)} collective-permute-done((f32[5,2048]{1,0:T(8,128)S(1)}, f32[5,2048]{1,0:T(8,128)S(1)}, u32[]{:S(2)}, u32[]{:S(2)}) %collective-permute-start.15) | collective-permute-done | bytes 40992 | tf_op jit(solution)/shard_map/ppermute | solution.py:62
  (53 shorter events, 7.7 us)
Async XLA Ops:
  0.0 21.7 %copy-start.1 = (f32[2048]{0:T(1024)S(1)}, f32[2048]{0:T(1024)}, u32[]{:S(2)}) copy-start(f32[2048]{0:T(1024)} %param.6) | copy-start | bytes 24580
  0.0 6.7 %collective-permute-start = (bf16[5,2048]{1,0:T(8,128)(2,1)}, bf16[5,2048]{1,0:T(8,128)(2,1)S(1)}, u32[]{:S(2)}, u32[]{:S(2)}) collective-permute-start(bf16[5,2048]{1,0:T(8,128)(2,1)} %param.5), channel_id=1, source_target_pairs={{0,4},{4,0},{8,12},{12,8},{1,5},{5,1},{9,13},{13,9},{2,6},{6,2},{1... | collective-permute-start | bytes 61448 | tf_op jit(solution)/shard_map/ppermute | solution.py:71
  3.0 8.1 %collective-permute-start.2 = (bf16[5,2048]{1,0:T(8,128)(2,1)}, bf16[5,2048]{1,0:T(8,128)(2,1)S(1)}, u32[]{:S(2)}, u32[]{:S(2)}) collective-permute-start(bf16[5,2048]{1,0:T(8,128)(2,1)} %param.5), channel_id=1, source_target_pairs={{0,12},{4,8},{8,4},{12,0},{1,13},{5,9},{9,5},{13,1},{2,14},{6,10},... | collective-permute-start | bytes 61448 | tf_op jit(solution)/shard_map/ppermute | solution.py:71
  5.5 5.4 %collective-permute-start.1 = (bf16[5,2048]{1,0:T(8,128)(2,1)}, bf16[5,2048]{1,0:T(8,128)(2,1)S(1)}, u32[]{:S(2)}, u32[]{:S(2)}) collective-permute-start(bf16[5,2048]{1,0:T(8,128)(2,1)} %param.5), channel_id=1, source_target_pairs={{0,8},{4,12},{8,0},{12,4},{1,9},{5,13},{9,1},{13,5},{2,10},{6,14},... | collective-permute-start | bytes 61448 | tf_op jit(solution)/shard_map/ppermute | solution.py:71
  11.6 3.0 %collective-permute-start.5 = (f32[20]{0:T(128)S(1)}, f32[20]{0:T(128)S(1)}, u32[]{:S(2)}, u32[]{:S(2)}) collective-permute-start(f32[20]{0:T(128)S(1)} %fusion.8), channel_id=1, source_target_pairs={{0,3},{1,2},{2,1},{3,0},{4,7},{5,6},{6,5},{7,4},{8,11},{9,10},{10,... | collective-permute-start | bytes 248 | tf_op jit(solution)/shard_map/ppermute | solution.py:78
  11.7 3.6 %collective-permute-start.4 = (f32[20]{0:T(128)S(1)}, f32[20]{0:T(128)S(1)}, u32[]{:S(2)}, u32[]{:S(2)}) collective-permute-start(f32[20]{0:T(128)S(1)} %fusion.8), channel_id=1, source_target_pairs={{0,2},{1,3},{2,0},{3,1},{4,6},{5,7},{6,4},{7,5},{8,10},{9,11},{10,... | collective-permute-start | bytes 248 | tf_op jit(solution)/shard_map/ppermute | solution.py:78
  13.2 2.1 %collective-permute-start.3 = (f32[20]{0:T(128)S(1)}, f32[20]{0:T(128)S(1)}, u32[]{:S(2)}, u32[]{:S(2)}) collective-permute-start(f32[20]{0:T(128)S(1)} %fusion.8), channel_id=1, source_target_pairs={{0,1},{1,0},{2,3},{3,2},{4,5},{5,4},{6,7},{7,6},{8,9},{9,8},{10,11... | collective-permute-start | bytes 248 | tf_op jit(solution)/shard_map/ppermute | solution.py:78
  16.0 15.5 %copy-start = (bf16[2048,6144]{1,0:T(8,128)(2,1)S(1)}, bf16[2048,6144]{1,0:T(8,128)(2,1)}, u32[]{:S(2)}) copy-start(bf16[2048,6144]{1,0:T(8,128)(2,1)} %param.7) | copy-start | bytes 75497472
  35.1 1.7 %collective-permute-start.10 = (f32[2,20,1536]{2,1,0:T(8,128)S(1)}, f32[2,20,1536]{2,1,0:T(8,128)S(1)}, u32[]{:S(2)}, u32[]{:S(2)}) collective-permute-start(f32[2,20,1536]{2,1,0:T(8,128)S(1)} %pad_maximum_fusion.1), channel_id=1, source_target_pairs={{0,1},{1,0},{2,3},{3,2},{4,5},{5,4},{6,7},{7,6},{8,9},{9,8},{10,11... | collective-permute-start | bytes 737288 | tf_op jit(solution)/shard_map/ppermute | solution.py:21
  35.6 2.8 %collective-permute-start.6 = (f32[2,20,1536]{2,1,0:T(8,128)S(1)}, f32[2,20,1536]{2,1,0:T(8,128)S(1)}, u32[]{:S(2)}, u32[]{:S(2)}) collective-permute-start(f32[2,20,1536]{2,1,0:T(8,128)S(1)} %pad_maximum_fusion), channel_id=1, source_target_pairs={{0,1},{1,0},{2,3},{3,2},{4,5},{5,4},{6,7},{7,6},{8,9},{9,8},{10,11... | collective-permute-start | bytes 737288 | tf_op jit(solution)/shard_map/ppermute | solution.py:21
  36.8 7.0 %collective-permute-start.11 = (f32[2,20,768]{2,1,0:T(8,128)S(1)}, f32[2,20,768]{2,1,0:T(8,128)S(1)}, u32[]{:S(2)}, u32[]{:S(2)}) collective-permute-start(f32[2,20,768]{2,1,0:T(8,128)S(1)} %pad_maximum_fusion.3), channel_id=1, source_target_pairs={{0,2},{1,3},{2,0},{3,1},{4,6},{5,7},{6,4},{7,5},{8,10},{9,11},{10,... | collective-permute-start | bytes 368648 | tf_op jit(solution)/shard_map/ppermute | solution.py:21
  38.5 7.7 %collective-permute-start.7 = (f32[2,20,768]{2,1,0:T(8,128)S(1)}, f32[2,20,768]{2,1,0:T(8,128)S(1)}, u32[]{:S(2)}, u32[]{:S(2)}) collective-permute-start(f32[2,20,768]{2,1,0:T(8,128)S(1)} %pad_maximum_fusion.2), channel_id=1, source_target_pairs={{0,2},{1,3},{2,0},{3,1},{4,6},{5,7},{6,4},{7,5},{8,10},{9,11},{10,... | collective-permute-start | bytes 368648 | tf_op jit(solution)/shard_map/ppermute | solution.py:21
  43.9 8.4 %collective-permute-start.12 = (bf16[20,768]{1,0:T(8,128)(2,1)S(1)}, bf16[20,768]{1,0:T(8,128)(2,1)S(1)}, u32[]{:S(2)}, u32[]{:S(2)}) collective-permute-start(bf16[20,768]{1,0:T(8,128)(2,1)S(1)} %fusion.30), channel_id=1, source_target_pairs={{0,2},{1,3},{2,0},{3,1},{4,6},{5,7},{6,4},{7,5},{8,10},{9,11},{10,... | collective-permute-start | bytes 92168 | tf_op jit(solution)/shard_map/ppermute | solution.py:21
  46.2 6.1 %collective-permute-start.8 = (bf16[20,768]{1,0:T(8,128)(2,1)S(1)}, bf16[20,768]{1,0:T(8,128)(2,1)S(1)}, u32[]{:S(2)}, u32[]{:S(2)}) collective-permute-start(bf16[20,768]{1,0:T(8,128)(2,1)S(1)} %fusion.34), channel_id=1, source_target_pairs={{0,2},{1,3},{2,0},{3,1},{4,6},{5,7},{6,4},{7,5},{8,10},{9,11},{10,... | collective-permute-start | bytes 92168 | tf_op jit(solution)/shard_map/ppermute | solution.py:21
  52.3 1.3 %collective-permute-start.13 = (bf16[20,1536]{1,0:T(8,128)(2,1)S(1)}, bf16[20,1536]{1,0:T(8,128)(2,1)S(1)}, u32[]{:S(2)}, u32[]{:S(2)}) collective-permute-start(bf16[20,1536]{1,0:T(8,128)(2,1)S(1)} %maximum_select_fusion.5), channel_id=1, source_target_pairs={{0,1},{1,0},{2,3},{3,2},{4,5},{5,4},{6,7},{7,6},{8,9},{9,8},{10,11... | collective-permute-start | bytes 184328 | tf_op jit(solution)/shard_map/ppermute | solution.py:21
  52.4 3.0 %collective-permute-start.9 = (bf16[20,1536]{1,0:T(8,128)(2,1)S(1)}, bf16[20,1536]{1,0:T(8,128)(2,1)S(1)}, u32[]{:S(2)}, u32[]{:S(2)}) collective-permute-start(bf16[20,1536]{1,0:T(8,128)(2,1)S(1)} %maximum_select_fusion.4), channel_id=1, source_target_pairs={{0,1},{1,0},{2,3},{3,2},{4,5},{5,4},{6,7},{7,6},{8,9},{9,8},{10,11... | collective-permute-start | bytes 184328 | tf_op jit(solution)/shard_map/ppermute | solution.py:21
  57.2 4.3 %collective-permute-start.14 = (f32[5,2048]{1,0:T(8,128)S(1)}, f32[5,2048]{1,0:T(8,128)S(1)}, u32[]{:S(2)}, u32[]{:S(2)}) collective-permute-start(f32[5,2048]{1,0:T(8,128)S(1)} %get-tuple-element.15), channel_id=1, source_target_pairs={{0,4},{4,0},{8,12},{12,8},{1,5},{5,1},{9,13},{13,9},{2,6},{6,2},{1... | collective-permute-start | bytes 122888 | tf_op jit(solution)/shard_map/ppermute | solution.py:62
  57.7 6.5 %collective-permute-start.16 = (f32[5,2048]{1,0:T(8,128)S(1)}, f32[5,2048]{1,0:T(8,128)S(1)}, u32[]{:S(2)}, u32[]{:S(2)}) collective-permute-start(f32[5,2048]{1,0:T(8,128)S(1)} %get-tuple-element.16), channel_id=1, source_target_pairs={{0,12},{4,8},{8,4},{12,0},{1,13},{5,9},{9,5},{13,1},{2,14},{6,10},... | collective-permute-start | bytes 122888 | tf_op jit(solution)/shard_map/ppermute | solution.py:62
  58.8 8.1 %collective-permute-start.15 = (f32[5,2048]{1,0:T(8,128)S(1)}, f32[5,2048]{1,0:T(8,128)S(1)}, u32[]{:S(2)}, u32[]{:S(2)}) collective-permute-start(f32[5,2048]{1,0:T(8,128)S(1)} %get-tuple-element.17), channel_id=1, source_target_pairs={{0,8},{4,12},{8,0},{12,4},{1,9},{5,13},{9,1},{13,5},{2,10},{6,14},... | collective-permute-start | bytes 122888 | tf_op jit(solution)/shard_map/ppermute | solution.py:62

commit v14 on v11

--- a/solution.py
+++ b/solution.py
@@ -9,7 +9,7 @@
 epsilon = 1e-06
 
 EXCHANGE_MAX = 8
-CHUNKS = 2
+CHUNKS = 1
 
 
 def pairwise(n):
@@ -122,6 +122,8 @@
     step = width // chunks
     gy_levels = list(range(ngy.bit_length() - 1))
     total = None
+    half = w_down.shape[0] // 2
+    staged = None
     for c in range(chunks):
         cols = slice(c * step, (c + 1) * step)
         gate_part = jnp.dot(piece, w_gate[:, cols], preferred_element_type=jnp.float32)
@@ -130,8 +132,11 @@
             first = xor_reduce_scatter([gate_part, up_part], "gy", ngy, 1, gy_levels[:1])
             if c == 0:
                 source, _ = lax.optimization_barrier((w_down, first[0]))
-                staged = [rows_to_vmem(source, k * step, step) for k in range(chunks)]
+                staged = [rows_to_vmem(source, 0, half)]
             gate, up = xor_reduce_scatter(first, "gy", ngy, 1, gy_levels[1:])
+            if c == 0:
+                source, _ = lax.optimization_barrier((w_down, gate))
+                staged.append(rows_to_vmem(source, half, half))
         else:
             gate = lax.psum_scatter(gate_part, "gy", scatter_dimension=1, tiled=True)
             up = lax.psum_scatter(up_part, "gy", scatter_dimension=1, tiled=True)
@@ -140,9 +145,17 @@
             hidden_all = xor_all_gather(hidden, "gy", ngy, 1, gy_levels[::-1])
         else:
             hidden_all = lax.all_gather(hidden, "gy", axis=1, tiled=True)
-        down = staged[c] if pairwise(ngy) else w_down[cols, :]
-        term = jnp.dot(hidden_all, down, preferred_element_type=jnp.float32)
-        total = term if total is None else total + term
+        for p in range(2):
+            lo, hi = max(c * step, p * half), min((c + 1) * step, (p + 1) * half)
+            if lo >= hi:
+                continue
+            if staged is None:
+                down = w_down[lo:hi, :]
+            else:
+                down = staged[p] if (lo, hi) == (p * half, (p + 1) * half) else staged[p][lo - p * half:hi - p * half]
+            h = hidden_all if (lo, hi) == (c * step, (c + 1) * step) else hidden_all[:, lo - c * step:hi - c * step]
+            term = jnp.dot(h, down, preferred_element_type=jnp.float32)
+            total = term if total is None else total + term
     if pairwise(ngx):
         result = fanout_reduce_scatter(total, "gx", ngx, gx_levels[::-1])
     else:

time: 72.4 us -> 77 us (1.064)
  waiting for transfers between devices: 20 us -> 24.5 us
  matrix products: 19.2 us -> 23.4 us
  local copies, waits for them, and re-layouts: 6 us -> 3.28 us
  starting transfers between devices: 16.4 us -> 14.5 us
    dot_general x2 -> x1, matrix products: 3.61 us -> 9.98 us  [local(): jnp.dot(piece, w_gate[:, cols], preferred_element_type=jnp.float32)]
    ppermute x8 -> x4, waiting for transfers between devices: 7.91 us -> 12.4 us  [exchange(): return lax.ppermute(x, axis, [(a, a ^ 1 << s) for a in range(n)])]
    unnamed x4 -> x2, local copies, waits for them, and re-layouts: 3.42 us -> 0.01 us
    dot_general x2 -> x1, matrix products: 12 us -> 9.98 us  [local(): up_part = jnp.dot(piece, w_up[:, cols], preferred_element_type=jnp.float32)]
    ppermute x8 -> x4, starting transfers between devices: 5.34 us -> 3.38 us  [exchange(): return lax.ppermute(x, axis, [(a, a ^ 1 << s) for a in range(n)])]
  transfers between devices with their start and end apart: 17 -> 13, of which waited for: 9 -> 9; matrix products, arithmetic and copies ran while one was open for 5% -> 2% of each run, Pallas kernels for 13% -> 12%
where the time goes in v14:
time: 77 us; the launch traced here: 76.8 us
  waiting for transfers between devices  24.5 us (32%)
  matrix products  23.4 us (30%)
  starting transfers between devices  14.5 us (19%)
  Pallas kernels  9.17 us (12%)
  local copies, waits for them, and re-layouts  3.28 us (4%)
  other arithmetic  1.69 us (2%)
    ppermute x4, waiting for transfers between devices, exchange(): return lax.ppermute(x, axis, [(a, a ^ 1 << s) for a in range(n)])  12.4 us
    dot_general x1, matrix products, local(): jnp.dot(piece, w_gate[:, cols], preferred_element_type=jnp.float32)  9.98 us
    dot_general x1, matrix products, local(): up_part = jnp.dot(piece, w_up[:, cols], preferred_element_type=jnp.float32)  9.98 us
    pallas_call x2, Pallas kernels, rows_to_vmem(): pl.pallas_call(kernel, out_shape=jax.ShapeDtypeStruct((count, w.shape[1])...  9.17 us
    ppermute x3, waiting for transfers between devices, fanout_reduce_scatter(): own = own + lax.ppermute(block, axis, [(a, a ^ k) for a in range(n)])  6.45 us
    ppermute x3, starting transfers between devices, fanout_all_gather(): lax.ppermute(x, axis, [(a, a ^ k) for a in range(n)])  5.62 us
    ppermute x3, waiting for transfers between devices, fanout_all_gather(): lax.ppermute(x, axis, [(a, a ^ k) for a in range(n)])  3.87 us
    ppermute x3, starting transfers between devices, fanout_reduce_scatter(): own = own + lax.ppermute(block, axis, [(a, a ^ k) for a in range(n)])  3.55 us
  transfers between devices with their start and end apart: 13, of which 9 were waited for; matrix products, arithmetic and copies ran while one was open for 2% of the time, Pallas kernels for 12%

profile of v14, /device:TPU:0, one launch (start us, length us, event | category | flops | bytes accessed | tf_op | source)
XLA Modules:
  0.0 76.8 jit_solution(10524973014020678540)
XLA Ops:
  0.0 3.0 %collective-permute-start = (bf16[5,2048]{1,0:T(8,128)(2,1)}, bf16[5,2048]{1,0:T(8,128)(2,1)S(1)}, u32[]{:S(2)}, u32[]{:S(2)}) collective-permute-start(bf16[5,2048]{1,0:T(8,128)(2,1)} %param.5), channel_id=1, source_target_pairs={{0,4},{4,0},{8,12},{12,8},{1,5},{5,1},{9,13},{13,9},{2,6},{6,2},{1... | collective-permute-start | bytes 61448 | tf_op jit(solution)/shard_map/ppermute | solution.py:70
  3.0 2.5 %collective-permute-start.2 = (bf16[5,2048]{1,0:T(8,128)(2,1)}, bf16[5,2048]{1,0:T(8,128)(2,1)S(1)}, u32[]{:S(2)}, u32[]{:S(2)}) collective-permute-start(bf16[5,2048]{1,0:T(8,128)(2,1)} %param.5), channel_id=1, source_target_pairs={{0,12},{4,8},{8,4},{12,0},{1,13},{5,9},{9,5},{13,1},{2,14},{6,10},... | collective-permute-start | bytes 61448 | tf_op jit(solution)/shard_map/ppermute | solution.py:70
  5.7 1.0 %dynamic_update_slice.12 = bf16[20,2048]{1,0:T(8,128)(2,1)S(1)} dynamic-update-slice(bf16[20,2048]{1,0:T(8,128)(2,1)S(1)} %broadcast_in_dim.15, bf16[5,2048]{1,0:T(8,128)(2,1)} %param.5, s32[]{:T(128)S(6)} %select_n.70, s32[]{:T(128)} %constant.19.clone.1) | dynamic-update-slice | bytes 40964 | tf_op jit(solution)/shard_map/dynamic_update_slice | solution.py:71
  7.0 3.9 %collective-permute-done.1 = bf16[5,2048]{1,0:T(8,128)(2,1)S(1)} collective-permute-done((bf16[5,2048]{1,0:T(8,128)(2,1)}, bf16[5,2048]{1,0:T(8,128)(2,1)S(1)}, u32[]{:S(2)}, u32[]{:S(2)}) %collective-permute-start.1) | collective-permute-done | bytes 20512 | tf_op jit(solution)/shard_map/ppermute | solution.py:70
  11.7 1.6 %collective-permute-start.4 = (f32[20]{0:T(128)S(1)}, f32[20]{0:T(128)S(1)}, u32[]{:S(2)}, u32[]{:S(2)}) collective-permute-start(f32[20]{0:T(128)S(1)} %fusion.2), channel_id=1, source_target_pairs={{0,2},{1,3},{2,0},{3,1},{4,6},{5,7},{6,4},{7,5},{8,10},{9,11},{10,... | collective-permute-start | bytes 248 | tf_op jit(solution)/shard_map/ppermute | solution.py:77
  13.5 1.1 %collective-permute-done.5 = f32[20]{0:T(128)S(1)} collective-permute-done((f32[20]{0:T(128)S(1)}, f32[20]{0:T(128)S(1)}, u32[]{:S(2)}, u32[]{:S(2)}) %collective-permute-start.5) | collective-permute-done | bytes 112 | tf_op jit(solution)/shard_map/ppermute | solution.py:77
  14.6 0.7 collective-permute-done.4
  16.0 10.0 %fusion.12 = f32[20,6144]{1,0:T(8,128)S(1)} fusion(bf16[2048,6144]{1,0:T(8,128)(2,1)} %param.8, bf16[20,2048]{1,0:T(8,128)(2,1)S(1)} %dynamic_update_slice.15, f32[2048]{0:T(1024)} %param.6, f32[20]{0:T(128)S(1)} %add_rsqrt_fusion), kind=kOutput, calls=%fused_computation.27 | convolution fusion | flops 503480320 | bytes 25747536 | tf_op jit(solution)/shard_map/dot_general | solution.py:130
  25.9 10.0 %fusion.14 = f32[20,6144]{1,0:T(8,128)S(1)} fusion(bf16[2048,6144]{1,0:T(8,128)(2,1)} %param.7, bf16[20,2048]{1,0:T(8,128)(2,1)S(1)} %dynamic_update_slice.15, f32[2048]{0:T(1024)S(1)} %copy-done, f32[20]{0:T(128)S(1)} %add_rsqrt_fusion), kind=kOutput, calls=%fused_computation.28 | convolution fusion | flops 503480320 | bytes 25747536 | tf_op jit(solution)/shard_map/dot_general | solution.py:129
  37.2 1.5 %collective-permute-done.6 = f32[2,20,3072]{2,0,1:T(2,128)S(1)} collective-permute-done((f32[2,20,3072]{2,0,1:T(2,128)S(1)}, f32[2,20,3072]{2,0,1:T(2,128)S(1)}, u32[]{:S(2)}, u32[]{:S(2)}) %collective-permute-start.6) | collective-permute-done | bytes 491552 | tf_op jit(solution)/shard_map/ppermute | solution.py:20
  39.3 1.6 %collective-permute-start.7 = (f32[2,20,1536]{2,1,0:T(8,128)S(1)}, f32[2,20,1536]{2,1,0:T(8,128)S(1)}, u32[]{:S(2)}, u32[]{:S(2)}) collective-permute-start(f32[2,20,1536]{2,1,0:T(8,128)S(1)} %pad_maximum_fusion.1), channel_id=1, source_target_pairs={{0,2},{1,3},{2,0},{3,1},{4,6},{5,7},{6,4},{7,5},{8,10},{9,11},{10,... | collective-permute-start | bytes 737288 | tf_op jit(solution)/shard_map/ppermute | solution.py:20
  40.9 7.8 %collective-permute-done.7 = f32[2,20,1536]{2,1,0:T(8,128)S(1)} collective-permute-done((f32[2,20,1536]{2,1,0:T(8,128)S(1)}, f32[2,20,1536]{2,1,0:T(8,128)S(1)}, u32[]{:S(2)}, u32[]{:S(2)}) %collective-permute-start.7) | collective-permute-done | bytes 245792 | tf_op jit(solution)/shard_map/ppermute | solution.py:20
  48.8 1.3 %collective-permute-start.8 = (bf16[20,1536]{1,0:T(8,128)(2,1)S(1)}, bf16[20,1536]{1,0:T(8,128)(2,1)S(1)}, u32[]{:S(2)}, u32[]{:S(2)}) collective-permute-start(bf16[20,1536]{1,0:T(8,128)(2,1)S(1)} %fusion.10), channel_id=1, source_target_pairs={{0,2},{1,3},{2,0},{3,1},{4,6},{5,7},{6,4},{7,5},{8,10},{9,11},{10,... | collective-permute-start | bytes 184328 | tf_op jit(solution)/shard_map/ppermute | solution.py:20
  50.1 3.1 %collective-permute-done.8 = bf16[20,1536]{1,0:T(8,128)(2,1)S(1)} collective-permute-done((bf16[20,1536]{1,0:T(8,128)(2,1)S(1)}, bf16[20,1536]{1,0:T(8,128)(2,1)S(1)}, u32[]{:S(2)}, u32[]{:S(2)}) %collective-permute-start.8) | collective-permute-done | bytes 61472 | tf_op jit(solution)/shard_map/ppermute | solution.py:20
  53.3 4.6 %shard_map.55 = bf16[3072,2048]{1,0:T(8,128)(2,1)S(1)} custom-call(bf16[6144,2048]{1,0:T(8,128)(2,1)} %src.1), custom_call_target="tpu_custom_call" | custom-call | bytes 25165824 | tf_op jit(solution)/shard_map/pallas_call | solution.py:90
  57.9 4.6 %shard_map.56 = bf16[3072,2048]{1,0:T(8,128)(2,1)S(1)} custom-call(bf16[6144,2048]{1,0:T(8,128)(2,1)} %src.1), custom_call_target="tpu_custom_call" | custom-call | bytes 25165824 | tf_op jit(solution)/shard_map/pallas_call | solution.py:90
  62.6 1.7 %fusion.5 = f32[20,2048]{1,0:T(8,128)S(1)} fusion(bf16[3072,2048]{1,0:T(8,128)(2,1)S(1)} %shard_map.56, bf16[20,6144]{1,0:T(8,128)(2,1)S(1)} %maximum_select_fusion), kind=kOutput, calls=%fused_computation.14 | convolution fusion | flops 251658240 | bytes 12894208 | tf_op jit(solution)/shard_map/dot_general | solution.py:157
  64.3 1.7 %convolution_add_fusion = f32[20,2048]{1,0:T(8,128)S(1)} fusion(f32[20,2048]{1,0:T(8,128)S(1)} %fusion.5, bf16[3072,2048]{1,0:T(8,128)(2,1)S(1)} %shard_map.55, bf16[20,6144]{1,0:T(8,128)(2,1)S(1)} %maximum_select_fusion), kind=kOutput, calls=%fused_computation.1 | convolution fusion | flops 251699200 | bytes 13090816 | tf_op jit(solution)/shard_map/dot_general | solution.py:157
  66.6 1.1 %collective-permute-start.12 = (f32[5,2048]{1,0:T(8,128)S(1)}, f32[5,2048]{1,0:T(8,128)S(1)}, u32[]{:S(2)}, u32[]{:S(2)}) collective-permute-start(f32[5,2048]{1,0:T(8,128)S(1)} %get-tuple-element.14), channel_id=1, source_target_pairs={{0,12},{4,8},{8,4},{12,0},{1,13},{5,9},{9,5},{13,1},{2,14},{6,10},... | collective-permute-start | bytes 122888 | tf_op jit(solution)/shard_map/ppermute | solution.py:61
  67.7 2.0 %collective-permute-start.11 = (f32[5,2048]{1,0:T(8,128)S(1)}, f32[5,2048]{1,0:T(8,128)S(1)}, u32[]{:S(2)}, u32[]{:S(2)}) collective-permute-start(f32[5,2048]{1,0:T(8,128)S(1)} %get-tuple-element.15), channel_id=1, source_target_pairs={{0,8},{4,12},{8,0},{12,4},{1,9},{5,13},{9,1},{13,5},{2,10},{6,14},... | collective-permute-start | bytes 122888 | tf_op jit(solution)/shard_map/ppermute | solution.py:61
  69.7 1.0 %collective-permute-done.10 = f32[5,2048]{1,0:T(8,128)S(1)} collective-permute-done((f32[5,2048]{1,0:T(8,128)S(1)}, f32[5,2048]{1,0:T(8,128)S(1)}, u32[]{:S(2)}, u32[]{:S(2)}) %collective-permute-start.10) | collective-permute-done | bytes 40992 | tf_op jit(solution)/shard_map/ppermute | solution.py:61
  70.7 2.7 %collective-permute-done.12 = f32[5,2048]{1,0:T(8,128)S(1)} collective-permute-done((f32[5,2048]{1,0:T(8,128)S(1)}, f32[5,2048]{1,0:T(8,128)S(1)}, u32[]{:S(2)}, u32[]{:S(2)}) %collective-permute-start.12) | collective-permute-done | bytes 40992 | tf_op jit(solution)/shard_map/ppermute | solution.py:61
  73.4 2.7 %collective-permute-done.11 = f32[5,2048]{1,0:T(8,128)S(1)} collective-permute-done((f32[5,2048]{1,0:T(8,128)S(1)}, f32[5,2048]{1,0:T(8,128)S(1)}, u32[]{:S(2)}, u32[]{:S(2)}) %collective-permute-start.11) | collective-permute-done | bytes 40992 | tf_op jit(solution)/shard_map/ppermute | solution.py:61
  76.1 0.6 add_convert_fusion
  (38 shorter events, 4.8 us)
Async XLA Ops:
  0.0 25.9 %copy-start = (f32[2048]{0:T(1024)S(1)}, f32[2048]{0:T(1024)}, u32[]{:S(2)}) copy-start(f32[2048]{0:T(1024)} %param.6) | copy-start | bytes 24580
  0.0 6.7 %collective-permute-start = (bf16[5,2048]{1,0:T(8,128)(2,1)}, bf16[5,2048]{1,0:T(8,128)(2,1)S(1)}, u32[]{:S(2)}, u32[]{:S(2)}) collective-permute-start(bf16[5,2048]{1,0:T(8,128)(2,1)} %param.5), channel_id=1, source_target_pairs={{0,4},{4,0},{8,12},{12,8},{1,5},{5,1},{9,13},{13,9},{2,6},{6,2},{1... | collective-permute-start | bytes 61448 | tf_op jit(solution)/shard_map/ppermute | solution.py:70
  3.0 8.1 %collective-permute-start.2 = (bf16[5,2048]{1,0:T(8,128)(2,1)}, bf16[5,2048]{1,0:T(8,128)(2,1)S(1)}, u32[]{:S(2)}, u32[]{:S(2)}) collective-permute-start(bf16[5,2048]{1,0:T(8,128)(2,1)} %param.5), channel_id=1, source_target_pairs={{0,12},{4,8},{8,4},{12,0},{1,13},{5,9},{9,5},{13,1},{2,14},{6,10},... | collective-permute-start | bytes 61448 | tf_op jit(solution)/shard_map/ppermute | solution.py:70
  5.5 5.4 %collective-permute-start.1 = (bf16[5,2048]{1,0:T(8,128)(2,1)}, bf16[5,2048]{1,0:T(8,128)(2,1)S(1)}, u32[]{:S(2)}, u32[]{:S(2)}) collective-permute-start(bf16[5,2048]{1,0:T(8,128)(2,1)} %param.5), channel_id=1, source_target_pairs={{0,8},{4,12},{8,0},{12,4},{1,9},{5,13},{9,1},{13,5},{2,10},{6,14},... | collective-permute-start | bytes 61448 | tf_op jit(solution)/shard_map/ppermute | solution.py:70
  11.6 3.0 %collective-permute-start.5 = (f32[20]{0:T(128)S(1)}, f32[20]{0:T(128)S(1)}, u32[]{:S(2)}, u32[]{:S(2)}) collective-permute-start(f32[20]{0:T(128)S(1)} %fusion.2), channel_id=1, source_target_pairs={{0,3},{1,2},{2,1},{3,0},{4,7},{5,6},{6,5},{7,4},{8,11},{9,10},{10,... | collective-permute-start | bytes 248 | tf_op jit(solution)/shard_map/ppermute | solution.py:77
  11.7 3.6 %collective-permute-start.4 = (f32[20]{0:T(128)S(1)}, f32[20]{0:T(128)S(1)}, u32[]{:S(2)}, u32[]{:S(2)}) collective-permute-start(f32[20]{0:T(128)S(1)} %fusion.2), channel_id=1, source_target_pairs={{0,2},{1,3},{2,0},{3,1},{4,6},{5,7},{6,4},{7,5},{8,10},{9,11},{10,... | collective-permute-start | bytes 248 | tf_op jit(solution)/shard_map/ppermute | solution.py:77
  13.2 2.1 %collective-permute-start.3 = (f32[20]{0:T(128)S(1)}, f32[20]{0:T(128)S(1)}, u32[]{:S(2)}, u32[]{:S(2)}) collective-permute-start(f32[20]{0:T(128)S(1)} %fusion.2), channel_id=1, source_target_pairs={{0,1},{1,0},{2,3},{3,2},{4,5},{5,4},{6,7},{7,6},{8,9},{9,8},{10,11... | collective-permute-start | bytes 248 | tf_op jit(solution)/shard_map/ppermute | solution.py:77
  36.8 1.9 %collective-permute-start.6 = (f32[2,20,3072]{2,0,1:T(2,128)S(1)}, f32[2,20,3072]{2,0,1:T(2,128)S(1)}, u32[]{:S(2)}, u32[]{:S(2)}) collective-permute-start(f32[2,20,3072]{2,0,1:T(2,128)S(1)} %pad_maximum_fusion), channel_id=1, source_target_pairs={{0,1},{1,0},{2,3},{3,2},{4,5},{5,4},{6,7},{7,6},{8,9},{9,8},{10,11... | collective-permute-start | bytes 1474568 | tf_op jit(solution)/shard_map/ppermute | solution.py:20
  39.3 9.4 %collective-permute-start.7 = (f32[2,20,1536]{2,1,0:T(8,128)S(1)}, f32[2,20,1536]{2,1,0:T(8,128)S(1)}, u32[]{:S(2)}, u32[]{:S(2)}) collective-permute-start(f32[2,20,1536]{2,1,0:T(8,128)S(1)} %pad_maximum_fusion.1), channel_id=1, source_target_pairs={{0,2},{1,3},{2,0},{3,1},{4,6},{5,7},{6,4},{7,5},{8,10},{9,11},{10,... | collective-permute-start | bytes 737288 | tf_op jit(solution)/shard_map/ppermute | solution.py:20
  48.8 4.4 %collective-permute-start.8 = (bf16[20,1536]{1,0:T(8,128)(2,1)S(1)}, bf16[20,1536]{1,0:T(8,128)(2,1)S(1)}, u32[]{:S(2)}, u32[]{:S(2)}) collective-permute-start(bf16[20,1536]{1,0:T(8,128)(2,1)S(1)} %fusion.10), channel_id=1, source_target_pairs={{0,2},{1,3},{2,0},{3,1},{4,6},{5,7},{6,4},{7,5},{8,10},{9,11},{10,... | collective-permute-start | bytes 184328 | tf_op jit(solution)/shard_map/ppermute | solution.py:20
  53.2 9.3 %collective-permute-start.9 = (bf16[20,3072]{1,0:T(8,128)(2,1)S(1)}, bf16[20,3072]{1,0:T(8,128)(2,1)S(1)}, u32[]{:S(2)}, u32[]{:S(2)}) collective-permute-start(bf16[20,3072]{1,0:T(8,128)(2,1)S(1)} %maximum_select_fusion.1), channel_id=1, source_target_pairs={{0,1},{1,0},{2,3},{3,2},{4,5},{5,4},{6,7},{7,6},{8,9},{9,8},{10,11... | collective-permute-start | bytes 368648 | tf_op jit(solution)/shard_map/ppermute | solution.py:20
  66.1 4.6 %collective-permute-start.10 = (f32[5,2048]{1,0:T(8,128)S(1)}, f32[5,2048]{1,0:T(8,128)S(1)}, u32[]{:S(2)}, u32[]{:S(2)}) collective-permute-start(f32[5,2048]{1,0:T(8,128)S(1)} %get-tuple-element.13), channel_id=1, source_target_pairs={{0,4},{4,0},{8,12},{12,8},{1,5},{5,1},{9,13},{13,9},{2,6},{6,2},{1... | collective-permute-start | bytes 122888 | tf_op jit(solution)/shard_map/ppermute | solution.py:61
  66.6 6.8 %collective-permute-start.12 = (f32[5,2048]{1,0:T(8,128)S(1)}, f32[5,2048]{1,0:T(8,128)S(1)}, u32[]{:S(2)}, u32[]{:S(2)}) collective-permute-start(f32[5,2048]{1,0:T(8,128)S(1)} %get-tuple-element.14), channel_id=1, source_target_pairs={{0,12},{4,8},{8,4},{12,0},{1,13},{5,9},{9,5},{13,1},{2,14},{6,10},... | collective-permute-start | bytes 122888 | tf_op jit(solution)/shard_map/ppermute | solution.py:61
  67.7 8.5 %collective-permute-start.11 = (f32[5,2048]{1,0:T(8,128)S(1)}, f32[5,2048]{1,0:T(8,128)S(1)}, u32[]{:S(2)}, u32[]{:S(2)}) collective-permute-start(f32[5,2048]{1,0:T(8,128)S(1)} %get-tuple-element.15), channel_id=1, source_target_pairs={{0,8},{4,12},{8,0},{12,4},{1,9},{5,13},{9,1},{13,5},{2,10},{6,14},... | collective-permute-start | bytes 122888 | tf_op jit(solution)/shard_map/ppermute | solution.py:61

commit v15 on v12

--- a/solution.py
+++ b/solution.py
@@ -98,13 +98,27 @@
     )(pltpu.with_memory_space_constraint(w, pltpu.HBM))
 
 
+def relative_all_gather(x, axis, n):
+    parts = [x] + [lax.ppermute(x, axis, [(a, a ^ k) for a in range(n)]) for k in range(1, n)]
+    return jnp.concatenate(parts, axis=0)
+
+
+def relative_reduce_scatter(x, axis, n):
+    rows = x.shape[0] // n
+    own = x[:rows]
+    for k in range(1, n):
+        block = x[k * rows:(k + 1) * rows]
+        own = own + lax.ppermute(block, axis, [(a, a ^ k) for a in range(n)])
+    return own
+
+
 def local(tokens, norm_gain, w_gate, w_up, w_down):
     ngx = lax.axis_size("gx")
     ngy = lax.axis_size("gy")
     features = tokens.shape[1] * ngy
     gx_levels = list(range(ngx.bit_length() - 1))
     if pairwise(ngx):
-        raw = fanout_all_gather(tokens, "gx", ngx, gx_levels[::-1])
+        raw = relative_all_gather(tokens, "gx", ngx)
     else:
         raw = lax.all_gather(tokens, "gx", axis=0, tiled=True)
     values = raw.astype(jnp.float32)
@@ -148,7 +162,7 @@
         term = jnp.dot(hidden_all, down, preferred_element_type=jnp.float32)
         total = term if total is None else total + term
     if pairwise(ngx):
-        result = fanout_reduce_scatter(total, "gx", ngx, gx_levels[::-1])
+        result = relative_reduce_scatter(total, "gx", ngx)
     else:
         result = lax.psum_scatter(total, "gx", scatter_dimension=0, tiled=True)
     return result.astype(jnp.bfloat16)

time: 67.7 us -> 71.1 us (1.050)
  matrix products: 19.2 us -> 23 us
  local copies, waits for them, and re-layouts: 6 us -> 3.58 us
  waiting for transfers between devices: 14.3 us -> 15.4 us
  other arithmetic: 1.18 us -> 1.97 us
    dot_general x2, matrix products: 3.61 us -> 11.4 us  [local(): jnp.dot(piece, w_gate[:, cols], preferred_element_type=jnp.float32)]
    dot_general x2, matrix products: 12 us -> 8.1 us  [local(): up_part = jnp.dot(piece, w_up[:, cols], preferred_element_type=jnp.float32)]
    ppermute x6, waiting for transfers between devices: 9.98 us -> 11.9 us  [the longest x3 6.06 us: relative_reduce_scatter(): own = own + lax.ppermute(block, axis, [(a, a ^ k) for a in range(n)])]
    dynamic_update_slice x4 -> x0, local copies, waits for them, and re-layouts: 1.87 us -> none  [fanout_all_gather(): lax.dynamic_update_slice_in_dim(out, block, gathered_position(me ^ k, bit...]
    ppermute x8, waiting for transfers between devices: 2.52 us -> 1.67 us  [exchange(): return lax.ppermute(x, axis, [(a, a ^ 1 << s) for a in range(n)])]
    reduce_sum x1, other arithmetic: 0.14 us -> 0.93 us  [local(): local_sq = jnp.sum(values * values, axis=1)]
    unnamed x4 -> x6, local copies, waits for them, and re-layouts: 3.42 us -> 2.89 us
  transfers between devices with their start and end apart: 17 -> 17, of which waited for: 9 -> 10; matrix products, arithmetic and copies ran while one was open for 5% -> 13% of each run, Pallas kernels for 14% -> 13%
where the time goes in v15:
time: 71.1 us; the launch traced here: 70.8 us
  matrix products  23 us (32%)
  starting transfers between devices  17.5 us (25%)
  waiting for transfers between devices  15.4 us (22%)
  Pallas kernels  9.17 us (13%)
  local copies, waits for them, and re-layouts  3.58 us (5%)
  other arithmetic  1.97 us (3%)
    dot_general x2, matrix products, local(): jnp.dot(piece, w_gate[:, cols], preferred_element_type=jnp.float32)  11.4 us
    pallas_call x2, Pallas kernels, rows_to_vmem(): pl.pallas_call(kernel, out_shape=jax.ShapeDtypeStruct((count, w.shape[1])...  9.17 us
    dot_general x2, matrix products, local(): up_part = jnp.dot(piece, w_up[:, cols], preferred_element_type=jnp.float32)  8.1 us
    ppermute x8, starting transfers between devices, exchange(): return lax.ppermute(x, axis, [(a, a ^ 1 << s) for a in range(n)])  6.43 us
    ppermute x3, waiting for transfers between devices, relative_reduce_scatter(): own = own + lax.ppermute(block, axis, [(a, a ^ k) for a in range(n)])  6.06 us
    ppermute x3, waiting for transfers between devices, relative_all_gather(): lax.ppermute(x, axis, [(a, a ^ k) for a in range(n)])  5.88 us
    ppermute x3, starting transfers between devices, relative_all_gather(): lax.ppermute(x, axis, [(a, a ^ k) for a in range(n)])  5.62 us
    ppermute x3, starting transfers between devices, relative_reduce_scatter(): own = own + lax.ppermute(block, axis, [(a, a ^ k) for a in range(n)])  3.55 us
  transfers between devices with their start and end apart: 17, of which 10 were waited for; matrix products, arithmetic and copies ran while one was open for 13% of the time, Pallas kernels for 13%

profile of v15, /device:TPU:0, one launch (start us, length us, event | category | flops | bytes accessed | tf_op | source)
XLA Modules:
  0.0 70.8 jit_solution(178372379664786852)
XLA Ops:
  0.0 4.0 %collective-permute-start.1 = (bf16[5,2048]{1,0:T(8,128)(2,1)}, bf16[5,2048]{1,0:T(8,128)(2,1)S(1)}, u32[]{:S(2)}, u32[]{:S(2)}) collective-permute-start(bf16[5,2048]{1,0:T(8,128)(2,1)} %param.5), channel_id=1, source_target_pairs={{0,8},{4,12},{8,0},{12,4},{1,9},{5,13},{9,1},{13,5},{2,10},{6,14},... | collective-permute-start | bytes 61448 | tf_op jit(solution)/shard_map/ppermute | solution.py:102
  4.0 1.6 %collective-permute-start = (bf16[5,2048]{1,0:T(8,128)(2,1)}, bf16[5,2048]{1,0:T(8,128)(2,1)S(1)}, u32[]{:S(2)}, u32[]{:S(2)}) collective-permute-start(bf16[5,2048]{1,0:T(8,128)(2,1)} %param.5), channel_id=1, source_target_pairs={{0,4},{4,0},{8,12},{12,8},{1,5},{5,1},{9,13},{13,9},{2,6},{6,2},{1... | collective-permute-start | bytes 61448 | tf_op jit(solution)/shard_map/ppermute | solution.py:102
  5.7 1.0 %collective-permute-done.1 = bf16[5,2048]{1,0:T(8,128)(2,1)S(1)} collective-permute-done((bf16[5,2048]{1,0:T(8,128)(2,1)}, bf16[5,2048]{1,0:T(8,128)(2,1)S(1)}, u32[]{:S(2)}, u32[]{:S(2)}) %collective-permute-start.1) | collective-permute-done | bytes 20512 | tf_op jit(solution)/shard_map/ppermute | solution.py:102
  6.7 1.5 %collective-permute-done = bf16[5,2048]{1,0:T(8,128)(2,1)S(1)} collective-permute-done((bf16[5,2048]{1,0:T(8,128)(2,1)}, bf16[5,2048]{1,0:T(8,128)(2,1)S(1)}, u32[]{:S(2)}, u32[]{:S(2)}) %collective-permute-start) | collective-permute-done | bytes 20512 | tf_op jit(solution)/shard_map/ppermute | solution.py:102
  8.2 3.4 %collective-permute-done.2 = bf16[5,2048]{1,0:T(8,128)(2,1)S(1)} collective-permute-done((bf16[5,2048]{1,0:T(8,128)(2,1)}, bf16[5,2048]{1,0:T(8,128)(2,1)S(1)}, u32[]{:S(2)}, u32[]{:S(2)}) %collective-permute-start.2) | collective-permute-done | bytes 20512 | tf_op jit(solution)/shard_map/ppermute | solution.py:102
  11.5 0.9 %fusion.8 = f32[20]{0:T(128)S(1)} fusion(bf16[5,2048]{1,0:T(8,128)(2,1)S(1)} %collective-permute-done.2, bf16[5,2048]{1,0:T(8,128)(2,1)S(1)} %collective-permute-done.1, bf16[5,2048]{1,0:T(8,128)(2,1)S(1)} %collective-permute-done, bf16[5,2048]{1,0:T(8,128)(2,1)} %param.5), kind=kLoop, calls=%fused_computation.14 | loop fusion | flops 409580 | bytes 82000 | tf_op jit(solution)/shard_map/reduce_sum | solution.py:125
  12.6 1.6 %collective-permute-start.4 = (f32[20]{0:T(128)S(1)}, f32[20]{0:T(128)S(1)}, u32[]{:S(2)}, u32[]{:S(2)}) collective-permute-start(f32[20]{0:T(128)S(1)} %fusion.8), channel_id=1, source_target_pairs={{0,2},{1,3},{2,0},{3,1},{4,6},{5,7},{6,4},{7,5},{8,10},{9,11},{10,... | collective-permute-start | bytes 248 | tf_op jit(solution)/shard_map/ppermute | solution.py:77
  14.4 1.1 %collective-permute-done.5 = f32[20]{0:T(128)S(1)} collective-permute-done((f32[20]{0:T(128)S(1)}, f32[20]{0:T(128)S(1)}, u32[]{:S(2)}, u32[]{:S(2)}) %collective-permute-start.5) | collective-permute-done | bytes 112 | tf_op jit(solution)/shard_map/ppermute | solution.py:77
  16.8 5.8 %fusion.2 = f32[20,3072]{1,0:T(8,128)S(1)} fusion(bf16[2048,6144]{1,0:T(8,128)(2,1)} %param.7, f32[2048]{0:T(1024)} %param.6, f32[20]{0:T(128)S(1)} %add_rsqrt_fusion, bf16[5,2048]{1,0:T(8,128)(2,1)S(1)} %collective-permute-done.2, bf16[5,2048]{1,0:T(8,128)(2,1)S(1)} %collective-permute-done.1, bf16[5,2048]{1,0:T(8,128)(2,1)S(1)} %collective-permute-done, ...), kind=kOutput, calls=%fused_computation.3 | convolution fusion | flops 252108800 | bytes 12931152 | tf_op jit(solution)/shard_map/dot_general | solution.py:141
  22.6 6.3 %fusion = f32[20,3072]{1,0:T(8,128)S(1)} fusion(bf16[2048,6144]{1,0:T(8,128)(2,1)} %param.8, f32[2048]{0:T(1024)S(1)} %copy-done.2, f32[20]{0:T(128)S(1)} %add_rsqrt_fusion, bf16[5,2048]{1,0:T(8,128)(2,1)S(1)} %collective-permute-done.2, bf16[5,2048]{1,0:T(8,128)(2,1)S(1)} %collective-permute-done.1, bf16[5,2048]{1,0:T(8,128)(2,1)S(1)} %collective-permute-done, ...), kind=kOutput, calls=%fused_computation.1 | convolution fusion | flops 252108800 | bytes 12918864 | tf_op jit(solution)/shard_map/dot_general | solution.py:142
  29.4 2.9 %copy-done.1 = bf16[2048,6144]{1,0:T(8,128)(2,1)S(1)} copy-done((bf16[2048,6144]{1,0:T(8,128)(2,1)S(1)}, bf16[2048,6144]{1,0:T(8,128)(2,1)}, u32[]{:S(2)}) %copy-start.1) | copy-done | bytes 25165848
  32.3 1.8 %fusion.4 = f32[20,3072]{1,0:T(8,128)S(1)} fusion(bf16[2048,6144]{1,0:T(8,128)(2,1)S(1)} %copy-done.1, f32[2048]{0:T(1024)S(1)} %copy-done.2, f32[20]{0:T(128)S(1)} %add_rsqrt_fusion, bf16[5,2048]{1,0:T(8,128)(2,1)S(1)} %collective-permute-done.2, bf16[5,2048]{1,0:T(8,128)(2,1)S(1)} %collective-permute-done.1, bf16[5,2048]{1,0:T(8,128)(2,1)S(1)} %collective-permute-done, ...), kind=kOutput, calls=%fused_computation.5 | convolution fusion | flops 252108800 | bytes 12968448 | tf_op jit(solution)/shard_map/dot_general | solution.py:142
  34.1 5.6 %fusion.6 = f32[20,3072]{1,0:T(8,128)S(1)} fusion(bf16[2048,6144]{1,0:T(8,128)(2,1)} %param.7, f32[2048]{0:T(1024)S(1)} %copy-done.2, f32[20]{0:T(128)S(1)} %add_rsqrt_fusion, bf16[5,2048]{1,0:T(8,128)(2,1)S(1)} %collective-permute-done.2, bf16[5,2048]{1,0:T(8,128)(2,1)S(1)} %collective-permute-done.1, bf16[5,2048]{1,0:T(8,128)(2,1)S(1)} %collective-permute-done, ...), kind=kOutput, calls=%fused_computation.7 | convolution fusion | flops 252108800 | bytes 12918864 | tf_op jit(solution)/shard_map/dot_general | solution.py:141
  40.4 1.2 %collective-permute-start.11 = (f32[2,20,768]{2,1,0:T(8,128)S(1)}, f32[2,20,768]{2,1,0:T(8,128)S(1)}, u32[]{:S(2)}, u32[]{:S(2)}) collective-permute-start(f32[2,20,768]{2,1,0:T(8,128)S(1)} %pad_maximum_fusion.3), channel_id=1, source_target_pairs={{0,2},{1,3},{2,0},{3,1},{4,6},{5,7},{6,4},{7,5},{8,10},{9,11},{10,... | collective-permute-start | bytes 368648 | tf_op jit(solution)/shard_map/ppermute | solution.py:20
  41.7 1.4 %collective-permute-start.7 = (f32[2,20,768]{2,1,0:T(8,128)S(1)}, f32[2,20,768]{2,1,0:T(8,128)S(1)}, u32[]{:S(2)}, u32[]{:S(2)}) collective-permute-start(f32[2,20,768]{2,1,0:T(8,128)S(1)} %pad_maximum_fusion.2), channel_id=1, source_target_pairs={{0,2},{1,3},{2,0},{3,1},{4,6},{5,7},{6,4},{7,5},{8,10},{9,11},{10,... | collective-permute-start | bytes 368648 | tf_op jit(solution)/shard_map/ppermute | solution.py:20
  43.1 4.6 %shard_map.55 = bf16[3072,2048]{1,0:T(8,128)(2,1)S(1)} custom-call(bf16[6144,2048]{1,0:T(8,128)(2,1)} %src.1), custom_call_target="tpu_custom_call" | custom-call | bytes 25165824 | tf_op jit(solution)/shard_map/pallas_call | solution.py:90
  48.5 1.0 %collective-permute-done.7 = f32[2,20,768]{2,1,0:T(8,128)S(1)} collective-permute-done((f32[2,20,768]{2,1,0:T(8,128)S(1)}, f32[2,20,768]{2,1,0:T(8,128)S(1)}, u32[]{:S(2)}, u32[]{:S(2)}) %collective-permute-start.7) | collective-permute-done | bytes 122912 | tf_op jit(solution)/shard_map/ppermute | solution.py:20
  49.5 1.6 %collective-permute-start.8 = (bf16[20,768]{1,0:T(8,128)(2,1)S(1)}, bf16[20,768]{1,0:T(8,128)(2,1)S(1)}, u32[]{:S(2)}, u32[]{:S(2)}) collective-permute-start(bf16[20,768]{1,0:T(8,128)(2,1)S(1)} %fusion.34), channel_id=1, source_target_pairs={{0,2},{1,3},{2,0},{3,1},{4,6},{5,7},{6,4},{7,5},{8,10},{9,11},{10,... | collective-permute-start | bytes 92168 | tf_op jit(solution)/shard_map/ppermute | solution.py:20
  51.1 4.6 %shard_map.56 = bf16[3072,2048]{1,0:T(8,128)(2,1)S(1)} custom-call(bf16[6144,2048]{1,0:T(8,128)(2,1)} %src.1), custom_call_target="tpu_custom_call" | custom-call | bytes 25165824 | tf_op jit(solution)/shard_map/pallas_call | solution.py:90
  57.0 1.7 %fusion.20 = f32[20,2048]{1,0:T(8,128)S(1)} fusion(bf16[3072,2048]{1,0:T(8,128)(2,1)S(1)} %shard_map.56, bf16[20,1536]{1,0:T(8,128)(2,1)S(1)} %collective-permute-done.13, bf16[20,1536]{1,0:T(8,128)(2,1)S(1)} %maximum_select_fusion.5, pred[]{:T(512)S(6)} %eq.8), kind=kOutput, calls=%fused_computation.34 | convolution fusion | flops 252211200 | bytes 12869633 | tf_op jit(solution)/shard_map/dot_general | solution.py:162
  58.8 1.8 %convolution_add_fusion = f32[20,2048]{1,0:T(8,128)S(1)} fusion(f32[20,2048]{1,0:T(8,128)S(1)} %fusion.20, bf16[3072,2048]{1,0:T(8,128)(2,1)S(1)} %shard_map.55, bf16[20,1536]{1,0:T(8,128)(2,1)S(1)} %collective-permute-done.9, bf16[20,1536]{1,0:T(8,128)(2,1)S(1)} %maximum_select_fusion.4, pred[]{:T(512)S(6)} %eq.8), kind=kOutput, calls=%fused_computation.9 | convolution fusion | flops 252252160 | bytes 13033473 | tf_op jit(solution)/shard_map/dot_general | solution.py:162
  61.1 3.1 %collective-permute-start.15 = (f32[5,2048]{1,0:T(8,128)S(1)}, f32[5,2048]{1,0:T(8,128)S(1)}, u32[]{:S(2)}, u32[]{:S(2)}) collective-permute-start(f32[5,2048]{1,0:T(8,128)S(1)} %get-tuple-element.17), channel_id=1, source_target_pairs={{0,8},{4,12},{8,0},{12,4},{1,9},{5,13},{9,1},{13,5},{2,10},{6,14},... | collective-permute-start | bytes 122888 | tf_op jit(solution)/shard_map/ppermute | solution.py:111
  64.9 2.6 %collective-permute-done.16 = f32[5,2048]{1,0:T(8,128)S(1)} collective-permute-done((f32[5,2048]{1,0:T(8,128)S(1)}, f32[5,2048]{1,0:T(8,128)S(1)}, u32[]{:S(2)}, u32[]{:S(2)}) %collective-permute-start.16) | collective-permute-done | bytes 40992 | tf_op jit(solution)/shard_map/ppermute | solution.py:111
  67.5 2.7 %collective-permute-done.15 = f32[5,2048]{1,0:T(8,128)S(1)} collective-permute-done((f32[5,2048]{1,0:T(8,128)S(1)}, f32[5,2048]{1,0:T(8,128)S(1)}, u32[]{:S(2)}, u32[]{:S(2)}) %collective-permute-start.15) | collective-permute-done | bytes 40992 | tf_op jit(solution)/shard_map/ppermute | solution.py:111
  (50 shorter events, 6.9 us)
Async XLA Ops:
  0.0 22.6 %copy-start = (bf16[5,2048]{1,0:T(8,128)(2,1)S(1)}, bf16[5,2048]{1,0:T(8,128)(2,1)}, u32[]{:S(2)}) copy-start(bf16[5,2048]{1,0:T(8,128)(2,1)} %param.5) | copy-start | bytes 61444
  0.0 22.6 %copy-start.2 = (f32[2048]{0:T(1024)S(1)}, f32[2048]{0:T(1024)}, u32[]{:S(2)}) copy-start(f32[2048]{0:T(1024)} %param.6) | copy-start | bytes 24580
  0.0 6.7 %collective-permute-start.1 = (bf16[5,2048]{1,0:T(8,128)(2,1)}, bf16[5,2048]{1,0:T(8,128)(2,1)S(1)}, u32[]{:S(2)}, u32[]{:S(2)}) collective-permute-start(bf16[5,2048]{1,0:T(8,128)(2,1)} %param.5), channel_id=1, source_target_pairs={{0,8},{4,12},{8,0},{12,4},{1,9},{5,13},{9,1},{13,5},{2,10},{6,14},... | collective-permute-start | bytes 61448 | tf_op jit(solution)/shard_map/ppermute | solution.py:102
  4.0 4.1 %collective-permute-start = (bf16[5,2048]{1,0:T(8,128)(2,1)}, bf16[5,2048]{1,0:T(8,128)(2,1)S(1)}, u32[]{:S(2)}, u32[]{:S(2)}) collective-permute-start(bf16[5,2048]{1,0:T(8,128)(2,1)} %param.5), channel_id=1, source_target_pairs={{0,4},{4,0},{8,12},{12,8},{1,5},{5,1},{9,13},{13,9},{2,6},{6,2},{1... | collective-permute-start | bytes 61448 | tf_op jit(solution)/shard_map/ppermute | solution.py:102
  5.6 5.9 %collective-permute-start.2 = (bf16[5,2048]{1,0:T(8,128)(2,1)}, bf16[5,2048]{1,0:T(8,128)(2,1)S(1)}, u32[]{:S(2)}, u32[]{:S(2)}) collective-permute-start(bf16[5,2048]{1,0:T(8,128)(2,1)} %param.5), channel_id=1, source_target_pairs={{0,12},{4,8},{8,4},{12,0},{1,13},{5,9},{9,5},{13,1},{2,14},{6,10},... | collective-permute-start | bytes 61448 | tf_op jit(solution)/shard_map/ppermute | solution.py:102
  12.5 3.0 %collective-permute-start.5 = (f32[20]{0:T(128)S(1)}, f32[20]{0:T(128)S(1)}, u32[]{:S(2)}, u32[]{:S(2)}) collective-permute-start(f32[20]{0:T(128)S(1)} %fusion.8), channel_id=1, source_target_pairs={{0,3},{1,2},{2,1},{3,0},{4,7},{5,6},{6,5},{7,4},{8,11},{9,10},{10,... | collective-permute-start | bytes 248 | tf_op jit(solution)/shard_map/ppermute | solution.py:77
  12.6 3.6 %collective-permute-start.4 = (f32[20]{0:T(128)S(1)}, f32[20]{0:T(128)S(1)}, u32[]{:S(2)}, u32[]{:S(2)}) collective-permute-start(f32[20]{0:T(128)S(1)} %fusion.8), channel_id=1, source_target_pairs={{0,2},{1,3},{2,0},{3,1},{4,6},{5,7},{6,4},{7,5},{8,10},{9,11},{10,... | collective-permute-start | bytes 248 | tf_op jit(solution)/shard_map/ppermute | solution.py:77
  14.1 2.1 %collective-permute-start.3 = (f32[20]{0:T(128)S(1)}, f32[20]{0:T(128)S(1)}, u32[]{:S(2)}, u32[]{:S(2)}) collective-permute-start(f32[20]{0:T(128)S(1)} %fusion.8), channel_id=1, source_target_pairs={{0,1},{1,0},{2,3},{3,2},{4,5},{5,4},{6,7},{7,6},{8,9},{9,8},{10,11... | collective-permute-start | bytes 248 | tf_op jit(solution)/shard_map/ppermute | solution.py:77
  16.8 15.5 %copy-start.1 = (bf16[2048,6144]{1,0:T(8,128)(2,1)S(1)}, bf16[2048,6144]{1,0:T(8,128)(2,1)}, u32[]{:S(2)}) copy-start(bf16[2048,6144]{1,0:T(8,128)(2,1)} %param.8) | copy-start | bytes 75497472
  29.0 11.3 %collective-permute-start.10 = (f32[2,20,1536]{2,1,0:T(8,128)S(1)}, f32[2,20,1536]{2,1,0:T(8,128)S(1)}, u32[]{:S(2)}, u32[]{:S(2)}) collective-permute-start(f32[2,20,1536]{2,1,0:T(8,128)S(1)} %pad_maximum_fusion.1), channel_id=1, source_target_pairs={{0,1},{1,0},{2,3},{3,2},{4,5},{5,4},{6,7},{7,6},{8,9},{9,8},{10,11... | collective-permute-start | bytes 737288 | tf_op jit(solution)/shard_map/ppermute | solution.py:20
  39.8 1.8 %collective-permute-start.6 = (f32[2,20,1536]{2,1,0:T(8,128)S(1)}, f32[2,20,1536]{2,1,0:T(8,128)S(1)}, u32[]{:S(2)}, u32[]{:S(2)}) collective-permute-start(f32[2,20,1536]{2,1,0:T(8,128)S(1)} %pad_maximum_fusion), channel_id=1, source_target_pairs={{0,1},{1,0},{2,3},{3,2},{4,5},{5,4},{6,7},{7,6},{8,9},{9,8},{10,11... | collective-permute-start | bytes 737288 | tf_op jit(solution)/shard_map/ppermute | solution.py:20
  40.4 7.4 %collective-permute-start.11 = (f32[2,20,768]{2,1,0:T(8,128)S(1)}, f32[2,20,768]{2,1,0:T(8,128)S(1)}, u32[]{:S(2)}, u32[]{:S(2)}) collective-permute-start(f32[2,20,768]{2,1,0:T(8,128)S(1)} %pad_maximum_fusion.3), channel_id=1, source_target_pairs={{0,2},{1,3},{2,0},{3,1},{4,6},{5,7},{6,4},{7,5},{8,10},{9,11},{10,... | collective-permute-start | bytes 368648 | tf_op jit(solution)/shard_map/ppermute | solution.py:20
  41.7 7.8 %collective-permute-start.7 = (f32[2,20,768]{2,1,0:T(8,128)S(1)}, f32[2,20,768]{2,1,0:T(8,128)S(1)}, u32[]{:S(2)}, u32[]{:S(2)}) collective-permute-start(f32[2,20,768]{2,1,0:T(8,128)S(1)} %pad_maximum_fusion.2), channel_id=1, source_target_pairs={{0,2},{1,3},{2,0},{3,1},{4,6},{5,7},{6,4},{7,5},{8,10},{9,11},{10,... | collective-permute-start | bytes 368648 | tf_op jit(solution)/shard_map/ppermute | solution.py:20
  47.8 7.9 %collective-permute-start.12 = (bf16[20,768]{1,0:T(8,128)(2,1)S(1)}, bf16[20,768]{1,0:T(8,128)(2,1)S(1)}, u32[]{:S(2)}, u32[]{:S(2)}) collective-permute-start(bf16[20,768]{1,0:T(8,128)(2,1)S(1)} %fusion.30), channel_id=1, source_target_pairs={{0,2},{1,3},{2,0},{3,1},{4,6},{5,7},{6,4},{7,5},{8,10},{9,11},{10,... | collective-permute-start | bytes 92168 | tf_op jit(solution)/shard_map/ppermute | solution.py:20
  49.5 6.3 %collective-permute-start.8 = (bf16[20,768]{1,0:T(8,128)(2,1)S(1)}, bf16[20,768]{1,0:T(8,128)(2,1)S(1)}, u32[]{:S(2)}, u32[]{:S(2)}) collective-permute-start(bf16[20,768]{1,0:T(8,128)(2,1)S(1)} %fusion.34), channel_id=1, source_target_pairs={{0,2},{1,3},{2,0},{3,1},{4,6},{5,7},{6,4},{7,5},{8,10},{9,11},{10,... | collective-permute-start | bytes 92168 | tf_op jit(solution)/shard_map/ppermute | solution.py:20
  55.7 1.3 %collective-permute-start.13 = (bf16[20,1536]{1,0:T(8,128)(2,1)S(1)}, bf16[20,1536]{1,0:T(8,128)(2,1)S(1)}, u32[]{:S(2)}, u32[]{:S(2)}) collective-permute-start(bf16[20,1536]{1,0:T(8,128)(2,1)S(1)} %maximum_select_fusion.5), channel_id=1, source_target_pairs={{0,1},{1,0},{2,3},{3,2},{4,5},{5,4},{6,7},{7,6},{8,9},{9,8},{10,11... | collective-permute-start | bytes 184328 | tf_op jit(solution)/shard_map/ppermute | solution.py:20
  55.8 3.0 %collective-permute-start.9 = (bf16[20,1536]{1,0:T(8,128)(2,1)S(1)}, bf16[20,1536]{1,0:T(8,128)(2,1)S(1)}, u32[]{:S(2)}, u32[]{:S(2)}) collective-permute-start(bf16[20,1536]{1,0:T(8,128)(2,1)S(1)} %maximum_select_fusion.4), channel_id=1, source_target_pairs={{0,1},{1,0},{2,3},{3,2},{4,5},{5,4},{6,7},{7,6},{8,9},{9,8},{10,11... | collective-permute-start | bytes 184328 | tf_op jit(solution)/shard_map/ppermute | solution.py:20
  60.6 4.3 %collective-permute-start.14 = (f32[5,2048]{1,0:T(8,128)S(1)}, f32[5,2048]{1,0:T(8,128)S(1)}, u32[]{:S(2)}, u32[]{:S(2)}) collective-permute-start(f32[5,2048]{1,0:T(8,128)S(1)} %get-tuple-element.15), channel_id=1, source_target_pairs={{0,4},{4,0},{8,12},{12,8},{1,5},{5,1},{9,13},{13,9},{2,6},{6,2},{1... | collective-permute-start | bytes 122888 | tf_op jit(solution)/shard_map/ppermute | solution.py:111
  60.6 6.8 %collective-permute-start.16 = (f32[5,2048]{1,0:T(8,128)S(1)}, f32[5,2048]{1,0:T(8,128)S(1)}, u32[]{:S(2)}, u32[]{:S(2)}) collective-permute-start(f32[5,2048]{1,0:T(8,128)S(1)} %get-tuple-element.16), channel_id=1, source_target_pairs={{0,12},{4,8},{8,4},{12,0},{1,13},{5,9},{9,5},{13,1},{2,14},{6,10},... | collective-permute-start | bytes 122888 | tf_op jit(solution)/shard_map/ppermute | solution.py:111
  61.1 9.1 %collective-permute-start.15 = (f32[5,2048]{1,0:T(8,128)S(1)}, f32[5,2048]{1,0:T(8,128)S(1)}, u32[]{:S(2)}, u32[]{:S(2)}) collective-permute-start(f32[5,2048]{1,0:T(8,128)S(1)} %get-tuple-element.17), channel_id=1, source_target_pairs={{0,8},{4,12},{8,0},{12,4},{1,9},{5,13},{9,1},{13,5},{2,10},{6,14},... | collective-permute-start | bytes 122888 | tf_op jit(solution)/shard_map/ppermute | solution.py:111

commit v16 on v12

--- a/solution.py
+++ b/solution.py
@@ -103,18 +103,18 @@
     ngy = lax.axis_size("gy")
     features = tokens.shape[1] * ngy
     gx_levels = list(range(ngx.bit_length() - 1))
-    if pairwise(ngx):
-        raw = fanout_all_gather(tokens, "gx", ngx, gx_levels[::-1])
-    else:
-        raw = lax.all_gather(tokens, "gx", axis=0, tiled=True)
-    values = raw.astype(jnp.float32)
+    values = tokens.astype(jnp.float32)
     local_sq = jnp.sum(values * values, axis=1)
     if pairwise(ngy):
         total_sq = fanout_all_reduce(local_sq, "gy", ngy)
     else:
         total_sq = lax.psum(local_sq, "gy")
     inverse = lax.rsqrt(total_sq / features + epsilon)
-    piece = (values * inverse[:, None] * norm_gain[None, :]).astype(jnp.bfloat16)
+    normed = (values * inverse[:, None] * norm_gain[None, :]).astype(jnp.bfloat16)
+    if pairwise(ngx):
+        piece = fanout_all_gather(normed, "gx", ngx, gx_levels[::-1])
+    else:
+        piece = lax.all_gather(normed, "gx", axis=0, tiled=True)
     rows = piece.shape[0]
 
     width = w_gate.shape[1]

time: 67.7 us -> 69.6 us (1.028)
  waiting for transfers between devices: 14.3 us -> 16.6 us
  other arithmetic: 1.18 us -> 2.77 us
  starting transfers between devices: 17.4 us -> 15.9 us
    ppermute x8, starting transfers between devices: 6.29 us -> 4.81 us  [exchange(): return lax.ppermute(x, axis, [(a, a ^ 1 << s) for a in range(n)])]
    ppermute x3, starting transfers between devices: 1.91 us -> 3.11 us  [fanout_all_reduce(): lax.ppermute(x, axis, [(a, a ^ k) for a in range(n)])]
    ppermute x3, starting transfers between devices: 5.62 us -> 4.45 us  [fanout_all_gather(): lax.ppermute(x, axis, [(a, a ^ k) for a in range(n)])]
    ppermute x3, waiting for transfers between devices: 1.76 us -> 2.84 us  [fanout_all_reduce(): lax.ppermute(x, axis, [(a, a ^ k) for a in range(n)])]
    convert_element_type x0 -> x1, other arithmetic: none -> 0.84 us  [local(): (values * inverse[:, None] * norm_gain[None, :]).astype(jnp.bfloat16)]
    reduce_sum x1, other arithmetic: 0.14 us -> 0.89 us  [local(): local_sq = jnp.sum(values * values, axis=1)]
    dynamic_update_slice x4, local copies, waits for them, and re-layouts: 1.87 us -> 1.14 us  [fanout_all_gather(): lax.dynamic_update_slice_in_dim(out, block, gathered_position(me ^ k, bit...]
    ppermute x3, waiting for transfers between devices: 3.86 us -> 4.57 us  [fanout_all_gather(): lax.ppermute(x, axis, [(a, a ^ k) for a in range(n)])]
  transfers between devices with their start and end apart: 17 -> 17, of which waited for: 9 -> 10; matrix products, arithmetic and copies ran while one was open for 5% -> 4% of each run, Pallas kernels for 14% -> 13%
where the time goes in v16:
time: 69.6 us; the launch traced here: 69.2 us
  matrix products  19.1 us (27%)
  waiting for transfers between devices  16.6 us (24%)
  starting transfers between devices  15.9 us (23%)
  Pallas kernels  9.17 us (13%)
  local copies, waits for them, and re-layouts  5.41 us (8%)
  other arithmetic  2.77 us (4%)
    dot_general x2, matrix products, local(): up_part = jnp.dot(piece, w_up[:, cols], preferred_element_type=jnp.float32)  11.9 us
    pallas_call x2, Pallas kernels, rows_to_vmem(): pl.pallas_call(kernel, out_shape=jax.ShapeDtypeStruct((count, w.shape[1])...  9.17 us
    ppermute x3, waiting for transfers between devices, fanout_reduce_scatter(): own = own + lax.ppermute(block, axis, [(a, a ^ k) for a in range(n)])  6.06 us
    ppermute x8, starting transfers between devices, exchange(): return lax.ppermute(x, axis, [(a, a ^ 1 << s) for a in range(n)])  4.81 us
    ppermute x3, waiting for transfers between devices, fanout_all_gather(): lax.ppermute(x, axis, [(a, a ^ k) for a in range(n)])  4.57 us
    ppermute x3, starting transfers between devices, fanout_all_gather(): lax.ppermute(x, axis, [(a, a ^ k) for a in range(n)])  4.45 us
    dot_general x2, matrix products, local(): jnp.dot(piece, w_gate[:, cols], preferred_element_type=jnp.float32)  3.77 us
    unnamed x2, local copies, waits for them, and re-layouts  3.55 us
  transfers between devices with their start and end apart: 17, of which 10 were waited for; matrix products, arithmetic and copies ran while one was open for 4% of the time, Pallas kernels for 13%

profile of v16, /device:TPU:0, one launch (start us, length us, event | category | flops | bytes accessed | tf_op | source)
XLA Modules:
  0.0 69.2 jit_solution(5992493244707227130)
XLA Ops:
  0.0 0.9 %fusion.33 = f32[5]{0:T(128)S(1)} fusion(bf16[5,2048]{1,0:T(8,128)(2,1)} %param.5), kind=kLoop, calls=%fused_computation.61 | loop fusion | flops 30715 | bytes 20500 | tf_op jit(solution)/shard_map/reduce_sum | solution.py:107
  0.9 2.4 %collective-permute-start.2 = (f32[5]{0:T(128)S(1)}, f32[5]{0:T(128)S(1)}, u32[]{:S(2)}, u32[]{:S(2)}) collective-permute-start(f32[5]{0:T(128)S(1)} %fusion.33), channel_id=1, source_target_pairs={{0,3},{1,2},{2,1},{3,0},{4,7},{5,6},{6,5},{7,4},{8,11},{9,10},{10,... | collective-permute-start | bytes 68 | tf_op jit(solution)/shard_map/ppermute | solution.py:77
  4.6 2.2 %collective-permute-done.1 = f32[5]{0:T(128)S(1)} collective-permute-done((f32[5]{0:T(128)S(1)}, f32[5]{0:T(128)S(1)}, u32[]{:S(2)}, u32[]{:S(2)}) %collective-permute-start.1) | collective-permute-done | bytes 52 | tf_op jit(solution)/shard_map/ppermute | solution.py:77
  7.5 0.8 %fusion.35 = bf16[5,2048]{1,0:T(8,128)(2,1)S(1)} fusion(bf16[5,2048]{1,0:T(8,128)(2,1)} %param.5, f32[2048]{0:T(1024)} %param.6, f32[5]{0:T(128)S(1)} %add_rsqrt_fusion), kind=kLoop, calls=%fused_computation.63 | loop fusion | flops 40960 | bytes 49172 | tf_op jit(solution)/shard_map/convert_element_type | solution.py:113
  8.4 1.6 %collective-permute-start.3 = (bf16[5,2048]{1,0:T(8,128)(2,1)S(1)}, bf16[5,2048]{1,0:T(8,128)(2,1)S(1)}, u32[]{:S(2)}, u32[]{:S(2)}) collective-permute-start(bf16[5,2048]{1,0:T(8,128)(2,1)S(1)} %fusion.35), channel_id=1, source_target_pairs={{0,4},{4,0},{8,12},{12,8},{1,5},{5,1},{9,13},{13,9},{2,6},{6,2},{1... | collective-permute-start | bytes 61448 | tf_op jit(solution)/shard_map/ppermute | solution.py:70
  10.0 2.6 %collective-permute-start.4 = (bf16[5,2048]{1,0:T(8,128)(2,1)S(1)}, bf16[5,2048]{1,0:T(8,128)(2,1)S(1)}, u32[]{:S(2)}, u32[]{:S(2)}) collective-permute-start(bf16[5,2048]{1,0:T(8,128)(2,1)S(1)} %fusion.35), channel_id=1, source_target_pairs={{0,8},{4,12},{8,0},{12,4},{1,9},{5,13},{9,1},{13,5},{2,10},{6,14},... | collective-permute-start | bytes 61448 | tf_op jit(solution)/shard_map/ppermute | solution.py:70
  13.5 1.6 %collective-permute-done.4 = bf16[5,2048]{1,0:T(8,128)(2,1)S(1)} collective-permute-done((bf16[5,2048]{1,0:T(8,128)(2,1)S(1)}, bf16[5,2048]{1,0:T(8,128)(2,1)S(1)}, u32[]{:S(2)}, u32[]{:S(2)}) %collective-permute-start.4) | collective-permute-done | bytes 20512 | tf_op jit(solution)/shard_map/ppermute | solution.py:70
  15.4 2.9 %collective-permute-done.5 = bf16[5,2048]{1,0:T(8,128)(2,1)S(1)} collective-permute-done((bf16[5,2048]{1,0:T(8,128)(2,1)S(1)}, bf16[5,2048]{1,0:T(8,128)(2,1)S(1)}, u32[]{:S(2)}, u32[]{:S(2)}) %collective-permute-start.5) | collective-permute-done | bytes 20512 | tf_op jit(solution)/shard_map/ppermute | solution.py:70
  18.6 5.7 %fusion = f32[20,3072]{1,0:T(8,128)S(1)} fusion(bf16[20,2048]{1,0:T(8,128)(2,1)S(1)} %dynamic_update_slice.15, bf16[2048,6144]{1,0:T(8,128)(2,1)} %param.8), kind=kOutput, calls=%fused_computation.1 | convolution fusion | flops 251658240 | bytes 12910592 | tf_op jit(solution)/shard_map/dot_general | solution.py:128
  24.3 6.2 %fusion.4 = f32[20,3072]{1,0:T(8,128)S(1)} fusion(bf16[20,2048]{1,0:T(8,128)(2,1)S(1)} %dynamic_update_slice.15, bf16[2048,6144]{1,0:T(8,128)(2,1)} %param.8), kind=kOutput, calls=%fused_computation.5 | convolution fusion | flops 251658240 | bytes 12910592 | tf_op jit(solution)/shard_map/dot_general | solution.py:128
  30.5 3.5 %copy-done = bf16[2048,6144]{1,0:T(8,128)(2,1)S(1)} copy-done((bf16[2048,6144]{1,0:T(8,128)(2,1)S(1)}, bf16[2048,6144]{1,0:T(8,128)(2,1)}, u32[]{:S(2)}) %copy-start) | copy-done | bytes 25165848
  34.0 1.9 %fusion.2 = f32[20,3072]{1,0:T(8,128)S(1)} fusion(bf16[20,2048]{1,0:T(8,128)(2,1)S(1)} %dynamic_update_slice.15, bf16[2048,6144]{1,0:T(8,128)(2,1)S(1)} %copy-done), kind=kOutput, calls=%fused_computation.3 | convolution fusion | flops 251658240 | bytes 12926976 | tf_op jit(solution)/shard_map/dot_general | solution.py:127
  35.9 1.9 %fusion.6 = f32[20,3072]{1,0:T(8,128)S(1)} fusion(bf16[20,2048]{1,0:T(8,128)(2,1)S(1)} %dynamic_update_slice.15, bf16[2048,6144]{1,0:T(8,128)(2,1)S(1)} %copy-done), kind=kOutput, calls=%fused_computation.7 | convolution fusion | flops 251658240 | bytes 12926976 | tf_op jit(solution)/shard_map/dot_general | solution.py:127
  38.6 1.0 %collective-permute-done.10 = f32[2,20,1536]{2,1,0:T(8,128)S(1)} collective-permute-done((f32[2,20,1536]{2,1,0:T(8,128)S(1)}, f32[2,20,1536]{2,1,0:T(8,128)S(1)}, u32[]{:S(2)}, u32[]{:S(2)}) %collective-permute-start.10) | collective-permute-done | bytes 245792 | tf_op jit(solution)/shard_map/ppermute | solution.py:20
  40.4 1.5 %collective-permute-start.7 = (f32[2,20,768]{2,1,0:T(8,128)S(1)}, f32[2,20,768]{2,1,0:T(8,128)S(1)}, u32[]{:S(2)}, u32[]{:S(2)}) collective-permute-start(f32[2,20,768]{2,1,0:T(8,128)S(1)} %pad_maximum_fusion.2), channel_id=1, source_target_pairs={{0,2},{1,3},{2,0},{3,1},{4,6},{5,7},{6,4},{7,5},{8,10},{9,11},{10,... | collective-permute-start | bytes 368648 | tf_op jit(solution)/shard_map/ppermute | solution.py:20
  41.9 4.6 %shard_map.55 = bf16[3072,2048]{1,0:T(8,128)(2,1)S(1)} custom-call(bf16[6144,2048]{1,0:T(8,128)(2,1)} %src.1), custom_call_target="tpu_custom_call" | custom-call | bytes 25165824 | tf_op jit(solution)/shard_map/pallas_call | solution.py:90
  47.2 1.5 %collective-permute-done.7 = f32[2,20,768]{2,1,0:T(8,128)S(1)} collective-permute-done((f32[2,20,768]{2,1,0:T(8,128)S(1)}, f32[2,20,768]{2,1,0:T(8,128)S(1)}, u32[]{:S(2)}, u32[]{:S(2)}) %collective-permute-start.7) | collective-permute-done | bytes 122912 | tf_op jit(solution)/shard_map/ppermute | solution.py:20
  49.5 4.6 %shard_map.56 = bf16[3072,2048]{1,0:T(8,128)(2,1)S(1)} custom-call(bf16[6144,2048]{1,0:T(8,128)(2,1)} %src.1), custom_call_target="tpu_custom_call" | custom-call | bytes 25165824 | tf_op jit(solution)/shard_map/pallas_call | solution.py:90
  55.4 1.7 %fusion.17 = f32[20,2048]{1,0:T(8,128)S(1)} fusion(bf16[3072,2048]{1,0:T(8,128)(2,1)S(1)} %shard_map.56, bf16[20,1536]{1,0:T(8,128)(2,1)S(1)} %collective-permute-done.13, bf16[20,1536]{1,0:T(8,128)(2,1)S(1)} %maximum_select_fusion.5, pred[]{:T(512)S(6)} %eq.8), kind=kOutput, calls=%fused_computation.29 | convolution fusion | flops 252211200 | bytes 12869633 | tf_op jit(solution)/shard_map/dot_general | solution.py:148
  57.2 1.8 %convolution_add_fusion = f32[20,2048]{1,0:T(8,128)S(1)} fusion(f32[20,2048]{1,0:T(8,128)S(1)} %fusion.17, bf16[3072,2048]{1,0:T(8,128)(2,1)S(1)} %shard_map.55, bf16[20,1536]{1,0:T(8,128)(2,1)S(1)} %collective-permute-done.9, bf16[20,1536]{1,0:T(8,128)(2,1)S(1)} %maximum_select_fusion.4, pred[]{:T(512)S(6)} %eq.8), kind=kOutput, calls=%fused_computation.9 | convolution fusion | flops 252252160 | bytes 13033473 | tf_op jit(solution)/shard_map/dot_general | solution.py:148
  59.1 0.9 %collective-permute-start.16 = (f32[5,2048]{1,0:T(8,128)S(1)}, f32[5,2048]{1,0:T(8,128)S(1)}, u32[]{:S(2)}, u32[]{:S(2)}) collective-permute-start(f32[5,2048]{1,0:T(8,128)S(1)} %get-tuple-element.16), channel_id=1, source_target_pairs={{0,12},{4,8},{8,4},{12,0},{1,13},{5,9},{9,5},{13,1},{2,14},{6,10},... | collective-permute-start | bytes 122888 | tf_op jit(solution)/shard_map/ppermute | solution.py:61
  59.9 2.6 %collective-permute-start.15 = (f32[5,2048]{1,0:T(8,128)S(1)}, f32[5,2048]{1,0:T(8,128)S(1)}, u32[]{:S(2)}, u32[]{:S(2)}) collective-permute-start(f32[5,2048]{1,0:T(8,128)S(1)} %get-tuple-element.17), channel_id=1, source_target_pairs={{0,8},{4,12},{8,0},{12,4},{1,9},{5,13},{9,1},{13,5},{2,10},{6,14},... | collective-permute-start | bytes 122888 | tf_op jit(solution)/shard_map/ppermute | solution.py:61
  63.3 2.6 %collective-permute-done.16 = f32[5,2048]{1,0:T(8,128)S(1)} collective-permute-done((f32[5,2048]{1,0:T(8,128)S(1)}, f32[5,2048]{1,0:T(8,128)S(1)}, u32[]{:S(2)}, u32[]{:S(2)}) %collective-permute-start.16) | collective-permute-done | bytes 40992 | tf_op jit(solution)/shard_map/ppermute | solution.py:61
  65.9 2.7 %collective-permute-done.15 = f32[5,2048]{1,0:T(8,128)S(1)} collective-permute-done((f32[5,2048]{1,0:T(8,128)S(1)}, f32[5,2048]{1,0:T(8,128)S(1)}, u32[]{:S(2)}, u32[]{:S(2)}) %collective-permute-start.15) | collective-permute-done | bytes 40992 | tf_op jit(solution)/shard_map/ppermute | solution.py:61
  (52 shorter events, 9.3 us)
Async XLA Ops:
  0.9 3.7 %collective-permute-start.2 = (f32[5]{0:T(128)S(1)}, f32[5]{0:T(128)S(1)}, u32[]{:S(2)}, u32[]{:S(2)}) collective-permute-start(f32[5]{0:T(128)S(1)} %fusion.33), channel_id=1, source_target_pairs={{0,3},{1,2},{2,1},{3,0},{4,7},{5,6},{6,5},{7,4},{8,11},{9,10},{10,... | collective-permute-start | bytes 68 | tf_op jit(solution)/shard_map/ppermute | solution.py:77
  3.3 3.5 %collective-permute-start.1 = (f32[5]{0:T(128)S(1)}, f32[5]{0:T(128)S(1)}, u32[]{:S(2)}, u32[]{:S(2)}) collective-permute-start(f32[5]{0:T(128)S(1)} %fusion.33), channel_id=1, source_target_pairs={{0,2},{1,3},{2,0},{3,1},{4,6},{5,7},{6,4},{7,5},{8,10},{9,11},{10,... | collective-permute-start | bytes 68 | tf_op jit(solution)/shard_map/ppermute | solution.py:77
  4.0 2.9 %collective-permute-start = (f32[5]{0:T(128)S(1)}, f32[5]{0:T(128)S(1)}, u32[]{:S(2)}, u32[]{:S(2)}) collective-permute-start(f32[5]{0:T(128)S(1)} %fusion.33), channel_id=1, source_target_pairs={{0,1},{1,0},{2,3},{3,2},{4,5},{5,4},{6,7},{7,6},{8,9},{9,8},{10,11... | collective-permute-start | bytes 68 | tf_op jit(solution)/shard_map/ppermute | solution.py:77
  8.4 4.8 %collective-permute-start.3 = (bf16[5,2048]{1,0:T(8,128)(2,1)S(1)}, bf16[5,2048]{1,0:T(8,128)(2,1)S(1)}, u32[]{:S(2)}, u32[]{:S(2)}) collective-permute-start(bf16[5,2048]{1,0:T(8,128)(2,1)S(1)} %fusion.35), channel_id=1, source_target_pairs={{0,4},{4,0},{8,12},{12,8},{1,5},{5,1},{9,13},{13,9},{2,6},{6,2},{1... | collective-permute-start | bytes 61448 | tf_op jit(solution)/shard_map/ppermute | solution.py:70
  10.0 5.1 %collective-permute-start.4 = (bf16[5,2048]{1,0:T(8,128)(2,1)S(1)}, bf16[5,2048]{1,0:T(8,128)(2,1)S(1)}, u32[]{:S(2)}, u32[]{:S(2)}) collective-permute-start(bf16[5,2048]{1,0:T(8,128)(2,1)S(1)} %fusion.35), channel_id=1, source_target_pairs={{0,8},{4,12},{8,0},{12,4},{1,9},{5,13},{9,1},{13,5},{2,10},{6,14},... | collective-permute-start | bytes 61448 | tf_op jit(solution)/shard_map/ppermute | solution.py:70
  12.6 5.7 %collective-permute-start.5 = (bf16[5,2048]{1,0:T(8,128)(2,1)S(1)}, bf16[5,2048]{1,0:T(8,128)(2,1)S(1)}, u32[]{:S(2)}, u32[]{:S(2)}) collective-permute-start(bf16[5,2048]{1,0:T(8,128)(2,1)S(1)} %fusion.35), channel_id=1, source_target_pairs={{0,12},{4,8},{8,4},{12,0},{1,13},{5,9},{9,5},{13,1},{2,14},{6,10},... | collective-permute-start | bytes 61448 | tf_op jit(solution)/shard_map/ppermute | solution.py:70
  18.6 15.4 %copy-start = (bf16[2048,6144]{1,0:T(8,128)(2,1)S(1)}, bf16[2048,6144]{1,0:T(8,128)(2,1)}, u32[]{:S(2)}) copy-start(bf16[2048,6144]{1,0:T(8,128)(2,1)} %param.7) | copy-start | bytes 75497472
  37.9 1.6 %collective-permute-start.10 = (f32[2,20,1536]{2,1,0:T(8,128)S(1)}, f32[2,20,1536]{2,1,0:T(8,128)S(1)}, u32[]{:S(2)}, u32[]{:S(2)}) collective-permute-start(f32[2,20,1536]{2,1,0:T(8,128)S(1)} %pad_maximum_fusion.1), channel_id=1, source_target_pairs={{0,1},{1,0},{2,3},{3,2},{4,5},{5,4},{6,7},{7,6},{8,9},{9,8},{10,11... | collective-permute-start | bytes 737288 | tf_op jit(solution)/shard_map/ppermute | solution.py:20
  38.0 2.3 %collective-permute-start.6 = (f32[2,20,1536]{2,1,0:T(8,128)S(1)}, f32[2,20,1536]{2,1,0:T(8,128)S(1)}, u32[]{:S(2)}, u32[]{:S(2)}) collective-permute-start(f32[2,20,1536]{2,1,0:T(8,128)S(1)} %pad_maximum_fusion), channel_id=1, source_target_pairs={{0,1},{1,0},{2,3},{3,2},{4,5},{5,4},{6,7},{7,6},{8,9},{9,8},{10,11... | collective-permute-start | bytes 737288 | tf_op jit(solution)/shard_map/ppermute | solution.py:20
  39.6 6.9 %collective-permute-start.11 = (f32[2,20,768]{2,1,0:T(8,128)S(1)}, f32[2,20,768]{2,1,0:T(8,128)S(1)}, u32[]{:S(2)}, u32[]{:S(2)}) collective-permute-start(f32[2,20,768]{2,1,0:T(8,128)S(1)} %pad_maximum_fusion.3), channel_id=1, source_target_pairs={{0,2},{1,3},{2,0},{3,1},{4,6},{5,7},{6,4},{7,5},{8,10},{9,11},{10,... | collective-permute-start | bytes 368648 | tf_op jit(solution)/shard_map/ppermute | solution.py:20
  40.4 8.3 %collective-permute-start.7 = (f32[2,20,768]{2,1,0:T(8,128)S(1)}, f32[2,20,768]{2,1,0:T(8,128)S(1)}, u32[]{:S(2)}, u32[]{:S(2)}) collective-permute-start(f32[2,20,768]{2,1,0:T(8,128)S(1)} %pad_maximum_fusion.2), channel_id=1, source_target_pairs={{0,2},{1,3},{2,0},{3,1},{4,6},{5,7},{6,4},{7,5},{8,10},{9,11},{10,... | collective-permute-start | bytes 368648 | tf_op jit(solution)/shard_map/ppermute | solution.py:20
  46.5 7.5 %collective-permute-start.12 = (bf16[20,768]{1,0:T(8,128)(2,1)S(1)}, bf16[20,768]{1,0:T(8,128)(2,1)S(1)}, u32[]{:S(2)}, u32[]{:S(2)}) collective-permute-start(bf16[20,768]{1,0:T(8,128)(2,1)S(1)} %fusion.27), channel_id=1, source_target_pairs={{0,2},{1,3},{2,0},{3,1},{4,6},{5,7},{6,4},{7,5},{8,10},{9,11},{10,... | collective-permute-start | bytes 92168 | tf_op jit(solution)/shard_map/ppermute | solution.py:20
  48.8 5.4 %collective-permute-start.8 = (bf16[20,768]{1,0:T(8,128)(2,1)S(1)}, bf16[20,768]{1,0:T(8,128)(2,1)S(1)}, u32[]{:S(2)}, u32[]{:S(2)}) collective-permute-start(bf16[20,768]{1,0:T(8,128)(2,1)S(1)} %fusion.31), channel_id=1, source_target_pairs={{0,2},{1,3},{2,0},{3,1},{4,6},{5,7},{6,4},{7,5},{8,10},{9,11},{10,... | collective-permute-start | bytes 92168 | tf_op jit(solution)/shard_map/ppermute | solution.py:20
  54.1 1.3 %collective-permute-start.13 = (bf16[20,1536]{1,0:T(8,128)(2,1)S(1)}, bf16[20,1536]{1,0:T(8,128)(2,1)S(1)}, u32[]{:S(2)}, u32[]{:S(2)}) collective-permute-start(bf16[20,1536]{1,0:T(8,128)(2,1)S(1)} %maximum_select_fusion.5), channel_id=1, source_target_pairs={{0,1},{1,0},{2,3},{3,2},{4,5},{5,4},{6,7},{7,6},{8,9},{9,8},{10,11... | collective-permute-start | bytes 184328 | tf_op jit(solution)/shard_map/ppermute | solution.py:20
  54.2 3.0 %collective-permute-start.9 = (bf16[20,1536]{1,0:T(8,128)(2,1)S(1)}, bf16[20,1536]{1,0:T(8,128)(2,1)S(1)}, u32[]{:S(2)}, u32[]{:S(2)}) collective-permute-start(bf16[20,1536]{1,0:T(8,128)(2,1)S(1)} %maximum_select_fusion.4), channel_id=1, source_target_pairs={{0,1},{1,0},{2,3},{3,2},{4,5},{5,4},{6,7},{7,6},{8,9},{9,8},{10,11... | collective-permute-start | bytes 184328 | tf_op jit(solution)/shard_map/ppermute | solution.py:20
  59.0 4.3 %collective-permute-start.14 = (f32[5,2048]{1,0:T(8,128)S(1)}, f32[5,2048]{1,0:T(8,128)S(1)}, u32[]{:S(2)}, u32[]{:S(2)}) collective-permute-start(f32[5,2048]{1,0:T(8,128)S(1)} %get-tuple-element.15), channel_id=1, source_target_pairs={{0,4},{4,0},{8,12},{12,8},{1,5},{5,1},{9,13},{13,9},{2,6},{6,2},{1... | collective-permute-start | bytes 122888 | tf_op jit(solution)/shard_map/ppermute | solution.py:61
  59.1 6.8 %collective-permute-start.16 = (f32[5,2048]{1,0:T(8,128)S(1)}, f32[5,2048]{1,0:T(8,128)S(1)}, u32[]{:S(2)}, u32[]{:S(2)}) collective-permute-start(f32[5,2048]{1,0:T(8,128)S(1)} %get-tuple-element.16), channel_id=1, source_target_pairs={{0,12},{4,8},{8,4},{12,0},{1,13},{5,9},{9,5},{13,1},{2,14},{6,10},... | collective-permute-start | bytes 122888 | tf_op jit(solution)/shard_map/ppermute | solution.py:61
  59.9 8.7 %collective-permute-start.15 = (f32[5,2048]{1,0:T(8,128)S(1)}, f32[5,2048]{1,0:T(8,128)S(1)}, u32[]{:S(2)}, u32[]{:S(2)}) collective-permute-start(f32[5,2048]{1,0:T(8,128)S(1)} %get-tuple-element.17), channel_id=1, source_target_pairs={{0,8},{4,12},{8,0},{12,4},{1,9},{5,13},{9,1},{13,5},{2,10},{6,14},... | collective-permute-start | bytes 122888 | tf_op jit(solution)/shard_map/ppermute | solution.py:61

commit v17 on v11

--- a/solution.py
+++ b/solution.py
@@ -122,16 +122,24 @@
     step = width // chunks
     gy_levels = list(range(ngy.bit_length() - 1))
     total = None
+    pieces = {}
+    staged = None
+    downs = []
     for c in range(chunks):
         cols = slice(c * step, (c + 1) * step)
         gate_part = jnp.dot(piece, w_gate[:, cols], preferred_element_type=jnp.float32)
         up_part = jnp.dot(piece, w_up[:, cols], preferred_element_type=jnp.float32)
         if pairwise(ngy):
             first = xor_reduce_scatter([gate_part, up_part], "gy", ngy, 1, gy_levels[:1])
-            if c == 0:
-                source, _ = lax.optimization_barrier((w_down, first[0]))
-                staged = [rows_to_vmem(source, k * step, step) for k in range(chunks)]
+            quarter = step // 2
+            source, _ = lax.optimization_barrier((w_down, first[0]))
+            pieces[c] = [rows_to_vmem(source, c * quarter, quarter)]
             gate, up = xor_reduce_scatter(first, "gy", ngy, 1, gy_levels[1:])
+            source, _ = lax.optimization_barrier((w_down, gate))
+            pieces[c].append(rows_to_vmem(source, (chunks + c) * quarter, quarter))
+            if c == chunks - 1:
+                flat = [pieces[k][0] for k in range(chunks)] + [pieces[k][1] for k in range(chunks)]
+                staged = [flat[2 * k:2 * k + 2] for k in range(chunks)]
         else:
             gate = lax.psum_scatter(gate_part, "gy", scatter_dimension=1, tiled=True)
             up = lax.psum_scatter(up_part, "gy", scatter_dimension=1, tiled=True)
@@ -140,8 +148,15 @@
             hidden_all = xor_all_gather(hidden, "gy", ngy, 1, gy_levels[::-1])
         else:
             hidden_all = lax.all_gather(hidden, "gy", axis=1, tiled=True)
-        down = staged[c] if pairwise(ngy) else w_down[cols, :]
-        term = jnp.dot(hidden_all, down, preferred_element_type=jnp.float32)
+        downs.append(hidden_all)
+    for c in range(chunks):
+        hidden_all = downs[c]
+        if pairwise(ngy):
+            half = step // 2
+            term = (jnp.dot(hidden_all[:, :half], staged[c][0], preferred_element_type=jnp.float32)
+                    + jnp.dot(hidden_all[:, half:], staged[c][1], preferred_element_type=jnp.float32))
+        else:
+            term = jnp.dot(hidden_all, w_down[c * step:(c + 1) * step, :], preferred_element_type=jnp.float32)
         total = term if total is None else total + term
     if pairwise(ngx):
         result = fanout_reduce_scatter(total, "gx", ngx, gx_levels[::-1])

time: 72.4 us -> 71.4 us (0.986)
  waiting for transfers between devices: 20 us -> 15.4 us
  Pallas kernels: 9.17 us -> 11.2 us
  starting transfers between devices: 16.4 us -> 17.5 us
    ppermute x3, waiting for transfers between devices: 6.45 us -> 3.67 us  [fanout_reduce_scatter(): own = own + lax.ppermute(block, axis, [(a, a ^ k) for a in range(n)])]
    ppermute x8, waiting for transfers between devices: 7.91 us -> 5.77 us  [exchange(): return lax.ppermute(x, axis, [(a, a ^ 1 << s) for a in range(n)])]
    pallas_call x2 -> x4, Pallas kernels: 9.17 us -> 11.2 us  [rows_to_vmem(): pl.pallas_call(kernel, out_shape=jax.ShapeDtypeStruct((count, w.shape[1])...]
    ppermute x3, starting transfers between devices: 3.55 us -> 4.45 us  [fanout_reduce_scatter(): own = own + lax.ppermute(block, axis, [(a, a ^ k) for a in range(n)])]
    dot_general x2 -> x4, matrix products: 3.53 us -> 3.76 us  [the longest x2 1.89 us: local(): jnp.dot(hidden_all[:, :half], staged[c][0], preferred_element_type=jnp.fl...]
  transfers between devices with their start and end apart: 17 -> 17, of which waited for: 9 -> 11; matrix products, arithmetic and copies ran while one was open for 5% -> 5% of each run, Pallas kernels for 13% -> 16%
where the time goes in v17:
time: 71.4 us; the launch traced here: 71.1 us
  matrix products  19.4 us (27%)
  starting transfers between devices  17.5 us (25%)
  waiting for transfers between devices  15.4 us (22%)
  Pallas kernels  11.2 us (16%)
  local copies, waits for them, and re-layouts  5.95 us (8%)
  other arithmetic  1.27 us (2%)
    dot_general x2, matrix products, local(): up_part = jnp.dot(piece, w_up[:, cols], preferred_element_type=jnp.float32)  12 us
    pallas_call x4, Pallas kernels, rows_to_vmem(): pl.pallas_call(kernel, out_shape=jax.ShapeDtypeStruct((count, w.shape[1])...  11.2 us
    ppermute x8, waiting for transfers between devices, exchange(): return lax.ppermute(x, axis, [(a, a ^ 1 << s) for a in range(n)])  5.77 us
    ppermute x3, starting transfers between devices, fanout_all_gather(): lax.ppermute(x, axis, [(a, a ^ k) for a in range(n)])  5.62 us
    ppermute x8, starting transfers between devices, exchange(): return lax.ppermute(x, axis, [(a, a ^ 1 << s) for a in range(n)])  5.56 us
    ppermute x3, starting transfers between devices, fanout_reduce_scatter(): own = own + lax.ppermute(block, axis, [(a, a ^ k) for a in range(n)])  4.45 us
    ppermute x3, waiting for transfers between devices, fanout_all_gather(): lax.ppermute(x, axis, [(a, a ^ k) for a in range(n)])  4.25 us
    ppermute x3, waiting for transfers between devices, fanout_reduce_scatter(): own = own + lax.ppermute(block, axis, [(a, a ^ k) for a in range(n)])  3.67 us
  transfers between devices with their start and end apart: 17, of which 11 were waited for; matrix products, arithmetic and copies ran while one was open for 5% of the time, Pallas kernels for 16%

profile of v17, /device:TPU:0, one launch (start us, length us, event | category | flops | bytes accessed | tf_op | source)
XLA Modules:
  0.0 71.1 jit_solution(14538891618098722929)
XLA Ops:
  0.0 3.0 %collective-permute-start = (bf16[5,2048]{1,0:T(8,128)(2,1)}, bf16[5,2048]{1,0:T(8,128)(2,1)S(1)}, u32[]{:S(2)}, u32[]{:S(2)}) collective-permute-start(bf16[5,2048]{1,0:T(8,128)(2,1)} %param.5), channel_id=1, source_target_pairs={{0,4},{4,0},{8,12},{12,8},{1,5},{5,1},{9,13},{13,9},{2,6},{6,2},{1... | collective-permute-start | bytes 61448 | tf_op jit(solution)/shard_map/ppermute | solution.py:70
  3.0 2.6 %collective-permute-start.1 = (bf16[5,2048]{1,0:T(8,128)(2,1)}, bf16[5,2048]{1,0:T(8,128)(2,1)S(1)}, u32[]{:S(2)}, u32[]{:S(2)}) collective-permute-start(bf16[5,2048]{1,0:T(8,128)(2,1)} %param.5), channel_id=1, source_target_pairs={{0,8},{4,12},{8,0},{12,4},{1,9},{5,13},{9,1},{13,5},{2,10},{6,14},... | collective-permute-start | bytes 61448 | tf_op jit(solution)/shard_map/ppermute | solution.py:70
  5.7 1.0 %dynamic_update_slice.12 = bf16[20,2048]{1,0:T(8,128)(2,1)S(1)} dynamic-update-slice(bf16[20,2048]{1,0:T(8,128)(2,1)S(1)} %broadcast_in_dim.15, bf16[5,2048]{1,0:T(8,128)(2,1)} %param.5, s32[]{:T(128)S(6)} %select_n.86, s32[]{:T(128)} %constant.19.clone.1) | dynamic-update-slice | bytes 40964 | tf_op jit(solution)/shard_map/dynamic_update_slice | solution.py:71
  7.0 1.6 %collective-permute-done.1 = bf16[5,2048]{1,0:T(8,128)(2,1)S(1)} collective-permute-done((bf16[5,2048]{1,0:T(8,128)(2,1)}, bf16[5,2048]{1,0:T(8,128)(2,1)S(1)}, u32[]{:S(2)}, u32[]{:S(2)}) %collective-permute-start.1) | collective-permute-done | bytes 20512 | tf_op jit(solution)/shard_map/ppermute | solution.py:70
  8.9 2.6 %collective-permute-done.2 = bf16[5,2048]{1,0:T(8,128)(2,1)S(1)} collective-permute-done((bf16[5,2048]{1,0:T(8,128)(2,1)}, bf16[5,2048]{1,0:T(8,128)(2,1)S(1)}, u32[]{:S(2)}, u32[]{:S(2)}) %collective-permute-start.2) | collective-permute-done | bytes 20512 | tf_op jit(solution)/shard_map/ppermute | solution.py:70
  12.0 1.6 %collective-permute-start.4 = (f32[20]{0:T(128)S(1)}, f32[20]{0:T(128)S(1)}, u32[]{:S(2)}, u32[]{:S(2)}) collective-permute-start(f32[20]{0:T(128)S(1)} %fusion.9), channel_id=1, source_target_pairs={{0,2},{1,3},{2,0},{3,1},{4,6},{5,7},{6,4},{7,5},{8,10},{9,11},{10,... | collective-permute-start | bytes 248 | tf_op jit(solution)/shard_map/ppermute | solution.py:77
  13.9 1.1 %collective-permute-done.5 = f32[20]{0:T(128)S(1)} collective-permute-done((f32[20]{0:T(128)S(1)}, f32[20]{0:T(128)S(1)}, u32[]{:S(2)}, u32[]{:S(2)}) %collective-permute-start.5) | collective-permute-done | bytes 112 | tf_op jit(solution)/shard_map/ppermute | solution.py:77
  16.3 5.8 %fusion = f32[20,3072]{1,0:T(8,128)S(1)} fusion(bf16[2048,6144]{1,0:T(8,128)(2,1)} %param.8, bf16[20,2048]{1,0:T(8,128)(2,1)S(1)} %dynamic_update_slice.15, f32[2048]{0:T(1024)} %param.6, f32[20]{0:T(128)S(1)} %add_rsqrt_fusion), kind=kOutput, calls=%fused_computation.1 | convolution fusion | flops 251822080 | bytes 12918864 | tf_op jit(solution)/shard_map/dot_general | solution.py:131
  22.1 6.3 %fusion.4 = f32[20,3072]{1,0:T(8,128)S(1)} fusion(bf16[2048,6144]{1,0:T(8,128)(2,1)} %param.8, bf16[20,2048]{1,0:T(8,128)(2,1)S(1)} %dynamic_update_slice.15, f32[2048]{0:T(1024)S(1)} %copy-done.1, f32[20]{0:T(128)S(1)} %add_rsqrt_fusion), kind=kOutput, calls=%fused_computation.5 | convolution fusion | flops 251822080 | bytes 12918864 | tf_op jit(solution)/shard_map/dot_general | solution.py:131
  28.3 3.4 %copy-done = bf16[2048,6144]{1,0:T(8,128)(2,1)S(1)} copy-done((bf16[2048,6144]{1,0:T(8,128)(2,1)S(1)}, bf16[2048,6144]{1,0:T(8,128)(2,1)}, u32[]{:S(2)}) %copy-start) | copy-done | bytes 25165848
  31.8 1.8 %fusion.2 = f32[20,3072]{1,0:T(8,128)S(1)} fusion(bf16[2048,6144]{1,0:T(8,128)(2,1)S(1)} %copy-done, bf16[20,2048]{1,0:T(8,128)(2,1)S(1)} %dynamic_update_slice.15, f32[2048]{0:T(1024)S(1)} %copy-done.1, f32[20]{0:T(128)S(1)} %add_rsqrt_fusion), kind=kOutput, calls=%fused_computation.3 | convolution fusion | flops 251822080 | bytes 12935680 | tf_op jit(solution)/shard_map/dot_general | solution.py:130
  33.6 1.8 %fusion.6 = f32[20,3072]{1,0:T(8,128)S(1)} fusion(bf16[2048,6144]{1,0:T(8,128)(2,1)S(1)} %copy-done, bf16[20,2048]{1,0:T(8,128)(2,1)S(1)} %dynamic_update_slice.15, f32[2048]{0:T(1024)S(1)} %copy-done.1, f32[20]{0:T(128)S(1)} %add_rsqrt_fusion), kind=kOutput, calls=%fused_computation.7 | convolution fusion | flops 251822080 | bytes 12935680 | tf_op jit(solution)/shard_map/dot_general | solution.py:130
  36.1 1.0 %collective-permute-done.6 = f32[2,20,1536]{2,1,0:T(8,128)S(1)} collective-permute-done((f32[2,20,1536]{2,1,0:T(8,128)S(1)}, f32[2,20,1536]{2,1,0:T(8,128)S(1)}, u32[]{:S(2)}, u32[]{:S(2)}) %collective-permute-start.6) | collective-permute-done | bytes 245792 | tf_op jit(solution)/shard_map/ppermute | solution.py:20
  37.2 1.6 %collective-permute-start.7 = (f32[2,20,768]{2,1,0:T(8,128)S(1)}, f32[2,20,768]{2,1,0:T(8,128)S(1)}, u32[]{:S(2)}, u32[]{:S(2)}) collective-permute-start(f32[2,20,768]{2,1,0:T(8,128)S(1)} %pad_maximum_fusion.2), channel_id=1, source_target_pairs={{0,2},{1,3},{2,0},{3,1},{4,6},{5,7},{6,4},{7,5},{8,10},{9,11},{10,... | collective-permute-start | bytes 368648 | tf_op jit(solution)/shard_map/ppermute | solution.py:20
  38.8 2.8 %shard_map.56 = bf16[1536,2048]{1,0:T(8,128)(2,1)S(1)} custom-call(bf16[6144,2048]{1,0:T(8,128)(2,1)} %src.3), custom_call_target="tpu_custom_call" | custom-call | bytes 12582912 | tf_op jit(solution)/shard_map/pallas_call | solution.py:90
  41.6 2.8 %shard_map.55 = bf16[1536,2048]{1,0:T(8,128)(2,1)S(1)} custom-call(bf16[6144,2048]{1,0:T(8,128)(2,1)} %src.3), custom_call_target="tpu_custom_call" | custom-call | bytes 12582912 | tf_op jit(solution)/shard_map/pallas_call | solution.py:90
  45.1 1.5 %collective-permute-start.8 = (bf16[20,768]{1,0:T(8,128)(2,1)S(1)}, bf16[20,768]{1,0:T(8,128)(2,1)S(1)}, u32[]{:S(2)}, u32[]{:S(2)}) collective-permute-start(bf16[20,768]{1,0:T(8,128)(2,1)S(1)} %fusion.28), channel_id=1, source_target_pairs={{0,2},{1,3},{2,0},{3,1},{4,6},{5,7},{6,4},{7,5},{8,10},{9,11},{10,... | collective-permute-start | bytes 92168 | tf_op jit(solution)/shard_map/ppermute | solution.py:20
  46.7 3.9 %collective-permute-done.11 = f32[2,20,768]{2,1,0:T(8,128)S(1)} collective-permute-done((f32[2,20,768]{2,1,0:T(8,128)S(1)}, f32[2,20,768]{2,1,0:T(8,128)S(1)}, u32[]{:S(2)}, u32[]{:S(2)}) %collective-permute-start.11) | collective-permute-done | bytes 122912 | tf_op jit(solution)/shard_map/ppermute | solution.py:20
  50.6 2.8 %shard_map.58 = bf16[1536,2048]{1,0:T(8,128)(2,1)S(1)} custom-call(bf16[6144,2048]{1,0:T(8,128)(2,1)} %src.3), custom_call_target="tpu_custom_call" | custom-call | bytes 12582912 | tf_op jit(solution)/shard_map/pallas_call | solution.py:90
  54.2 2.8 %shard_map.57 = bf16[1536,2048]{1,0:T(8,128)(2,1)S(1)} custom-call(bf16[6144,2048]{1,0:T(8,128)(2,1)} %src.3), custom_call_target="tpu_custom_call" | custom-call | bytes 12582912 | tf_op jit(solution)/shard_map/pallas_call | solution.py:90
  61.3 0.9 %fusion.8 = f32[20,2048]{1,0:T(8,128)S(1)} fusion(f32[20,2048]{1,0:T(8,128)S(1)} %convolution_add_fusion.1, f32[20,2048]{1,0:T(8,128)S(1)} %fusion.16, bf16[1536,2048]{1,0:T(8,128)(2,1)S(1)} %shard_map.57, bf16[20,3072]{1,0:T(8,128)(2,1)S(1)} %maximum_select_fusion.1), kind=kOutput, calls=%fused_computation.10 | convolution fusion | flops 125911040 | bytes 6922240 | tf_op jit(solution)/shard_map/dot_general | solution.py:156
  62.8 3.9 %collective-permute-start.14 = (f32[5,2048]{1,0:T(8,128)S(1)}, f32[5,2048]{1,0:T(8,128)S(1)}, u32[]{:S(2)}, u32[]{:S(2)}) collective-permute-start(f32[5,2048]{1,0:T(8,128)S(1)} %get-tuple-element.21), channel_id=1, source_target_pairs={{0,4},{4,0},{8,12},{12,8},{1,5},{5,1},{9,13},{13,9},{2,6},{6,2},{1... | collective-permute-start | bytes 122888 | tf_op jit(solution)/shard_map/ppermute | solution.py:61
  66.8 2.4 %collective-permute-done.16 = f32[5,2048]{1,0:T(8,128)S(1)} collective-permute-done((f32[5,2048]{1,0:T(8,128)S(1)}, f32[5,2048]{1,0:T(8,128)S(1)}, u32[]{:S(2)}, u32[]{:S(2)}) %collective-permute-start.16) | collective-permute-done | bytes 40992 | tf_op jit(solution)/shard_map/ppermute | solution.py:61
  69.2 1.2 %collective-permute-done.15 = f32[5,2048]{1,0:T(8,128)S(1)} collective-permute-done((f32[5,2048]{1,0:T(8,128)S(1)}, f32[5,2048]{1,0:T(8,128)S(1)}, u32[]{:S(2)}, u32[]{:S(2)}) %collective-permute-start.15) | collective-permute-done | bytes 40992 | tf_op jit(solution)/shard_map/ppermute | solution.py:61
  (59 shorter events, 10.7 us)
Async XLA Ops:
  0.0 22.1 %copy-start.1 = (f32[2048]{0:T(1024)S(1)}, f32[2048]{0:T(1024)}, u32[]{:S(2)}) copy-start(f32[2048]{0:T(1024)} %param.6) | copy-start | bytes 24580
  0.0 6.7 %collective-permute-start = (bf16[5,2048]{1,0:T(8,128)(2,1)}, bf16[5,2048]{1,0:T(8,128)(2,1)S(1)}, u32[]{:S(2)}, u32[]{:S(2)}) collective-permute-start(bf16[5,2048]{1,0:T(8,128)(2,1)} %param.5), channel_id=1, source_target_pairs={{0,4},{4,0},{8,12},{12,8},{1,5},{5,1},{9,13},{13,9},{2,6},{6,2},{1... | collective-permute-start | bytes 61448 | tf_op jit(solution)/shard_map/ppermute | solution.py:70
  3.0 5.6 %collective-permute-start.1 = (bf16[5,2048]{1,0:T(8,128)(2,1)}, bf16[5,2048]{1,0:T(8,128)(2,1)S(1)}, u32[]{:S(2)}, u32[]{:S(2)}) collective-permute-start(bf16[5,2048]{1,0:T(8,128)(2,1)} %param.5), channel_id=1, source_target_pairs={{0,8},{4,12},{8,0},{12,4},{1,9},{5,13},{9,1},{13,5},{2,10},{6,14},... | collective-permute-start | bytes 61448 | tf_op jit(solution)/shard_map/ppermute | solution.py:70
  5.6 5.9 %collective-permute-start.2 = (bf16[5,2048]{1,0:T(8,128)(2,1)}, bf16[5,2048]{1,0:T(8,128)(2,1)S(1)}, u32[]{:S(2)}, u32[]{:S(2)}) collective-permute-start(bf16[5,2048]{1,0:T(8,128)(2,1)} %param.5), channel_id=1, source_target_pairs={{0,12},{4,8},{8,4},{12,0},{1,13},{5,9},{9,5},{13,1},{2,14},{6,10},... | collective-permute-start | bytes 61448 | tf_op jit(solution)/shard_map/ppermute | solution.py:70
  11.9 3.0 %collective-permute-start.5 = (f32[20]{0:T(128)S(1)}, f32[20]{0:T(128)S(1)}, u32[]{:S(2)}, u32[]{:S(2)}) collective-permute-start(f32[20]{0:T(128)S(1)} %fusion.9), channel_id=1, source_target_pairs={{0,3},{1,2},{2,1},{3,0},{4,7},{5,6},{6,5},{7,4},{8,11},{9,10},{10,... | collective-permute-start | bytes 248 | tf_op jit(solution)/shard_map/ppermute | solution.py:77
  12.0 3.6 %collective-permute-start.4 = (f32[20]{0:T(128)S(1)}, f32[20]{0:T(128)S(1)}, u32[]{:S(2)}, u32[]{:S(2)}) collective-permute-start(f32[20]{0:T(128)S(1)} %fusion.9), channel_id=1, source_target_pairs={{0,2},{1,3},{2,0},{3,1},{4,6},{5,7},{6,4},{7,5},{8,10},{9,11},{10,... | collective-permute-start | bytes 248 | tf_op jit(solution)/shard_map/ppermute | solution.py:77
  13.6 2.1 %collective-permute-start.3 = (f32[20]{0:T(128)S(1)}, f32[20]{0:T(128)S(1)}, u32[]{:S(2)}, u32[]{:S(2)}) collective-permute-start(f32[20]{0:T(128)S(1)} %fusion.9), channel_id=1, source_target_pairs={{0,1},{1,0},{2,3},{3,2},{4,5},{5,4},{6,7},{7,6},{8,9},{9,8},{10,11... | collective-permute-start | bytes 248 | tf_op jit(solution)/shard_map/ppermute | solution.py:77
  16.3 15.5 %copy-start = (bf16[2048,6144]{1,0:T(8,128)(2,1)S(1)}, bf16[2048,6144]{1,0:T(8,128)(2,1)}, u32[]{:S(2)}) copy-start(bf16[2048,6144]{1,0:T(8,128)(2,1)} %param.7) | copy-start | bytes 75497472
  35.4 1.7 %collective-permute-start.6 = (f32[2,20,1536]{2,1,0:T(8,128)S(1)}, f32[2,20,1536]{2,1,0:T(8,128)S(1)}, u32[]{:S(2)}, u32[]{:S(2)}) collective-permute-start(f32[2,20,1536]{2,1,0:T(8,128)S(1)} %pad_maximum_fusion), channel_id=1, source_target_pairs={{0,1},{1,0},{2,3},{3,2},{4,5},{5,4},{6,7},{7,6},{8,9},{9,8},{10,11... | collective-permute-start | bytes 737288 | tf_op jit(solution)/shard_map/ppermute | solution.py:20
  35.9 2.8 %collective-permute-start.10 = (f32[2,20,1536]{2,1,0:T(8,128)S(1)}, f32[2,20,1536]{2,1,0:T(8,128)S(1)}, u32[]{:S(2)}, u32[]{:S(2)}) collective-permute-start(f32[2,20,1536]{2,1,0:T(8,128)S(1)} %pad_maximum_fusion.1), channel_id=1, source_target_pairs={{0,1},{1,0},{2,3},{3,2},{4,5},{5,4},{6,7},{7,6},{8,9},{9,8},{10,11... | collective-permute-start | bytes 737288 | tf_op jit(solution)/shard_map/ppermute | solution.py:20
  37.2 7.9 %collective-permute-start.7 = (f32[2,20,768]{2,1,0:T(8,128)S(1)}, f32[2,20,768]{2,1,0:T(8,128)S(1)}, u32[]{:S(2)}, u32[]{:S(2)}) collective-permute-start(f32[2,20,768]{2,1,0:T(8,128)S(1)} %pad_maximum_fusion.2), channel_id=1, source_target_pairs={{0,2},{1,3},{2,0},{3,1},{4,6},{5,7},{6,4},{7,5},{8,10},{9,11},{10,... | collective-permute-start | bytes 368648 | tf_op jit(solution)/shard_map/ppermute | solution.py:20
  44.5 6.1 %collective-permute-start.11 = (f32[2,20,768]{2,1,0:T(8,128)S(1)}, f32[2,20,768]{2,1,0:T(8,128)S(1)}, u32[]{:S(2)}, u32[]{:S(2)}) collective-permute-start(f32[2,20,768]{2,1,0:T(8,128)S(1)} %pad_maximum_fusion.3), channel_id=1, source_target_pairs={{0,2},{1,3},{2,0},{3,1},{4,6},{5,7},{6,4},{7,5},{8,10},{9,11},{10,... | collective-permute-start | bytes 368648 | tf_op jit(solution)/shard_map/ppermute | solution.py:20
  45.1 11.9 %collective-permute-start.8 = (bf16[20,768]{1,0:T(8,128)(2,1)S(1)}, bf16[20,768]{1,0:T(8,128)(2,1)S(1)}, u32[]{:S(2)}, u32[]{:S(2)}) collective-permute-start(bf16[20,768]{1,0:T(8,128)(2,1)S(1)} %fusion.28), channel_id=1, source_target_pairs={{0,2},{1,3},{2,0},{3,1},{4,6},{5,7},{6,4},{7,5},{8,10},{9,11},{10,... | collective-permute-start | bytes 92168 | tf_op jit(solution)/shard_map/ppermute | solution.py:20
  53.4 4.0 %collective-permute-start.12 = (bf16[20,768]{1,0:T(8,128)(2,1)S(1)}, bf16[20,768]{1,0:T(8,128)(2,1)S(1)}, u32[]{:S(2)}, u32[]{:S(2)}) collective-permute-start(bf16[20,768]{1,0:T(8,128)(2,1)S(1)} %fusion.21), channel_id=1, source_target_pairs={{0,2},{1,3},{2,0},{3,1},{4,6},{5,7},{6,4},{7,5},{8,10},{9,11},{10,... | collective-permute-start | bytes 92168 | tf_op jit(solution)/shard_map/ppermute | solution.py:20
  57.1 1.3 %collective-permute-start.9 = (bf16[20,1536]{1,0:T(8,128)(2,1)S(1)}, bf16[20,1536]{1,0:T(8,128)(2,1)S(1)}, u32[]{:S(2)}, u32[]{:S(2)}) collective-permute-start(bf16[20,1536]{1,0:T(8,128)(2,1)S(1)} %maximum_select_fusion.2), channel_id=1, source_target_pairs={{0,1},{1,0},{2,3},{3,2},{4,5},{5,4},{6,7},{7,6},{8,9},{9,8},{10,11... | collective-permute-start | bytes 184328 | tf_op jit(solution)/shard_map/ppermute | solution.py:20
  57.4 2.9 %collective-permute-start.13 = (bf16[20,1536]{1,0:T(8,128)(2,1)S(1)}, bf16[20,1536]{1,0:T(8,128)(2,1)S(1)}, u32[]{:S(2)}, u32[]{:S(2)}) collective-permute-start(bf16[20,1536]{1,0:T(8,128)(2,1)S(1)} %maximum_select_fusion.3), channel_id=1, source_target_pairs={{0,1},{1,0},{2,3},{3,2},{4,5},{5,4},{6,7},{7,6},{8,9},{9,8},{10,11... | collective-permute-start | bytes 184328 | tf_op jit(solution)/shard_map/ppermute | solution.py:20
  62.3 6.8 %collective-permute-start.16 = (f32[5,2048]{1,0:T(8,128)S(1)}, f32[5,2048]{1,0:T(8,128)S(1)}, u32[]{:S(2)}, u32[]{:S(2)}) collective-permute-start(f32[5,2048]{1,0:T(8,128)S(1)} %get-tuple-element.22), channel_id=1, source_target_pairs={{0,12},{4,8},{8,4},{12,0},{1,13},{5,9},{9,5},{13,1},{2,14},{6,10},... | collective-permute-start | bytes 122888 | tf_op jit(solution)/shard_map/ppermute | solution.py:61
  62.7 7.6 %collective-permute-start.15 = (f32[5,2048]{1,0:T(8,128)S(1)}, f32[5,2048]{1,0:T(8,128)S(1)}, u32[]{:S(2)}, u32[]{:S(2)}) collective-permute-start(f32[5,2048]{1,0:T(8,128)S(1)} %get-tuple-element.23), channel_id=1, source_target_pairs={{0,8},{4,12},{8,0},{12,4},{1,9},{5,13},{9,1},{13,5},{2,10},{6,14},... | collective-permute-start | bytes 122888 | tf_op jit(solution)/shard_map/ppermute | solution.py:61
  62.8 7.6 %collective-permute-start.14 = (f32[5,2048]{1,0:T(8,128)S(1)}, f32[5,2048]{1,0:T(8,128)S(1)}, u32[]{:S(2)}, u32[]{:S(2)}) collective-permute-start(f32[5,2048]{1,0:T(8,128)S(1)} %get-tuple-element.21), channel_id=1, source_target_pairs={{0,4},{4,0},{8,12},{12,8},{1,5},{5,1},{9,13},{13,9},{2,6},{6,2},{1... | collective-permute-start | bytes 122888 | tf_op jit(solution)/shard_map/ppermute | solution.py:61

commit v18 on v12

--- a/solution.py
+++ b/solution.py
@@ -64,12 +64,10 @@
 
 def fanout_all_gather(x, axis, n, bits):
     me = lax.axis_index(axis)
-    rows = x.shape[0]
-    out = jnp.zeros((n * rows,) + x.shape[1:], x.dtype)
-    for k in range(n):
-        block = x if k == 0 else lax.ppermute(x, axis, [(a, a ^ k) for a in range(n)])
-        out = lax.dynamic_update_slice_in_dim(out, block, gathered_position(me ^ k, bits) * rows, axis=0)
-    return out
+    blocks = jnp.stack([x] + [lax.ppermute(x, axis, [(a, a ^ k) for a in range(n)]) for k in range(1, n)])
+    owner = [next(d for d in range(n) if gathered_position(d, bits) == p) for p in range(n)]
+    ordered = jnp.take(blocks, jnp.asarray(owner, jnp.int32) ^ me, axis=0)
+    return ordered.reshape((n * x.shape[0],) + x.shape[1:])
 
 
 def fanout_all_reduce(x, axis, n):

time: 67.7 us -> 68.7 us (1.015)
  other arithmetic: 1.18 us -> 2.69 us
  local copies, waits for them, and re-layouts: 6 us -> 5.03 us
    dynamic_update_slice x4 -> x0, local copies, waits for them, and re-layouts: 1.87 us -> none  [fanout_all_gather(): lax.dynamic_update_slice_in_dim(out, block, gathered_position(me ^ k, bit...]
    another operation x0 -> x1, other arithmetic: none -> 0.79 us  [fanout_all_gather(): jnp.stack([x] + [lax.ppermute(x, axis, [(a, a ^ k) for a in range(n)]) fo...]
  transfers between devices with their start and end apart: 17 -> 17, of which waited for: 9 -> 10; matrix products, arithmetic and copies ran while one was open for 5% -> 4% of each run, Pallas kernels for 14% -> 13%
where the time goes in v18:
time: 68.7 us; the launch traced here: 68.4 us
  matrix products  19.2 us (28%)
  starting transfers between devices  17.3 us (25%)
  waiting for transfers between devices  14.8 us (22%)
  Pallas kernels  9.17 us (13%)
  local copies, waits for them, and re-layouts  5.03 us (7%)
  other arithmetic  2.69 us (4%)
    dot_general x2, matrix products, local(): up_part = jnp.dot(piece, w_up[:, cols], preferred_element_type=jnp.float32)  12 us
    pallas_call x2, Pallas kernels, rows_to_vmem(): pl.pallas_call(kernel, out_shape=jax.ShapeDtypeStruct((count, w.shape[1])...  9.17 us
    ppermute x8, starting transfers between devices, exchange(): return lax.ppermute(x, axis, [(a, a ^ 1 << s) for a in range(n)])  6.26 us
    ppermute x3, waiting for transfers between devices, fanout_reduce_scatter(): own = own + lax.ppermute(block, axis, [(a, a ^ k) for a in range(n)])  6.12 us
    ppermute x3, starting transfers between devices, fanout_all_gather(): lax.ppermute(x, axis, [(a, a ^ k) for a in range(n)])  5.62 us
    ppermute x3, waiting for transfers between devices, fanout_all_gather(): lax.ppermute(x, axis, [(a, a ^ k) for a in range(n)])  4.36 us
    dot_general x2, matrix products, local(): jnp.dot(piece, w_gate[:, cols], preferred_element_type=jnp.float32)  3.67 us
    ppermute x3, starting transfers between devices, fanout_reduce_scatter(): own = own + lax.ppermute(block, axis, [(a, a ^ k) for a in range(n)])  3.55 us
  transfers between devices with their start and end apart: 17, of which 10 were waited for; matrix products, arithmetic and copies ran while one was open for 4% of the time, Pallas kernels for 13%

profile of v18, /device:TPU:0, one launch (start us, length us, event | category | flops | bytes accessed | tf_op | source)
XLA Modules:
  0.0 68.4 jit_solution(11087180756801482449)
XLA Ops:
  0.0 3.0 %collective-permute-start = (bf16[5,2048]{1,0:T(8,128)(2,1)}, bf16[5,2048]{1,0:T(8,128)(2,1)S(1)}, u32[]{:S(2)}, u32[]{:S(2)}) collective-permute-start(bf16[5,2048]{1,0:T(8,128)(2,1)} %param.6), channel_id=1, source_target_pairs={{0,4},{4,0},{8,12},{12,8},{1,5},{5,1},{9,13},{13,9},{2,6},{6,2},{1... | collective-permute-start | bytes 61448 | tf_op jit(solution)/shard_map/ppermute | solution.py:67
  3.0 2.5 %collective-permute-start.2 = (bf16[5,2048]{1,0:T(8,128)(2,1)}, bf16[5,2048]{1,0:T(8,128)(2,1)S(1)}, u32[]{:S(2)}, u32[]{:S(2)}) collective-permute-start(bf16[5,2048]{1,0:T(8,128)(2,1)} %param.6), channel_id=1, source_target_pairs={{0,12},{4,8},{8,4},{12,0},{1,13},{5,9},{9,5},{13,1},{2,14},{6,10},... | collective-permute-start | bytes 61448 | tf_op jit(solution)/shard_map/ppermute | solution.py:67
  6.5 2.9 %collective-permute-done.2 = bf16[5,2048]{1,0:T(8,128)(2,1)S(1)} collective-permute-done((bf16[5,2048]{1,0:T(8,128)(2,1)}, bf16[5,2048]{1,0:T(8,128)(2,1)S(1)}, u32[]{:S(2)}, u32[]{:S(2)}) %collective-permute-start.2) | collective-permute-done | bytes 20512 | tf_op jit(solution)/shard_map/ppermute | solution.py:67
  9.4 1.5 %collective-permute-done.1 = bf16[5,2048]{1,0:T(8,128)(2,1)S(1)} collective-permute-done((bf16[5,2048]{1,0:T(8,128)(2,1)}, bf16[5,2048]{1,0:T(8,128)(2,1)S(1)}, u32[]{:S(2)}, u32[]{:S(2)}) %collective-permute-start.1) | collective-permute-done | bytes 20512 | tf_op jit(solution)/shard_map/ppermute | solution.py:67
  12.6 1.6 %collective-permute-start.4 = (f32[20]{0:T(128)S(1)}, f32[20]{0:T(128)S(1)}, u32[]{:S(2)}, u32[]{:S(2)}) collective-permute-start(f32[20]{0:T(128)S(1)} %reduce_sum.21), channel_id=1, source_target_pairs={{0,2},{1,3},{2,0},{3,1},{4,6},{5,7},{6,4},{7,5},{8,10},{9,11},{10,... | collective-permute-start | bytes 248 | tf_op jit(solution)/shard_map/ppermute | solution.py:75
  14.5 1.1 %collective-permute-done.5 = f32[20]{0:T(128)S(1)} collective-permute-done((f32[20]{0:T(128)S(1)}, f32[20]{0:T(128)S(1)}, u32[]{:S(2)}, u32[]{:S(2)}) %collective-permute-start.5) | collective-permute-done | bytes 112 | tf_op jit(solution)/shard_map/ppermute | solution.py:75
  16.9 5.8 %fusion.4 = f32[20,3072]{1,0:T(8,128)S(1)} fusion(bf16[2048,6144]{1,0:T(8,128)(2,1)} %param.9, f32[2048]{0:T(1024)} %param.7, f32[20]{0:T(128)S(1)} %add_rsqrt_fusion, bf16[20,2048]{1,0:T(8,128)(2,1)S(1)} %gather.11, pred[20]{0:T(512)(128)(4,1)S(1)} %broadcast_in_dim.33), kind=kOutput, calls=%fused_computation.6 | convolution fusion | flops 251863040 | bytes 12918884 | tf_op jit(solution)/shard_map/dot_general | solution.py:126
  22.7 6.3 %fusion = f32[20,3072]{1,0:T(8,128)S(1)} fusion(bf16[2048,6144]{1,0:T(8,128)(2,1)} %param.9, f32[2048]{0:T(1024)S(1)} %copy-done.1, f32[20]{0:T(128)S(1)} %add_rsqrt_fusion, bf16[20,2048]{1,0:T(8,128)(2,1)S(1)} %gather.11, pred[20]{0:T(512)(128)(4,1)S(1)} %broadcast_in_dim.33), kind=kOutput, calls=%fused_computation.2 | convolution fusion | flops 251863040 | bytes 12918884 | tf_op jit(solution)/shard_map/dot_general | solution.py:126
  29.0 3.4 %copy-done = bf16[2048,6144]{1,0:T(8,128)(2,1)S(1)} copy-done((bf16[2048,6144]{1,0:T(8,128)(2,1)S(1)}, bf16[2048,6144]{1,0:T(8,128)(2,1)}, u32[]{:S(2)}) %copy-start) | copy-done | bytes 25165848
  32.4 1.8 %fusion.2 = f32[20,3072]{1,0:T(8,128)S(1)} fusion(bf16[2048,6144]{1,0:T(8,128)(2,1)S(1)} %copy-done, f32[2048]{0:T(1024)S(1)} %copy-done.1, f32[20]{0:T(128)S(1)} %add_rsqrt_fusion, bf16[20,2048]{1,0:T(8,128)(2,1)S(1)} %gather.11, pred[20]{0:T(512)(128)(4,1)S(1)} %broadcast_in_dim.33), kind=kOutput, calls=%fused_computation.4 | convolution fusion | flops 251863040 | bytes 12936192 | tf_op jit(solution)/shard_map/dot_general | solution.py:125
  34.2 1.8 %fusion.6 = f32[20,3072]{1,0:T(8,128)S(1)} fusion(bf16[2048,6144]{1,0:T(8,128)(2,1)S(1)} %copy-done, f32[2048]{0:T(1024)S(1)} %copy-done.1, f32[20]{0:T(128)S(1)} %add_rsqrt_fusion, bf16[20,2048]{1,0:T(8,128)(2,1)S(1)} %gather.11, pred[20]{0:T(512)(128)(4,1)S(1)} %broadcast_in_dim.33), kind=kOutput, calls=%fused_computation.8 | convolution fusion | flops 251863040 | bytes 12936192 | tf_op jit(solution)/shard_map/dot_general | solution.py:125
  36.8 1.0 %collective-permute-done.10 = f32[2,20,1536]{2,1,0:T(8,128)S(1)} collective-permute-done((f32[2,20,1536]{2,1,0:T(8,128)S(1)}, f32[2,20,1536]{2,1,0:T(8,128)S(1)}, u32[]{:S(2)}, u32[]{:S(2)}) %collective-permute-start.10) | collective-permute-done | bytes 245792 | tf_op jit(solution)/shard_map/ppermute | solution.py:20
  37.9 1.5 %collective-permute-start.11 = (f32[2,20,768]{2,1,0:T(8,128)S(1)}, f32[2,20,768]{2,1,0:T(8,128)S(1)}, u32[]{:S(2)}, u32[]{:S(2)}) collective-permute-start(f32[2,20,768]{2,1,0:T(8,128)S(1)} %pad_maximum_fusion.3), channel_id=1, source_target_pairs={{0,2},{1,3},{2,0},{3,1},{4,6},{5,7},{6,4},{7,5},{8,10},{9,11},{10,... | collective-permute-start | bytes 368648 | tf_op jit(solution)/shard_map/ppermute | solution.py:20
  40.2 4.6 %shard_map.64 = bf16[3072,2048]{1,0:T(8,128)(2,1)S(1)} custom-call(bf16[6144,2048]{1,0:T(8,128)(2,1)} %src.1), custom_call_target="tpu_custom_call" | custom-call | bytes 25165824 | tf_op jit(solution)/shard_map/pallas_call | solution.py:88
  44.8 1.5 %collective-permute-start.12 = (bf16[20,768]{1,0:T(8,128)(2,1)S(1)}, bf16[20,768]{1,0:T(8,128)(2,1)S(1)}, u32[]{:S(2)}, u32[]{:S(2)}) collective-permute-start(bf16[20,768]{1,0:T(8,128)(2,1)S(1)} %fusion.27), channel_id=1, source_target_pairs={{0,2},{1,3},{2,0},{3,1},{4,6},{5,7},{6,4},{7,5},{8,10},{9,11},{10,... | collective-permute-start | bytes 92168 | tf_op jit(solution)/shard_map/ppermute | solution.py:20
  46.3 0.9 %collective-permute-done.7 = f32[2,20,768]{2,1,0:T(8,128)S(1)} collective-permute-done((f32[2,20,768]{2,1,0:T(8,128)S(1)}, f32[2,20,768]{2,1,0:T(8,128)S(1)}, u32[]{:S(2)}, u32[]{:S(2)}) %collective-permute-start.7) | collective-permute-done | bytes 122912 | tf_op jit(solution)/shard_map/ppermute | solution.py:20
  47.3 1.3 %collective-permute-start.8 = (bf16[20,768]{1,0:T(8,128)(2,1)S(1)}, bf16[20,768]{1,0:T(8,128)(2,1)S(1)}, u32[]{:S(2)}, u32[]{:S(2)}) collective-permute-start(bf16[20,768]{1,0:T(8,128)(2,1)S(1)} %fusion.31), channel_id=1, source_target_pairs={{0,2},{1,3},{2,0},{3,1},{4,6},{5,7},{6,4},{7,5},{8,10},{9,11},{10,... | collective-permute-start | bytes 92168 | tf_op jit(solution)/shard_map/ppermute | solution.py:20
  48.6 4.6 %shard_map.65 = bf16[3072,2048]{1,0:T(8,128)(2,1)S(1)} custom-call(bf16[6144,2048]{1,0:T(8,128)(2,1)} %src.1), custom_call_target="tpu_custom_call" | custom-call | bytes 25165824 | tf_op jit(solution)/shard_map/pallas_call | solution.py:88
  54.5 1.7 %fusion.17 = f32[20,2048]{1,0:T(8,128)S(1)} fusion(bf16[3072,2048]{1,0:T(8,128)(2,1)S(1)} %shard_map.65, bf16[20,1536]{1,0:T(8,128)(2,1)S(1)} %collective-permute-done.13, bf16[20,1536]{1,0:T(8,128)(2,1)S(1)} %maximum_select_fusion.5, pred[]{:T(512)S(6)} %eq.8), kind=kOutput, calls=%fused_computation.32 | convolution fusion | flops 252211200 | bytes 12869633 | tf_op jit(solution)/shard_map/dot_general | solution.py:146
  56.3 1.8 %convolution_add_fusion = f32[20,2048]{1,0:T(8,128)S(1)} fusion(f32[20,2048]{1,0:T(8,128)S(1)} %fusion.17, bf16[3072,2048]{1,0:T(8,128)(2,1)S(1)} %shard_map.64, bf16[20,1536]{1,0:T(8,128)(2,1)S(1)} %collective-permute-done.9, bf16[20,1536]{1,0:T(8,128)(2,1)S(1)} %maximum_select_fusion.4, pred[]{:T(512)S(6)} %eq.8), kind=kOutput, calls=%fused_computation.10 | convolution fusion | flops 252252160 | bytes 13033473 | tf_op jit(solution)/shard_map/dot_general | solution.py:146
  58.6 1.1 %collective-permute-start.16 = (f32[5,2048]{1,0:T(8,128)S(1)}, f32[5,2048]{1,0:T(8,128)S(1)}, u32[]{:S(2)}, u32[]{:S(2)}) collective-permute-start(f32[5,2048]{1,0:T(8,128)S(1)} %get-tuple-element.18), channel_id=1, source_target_pairs={{0,12},{4,8},{8,4},{12,0},{1,13},{5,9},{9,5},{13,1},{2,14},{6,10},... | collective-permute-start | bytes 122888 | tf_op jit(solution)/shard_map/ppermute | solution.py:61
  59.6 2.0 %collective-permute-start.15 = (f32[5,2048]{1,0:T(8,128)S(1)}, f32[5,2048]{1,0:T(8,128)S(1)}, u32[]{:S(2)}, u32[]{:S(2)}) collective-permute-start(f32[5,2048]{1,0:T(8,128)S(1)} %get-tuple-element.19), channel_id=1, source_target_pairs={{0,8},{4,12},{8,0},{12,4},{1,9},{5,13},{9,1},{13,5},{2,10},{6,14},... | collective-permute-start | bytes 122888 | tf_op jit(solution)/shard_map/ppermute | solution.py:61
  62.4 2.6 %collective-permute-done.16 = f32[5,2048]{1,0:T(8,128)S(1)} collective-permute-done((f32[5,2048]{1,0:T(8,128)S(1)}, f32[5,2048]{1,0:T(8,128)S(1)}, u32[]{:S(2)}, u32[]{:S(2)}) %collective-permute-start.16) | collective-permute-done | bytes 40992 | tf_op jit(solution)/shard_map/ppermute | solution.py:61
  65.1 2.7 %collective-permute-done.15 = f32[5,2048]{1,0:T(8,128)S(1)} collective-permute-done((f32[5,2048]{1,0:T(8,128)S(1)}, f32[5,2048]{1,0:T(8,128)S(1)}, u32[]{:S(2)}, u32[]{:S(2)}) %collective-permute-start.15) | collective-permute-done | bytes 40992 | tf_op jit(solution)/shard_map/ppermute | solution.py:61
  (57 shorter events, 9.2 us)
Async XLA Ops:
  0.0 22.7 %copy-start.1 = (f32[2048]{0:T(1024)S(1)}, f32[2048]{0:T(1024)}, u32[]{:S(2)}) copy-start(f32[2048]{0:T(1024)} %param.7) | copy-start | bytes 24580
  0.0 6.5 %collective-permute-start = (bf16[5,2048]{1,0:T(8,128)(2,1)}, bf16[5,2048]{1,0:T(8,128)(2,1)S(1)}, u32[]{:S(2)}, u32[]{:S(2)}) collective-permute-start(bf16[5,2048]{1,0:T(8,128)(2,1)} %param.6), channel_id=1, source_target_pairs={{0,4},{4,0},{8,12},{12,8},{1,5},{5,1},{9,13},{13,9},{2,6},{6,2},{1... | collective-permute-start | bytes 61448 | tf_op jit(solution)/shard_map/ppermute | solution.py:67
  3.0 6.4 %collective-permute-start.2 = (bf16[5,2048]{1,0:T(8,128)(2,1)}, bf16[5,2048]{1,0:T(8,128)(2,1)S(1)}, u32[]{:S(2)}, u32[]{:S(2)}) collective-permute-start(bf16[5,2048]{1,0:T(8,128)(2,1)} %param.6), channel_id=1, source_target_pairs={{0,12},{4,8},{8,4},{12,0},{1,13},{5,9},{9,5},{13,1},{2,14},{6,10},... | collective-permute-start | bytes 61448 | tf_op jit(solution)/shard_map/ppermute | solution.py:67
  5.5 5.4 %collective-permute-start.1 = (bf16[5,2048]{1,0:T(8,128)(2,1)}, bf16[5,2048]{1,0:T(8,128)(2,1)S(1)}, u32[]{:S(2)}, u32[]{:S(2)}) collective-permute-start(bf16[5,2048]{1,0:T(8,128)(2,1)} %param.6), channel_id=1, source_target_pairs={{0,8},{4,12},{8,0},{12,4},{1,9},{5,13},{9,1},{13,5},{2,10},{6,14},... | collective-permute-start | bytes 61448 | tf_op jit(solution)/shard_map/ppermute | solution.py:67
  12.6 3.0 %collective-permute-start.5 = (f32[20]{0:T(128)S(1)}, f32[20]{0:T(128)S(1)}, u32[]{:S(2)}, u32[]{:S(2)}) collective-permute-start(f32[20]{0:T(128)S(1)} %reduce_sum.21), channel_id=1, source_target_pairs={{0,3},{1,2},{2,1},{3,0},{4,7},{5,6},{6,5},{7,4},{8,11},{9,10},{10,... | collective-permute-start | bytes 248 | tf_op jit(solution)/shard_map/ppermute | solution.py:75
  12.6 3.6 %collective-permute-start.4 = (f32[20]{0:T(128)S(1)}, f32[20]{0:T(128)S(1)}, u32[]{:S(2)}, u32[]{:S(2)}) collective-permute-start(f32[20]{0:T(128)S(1)} %reduce_sum.21), channel_id=1, source_target_pairs={{0,2},{1,3},{2,0},{3,1},{4,6},{5,7},{6,4},{7,5},{8,10},{9,11},{10,... | collective-permute-start | bytes 248 | tf_op jit(solution)/shard_map/ppermute | solution.py:75
  14.2 2.1 %collective-permute-start.3 = (f32[20]{0:T(128)S(1)}, f32[20]{0:T(128)S(1)}, u32[]{:S(2)}, u32[]{:S(2)}) collective-permute-start(f32[20]{0:T(128)S(1)} %reduce_sum.21), channel_id=1, source_target_pairs={{0,1},{1,0},{2,3},{3,2},{4,5},{5,4},{6,7},{7,6},{8,9},{9,8},{10,11... | collective-permute-start | bytes 248 | tf_op jit(solution)/shard_map/ppermute | solution.py:75
  16.9 15.5 %copy-start = (bf16[2048,6144]{1,0:T(8,128)(2,1)S(1)}, bf16[2048,6144]{1,0:T(8,128)(2,1)}, u32[]{:S(2)}) copy-start(bf16[2048,6144]{1,0:T(8,128)(2,1)} %param.8) | copy-start | bytes 75497472
  36.1 1.7 %collective-permute-start.10 = (f32[2,20,1536]{2,1,0:T(8,128)S(1)}, f32[2,20,1536]{2,1,0:T(8,128)S(1)}, u32[]{:S(2)}, u32[]{:S(2)}) collective-permute-start(f32[2,20,1536]{2,1,0:T(8,128)S(1)} %pad_maximum_fusion.1), channel_id=1, source_target_pairs={{0,1},{1,0},{2,3},{3,2},{4,5},{5,4},{6,7},{7,6},{8,9},{9,8},{10,11... | collective-permute-start | bytes 737288 | tf_op jit(solution)/shard_map/ppermute | solution.py:20
  36.6 2.8 %collective-permute-start.6 = (f32[2,20,1536]{2,1,0:T(8,128)S(1)}, f32[2,20,1536]{2,1,0:T(8,128)S(1)}, u32[]{:S(2)}, u32[]{:S(2)}) collective-permute-start(f32[2,20,1536]{2,1,0:T(8,128)S(1)} %pad_maximum_fusion), channel_id=1, source_target_pairs={{0,1},{1,0},{2,3},{3,2},{4,5},{5,4},{6,7},{7,6},{8,9},{9,8},{10,11... | collective-permute-start | bytes 737288 | tf_op jit(solution)/shard_map/ppermute | solution.py:20
  37.9 6.9 %collective-permute-start.11 = (f32[2,20,768]{2,1,0:T(8,128)S(1)}, f32[2,20,768]{2,1,0:T(8,128)S(1)}, u32[]{:S(2)}, u32[]{:S(2)}) collective-permute-start(f32[2,20,768]{2,1,0:T(8,128)S(1)} %pad_maximum_fusion.3), channel_id=1, source_target_pairs={{0,2},{1,3},{2,0},{3,1},{4,6},{5,7},{6,4},{7,5},{8,10},{9,11},{10,... | collective-permute-start | bytes 368648 | tf_op jit(solution)/shard_map/ppermute | solution.py:20
  39.5 7.7 %collective-permute-start.7 = (f32[2,20,768]{2,1,0:T(8,128)S(1)}, f32[2,20,768]{2,1,0:T(8,128)S(1)}, u32[]{:S(2)}, u32[]{:S(2)}) collective-permute-start(f32[2,20,768]{2,1,0:T(8,128)S(1)} %pad_maximum_fusion.2), channel_id=1, source_target_pairs={{0,2},{1,3},{2,0},{3,1},{4,6},{5,7},{6,4},{7,5},{8,10},{9,11},{10,... | collective-permute-start | bytes 368648 | tf_op jit(solution)/shard_map/ppermute | solution.py:20
  44.8 8.4 %collective-permute-start.12 = (bf16[20,768]{1,0:T(8,128)(2,1)S(1)}, bf16[20,768]{1,0:T(8,128)(2,1)S(1)}, u32[]{:S(2)}, u32[]{:S(2)}) collective-permute-start(bf16[20,768]{1,0:T(8,128)(2,1)S(1)} %fusion.27), channel_id=1, source_target_pairs={{0,2},{1,3},{2,0},{3,1},{4,6},{5,7},{6,4},{7,5},{8,10},{9,11},{10,... | collective-permute-start | bytes 92168 | tf_op jit(solution)/shard_map/ppermute | solution.py:20
  47.3 6.0 %collective-permute-start.8 = (bf16[20,768]{1,0:T(8,128)(2,1)S(1)}, bf16[20,768]{1,0:T(8,128)(2,1)S(1)}, u32[]{:S(2)}, u32[]{:S(2)}) collective-permute-start(bf16[20,768]{1,0:T(8,128)(2,1)S(1)} %fusion.31), channel_id=1, source_target_pairs={{0,2},{1,3},{2,0},{3,1},{4,6},{5,7},{6,4},{7,5},{8,10},{9,11},{10,... | collective-permute-start | bytes 92168 | tf_op jit(solution)/shard_map/ppermute | solution.py:20
  53.2 1.3 %collective-permute-start.13 = (bf16[20,1536]{1,0:T(8,128)(2,1)S(1)}, bf16[20,1536]{1,0:T(8,128)(2,1)S(1)}, u32[]{:S(2)}, u32[]{:S(2)}) collective-permute-start(bf16[20,1536]{1,0:T(8,128)(2,1)S(1)} %maximum_select_fusion.5), channel_id=1, source_target_pairs={{0,1},{1,0},{2,3},{3,2},{4,5},{5,4},{6,7},{7,6},{8,9},{9,8},{10,11... | collective-permute-start | bytes 184328 | tf_op jit(solution)/shard_map/ppermute | solution.py:20
  53.3 3.0 %collective-permute-start.9 = (bf16[20,1536]{1,0:T(8,128)(2,1)S(1)}, bf16[20,1536]{1,0:T(8,128)(2,1)S(1)}, u32[]{:S(2)}, u32[]{:S(2)}) collective-permute-start(bf16[20,1536]{1,0:T(8,128)(2,1)S(1)} %maximum_select_fusion.4), channel_id=1, source_target_pairs={{0,1},{1,0},{2,3},{3,2},{4,5},{5,4},{6,7},{7,6},{8,9},{9,8},{10,11... | collective-permute-start | bytes 184328 | tf_op jit(solution)/shard_map/ppermute | solution.py:20
  58.1 4.3 %collective-permute-start.14 = (f32[5,2048]{1,0:T(8,128)S(1)}, f32[5,2048]{1,0:T(8,128)S(1)}, u32[]{:S(2)}, u32[]{:S(2)}) collective-permute-start(f32[5,2048]{1,0:T(8,128)S(1)} %get-tuple-element.17), channel_id=1, source_target_pairs={{0,4},{4,0},{8,12},{12,8},{1,5},{5,1},{9,13},{13,9},{2,6},{6,2},{1... | collective-permute-start | bytes 122888 | tf_op jit(solution)/shard_map/ppermute | solution.py:61
  58.6 6.5 %collective-permute-start.16 = (f32[5,2048]{1,0:T(8,128)S(1)}, f32[5,2048]{1,0:T(8,128)S(1)}, u32[]{:S(2)}, u32[]{:S(2)}) collective-permute-start(f32[5,2048]{1,0:T(8,128)S(1)} %get-tuple-element.18), channel_id=1, source_target_pairs={{0,12},{4,8},{8,4},{12,0},{1,13},{5,9},{9,5},{13,1},{2,14},{6,10},... | collective-permute-start | bytes 122888 | tf_op jit(solution)/shard_map/ppermute | solution.py:61
  59.6 8.1 %collective-permute-start.15 = (f32[5,2048]{1,0:T(8,128)S(1)}, f32[5,2048]{1,0:T(8,128)S(1)}, u32[]{:S(2)}, u32[]{:S(2)}) collective-permute-start(f32[5,2048]{1,0:T(8,128)S(1)} %get-tuple-element.19), channel_id=1, source_target_pairs={{0,8},{4,12},{8,0},{12,4},{1,9},{5,13},{9,1},{13,5},{2,10},{6,14},... | collective-permute-start | bytes 122888 | tf_op jit(solution)/shard_map/ppermute | solution.py:61

commit v19 on v12

--- a/solution.py
+++ b/solution.py
@@ -132,7 +132,7 @@
                 source, _ = lax.optimization_barrier((w_down, first[0]))
                 staged = [rows_to_vmem(source, 0, step)]
             gate, up = xor_reduce_scatter(first, "gy", ngy, 1, gy_levels[1:])
-            if c == 0:
+            if c == chunks - 1:
                 for k in range(1, chunks):
                     source, _ = lax.optimization_barrier((w_down, gate))
                     staged.append(rows_to_vmem(source, k * step, step))

time: 67.7 us -> 71.2 us (1.052)
  waiting for transfers between devices: 14.3 us -> 17.9 us
    ppermute x8, waiting for transfers between devices: 2.52 us -> 7.91 us  [exchange(): return lax.ppermute(x, axis, [(a, a ^ 1 << s) for a in range(n)])]
    ppermute x3, waiting for transfers between devices: 6.12 us -> 3.94 us  [fanout_reduce_scatter(): own = own + lax.ppermute(block, axis, [(a, a ^ k) for a in range(n)])]
    ppermute x8, starting transfers between devices: 6.29 us -> 5.33 us  [exchange(): return lax.ppermute(x, axis, [(a, a ^ 1 << s) for a in range(n)])]
    ppermute x3, starting transfers between devices: 3.55 us -> 4.45 us  [fanout_reduce_scatter(): own = own + lax.ppermute(block, axis, [(a, a ^ k) for a in range(n)])]
  transfers between devices with their start and end apart: 17 -> 17, of which waited for: 9 -> 9; matrix products, arithmetic and copies ran while one was open for 5% -> 5% of each run, Pallas kernels for 14% -> 13%
where the time goes in v19:
time: 71.2 us; the launch traced here: 70.9 us
  matrix products  19.2 us (27%)
  waiting for transfers between devices  17.9 us (25%)
  starting transfers between devices  17.3 us (24%)
  Pallas kernels  9.17 us (13%)
  local copies, waits for them, and re-layouts  5.95 us (8%)
  other arithmetic  1.17 us (2%)
    dot_general x2, matrix products, local(): up_part = jnp.dot(piece, w_up[:, cols], preferred_element_type=jnp.float32)  12 us
    pallas_call x2, Pallas kernels, rows_to_vmem(): pl.pallas_call(kernel, out_shape=jax.ShapeDtypeStruct((count, w.shape[1])...  9.17 us
    ppermute x8, waiting for transfers between devices, exchange(): return lax.ppermute(x, axis, [(a, a ^ 1 << s) for a in range(n)])  7.91 us
    ppermute x3, starting transfers between devices, fanout_all_gather(): lax.ppermute(x, axis, [(a, a ^ k) for a in range(n)])  5.62 us
    ppermute x8, starting transfers between devices, exchange(): return lax.ppermute(x, axis, [(a, a ^ 1 << s) for a in range(n)])  5.33 us
    ppermute x3, starting transfers between devices, fanout_reduce_scatter(): own = own + lax.ppermute(block, axis, [(a, a ^ k) for a in range(n)])  4.45 us
    ppermute x3, waiting for transfers between devices, fanout_all_gather(): lax.ppermute(x, axis, [(a, a ^ k) for a in range(n)])  4.25 us
    ppermute x3, waiting for transfers between devices, fanout_reduce_scatter(): own = own + lax.ppermute(block, axis, [(a, a ^ k) for a in range(n)])  3.94 us
  transfers between devices with their start and end apart: 17, of which 9 were waited for; matrix products, arithmetic and copies ran while one was open for 5% of the time, Pallas kernels for 13%

profile of v19, /device:TPU:0, one launch (start us, length us, event | category | flops | bytes accessed | tf_op | source)
XLA Modules:
  0.0 70.9 jit_solution(14181179866524954298)
XLA Ops:
  0.0 3.0 %collective-permute-start = (bf16[5,2048]{1,0:T(8,128)(2,1)}, bf16[5,2048]{1,0:T(8,128)(2,1)S(1)}, u32[]{:S(2)}, u32[]{:S(2)}) collective-permute-start(bf16[5,2048]{1,0:T(8,128)(2,1)} %param.5), channel_id=1, source_target_pairs={{0,4},{4,0},{8,12},{12,8},{1,5},{5,1},{9,13},{13,9},{2,6},{6,2},{1... | collective-permute-start | bytes 61448 | tf_op jit(solution)/shard_map/ppermute | solution.py:70
  3.0 2.6 %collective-permute-start.1 = (bf16[5,2048]{1,0:T(8,128)(2,1)}, bf16[5,2048]{1,0:T(8,128)(2,1)S(1)}, u32[]{:S(2)}, u32[]{:S(2)}) collective-permute-start(bf16[5,2048]{1,0:T(8,128)(2,1)} %param.5), channel_id=1, source_target_pairs={{0,8},{4,12},{8,0},{12,4},{1,9},{5,13},{9,1},{13,5},{2,10},{6,14},... | collective-permute-start | bytes 61448 | tf_op jit(solution)/shard_map/ppermute | solution.py:70
  5.7 1.0 %dynamic_update_slice.12 = bf16[20,2048]{1,0:T(8,128)(2,1)S(1)} dynamic-update-slice(bf16[20,2048]{1,0:T(8,128)(2,1)S(1)} %broadcast_in_dim.15, bf16[5,2048]{1,0:T(8,128)(2,1)} %param.5, s32[]{:T(128)S(6)} %select_n.86, s32[]{:T(128)} %constant.19.clone.1) | dynamic-update-slice | bytes 40964 | tf_op jit(solution)/shard_map/dynamic_update_slice | solution.py:71
  7.0 1.6 %collective-permute-done.1 = bf16[5,2048]{1,0:T(8,128)(2,1)S(1)} collective-permute-done((bf16[5,2048]{1,0:T(8,128)(2,1)}, bf16[5,2048]{1,0:T(8,128)(2,1)S(1)}, u32[]{:S(2)}, u32[]{:S(2)}) %collective-permute-start.1) | collective-permute-done | bytes 20512 | tf_op jit(solution)/shard_map/ppermute | solution.py:70
  8.9 2.6 %collective-permute-done.2 = bf16[5,2048]{1,0:T(8,128)(2,1)S(1)} collective-permute-done((bf16[5,2048]{1,0:T(8,128)(2,1)}, bf16[5,2048]{1,0:T(8,128)(2,1)S(1)}, u32[]{:S(2)}, u32[]{:S(2)}) %collective-permute-start.2) | collective-permute-done | bytes 20512 | tf_op jit(solution)/shard_map/ppermute | solution.py:70
  12.0 1.6 %collective-permute-start.4 = (f32[20]{0:T(128)S(1)}, f32[20]{0:T(128)S(1)}, u32[]{:S(2)}, u32[]{:S(2)}) collective-permute-start(f32[20]{0:T(128)S(1)} %fusion.8), channel_id=1, source_target_pairs={{0,2},{1,3},{2,0},{3,1},{4,6},{5,7},{6,4},{7,5},{8,10},{9,11},{10,... | collective-permute-start | bytes 248 | tf_op jit(solution)/shard_map/ppermute | solution.py:77
  13.9 1.1 %collective-permute-done.5 = f32[20]{0:T(128)S(1)} collective-permute-done((f32[20]{0:T(128)S(1)}, f32[20]{0:T(128)S(1)}, u32[]{:S(2)}, u32[]{:S(2)}) %collective-permute-start.5) | collective-permute-done | bytes 112 | tf_op jit(solution)/shard_map/ppermute | solution.py:77
  16.3 5.8 %fusion = f32[20,3072]{1,0:T(8,128)S(1)} fusion(bf16[2048,6144]{1,0:T(8,128)(2,1)} %param.8, bf16[20,2048]{1,0:T(8,128)(2,1)S(1)} %dynamic_update_slice.15, f32[2048]{0:T(1024)} %param.6, f32[20]{0:T(128)S(1)} %add_rsqrt_fusion), kind=kOutput, calls=%fused_computation.1 | convolution fusion | flops 251822080 | bytes 12918864 | tf_op jit(solution)/shard_map/dot_general | solution.py:128
  22.1 6.3 %fusion.4 = f32[20,3072]{1,0:T(8,128)S(1)} fusion(bf16[2048,6144]{1,0:T(8,128)(2,1)} %param.8, bf16[20,2048]{1,0:T(8,128)(2,1)S(1)} %dynamic_update_slice.15, f32[2048]{0:T(1024)S(1)} %copy-done.1, f32[20]{0:T(128)S(1)} %add_rsqrt_fusion), kind=kOutput, calls=%fused_computation.5 | convolution fusion | flops 251822080 | bytes 12918864 | tf_op jit(solution)/shard_map/dot_general | solution.py:128
  28.3 3.4 %copy-done = bf16[2048,6144]{1,0:T(8,128)(2,1)S(1)} copy-done((bf16[2048,6144]{1,0:T(8,128)(2,1)S(1)}, bf16[2048,6144]{1,0:T(8,128)(2,1)}, u32[]{:S(2)}) %copy-start) | copy-done | bytes 25165848
  31.8 1.8 %fusion.2 = f32[20,3072]{1,0:T(8,128)S(1)} fusion(bf16[2048,6144]{1,0:T(8,128)(2,1)S(1)} %copy-done, bf16[20,2048]{1,0:T(8,128)(2,1)S(1)} %dynamic_update_slice.15, f32[2048]{0:T(1024)S(1)} %copy-done.1, f32[20]{0:T(128)S(1)} %add_rsqrt_fusion), kind=kOutput, calls=%fused_computation.3 | convolution fusion | flops 251822080 | bytes 12935680 | tf_op jit(solution)/shard_map/dot_general | solution.py:127
  33.6 1.8 %fusion.6 = f32[20,3072]{1,0:T(8,128)S(1)} fusion(bf16[2048,6144]{1,0:T(8,128)(2,1)S(1)} %copy-done, bf16[20,2048]{1,0:T(8,128)(2,1)S(1)} %dynamic_update_slice.15, f32[2048]{0:T(1024)S(1)} %copy-done.1, f32[20]{0:T(128)S(1)} %add_rsqrt_fusion), kind=kOutput, calls=%fused_computation.7 | convolution fusion | flops 251822080 | bytes 12935680 | tf_op jit(solution)/shard_map/dot_general | solution.py:127
  36.1 1.0 %collective-permute-done.10 = f32[2,20,1536]{2,1,0:T(8,128)S(1)} collective-permute-done((f32[2,20,1536]{2,1,0:T(8,128)S(1)}, f32[2,20,1536]{2,1,0:T(8,128)S(1)}, u32[]{:S(2)}, u32[]{:S(2)}) %collective-permute-start.10) | collective-permute-done | bytes 245792 | tf_op jit(solution)/shard_map/ppermute | solution.py:20
  37.2 1.6 %collective-permute-start.11 = (f32[2,20,768]{2,1,0:T(8,128)S(1)}, f32[2,20,768]{2,1,0:T(8,128)S(1)}, u32[]{:S(2)}, u32[]{:S(2)}) collective-permute-start(f32[2,20,768]{2,1,0:T(8,128)S(1)} %pad_maximum_fusion.3), channel_id=1, source_target_pairs={{0,2},{1,3},{2,0},{3,1},{4,6},{5,7},{6,4},{7,5},{8,10},{9,11},{10,... | collective-permute-start | bytes 368648 | tf_op jit(solution)/shard_map/ppermute | solution.py:20
  38.8 4.6 %shard_map.55 = bf16[3072,2048]{1,0:T(8,128)(2,1)S(1)} custom-call(bf16[6144,2048]{1,0:T(8,128)(2,1)} %src.1), custom_call_target="tpu_custom_call" | custom-call | bytes 25165824 | tf_op jit(solution)/shard_map/pallas_call | solution.py:90
  44.1 1.5 %collective-permute-start.12 = (bf16[20,768]{1,0:T(8,128)(2,1)S(1)}, bf16[20,768]{1,0:T(8,128)(2,1)S(1)}, u32[]{:S(2)}, u32[]{:S(2)}) collective-permute-start(bf16[20,768]{1,0:T(8,128)(2,1)S(1)} %fusion.30), channel_id=1, source_target_pairs={{0,2},{1,3},{2,0},{3,1},{4,6},{5,7},{6,4},{7,5},{8,10},{9,11},{10,... | collective-permute-start | bytes 92168 | tf_op jit(solution)/shard_map/ppermute | solution.py:20
  45.6 3.9 %collective-permute-done.7 = f32[2,20,768]{2,1,0:T(8,128)S(1)} collective-permute-done((f32[2,20,768]{2,1,0:T(8,128)S(1)}, f32[2,20,768]{2,1,0:T(8,128)S(1)}, u32[]{:S(2)}, u32[]{:S(2)}) %collective-permute-start.7) | collective-permute-done | bytes 122912 | tf_op jit(solution)/shard_map/ppermute | solution.py:20
  49.6 4.6 %shard_map.56 = bf16[3072,2048]{1,0:T(8,128)(2,1)S(1)} custom-call(bf16[6144,2048]{1,0:T(8,128)(2,1)} %src.1), custom_call_target="tpu_custom_call" | custom-call | bytes 25165824 | tf_op jit(solution)/shard_map/pallas_call | solution.py:90
  55.1 3.1 %collective-permute-done.8 = bf16[20,768]{1,0:T(8,128)(2,1)S(1)} collective-permute-done((bf16[20,768]{1,0:T(8,128)(2,1)S(1)}, bf16[20,768]{1,0:T(8,128)(2,1)S(1)}, u32[]{:S(2)}, u32[]{:S(2)}) %collective-permute-start.8) | collective-permute-done | bytes 30752 | tf_op jit(solution)/shard_map/ppermute | solution.py:20
  58.3 1.8 %fusion.20 = f32[20,2048]{1,0:T(8,128)S(1)} fusion(bf16[3072,2048]{1,0:T(8,128)(2,1)S(1)} %shard_map.56, bf16[20,1536]{1,0:T(8,128)(2,1)S(1)} %collective-permute-done.13, bf16[20,1536]{1,0:T(8,128)(2,1)S(1)} %maximum_select_fusion.5, pred[]{:T(512)S(6)} %eq.8), kind=kOutput, calls=%fused_computation.34 | convolution fusion | flops 252211200 | bytes 12869633 | tf_op jit(solution)/shard_map/dot_general | solution.py:148
  60.0 1.8 %convolution_add_fusion = f32[20,2048]{1,0:T(8,128)S(1)} fusion(f32[20,2048]{1,0:T(8,128)S(1)} %fusion.20, bf16[3072,2048]{1,0:T(8,128)(2,1)S(1)} %shard_map.55, bf16[20,1536]{1,0:T(8,128)(2,1)S(1)} %collective-permute-done.9, bf16[20,1536]{1,0:T(8,128)(2,1)S(1)} %maximum_select_fusion.4, pred[]{:T(512)S(6)} %eq.8), kind=kOutput, calls=%fused_computation.9 | convolution fusion | flops 252252160 | bytes 13033473 | tf_op jit(solution)/shard_map/dot_general | solution.py:148
  62.4 3.9 %collective-permute-start.14 = (f32[5,2048]{1,0:T(8,128)S(1)}, f32[5,2048]{1,0:T(8,128)S(1)}, u32[]{:S(2)}, u32[]{:S(2)}) collective-permute-start(f32[5,2048]{1,0:T(8,128)S(1)} %get-tuple-element.15), channel_id=1, source_target_pairs={{0,4},{4,0},{8,12},{12,8},{1,5},{5,1},{9,13},{13,9},{2,6},{6,2},{1... | collective-permute-start | bytes 122888 | tf_op jit(solution)/shard_map/ppermute | solution.py:61
  66.3 2.4 %collective-permute-done.16 = f32[5,2048]{1,0:T(8,128)S(1)} collective-permute-done((f32[5,2048]{1,0:T(8,128)S(1)}, f32[5,2048]{1,0:T(8,128)S(1)}, u32[]{:S(2)}, u32[]{:S(2)}) %collective-permute-start.16) | collective-permute-done | bytes 40992 | tf_op jit(solution)/shard_map/ppermute | solution.py:61
  68.7 1.5 %collective-permute-done.15 = f32[5,2048]{1,0:T(8,128)S(1)} collective-permute-done((f32[5,2048]{1,0:T(8,128)S(1)}, f32[5,2048]{1,0:T(8,128)S(1)}, u32[]{:S(2)}, u32[]{:S(2)}) %collective-permute-start.15) | collective-permute-done | bytes 40992 | tf_op jit(solution)/shard_map/ppermute | solution.py:61
  (53 shorter events, 6.5 us)
Async XLA Ops:
  0.0 22.1 %copy-start.1 = (f32[2048]{0:T(1024)S(1)}, f32[2048]{0:T(1024)}, u32[]{:S(2)}) copy-start(f32[2048]{0:T(1024)} %param.6) | copy-start | bytes 24580
  0.0 6.7 %collective-permute-start = (bf16[5,2048]{1,0:T(8,128)(2,1)}, bf16[5,2048]{1,0:T(8,128)(2,1)S(1)}, u32[]{:S(2)}, u32[]{:S(2)}) collective-permute-start(bf16[5,2048]{1,0:T(8,128)(2,1)} %param.5), channel_id=1, source_target_pairs={{0,4},{4,0},{8,12},{12,8},{1,5},{5,1},{9,13},{13,9},{2,6},{6,2},{1... | collective-permute-start | bytes 61448 | tf_op jit(solution)/shard_map/ppermute | solution.py:70
  3.0 5.6 %collective-permute-start.1 = (bf16[5,2048]{1,0:T(8,128)(2,1)}, bf16[5,2048]{1,0:T(8,128)(2,1)S(1)}, u32[]{:S(2)}, u32[]{:S(2)}) collective-permute-start(bf16[5,2048]{1,0:T(8,128)(2,1)} %param.5), channel_id=1, source_target_pairs={{0,8},{4,12},{8,0},{12,4},{1,9},{5,13},{9,1},{13,5},{2,10},{6,14},... | collective-permute-start | bytes 61448 | tf_op jit(solution)/shard_map/ppermute | solution.py:70
  5.6 5.9 %collective-permute-start.2 = (bf16[5,2048]{1,0:T(8,128)(2,1)}, bf16[5,2048]{1,0:T(8,128)(2,1)S(1)}, u32[]{:S(2)}, u32[]{:S(2)}) collective-permute-start(bf16[5,2048]{1,0:T(8,128)(2,1)} %param.5), channel_id=1, source_target_pairs={{0,12},{4,8},{8,4},{12,0},{1,13},{5,9},{9,5},{13,1},{2,14},{6,10},... | collective-permute-start | bytes 61448 | tf_op jit(solution)/shard_map/ppermute | solution.py:70
  11.9 3.0 %collective-permute-start.5 = (f32[20]{0:T(128)S(1)}, f32[20]{0:T(128)S(1)}, u32[]{:S(2)}, u32[]{:S(2)}) collective-permute-start(f32[20]{0:T(128)S(1)} %fusion.8), channel_id=1, source_target_pairs={{0,3},{1,2},{2,1},{3,0},{4,7},{5,6},{6,5},{7,4},{8,11},{9,10},{10,... | collective-permute-start | bytes 248 | tf_op jit(solution)/shard_map/ppermute | solution.py:77
  12.0 3.6 %collective-permute-start.4 = (f32[20]{0:T(128)S(1)}, f32[20]{0:T(128)S(1)}, u32[]{:S(2)}, u32[]{:S(2)}) collective-permute-start(f32[20]{0:T(128)S(1)} %fusion.8), channel_id=1, source_target_pairs={{0,2},{1,3},{2,0},{3,1},{4,6},{5,7},{6,4},{7,5},{8,10},{9,11},{10,... | collective-permute-start | bytes 248 | tf_op jit(solution)/shard_map/ppermute | solution.py:77
  13.6 2.1 %collective-permute-start.3 = (f32[20]{0:T(128)S(1)}, f32[20]{0:T(128)S(1)}, u32[]{:S(2)}, u32[]{:S(2)}) collective-permute-start(f32[20]{0:T(128)S(1)} %fusion.8), channel_id=1, source_target_pairs={{0,1},{1,0},{2,3},{3,2},{4,5},{5,4},{6,7},{7,6},{8,9},{9,8},{10,11... | collective-permute-start | bytes 248 | tf_op jit(solution)/shard_map/ppermute | solution.py:77
  16.3 15.5 %copy-start = (bf16[2048,6144]{1,0:T(8,128)(2,1)S(1)}, bf16[2048,6144]{1,0:T(8,128)(2,1)}, u32[]{:S(2)}) copy-start(bf16[2048,6144]{1,0:T(8,128)(2,1)} %param.7) | copy-start | bytes 75497472
  35.4 1.7 %collective-permute-start.10 = (f32[2,20,1536]{2,1,0:T(8,128)S(1)}, f32[2,20,1536]{2,1,0:T(8,128)S(1)}, u32[]{:S(2)}, u32[]{:S(2)}) collective-permute-start(f32[2,20,1536]{2,1,0:T(8,128)S(1)} %pad_maximum_fusion.1), channel_id=1, source_target_pairs={{0,1},{1,0},{2,3},{3,2},{4,5},{5,4},{6,7},{7,6},{8,9},{9,8},{10,11... | collective-permute-start | bytes 737288 | tf_op jit(solution)/shard_map/ppermute | solution.py:20
  35.9 2.8 %collective-permute-start.6 = (f32[2,20,1536]{2,1,0:T(8,128)S(1)}, f32[2,20,1536]{2,1,0:T(8,128)S(1)}, u32[]{:S(2)}, u32[]{:S(2)}) collective-permute-start(f32[2,20,1536]{2,1,0:T(8,128)S(1)} %pad_maximum_fusion), channel_id=1, source_target_pairs={{0,1},{1,0},{2,3},{3,2},{4,5},{5,4},{6,7},{7,6},{8,9},{9,8},{10,11... | collective-permute-start | bytes 737288 | tf_op jit(solution)/shard_map/ppermute | solution.py:20
  37.2 6.9 %collective-permute-start.11 = (f32[2,20,768]{2,1,0:T(8,128)S(1)}, f32[2,20,768]{2,1,0:T(8,128)S(1)}, u32[]{:S(2)}, u32[]{:S(2)}) collective-permute-start(f32[2,20,768]{2,1,0:T(8,128)S(1)} %pad_maximum_fusion.3), channel_id=1, source_target_pairs={{0,2},{1,3},{2,0},{3,1},{4,6},{5,7},{6,4},{7,5},{8,10},{9,11},{10,... | collective-permute-start | bytes 368648 | tf_op jit(solution)/shard_map/ppermute | solution.py:20
  43.4 6.1 %collective-permute-start.7 = (f32[2,20,768]{2,1,0:T(8,128)S(1)}, f32[2,20,768]{2,1,0:T(8,128)S(1)}, u32[]{:S(2)}, u32[]{:S(2)}) collective-permute-start(f32[2,20,768]{2,1,0:T(8,128)S(1)} %pad_maximum_fusion.2), channel_id=1, source_target_pairs={{0,2},{1,3},{2,0},{3,1},{4,6},{5,7},{6,4},{7,5},{8,10},{9,11},{10,... | collective-permute-start | bytes 368648 | tf_op jit(solution)/shard_map/ppermute | solution.py:20
  44.1 10.9 %collective-permute-start.12 = (bf16[20,768]{1,0:T(8,128)(2,1)S(1)}, bf16[20,768]{1,0:T(8,128)(2,1)S(1)}, u32[]{:S(2)}, u32[]{:S(2)}) collective-permute-start(bf16[20,768]{1,0:T(8,128)(2,1)S(1)} %fusion.30), channel_id=1, source_target_pairs={{0,2},{1,3},{2,0},{3,1},{4,6},{5,7},{6,4},{7,5},{8,10},{9,11},{10,... | collective-permute-start | bytes 92168 | tf_op jit(solution)/shard_map/ppermute | solution.py:20
  54.1 4.0 %collective-permute-start.8 = (bf16[20,768]{1,0:T(8,128)(2,1)S(1)}, bf16[20,768]{1,0:T(8,128)(2,1)S(1)}, u32[]{:S(2)}, u32[]{:S(2)}) collective-permute-start(bf16[20,768]{1,0:T(8,128)(2,1)S(1)} %fusion.34), channel_id=1, source_target_pairs={{0,2},{1,3},{2,0},{3,1},{4,6},{5,7},{6,4},{7,5},{8,10},{9,11},{10,... | collective-permute-start | bytes 92168 | tf_op jit(solution)/shard_map/ppermute | solution.py:20
  55.0 3.3 %collective-permute-start.13 = (bf16[20,1536]{1,0:T(8,128)(2,1)S(1)}, bf16[20,1536]{1,0:T(8,128)(2,1)S(1)}, u32[]{:S(2)}, u32[]{:S(2)}) collective-permute-start(bf16[20,1536]{1,0:T(8,128)(2,1)S(1)} %maximum_select_fusion.5), channel_id=1, source_target_pairs={{0,1},{1,0},{2,3},{3,2},{4,5},{5,4},{6,7},{7,6},{8,9},{9,8},{10,11... | collective-permute-start | bytes 184328 | tf_op jit(solution)/shard_map/ppermute | solution.py:20
  58.2 1.8 %collective-permute-start.9 = (bf16[20,1536]{1,0:T(8,128)(2,1)S(1)}, bf16[20,1536]{1,0:T(8,128)(2,1)S(1)}, u32[]{:S(2)}, u32[]{:S(2)}) collective-permute-start(bf16[20,1536]{1,0:T(8,128)(2,1)S(1)} %maximum_select_fusion.4), channel_id=1, source_target_pairs={{0,1},{1,0},{2,3},{3,2},{4,5},{5,4},{6,7},{7,6},{8,9},{9,8},{10,11... | collective-permute-start | bytes 184328 | tf_op jit(solution)/shard_map/ppermute | solution.py:20
  61.9 6.8 %collective-permute-start.16 = (f32[5,2048]{1,0:T(8,128)S(1)}, f32[5,2048]{1,0:T(8,128)S(1)}, u32[]{:S(2)}, u32[]{:S(2)}) collective-permute-start(f32[5,2048]{1,0:T(8,128)S(1)} %get-tuple-element.16), channel_id=1, source_target_pairs={{0,12},{4,8},{8,4},{12,0},{1,13},{5,9},{9,5},{13,1},{2,14},{6,10},... | collective-permute-start | bytes 122888 | tf_op jit(solution)/shard_map/ppermute | solution.py:61
  62.3 8.0 %collective-permute-start.15 = (f32[5,2048]{1,0:T(8,128)S(1)}, f32[5,2048]{1,0:T(8,128)S(1)}, u32[]{:S(2)}, u32[]{:S(2)}) collective-permute-start(f32[5,2048]{1,0:T(8,128)S(1)} %get-tuple-element.17), channel_id=1, source_target_pairs={{0,8},{4,12},{8,0},{12,4},{1,9},{5,13},{9,1},{13,5},{2,10},{6,14},... | collective-permute-start | bytes 122888 | tf_op jit(solution)/shard_map/ppermute | solution.py:61
  62.4 7.9 %collective-permute-start.14 = (f32[5,2048]{1,0:T(8,128)S(1)}, f32[5,2048]{1,0:T(8,128)S(1)}, u32[]{:S(2)}, u32[]{:S(2)}) collective-permute-start(f32[5,2048]{1,0:T(8,128)S(1)} %get-tuple-element.15), channel_id=1, source_target_pairs={{0,4},{4,0},{8,12},{12,8},{1,5},{5,1},{9,13},{13,9},{2,6},{6,2},{1... | collective-permute-start | bytes 122888 | tf_op jit(solution)/shard_map/ppermute | solution.py:61

commit v20 on v19

--- a/solution.py
+++ b/solution.py
@@ -122,31 +122,52 @@
     step = width // chunks
     gy_levels = list(range(ngy.bit_length() - 1))
     total = None
-    for c in range(chunks):
-        cols = slice(c * step, (c + 1) * step)
-        gate_part = jnp.dot(piece, w_gate[:, cols], preferred_element_type=jnp.float32)
-        up_part = jnp.dot(piece, w_up[:, cols], preferred_element_type=jnp.float32)
-        if pairwise(ngy):
-            first = xor_reduce_scatter([gate_part, up_part], "gy", ngy, 1, gy_levels[:1])
+    if pairwise(ngy) and ngy >= 4:
+        me = lax.axis_index("gy")
+        parts = []
+        for c in range(chunks):
+            cols = slice(c * step, (c + 1) * step)
+            parts.append(jnp.dot(piece, w_gate[:, cols], preferred_element_type=jnp.float32))
+            parts.append(jnp.dot(piece, w_up[:, cols], preferred_element_type=jnp.float32))
+        first = xor_reduce_scatter(parts, "gy", ngy, 1, gy_levels[:1])
+        source, _ = lax.optimization_barrier((w_down, first[0]))
+        staged = [rows_to_vmem(source, 0, step)]
+        sums = []
+        for c in range(chunks):
+            sums.append(xor_reduce_scatter(first[2 * c:2 * c + 2], "gy", ngy, 1, gy_levels[1:]))
             if c == 0:
-                source, _ = lax.optimization_barrier((w_down, first[0]))
-                staged = [rows_to_vmem(source, 0, step)]
-            gate, up = xor_reduce_scatter(first, "gy", ngy, 1, gy_levels[1:])
-            if c == chunks - 1:
                 for k in range(1, chunks):
-                    source, _ = lax.optimization_barrier((w_down, gate))
+                    source, _ = lax.optimization_barrier((w_down, sums[0][0]))
                     staged.append(rows_to_vmem(source, k * step, step))
-        else:
-            gate = lax.psum_scatter(gate_part, "gy", scatter_dimension=1, tiled=True)
-            up = lax.psum_scatter(up_part, "gy", scatter_dimension=1, tiled=True)
-        hidden = (jax.nn.silu(gate) * up).astype(jnp.bfloat16)
-        if pairwise(ngy):
-            hidden_all = xor_all_gather(hidden, "gy", ngy, 1, gy_levels[::-1])
-        else:
-            hidden_all = lax.all_gather(hidden, "gy", axis=1, tiled=True)
-        down = staged[c] if pairwise(ngy) else w_down[cols, :]
-        term = jnp.dot(hidden_all, down, preferred_element_type=jnp.float32)
-        total = term if total is None else total + term
+        halves = []
+        for gate, up in sums:
+            hidden = (jax.nn.silu(gate) * up).astype(jnp.bfloat16)
+            halves.append(xor_all_gather(hidden, "gy", ngy, 1, gy_levels[1:][::-1]))
+        others = exchange(jnp.stack(halves), "gy", ngy, gy_levels[0])
+        low = (me & 1) == 0
+        for c in range(chunks):
+            mine, other = halves[c], others[c]
+            hidden_all = jnp.where(low, jnp.concatenate([mine, other], axis=1),
+                                   jnp.concatenate([other, mine], axis=1))
+            term = jnp.dot(hidden_all, staged[c], preferred_element_type=jnp.float32)
+            total = term if total is None else total + term
+    else:
+        for c in range(chunks):
+            cols = slice(c * step, (c + 1) * step)
+            gate_part = jnp.dot(piece, w_gate[:, cols], preferred_element_type=jnp.float32)
+            up_part = jnp.dot(piece, w_up[:, cols], preferred_element_type=jnp.float32)
+            if pairwise(ngy):
+                gate, up = xor_reduce_scatter([gate_part, up_part], "gy", ngy, 1, gy_levels)
+            else:
+                gate = lax.psum_scatter(gate_part, "gy", scatter_dimension=1, tiled=True)
+                up = lax.psum_scatter(up_part, "gy", scatter_dimension=1, tiled=True)
+            hidden = (jax.nn.silu(gate) * up).astype(jnp.bfloat16)
+            if pairwise(ngy):
+                hidden_all = xor_all_gather(hidden, "gy", ngy, 1, gy_levels[::-1])
+            else:
+                hidden_all = lax.all_gather(hidden, "gy", axis=1, tiled=True)
+            term = jnp.dot(hidden_all, w_down[cols, :], preferred_element_type=jnp.float32)
+            total = term if total is None else total + term
     if pairwise(ngx):
         result = fanout_reduce_scatter(total, "gx", ngx, gx_levels[::-1])
     else:

time: 71.2 us -> 70.7 us (level)
  waiting for transfers between devices: 17.9 us -> 16.3 us
  local copies, waits for them, and re-layouts: 5.95 us -> 6.67 us
    ppermute x8 -> x6, waiting for transfers between devices: 7.91 us -> 6.67 us  [exchange(): return lax.ppermute(x, axis, [(a, a ^ 1 << s) for a in range(n)])]
    ppermute x8 -> x6, starting transfers between devices: 5.33 us -> 5.07 us  [exchange(): return lax.ppermute(x, axis, [(a, a ^ 1 << s) for a in range(n)])]
  transfers between devices with their start and end apart: 17 -> 15, of which waited for: 9 -> 10; matrix products, arithmetic and copies ran while one was open for 5% -> 3% of each run, Pallas kernels for 13% -> 13%
where the time goes in v20:
time: 70.7 us; the launch traced here: 70.4 us
  matrix products  19.2 us (27%)
  starting transfers between devices  17 us (24%)
  waiting for transfers between devices  16.3 us (23%)
  Pallas kernels  9.17 us (13%)
  local copies, waits for them, and re-layouts  6.67 us (9%)
  other arithmetic  1.68 us (2%)
    dot_general x2, matrix products, local(): jnp.dot(piece, w_up[:, cols], preferred_element_type=jnp.float32)  12 us
    pallas_call x2, Pallas kernels, rows_to_vmem(): pl.pallas_call(kernel, out_shape=jax.ShapeDtypeStruct((count, w.shape[1])...  9.17 us
    ppermute x6, waiting for transfers between devices, exchange(): return lax.ppermute(x, axis, [(a, a ^ 1 << s) for a in range(n)])  6.67 us
    ppermute x3, starting transfers between devices, fanout_all_gather(): lax.ppermute(x, axis, [(a, a ^ k) for a in range(n)])  5.62 us
    ppermute x6, starting transfers between devices, exchange(): return lax.ppermute(x, axis, [(a, a ^ 1 << s) for a in range(n)])  5.07 us
    ppermute x3, starting transfers between devices, fanout_reduce_scatter(): own = own + lax.ppermute(block, axis, [(a, a ^ k) for a in range(n)])  4.45 us
    ppermute x3, waiting for transfers between devices, fanout_all_gather(): lax.ppermute(x, axis, [(a, a ^ k) for a in range(n)])  4.26 us
    ppermute x3, waiting for transfers between devices, fanout_reduce_scatter(): own = own + lax.ppermute(block, axis, [(a, a ^ k) for a in range(n)])  3.66 us
  transfers between devices with their start and end apart: 15, of which 10 were waited for; matrix products, arithmetic and copies ran while one was open for 3% of the time, Pallas kernels for 13%

profile of v20, /device:TPU:0, one launch (start us, length us, event | category | flops | bytes accessed | tf_op | source)
XLA Modules:
  0.0 70.4 jit_solution(4312901667950255440)
XLA Ops:
  0.0 3.0 %collective-permute-start = (bf16[5,2048]{1,0:T(8,128)(2,1)}, bf16[5,2048]{1,0:T(8,128)(2,1)S(1)}, u32[]{:S(2)}, u32[]{:S(2)}) collective-permute-start(bf16[5,2048]{1,0:T(8,128)(2,1)} %param.5), channel_id=1, source_target_pairs={{0,4},{4,0},{8,12},{12,8},{1,5},{5,1},{9,13},{13,9},{2,6},{6,2},{1... | collective-permute-start | bytes 61448 | tf_op jit(solution)/shard_map/ppermute | solution.py:70
  3.0 2.6 %collective-permute-start.1 = (bf16[5,2048]{1,0:T(8,128)(2,1)}, bf16[5,2048]{1,0:T(8,128)(2,1)S(1)}, u32[]{:S(2)}, u32[]{:S(2)}) collective-permute-start(bf16[5,2048]{1,0:T(8,128)(2,1)} %param.5), channel_id=1, source_target_pairs={{0,8},{4,12},{8,0},{12,4},{1,9},{5,13},{9,1},{13,5},{2,10},{6,14},... | collective-permute-start | bytes 61448 | tf_op jit(solution)/shard_map/ppermute | solution.py:70
  5.7 1.0 %dynamic_update_slice.12 = bf16[20,2048]{1,0:T(8,128)(2,1)S(1)} dynamic-update-slice(bf16[20,2048]{1,0:T(8,128)(2,1)S(1)} %broadcast_in_dim.15, bf16[5,2048]{1,0:T(8,128)(2,1)} %param.5, s32[]{:T(128)S(6)} %select_n.106, s32[]{:T(128)} %constant.20.clone.1) | dynamic-update-slice | bytes 40964 | tf_op jit(solution)/shard_map/dynamic_update_slice | solution.py:71
  7.0 1.6 %collective-permute-done.1 = bf16[5,2048]{1,0:T(8,128)(2,1)S(1)} collective-permute-done((bf16[5,2048]{1,0:T(8,128)(2,1)}, bf16[5,2048]{1,0:T(8,128)(2,1)S(1)}, u32[]{:S(2)}, u32[]{:S(2)}) %collective-permute-start.1) | collective-permute-done | bytes 20512 | tf_op jit(solution)/shard_map/ppermute | solution.py:70
  8.9 2.6 %collective-permute-done.2 = bf16[5,2048]{1,0:T(8,128)(2,1)S(1)} collective-permute-done((bf16[5,2048]{1,0:T(8,128)(2,1)}, bf16[5,2048]{1,0:T(8,128)(2,1)S(1)}, u32[]{:S(2)}, u32[]{:S(2)}) %collective-permute-start.2) | collective-permute-done | bytes 20512 | tf_op jit(solution)/shard_map/ppermute | solution.py:70
  12.0 1.6 %collective-permute-start.4 = (f32[20]{0:T(128)S(1)}, f32[20]{0:T(128)S(1)}, u32[]{:S(2)}, u32[]{:S(2)}) collective-permute-start(f32[20]{0:T(128)S(1)} %fusion.8), channel_id=1, source_target_pairs={{0,2},{1,3},{2,0},{3,1},{4,6},{5,7},{6,4},{7,5},{8,10},{9,11},{10,... | collective-permute-start | bytes 248 | tf_op jit(solution)/shard_map/ppermute | solution.py:77
  13.9 1.1 %collective-permute-done.5 = f32[20]{0:T(128)S(1)} collective-permute-done((f32[20]{0:T(128)S(1)}, f32[20]{0:T(128)S(1)}, u32[]{:S(2)}, u32[]{:S(2)}) %collective-permute-start.5) | collective-permute-done | bytes 112 | tf_op jit(solution)/shard_map/ppermute | solution.py:77
  16.3 5.8 %fusion = f32[20,3072]{1,0:T(8,128)S(1)} fusion(bf16[2048,6144]{1,0:T(8,128)(2,1)} %param.8, bf16[20,2048]{1,0:T(8,128)(2,1)S(1)} %dynamic_update_slice.15, f32[2048]{0:T(1024)} %param.6, f32[20]{0:T(128)S(1)} %add_rsqrt_fusion), kind=kOutput, calls=%fused_computation.1 | convolution fusion | flops 251822080 | bytes 12918864 | tf_op jit(solution)/shard_map/dot_general | solution.py:131
  22.1 6.3 %fusion.4 = f32[20,3072]{1,0:T(8,128)S(1)} fusion(bf16[2048,6144]{1,0:T(8,128)(2,1)} %param.8, bf16[20,2048]{1,0:T(8,128)(2,1)S(1)} %dynamic_update_slice.15, f32[2048]{0:T(1024)S(1)} %copy-done.1, f32[20]{0:T(128)S(1)} %add_rsqrt_fusion), kind=kOutput, calls=%fused_computation.5 | convolution fusion | flops 251822080 | bytes 12918864 | tf_op jit(solution)/shard_map/dot_general | solution.py:131
  28.3 3.4 %copy-done = bf16[2048,6144]{1,0:T(8,128)(2,1)S(1)} copy-done((bf16[2048,6144]{1,0:T(8,128)(2,1)S(1)}, bf16[2048,6144]{1,0:T(8,128)(2,1)}, u32[]{:S(2)}) %copy-start) | copy-done | bytes 25165848
  31.8 1.8 %fusion.2 = f32[20,3072]{1,0:T(8,128)S(1)} fusion(bf16[2048,6144]{1,0:T(8,128)(2,1)S(1)} %copy-done, bf16[20,2048]{1,0:T(8,128)(2,1)S(1)} %dynamic_update_slice.15, f32[2048]{0:T(1024)S(1)} %copy-done.1, f32[20]{0:T(128)S(1)} %add_rsqrt_fusion), kind=kOutput, calls=%fused_computation.3 | convolution fusion | flops 251822080 | bytes 12935680 | tf_op jit(solution)/shard_map/dot_general | solution.py:130
  33.6 1.8 %fusion.6 = f32[20,3072]{1,0:T(8,128)S(1)} fusion(bf16[2048,6144]{1,0:T(8,128)(2,1)S(1)} %copy-done, bf16[20,2048]{1,0:T(8,128)(2,1)S(1)} %dynamic_update_slice.15, f32[2048]{0:T(1024)S(1)} %copy-done.1, f32[20]{0:T(128)S(1)} %add_rsqrt_fusion), kind=kOutput, calls=%fused_computation.7 | convolution fusion | flops 251822080 | bytes 12935680 | tf_op jit(solution)/shard_map/dot_general | solution.py:130
  36.8 1.5 %collective-permute-done.6 = f32[4,20,1536]{2,0,1:T(4,128)S(1)} collective-permute-done((f32[4,20,1536]{2,0,1:T(4,128)S(1)}, f32[4,20,1536]{2,0,1:T(4,128)S(1)}, u32[]{:S(2)}, u32[]{:S(2)}) %collective-permute-start.6) | collective-permute-done | bytes 491552 | tf_op jit(solution)/shard_map/ppermute | solution.py:20
  38.8 1.6 %collective-permute-start.9 = (f32[2,20,768]{2,1,0:T(8,128)S(1)}, f32[2,20,768]{2,1,0:T(8,128)S(1)}, u32[]{:S(2)}, u32[]{:S(2)}) collective-permute-start(f32[2,20,768]{2,1,0:T(8,128)S(1)} %pad_maximum_fusion.2), channel_id=1, source_target_pairs={{0,2},{1,3},{2,0},{3,1},{4,6},{5,7},{6,4},{7,5},{8,10},{9,11},{10,... | collective-permute-start | bytes 368648 | tf_op jit(solution)/shard_map/ppermute | solution.py:20
  40.4 4.6 %shard_map.55 = bf16[3072,2048]{1,0:T(8,128)(2,1)S(1)} custom-call(bf16[6144,2048]{1,0:T(8,128)(2,1)} %src.1), custom_call_target="tpu_custom_call" | custom-call | bytes 25165824 | tf_op jit(solution)/shard_map/pallas_call | solution.py:90
  45.7 1.5 %collective-permute-start.10 = (bf16[20,768]{1,0:T(8,128)(2,1)S(1)}, bf16[20,768]{1,0:T(8,128)(2,1)S(1)}, u32[]{:S(2)}, u32[]{:S(2)}) collective-permute-start(bf16[20,768]{1,0:T(8,128)(2,1)S(1)} %fusion.30), channel_id=1, source_target_pairs={{0,2},{1,3},{2,0},{3,1},{4,6},{5,7},{6,4},{7,5},{8,10},{9,11},{10,... | collective-permute-start | bytes 92168 | tf_op jit(solution)/shard_map/ppermute | solution.py:20
  47.2 3.9 %collective-permute-done.7 = f32[2,20,768]{2,1,0:T(8,128)S(1)} collective-permute-done((f32[2,20,768]{2,1,0:T(8,128)S(1)}, f32[2,20,768]{2,1,0:T(8,128)S(1)}, u32[]{:S(2)}, u32[]{:S(2)}) %collective-permute-start.7) | collective-permute-done | bytes 122912 | tf_op jit(solution)/shard_map/ppermute | solution.py:20
  52.0 4.6 %shard_map.56 = bf16[3072,2048]{1,0:T(8,128)(2,1)S(1)} custom-call(bf16[6144,2048]{1,0:T(8,128)(2,1)} %src.1), custom_call_target="tpu_custom_call" | custom-call | bytes 25165824 | tf_op jit(solution)/shard_map/pallas_call | solution.py:90
  56.8 1.3 %collective-permute-done.11 = bf16[2,20,1536]{2,1,0:T(8,128)(2,1)S(1)} collective-permute-done((bf16[2,20,1536]{2,1,0:T(8,128)(2,1)S(1)}, bf16[2,20,1536]{2,1,0:T(8,128)(2,1)S(1)}, u32[]{:S(2)}, u32[]{:S(2)}) %collective-permute-start.11) | collective-permute-done | bytes 122912 | tf_op jit(solution)/shard_map/ppermute | solution.py:20
  58.1 1.8 %fusion.11 = f32[20,2048]{1,0:T(8,128)S(1)} fusion(bf16[3072,2048]{1,0:T(8,128)(2,1)S(1)} %shard_map.55, bf16[20,1536]{1,0:T(8,128)(2,1)S(1)} %get-tuple-element.19, bf16[20,1536]{1,0:T(8,128)(2,1)S(1)} %maximum_select_fusion.4, pred[]{:T(512)S(6)} %eq.7), kind=kOutput, calls=%fused_computation.20 | convolution fusion | flops 252211200 | bytes 12869633 | tf_op jit(solution)/shard_map/dot_general | solution.py:152
  59.9 1.8 %convolution_add_fusion = f32[20,2048]{1,0:T(8,128)S(1)} fusion(f32[20,2048]{1,0:T(8,128)S(1)} %fusion.11, bf16[3072,2048]{1,0:T(8,128)(2,1)S(1)} %shard_map.56, bf16[20,1536]{1,0:T(8,128)(2,1)S(1)} %get-tuple-element.18, bf16[20,1536]{1,0:T(8,128)(2,1)S(1)} %maximum_select_fusion.7, pred[]{:T(512)S(6)} %eq.7), kind=kOutput, calls=%fused_computation.9 | convolution fusion | flops 252252160 | bytes 13033473 | tf_op jit(solution)/shard_map/dot_general | solution.py:152
  62.2 3.9 %collective-permute-start.12 = (f32[5,2048]{1,0:T(8,128)S(1)}, f32[5,2048]{1,0:T(8,128)S(1)}, u32[]{:S(2)}, u32[]{:S(2)}) collective-permute-start(f32[5,2048]{1,0:T(8,128)S(1)} %get-tuple-element.15), channel_id=1, source_target_pairs={{0,4},{4,0},{8,12},{12,8},{1,5},{5,1},{9,13},{13,9},{2,6},{6,2},{1... | collective-permute-start | bytes 122888 | tf_op jit(solution)/shard_map/ppermute | solution.py:61
  66.1 2.4 %collective-permute-done.14 = f32[5,2048]{1,0:T(8,128)S(1)} collective-permute-done((f32[5,2048]{1,0:T(8,128)S(1)}, f32[5,2048]{1,0:T(8,128)S(1)}, u32[]{:S(2)}, u32[]{:S(2)}) %collective-permute-start.14) | collective-permute-done | bytes 40992 | tf_op jit(solution)/shard_map/ppermute | solution.py:61
  68.5 1.1 %collective-permute-done.13 = f32[5,2048]{1,0:T(8,128)S(1)} collective-permute-done((f32[5,2048]{1,0:T(8,128)S(1)}, f32[5,2048]{1,0:T(8,128)S(1)}, u32[]{:S(2)}, u32[]{:S(2)}) %collective-permute-start.13) | collective-permute-done | bytes 40992 | tf_op jit(solution)/shard_map/ppermute | solution.py:61
  (59 shorter events, 7.6 us)
Async XLA Ops:
  0.0 22.1 %copy-start.1 = (f32[2048]{0:T(1024)S(1)}, f32[2048]{0:T(1024)}, u32[]{:S(2)}) copy-start(f32[2048]{0:T(1024)} %param.6) | copy-start | bytes 24580
  0.0 6.7 %collective-permute-start = (bf16[5,2048]{1,0:T(8,128)(2,1)}, bf16[5,2048]{1,0:T(8,128)(2,1)S(1)}, u32[]{:S(2)}, u32[]{:S(2)}) collective-permute-start(bf16[5,2048]{1,0:T(8,128)(2,1)} %param.5), channel_id=1, source_target_pairs={{0,4},{4,0},{8,12},{12,8},{1,5},{5,1},{9,13},{13,9},{2,6},{6,2},{1... | collective-permute-start | bytes 61448 | tf_op jit(solution)/shard_map/ppermute | solution.py:70
  3.0 5.6 %collective-permute-start.1 = (bf16[5,2048]{1,0:T(8,128)(2,1)}, bf16[5,2048]{1,0:T(8,128)(2,1)S(1)}, u32[]{:S(2)}, u32[]{:S(2)}) collective-permute-start(bf16[5,2048]{1,0:T(8,128)(2,1)} %param.5), channel_id=1, source_target_pairs={{0,8},{4,12},{8,0},{12,4},{1,9},{5,13},{9,1},{13,5},{2,10},{6,14},... | collective-permute-start | bytes 61448 | tf_op jit(solution)/shard_map/ppermute | solution.py:70
  5.6 5.9 %collective-permute-start.2 = (bf16[5,2048]{1,0:T(8,128)(2,1)}, bf16[5,2048]{1,0:T(8,128)(2,1)S(1)}, u32[]{:S(2)}, u32[]{:S(2)}) collective-permute-start(bf16[5,2048]{1,0:T(8,128)(2,1)} %param.5), channel_id=1, source_target_pairs={{0,12},{4,8},{8,4},{12,0},{1,13},{5,9},{9,5},{13,1},{2,14},{6,10},... | collective-permute-start | bytes 61448 | tf_op jit(solution)/shard_map/ppermute | solution.py:70
  11.9 3.0 %collective-permute-start.5 = (f32[20]{0:T(128)S(1)}, f32[20]{0:T(128)S(1)}, u32[]{:S(2)}, u32[]{:S(2)}) collective-permute-start(f32[20]{0:T(128)S(1)} %fusion.8), channel_id=1, source_target_pairs={{0,3},{1,2},{2,1},{3,0},{4,7},{5,6},{6,5},{7,4},{8,11},{9,10},{10,... | collective-permute-start | bytes 248 | tf_op jit(solution)/shard_map/ppermute | solution.py:77
  12.0 3.6 %collective-permute-start.4 = (f32[20]{0:T(128)S(1)}, f32[20]{0:T(128)S(1)}, u32[]{:S(2)}, u32[]{:S(2)}) collective-permute-start(f32[20]{0:T(128)S(1)} %fusion.8), channel_id=1, source_target_pairs={{0,2},{1,3},{2,0},{3,1},{4,6},{5,7},{6,4},{7,5},{8,10},{9,11},{10,... | collective-permute-start | bytes 248 | tf_op jit(solution)/shard_map/ppermute | solution.py:77
  13.6 2.1 %collective-permute-start.3 = (f32[20]{0:T(128)S(1)}, f32[20]{0:T(128)S(1)}, u32[]{:S(2)}, u32[]{:S(2)}) collective-permute-start(f32[20]{0:T(128)S(1)} %fusion.8), channel_id=1, source_target_pairs={{0,1},{1,0},{2,3},{3,2},{4,5},{5,4},{6,7},{7,6},{8,9},{9,8},{10,11... | collective-permute-start | bytes 248 | tf_op jit(solution)/shard_map/ppermute | solution.py:77
  16.3 15.5 %copy-start = (bf16[2048,6144]{1,0:T(8,128)(2,1)S(1)}, bf16[2048,6144]{1,0:T(8,128)(2,1)}, u32[]{:S(2)}) copy-start(bf16[2048,6144]{1,0:T(8,128)(2,1)} %param.7) | copy-start | bytes 75497472
  36.3 1.9 %collective-permute-start.6 = (f32[4,20,1536]{2,0,1:T(4,128)S(1)}, f32[4,20,1536]{2,0,1:T(4,128)S(1)}, u32[]{:S(2)}, u32[]{:S(2)}) collective-permute-start(f32[4,20,1536]{2,0,1:T(4,128)S(1)} %pad_maximum_fusion), channel_id=1, source_target_pairs={{0,1},{1,0},{2,3},{3,2},{4,5},{5,4},{6,7},{7,6},{8,9},{9,8},{10,11... | collective-permute-start | bytes 1474568 | tf_op jit(solution)/shard_map/ppermute | solution.py:20
  38.8 6.9 %collective-permute-start.9 = (f32[2,20,768]{2,1,0:T(8,128)S(1)}, f32[2,20,768]{2,1,0:T(8,128)S(1)}, u32[]{:S(2)}, u32[]{:S(2)}) collective-permute-start(f32[2,20,768]{2,1,0:T(8,128)S(1)} %pad_maximum_fusion.2), channel_id=1, source_target_pairs={{0,2},{1,3},{2,0},{3,1},{4,6},{5,7},{6,4},{7,5},{8,10},{9,11},{10,... | collective-permute-start | bytes 368648 | tf_op jit(solution)/shard_map/ppermute | solution.py:20
  45.0 6.1 %collective-permute-start.7 = (f32[2,20,768]{2,1,0:T(8,128)S(1)}, f32[2,20,768]{2,1,0:T(8,128)S(1)}, u32[]{:S(2)}, u32[]{:S(2)}) collective-permute-start(f32[2,20,768]{2,1,0:T(8,128)S(1)} %pad_maximum_fusion.1), channel_id=1, source_target_pairs={{0,2},{1,3},{2,0},{3,1},{4,6},{5,7},{6,4},{7,5},{8,10},{9,11},{10,... | collective-permute-start | bytes 368648 | tf_op jit(solution)/shard_map/ppermute | solution.py:20
  45.7 10.9 %collective-permute-start.10 = (bf16[20,768]{1,0:T(8,128)(2,1)S(1)}, bf16[20,768]{1,0:T(8,128)(2,1)S(1)}, u32[]{:S(2)}, u32[]{:S(2)}) collective-permute-start(bf16[20,768]{1,0:T(8,128)(2,1)S(1)} %fusion.30), channel_id=1, source_target_pairs={{0,2},{1,3},{2,0},{3,1},{4,6},{5,7},{6,4},{7,5},{8,10},{9,11},{10,... | collective-permute-start | bytes 92168 | tf_op jit(solution)/shard_map/ppermute | solution.py:20
  51.1 5.5 %collective-permute-start.8 = (bf16[20,768]{1,0:T(8,128)(2,1)S(1)}, bf16[20,768]{1,0:T(8,128)(2,1)S(1)}, u32[]{:S(2)}, u32[]{:S(2)}) collective-permute-start(bf16[20,768]{1,0:T(8,128)(2,1)S(1)} %fusion.34), channel_id=1, source_target_pairs={{0,2},{1,3},{2,0},{3,1},{4,6},{5,7},{6,4},{7,5},{8,10},{9,11},{10,... | collective-permute-start | bytes 92168 | tf_op jit(solution)/shard_map/ppermute | solution.py:20
  56.7 1.4 %collective-permute-start.11 = (bf16[2,20,1536]{2,1,0:T(8,128)(2,1)S(1)}, bf16[2,20,1536]{2,1,0:T(8,128)(2,1)S(1)}, u32[]{:S(2)}, u32[]{:S(2)}) collective-permute-start(bf16[2,20,1536]{2,1,0:T(8,128)(2,1)S(1)} %pad_maximum_fusion.3), channel_id=1, source_target_pairs={{0,1},{1,0},{2,3},{3,2},{4,5},{5,4},{6,7},{7,6},{8,9},{9,8},{10,11... | collective-permute-start | bytes 368648 | tf_op jit(solution)/shard_map/ppermute | solution.py:20
  61.7 6.8 %collective-permute-start.14 = (f32[5,2048]{1,0:T(8,128)S(1)}, f32[5,2048]{1,0:T(8,128)S(1)}, u32[]{:S(2)}, u32[]{:S(2)}) collective-permute-start(f32[5,2048]{1,0:T(8,128)S(1)} %get-tuple-element.16), channel_id=1, source_target_pairs={{0,12},{4,8},{8,4},{12,0},{1,13},{5,9},{9,5},{13,1},{2,14},{6,10},... | collective-permute-start | bytes 122888 | tf_op jit(solution)/shard_map/ppermute | solution.py:61
  62.1 7.6 %collective-permute-start.13 = (f32[5,2048]{1,0:T(8,128)S(1)}, f32[5,2048]{1,0:T(8,128)S(1)}, u32[]{:S(2)}, u32[]{:S(2)}) collective-permute-start(f32[5,2048]{1,0:T(8,128)S(1)} %get-tuple-element.17), channel_id=1, source_target_pairs={{0,8},{4,12},{8,0},{12,4},{1,9},{5,13},{9,1},{13,5},{2,10},{6,14},... | collective-permute-start | bytes 122888 | tf_op jit(solution)/shard_map/ppermute | solution.py:61
  62.2 7.6 %collective-permute-start.12 = (f32[5,2048]{1,0:T(8,128)S(1)}, f32[5,2048]{1,0:T(8,128)S(1)}, u32[]{:S(2)}, u32[]{:S(2)}) collective-permute-start(f32[5,2048]{1,0:T(8,128)S(1)} %get-tuple-element.15), channel_id=1, source_target_pairs={{0,4},{4,0},{8,12},{12,8},{1,5},{5,1},{9,13},{13,9},{2,6},{6,2},{1... | collective-permute-start | bytes 122888 | tf_op jit(solution)/shard_map/ppermute | solution.py:61

commit v21 on v12

--- a/solution.py
+++ b/solution.py
@@ -9,7 +9,7 @@
 epsilon = 1e-06
 
 EXCHANGE_MAX = 8
-CHUNKS = 2
+CHUNKS = 3
 
 
 def pairwise(n):

time: 67.7 us -> 76.8 us (1.13)
  matrix products: 19.2 us -> 26.4 us
  local copies, waits for them, and re-layouts: 6 us -> 2.61 us
  waiting for transfers between devices: 14.3 us -> 16.9 us
  starting transfers between devices: 17.4 us -> 18.8 us
  Pallas kernels: 9.17 us -> 10.2 us
    dot_general x2 -> x3, matrix products: 3.61 us -> 7.91 us  [local(): jnp.dot(piece, w_gate[:, cols], preferred_element_type=jnp.float32)]
    unnamed x4, local copies, waits for them, and re-layouts: 3.42 us -> 0.01 us
    dot_general x2 -> x3, matrix products: 12 us -> 14.8 us  [local(): up_part = jnp.dot(piece, w_up[:, cols], preferred_element_type=jnp.float32)]
    ppermute x8 -> x12, waiting for transfers between devices: 2.52 us -> 4.87 us  [exchange(): return lax.ppermute(x, axis, [(a, a ^ 1 << s) for a in range(n)])]
    ppermute x8 -> x12, starting transfers between devices: 6.29 us -> 7.72 us  [exchange(): return lax.ppermute(x, axis, [(a, a ^ 1 << s) for a in range(n)])]
    pallas_call x2 -> x3, Pallas kernels: 9.17 us -> 10.2 us  [rows_to_vmem(): pl.pallas_call(kernel, out_shape=jax.ShapeDtypeStruct((count, w.shape[1])...]
    dot_general x2 -> x3, matrix products: 3.53 us -> 3.64 us  [local(): term = jnp.dot(hidden_all, down, preferred_element_type=jnp.float32)]
  transfers between devices with their start and end apart: 17 -> 21, of which waited for: 9 -> 10; matrix products, arithmetic and copies ran while one was open for 5% -> 6% of each run, Pallas kernels for 14% -> 13%
where the time goes in v21:
time: 76.8 us; the launch traced here: 76.5 us
  matrix products  26.4 us (34%)
  starting transfers between devices  18.8 us (24%)
  waiting for transfers between devices  16.9 us (22%)
  Pallas kernels  10.2 us (13%)
  local copies, waits for them, and re-layouts  2.61 us (3%)
  other arithmetic  1.21 us (2%)
    dot_general x3, matrix products, local(): up_part = jnp.dot(piece, w_up[:, cols], preferred_element_type=jnp.float32)  14.8 us
    pallas_call x3, Pallas kernels, rows_to_vmem(): pl.pallas_call(kernel, out_shape=jax.ShapeDtypeStruct((count, w.shape[1])...  10.2 us
    dot_general x3, matrix products, local(): jnp.dot(piece, w_gate[:, cols], preferred_element_type=jnp.float32)  7.91 us
    ppermute x12, starting transfers between devices, exchange(): return lax.ppermute(x, axis, [(a, a ^ 1 << s) for a in range(n)])  7.72 us
    ppermute x3, waiting for transfers between devices, fanout_reduce_scatter(): own = own + lax.ppermute(block, axis, [(a, a ^ k) for a in range(n)])  6.45 us
    ppermute x3, starting transfers between devices, fanout_all_gather(): lax.ppermute(x, axis, [(a, a ^ k) for a in range(n)])  5.62 us
    ppermute x12, waiting for transfers between devices, exchange(): return lax.ppermute(x, axis, [(a, a ^ 1 << s) for a in range(n)])  4.87 us
    ppermute x3, waiting for transfers between devices, fanout_all_gather(): lax.ppermute(x, axis, [(a, a ^ k) for a in range(n)])  3.86 us
  transfers between devices with their start and end apart: 21, of which 10 were waited for; matrix products, arithmetic and copies ran while one was open for 6% of the time, Pallas kernels for 13%

profile of v21, /device:TPU:0, one launch (start us, length us, event | category | flops | bytes accessed | tf_op | source)
XLA Modules:
  0.0 76.5 jit_solution(17669782872789128798)
XLA Ops:
  0.0 3.0 %collective-permute-start = (bf16[5,2048]{1,0:T(8,128)(2,1)}, bf16[5,2048]{1,0:T(8,128)(2,1)S(1)}, u32[]{:S(2)}, u32[]{:S(2)}) collective-permute-start(bf16[5,2048]{1,0:T(8,128)(2,1)} %param.5), channel_id=1, source_target_pairs={{0,4},{4,0},{8,12},{12,8},{1,5},{5,1},{9,13},{13,9},{2,6},{6,2},{1... | collective-permute-start | bytes 61448 | tf_op jit(solution)/shard_map/ppermute | solution.py:70
  3.0 2.5 %collective-permute-start.2 = (bf16[5,2048]{1,0:T(8,128)(2,1)}, bf16[5,2048]{1,0:T(8,128)(2,1)S(1)}, u32[]{:S(2)}, u32[]{:S(2)}) collective-permute-start(bf16[5,2048]{1,0:T(8,128)(2,1)} %param.5), channel_id=1, source_target_pairs={{0,12},{4,8},{8,4},{12,0},{1,13},{5,9},{9,5},{13,1},{2,14},{6,10},... | collective-permute-start | bytes 61448 | tf_op jit(solution)/shard_map/ppermute | solution.py:70
  7.0 3.9 %collective-permute-done.1 = bf16[5,2048]{1,0:T(8,128)(2,1)S(1)} collective-permute-done((bf16[5,2048]{1,0:T(8,128)(2,1)}, bf16[5,2048]{1,0:T(8,128)(2,1)S(1)}, u32[]{:S(2)}, u32[]{:S(2)}) %collective-permute-start.1) | collective-permute-done | bytes 20512 | tf_op jit(solution)/shard_map/ppermute | solution.py:70
  11.7 1.6 %collective-permute-start.4 = (f32[20]{0:T(128)S(1)}, f32[20]{0:T(128)S(1)}, u32[]{:S(2)}, u32[]{:S(2)}) collective-permute-start(f32[20]{0:T(128)S(1)} %fusion.13), channel_id=1, source_target_pairs={{0,2},{1,3},{2,0},{3,1},{4,6},{5,7},{6,4},{7,5},{8,10},{9,11},{10,... | collective-permute-start | bytes 248 | tf_op jit(solution)/shard_map/ppermute | solution.py:77
  16.0 4.8 %fusion.8 = f32[20,2048]{1,0:T(8,128)S(1)} fusion(bf16[2048,6144]{1,0:T(8,128)(2,1)} %param.8, bf16[20,2048]{1,0:T(8,128)(2,1)S(1)} %dynamic_update_slice.15, f32[2048]{0:T(1024)} %param.6, f32[20]{0:T(128)S(1)} %add_rsqrt_fusion), kind=kOutput, calls=%fused_computation.9 | convolution fusion | flops 167936000 | bytes 8642640 | tf_op jit(solution)/shard_map/dot_general | solution.py:128
  20.8 5.4 %fusion.4 = f32[20,2048]{1,0:T(8,128)S(1)} fusion(bf16[2048,6144]{1,0:T(8,128)(2,1)} %param.8, bf16[20,2048]{1,0:T(8,128)(2,1)S(1)} %dynamic_update_slice.15, f32[2048]{0:T(1024)S(1)} %copy-done.1, f32[20]{0:T(128)S(1)} %add_rsqrt_fusion), kind=kOutput, calls=%fused_computation.5 | convolution fusion | flops 167936000 | bytes 8642640 | tf_op jit(solution)/shard_map/dot_general | solution.py:128
  26.2 5.4 %fusion.6 = f32[20,2048]{1,0:T(8,128)S(1)} fusion(bf16[2048,6144]{1,0:T(8,128)(2,1)} %param.7, bf16[20,2048]{1,0:T(8,128)(2,1)S(1)} %dynamic_update_slice.15, f32[2048]{0:T(1024)S(1)} %copy-done.1, f32[20]{0:T(128)S(1)} %add_rsqrt_fusion), kind=kOutput, calls=%fused_computation.7 | convolution fusion | flops 167936000 | bytes 8642640 | tf_op jit(solution)/shard_map/dot_general | solution.py:127
  31.6 1.3 %fusion.2 = f32[20,2048]{1,0:T(8,128)S(1)} fusion(bf16[2048,6144]{1,0:T(8,128)(2,1)S(1)} %copy-done, bf16[20,2048]{1,0:T(8,128)(2,1)S(1)} %dynamic_update_slice.15, f32[2048]{0:T(1024)S(1)} %copy-done.1, f32[20]{0:T(128)S(1)} %add_rsqrt_fusion), kind=kOutput, calls=%fused_computation.3 | convolution fusion | flops 167936000 | bytes 8659456 | tf_op jit(solution)/shard_map/dot_general | solution.py:127
  32.8 4.6 %fusion = f32[20,2048]{1,0:T(8,128)S(1)} fusion(bf16[2048,6144]{1,0:T(8,128)(2,1)} %param.8, bf16[20,2048]{1,0:T(8,128)(2,1)S(1)} %dynamic_update_slice.15, f32[2048]{0:T(1024)S(1)} %copy-done.1, f32[20]{0:T(128)S(1)} %add_rsqrt_fusion), kind=kOutput, calls=%fused_computation.1 | convolution fusion | flops 167936000 | bytes 8642640 | tf_op jit(solution)/shard_map/dot_general | solution.py:128
  37.5 1.3 %fusion.10 = f32[20,2048]{1,0:T(8,128)S(1)} fusion(bf16[2048,6144]{1,0:T(8,128)(2,1)S(1)} %copy-done, bf16[20,2048]{1,0:T(8,128)(2,1)S(1)} %dynamic_update_slice.15, f32[2048]{0:T(1024)S(1)} %copy-done.1, f32[20]{0:T(128)S(1)} %add_rsqrt_fusion), kind=kOutput, calls=%fused_computation.11 | convolution fusion | flops 167936000 | bytes 8659456 | tf_op jit(solution)/shard_map/dot_general | solution.py:127
  40.4 1.5 %collective-permute-start.11 = (f32[2,20,512]{2,1,0:T(8,128)S(1)}, f32[2,20,512]{2,1,0:T(8,128)S(1)}, u32[]{:S(2)}, u32[]{:S(2)}) collective-permute-start(f32[2,20,512]{2,1,0:T(8,128)S(1)} %pad_maximum_fusion.4), channel_id=1, source_target_pairs={{0,2},{1,3},{2,0},{3,1},{4,6},{5,7},{6,4},{7,5},{8,10},{9,11},{10,... | collective-permute-start | bytes 245768 | tf_op jit(solution)/shard_map/ppermute | solution.py:20
  42.7 1.5 %collective-permute-start.7 = (f32[2,20,512]{2,1,0:T(8,128)S(1)}, f32[2,20,512]{2,1,0:T(8,128)S(1)}, u32[]{:S(2)}, u32[]{:S(2)}) collective-permute-start(f32[2,20,512]{2,1,0:T(8,128)S(1)} %pad_maximum_fusion.3), channel_id=1, source_target_pairs={{0,2},{1,3},{2,0},{3,1},{4,6},{5,7},{6,4},{7,5},{8,10},{9,11},{10,... | collective-permute-start | bytes 245768 | tf_op jit(solution)/shard_map/ppermute | solution.py:20
  44.3 3.4 %shard_map.55 = bf16[2048,2048]{1,0:T(8,128)(2,1)S(1)} custom-call(bf16[6144,2048]{1,0:T(8,128)(2,1)} %src.2), custom_call_target="tpu_custom_call" | custom-call | bytes 16777216 | tf_op jit(solution)/shard_map/pallas_call | solution.py:90
  48.3 1.4 %collective-permute-done.7 = f32[2,20,512]{2,1,0:T(8,128)S(1)} collective-permute-done((f32[2,20,512]{2,1,0:T(8,128)S(1)}, f32[2,20,512]{2,1,0:T(8,128)S(1)}, u32[]{:S(2)}, u32[]{:S(2)}) %collective-permute-start.7) | collective-permute-done | bytes 81952 | tf_op jit(solution)/shard_map/ppermute | solution.py:20
  49.8 3.4 %shard_map.57 = bf16[2048,2048]{1,0:T(8,128)(2,1)S(1)} custom-call(bf16[6144,2048]{1,0:T(8,128)(2,1)} %src.2), custom_call_target="tpu_custom_call" | custom-call | bytes 16777216 | tf_op jit(solution)/shard_map/pallas_call | solution.py:90
  53.2 3.4 %shard_map.56 = bf16[2048,2048]{1,0:T(8,128)(2,1)S(1)} custom-call(bf16[6144,2048]{1,0:T(8,128)(2,1)} %src.2), custom_call_target="tpu_custom_call" | custom-call | bytes 16777216 | tf_op jit(solution)/shard_map/pallas_call | solution.py:90
  56.6 1.6 %collective-permute-start.16 = (bf16[20,512]{1,0:T(8,128)(2,1)S(1)}, bf16[20,512]{1,0:T(8,128)(2,1)S(1)}, u32[]{:S(2)}, u32[]{:S(2)}) collective-permute-start(bf16[20,512]{1,0:T(8,128)(2,1)S(1)} %fusion.44), channel_id=1, source_target_pairs={{0,2},{1,3},{2,0},{3,1},{4,6},{5,7},{6,4},{7,5},{8,10},{9,11},{10,... | collective-permute-start | bytes 61448 | tf_op jit(solution)/shard_map/ppermute | solution.py:20
  58.8 1.7 %collective-permute-done.16 = bf16[20,512]{1,0:T(8,128)(2,1)S(1)} collective-permute-done((bf16[20,512]{1,0:T(8,128)(2,1)S(1)}, bf16[20,512]{1,0:T(8,128)(2,1)S(1)}, u32[]{:S(2)}, u32[]{:S(2)}) %collective-permute-start.16) | collective-permute-done | bytes 20512 | tf_op jit(solution)/shard_map/ppermute | solution.py:20
  60.6 1.4 %collective-permute-done.8 = bf16[20,512]{1,0:T(8,128)(2,1)S(1)} collective-permute-done((bf16[20,512]{1,0:T(8,128)(2,1)S(1)}, bf16[20,512]{1,0:T(8,128)(2,1)S(1)}, u32[]{:S(2)}, u32[]{:S(2)}) %collective-permute-start.8) | collective-permute-done | bytes 20512 | tf_op jit(solution)/shard_map/ppermute | solution.py:20
  63.3 1.2 %fusion.27 = f32[20,2048]{1,0:T(8,128)S(1)} fusion(bf16[2048,2048]{1,0:T(8,128)(2,1)S(1)} %shard_map.56, bf16[20,1024]{1,0:T(8,128)(2,1)S(1)} %collective-permute-done.13, bf16[20,1024]{1,0:T(8,128)(2,1)S(1)} %maximum_select_fusion.7, pred[]{:T(512)S(6)} %eq.4), kind=kOutput, calls=%fused_computation.44 | convolution fusion | flops 168140800 | bytes 8634369 | tf_op jit(solution)/shard_map/dot_general | solution.py:148
  64.6 1.2 %fusion.12 = f32[20,2048]{1,0:T(8,128)S(1)} fusion(f32[20,2048]{1,0:T(8,128)S(1)} %fusion.33, f32[20,2048]{1,0:T(8,128)S(1)} %fusion.27, bf16[2048,2048]{1,0:T(8,128)(2,1)S(1)} %shard_map.55, bf16[20,1024]{1,0:T(8,128)(2,1)S(1)} %collective-permute-done.9, bf16[20,1024]{1,0:T(8,128)(2,1)S(1)} %maximum_select_fusion.6, pred[]{:T(512)S(6)} %eq.4), kind=kOutput, calls=%fused_computation.14 | convolution fusion | flops 168222720 | bytes 8962049 | tf_op jit(solution)/shard_map/dot_general | solution.py:148
  67.4 2.0 %collective-permute-start.19 = (f32[5,2048]{1,0:T(8,128)S(1)}, f32[5,2048]{1,0:T(8,128)S(1)}, u32[]{:S(2)}, u32[]{:S(2)}) collective-permute-start(f32[5,2048]{1,0:T(8,128)S(1)} %get-tuple-element.13), channel_id=1, source_target_pairs={{0,8},{4,12},{8,0},{12,4},{1,9},{5,13},{9,1},{13,5},{2,10},{6,14},... | collective-permute-start | bytes 122888 | tf_op jit(solution)/shard_map/ppermute | solution.py:61
  70.4 2.7 %collective-permute-done.20 = f32[5,2048]{1,0:T(8,128)S(1)} collective-permute-done((f32[5,2048]{1,0:T(8,128)S(1)}, f32[5,2048]{1,0:T(8,128)S(1)}, u32[]{:S(2)}, u32[]{:S(2)}) %collective-permute-start.20) | collective-permute-done | bytes 40992 | tf_op jit(solution)/shard_map/ppermute | solution.py:61
  73.1 2.7 %collective-permute-done.19 = f32[5,2048]{1,0:T(8,128)S(1)} collective-permute-done((f32[5,2048]{1,0:T(8,128)S(1)}, f32[5,2048]{1,0:T(8,128)S(1)}, u32[]{:S(2)}, u32[]{:S(2)}) %collective-permute-start.19) | collective-permute-done | bytes 40992 | tf_op jit(solution)/shard_map/ppermute | solution.py:61
  (73 shorter events, 13.2 us)
Async XLA Ops:
  0.0 20.8 %copy-start.1 = (f32[2048]{0:T(1024)S(1)}, f32[2048]{0:T(1024)}, u32[]{:S(2)}) copy-start(f32[2048]{0:T(1024)} %param.6) | copy-start | bytes 24580
  0.0 6.7 %collective-permute-start = (bf16[5,2048]{1,0:T(8,128)(2,1)}, bf16[5,2048]{1,0:T(8,128)(2,1)S(1)}, u32[]{:S(2)}, u32[]{:S(2)}) collective-permute-start(bf16[5,2048]{1,0:T(8,128)(2,1)} %param.5), channel_id=1, source_target_pairs={{0,4},{4,0},{8,12},{12,8},{1,5},{5,1},{9,13},{13,9},{2,6},{6,2},{1... | collective-permute-start | bytes 61448 | tf_op jit(solution)/shard_map/ppermute | solution.py:70
  3.0 8.1 %collective-permute-start.2 = (bf16[5,2048]{1,0:T(8,128)(2,1)}, bf16[5,2048]{1,0:T(8,128)(2,1)S(1)}, u32[]{:S(2)}, u32[]{:S(2)}) collective-permute-start(bf16[5,2048]{1,0:T(8,128)(2,1)} %param.5), channel_id=1, source_target_pairs={{0,12},{4,8},{8,4},{12,0},{1,13},{5,9},{9,5},{13,1},{2,14},{6,10},... | collective-permute-start | bytes 61448 | tf_op jit(solution)/shard_map/ppermute | solution.py:70
  5.5 5.4 %collective-permute-start.1 = (bf16[5,2048]{1,0:T(8,128)(2,1)}, bf16[5,2048]{1,0:T(8,128)(2,1)S(1)}, u32[]{:S(2)}, u32[]{:S(2)}) collective-permute-start(bf16[5,2048]{1,0:T(8,128)(2,1)} %param.5), channel_id=1, source_target_pairs={{0,8},{4,12},{8,0},{12,4},{1,9},{5,13},{9,1},{13,5},{2,10},{6,14},... | collective-permute-start | bytes 61448 | tf_op jit(solution)/shard_map/ppermute | solution.py:70
  11.6 3.0 %collective-permute-start.5 = (f32[20]{0:T(128)S(1)}, f32[20]{0:T(128)S(1)}, u32[]{:S(2)}, u32[]{:S(2)}) collective-permute-start(f32[20]{0:T(128)S(1)} %fusion.13), channel_id=1, source_target_pairs={{0,3},{1,2},{2,1},{3,0},{4,7},{5,6},{6,5},{7,4},{8,11},{9,10},{10,... | collective-permute-start | bytes 248 | tf_op jit(solution)/shard_map/ppermute | solution.py:77
  11.7 3.6 %collective-permute-start.4 = (f32[20]{0:T(128)S(1)}, f32[20]{0:T(128)S(1)}, u32[]{:S(2)}, u32[]{:S(2)}) collective-permute-start(f32[20]{0:T(128)S(1)} %fusion.13), channel_id=1, source_target_pairs={{0,2},{1,3},{2,0},{3,1},{4,6},{5,7},{6,4},{7,5},{8,10},{9,11},{10,... | collective-permute-start | bytes 248 | tf_op jit(solution)/shard_map/ppermute | solution.py:77
  13.2 2.1 %collective-permute-start.3 = (f32[20]{0:T(128)S(1)}, f32[20]{0:T(128)S(1)}, u32[]{:S(2)}, u32[]{:S(2)}) collective-permute-start(f32[20]{0:T(128)S(1)} %fusion.13), channel_id=1, source_target_pairs={{0,1},{1,0},{2,3},{3,2},{4,5},{5,4},{6,7},{7,6},{8,9},{9,8},{10,11... | collective-permute-start | bytes 248 | tf_op jit(solution)/shard_map/ppermute | solution.py:77
  16.0 15.6 %copy-start = (bf16[2048,6144]{1,0:T(8,128)(2,1)S(1)}, bf16[2048,6144]{1,0:T(8,128)(2,1)}, u32[]{:S(2)}) copy-start(bf16[2048,6144]{1,0:T(8,128)(2,1)} %param.7) | copy-start | bytes 75497472
  38.8 1.5 %collective-permute-start.10 = (f32[2,20,1024]{2,1,0:T(8,128)S(1)}, f32[2,20,1024]{2,1,0:T(8,128)S(1)}, u32[]{:S(2)}, u32[]{:S(2)}) collective-permute-start(f32[2,20,1024]{2,1,0:T(8,128)S(1)} %pad_maximum_fusion.1), channel_id=1, source_target_pairs={{0,1},{1,0},{2,3},{3,2},{4,5},{5,4},{6,7},{7,6},{8,9},{9,8},{10,11... | collective-permute-start | bytes 491528 | tf_op jit(solution)/shard_map/ppermute | solution.py:20
  39.3 2.7 %collective-permute-start.14 = (f32[2,20,1024]{2,1,0:T(8,128)S(1)}, f32[2,20,1024]{2,1,0:T(8,128)S(1)}, u32[]{:S(2)}, u32[]{:S(2)}) collective-permute-start(f32[2,20,1024]{2,1,0:T(8,128)S(1)} %pad_maximum_fusion.2), channel_id=1, source_target_pairs={{0,1},{1,0},{2,3},{3,2},{4,5},{5,4},{6,7},{7,6},{8,9},{9,8},{10,11... | collective-permute-start | bytes 491528 | tf_op jit(solution)/shard_map/ppermute | solution.py:20
  39.5 3.1 %collective-permute-start.6 = (f32[2,20,1024]{2,1,0:T(8,128)S(1)}, f32[2,20,1024]{2,1,0:T(8,128)S(1)}, u32[]{:S(2)}, u32[]{:S(2)}) collective-permute-start(f32[2,20,1024]{2,1,0:T(8,128)S(1)} %pad_maximum_fusion), channel_id=1, source_target_pairs={{0,1},{1,0},{2,3},{3,2},{4,5},{5,4},{6,7},{7,6},{8,9},{9,8},{10,11... | collective-permute-start | bytes 491528 | tf_op jit(solution)/shard_map/ppermute | solution.py:20
  40.4 7.3 %collective-permute-start.11 = (f32[2,20,512]{2,1,0:T(8,128)S(1)}, f32[2,20,512]{2,1,0:T(8,128)S(1)}, u32[]{:S(2)}, u32[]{:S(2)}) collective-permute-start(f32[2,20,512]{2,1,0:T(8,128)S(1)} %pad_maximum_fusion.4), channel_id=1, source_target_pairs={{0,2},{1,3},{2,0},{3,1},{4,6},{5,7},{6,4},{7,5},{8,10},{9,11},{10,... | collective-permute-start | bytes 245768 | tf_op jit(solution)/shard_map/ppermute | solution.py:20
  42.0 7.7 %collective-permute-start.15 = (f32[2,20,512]{2,1,0:T(8,128)S(1)}, f32[2,20,512]{2,1,0:T(8,128)S(1)}, u32[]{:S(2)}, u32[]{:S(2)}) collective-permute-start(f32[2,20,512]{2,1,0:T(8,128)S(1)} %pad_maximum_fusion.5), channel_id=1, source_target_pairs={{0,2},{1,3},{2,0},{3,1},{4,6},{5,7},{6,4},{7,5},{8,10},{9,11},{10,... | collective-permute-start | bytes 245768 | tf_op jit(solution)/shard_map/ppermute | solution.py:20
  42.7 7.0 %collective-permute-start.7 = (f32[2,20,512]{2,1,0:T(8,128)S(1)}, f32[2,20,512]{2,1,0:T(8,128)S(1)}, u32[]{:S(2)}, u32[]{:S(2)}) collective-permute-start(f32[2,20,512]{2,1,0:T(8,128)S(1)} %pad_maximum_fusion.3), channel_id=1, source_target_pairs={{0,2},{1,3},{2,0},{3,1},{4,6},{5,7},{6,4},{7,5},{8,10},{9,11},{10,... | collective-permute-start | bytes 245768 | tf_op jit(solution)/shard_map/ppermute | solution.py:20
  47.7 11.0 %collective-permute-start.12 = (bf16[20,512]{1,0:T(8,128)(2,1)S(1)}, bf16[20,512]{1,0:T(8,128)(2,1)S(1)}, u32[]{:S(2)}, u32[]{:S(2)}) collective-permute-start(bf16[20,512]{1,0:T(8,128)(2,1)S(1)} %fusion.48), channel_id=1, source_target_pairs={{0,2},{1,3},{2,0},{3,1},{4,6},{5,7},{6,4},{7,5},{8,10},{9,11},{10,... | collective-permute-start | bytes 61448 | tf_op jit(solution)/shard_map/ppermute | solution.py:20
  56.6 3.9 %collective-permute-start.16 = (bf16[20,512]{1,0:T(8,128)(2,1)S(1)}, bf16[20,512]{1,0:T(8,128)(2,1)S(1)}, u32[]{:S(2)}, u32[]{:S(2)}) collective-permute-start(bf16[20,512]{1,0:T(8,128)(2,1)S(1)} %fusion.44), channel_id=1, source_target_pairs={{0,2},{1,3},{2,0},{3,1},{4,6},{5,7},{6,4},{7,5},{8,10},{9,11},{10,... | collective-permute-start | bytes 61448 | tf_op jit(solution)/shard_map/ppermute | solution.py:20
  58.2 3.8 %collective-permute-start.8 = (bf16[20,512]{1,0:T(8,128)(2,1)S(1)}, bf16[20,512]{1,0:T(8,128)(2,1)S(1)}, u32[]{:S(2)}, u32[]{:S(2)}) collective-permute-start(bf16[20,512]{1,0:T(8,128)(2,1)S(1)} %fusion.52), channel_id=1, source_target_pairs={{0,2},{1,3},{2,0},{3,1},{4,6},{5,7},{6,4},{7,5},{8,10},{9,11},{10,... | collective-permute-start | bytes 61448 | tf_op jit(solution)/shard_map/ppermute | solution.py:20
  58.7 4.6 %collective-permute-start.13 = (bf16[20,1024]{1,0:T(8,128)(2,1)S(1)}, bf16[20,1024]{1,0:T(8,128)(2,1)S(1)}, u32[]{:S(2)}, u32[]{:S(2)}) collective-permute-start(bf16[20,1024]{1,0:T(8,128)(2,1)S(1)} %maximum_select_fusion.7), channel_id=1, source_target_pairs={{0,1},{1,0},{2,3},{3,2},{4,5},{5,4},{6,7},{7,6},{8,9},{9,8},{10,11... | collective-permute-start | bytes 122888 | tf_op jit(solution)/shard_map/ppermute | solution.py:20
  60.5 1.6 %collective-permute-start.17 = (bf16[20,1024]{1,0:T(8,128)(2,1)S(1)}, bf16[20,1024]{1,0:T(8,128)(2,1)S(1)}, u32[]{:S(2)}, u32[]{:S(2)}) collective-permute-start(bf16[20,1024]{1,0:T(8,128)(2,1)S(1)} %maximum_select_fusion.8), channel_id=1, source_target_pairs={{0,1},{1,0},{2,3},{3,2},{4,5},{5,4},{6,7},{7,6},{8,9},{9,8},{10,11... | collective-permute-start | bytes 122888 | tf_op jit(solution)/shard_map/ppermute | solution.py:20
  62.0 2.5 %collective-permute-start.9 = (bf16[20,1024]{1,0:T(8,128)(2,1)S(1)}, bf16[20,1024]{1,0:T(8,128)(2,1)S(1)}, u32[]{:S(2)}, u32[]{:S(2)}) collective-permute-start(bf16[20,1024]{1,0:T(8,128)(2,1)S(1)} %maximum_select_fusion.6), channel_id=1, source_target_pairs={{0,1},{1,0},{2,3},{3,2},{4,5},{5,4},{6,7},{7,6},{8,9},{9,8},{10,11... | collective-permute-start | bytes 122888 | tf_op jit(solution)/shard_map/ppermute | solution.py:20
  65.8 4.6 %collective-permute-start.18 = (f32[5,2048]{1,0:T(8,128)S(1)}, f32[5,2048]{1,0:T(8,128)S(1)}, u32[]{:S(2)}, u32[]{:S(2)}) collective-permute-start(f32[5,2048]{1,0:T(8,128)S(1)} %get-tuple-element.11), channel_id=1, source_target_pairs={{0,4},{4,0},{8,12},{12,8},{1,5},{5,1},{9,13},{13,9},{2,6},{6,2},{1... | collective-permute-start | bytes 122888 | tf_op jit(solution)/shard_map/ppermute | solution.py:61
  66.3 6.8 %collective-permute-start.20 = (f32[5,2048]{1,0:T(8,128)S(1)}, f32[5,2048]{1,0:T(8,128)S(1)}, u32[]{:S(2)}, u32[]{:S(2)}) collective-permute-start(f32[5,2048]{1,0:T(8,128)S(1)} %get-tuple-element.12), channel_id=1, source_target_pairs={{0,12},{4,8},{8,4},{12,0},{1,13},{5,9},{9,5},{13,1},{2,14},{6,10},... | collective-permute-start | bytes 122888 | tf_op jit(solution)/shard_map/ppermute | solution.py:61
  67.4 8.5 %collective-permute-start.19 = (f32[5,2048]{1,0:T(8,128)S(1)}, f32[5,2048]{1,0:T(8,128)S(1)}, u32[]{:S(2)}, u32[]{:S(2)}) collective-permute-start(f32[5,2048]{1,0:T(8,128)S(1)} %get-tuple-element.13), channel_id=1, source_target_pairs={{0,8},{4,12},{8,0},{12,4},{1,9},{5,13},{9,1},{13,5},{2,10},{6,14},... | collective-permute-start | bytes 122888 | tf_op jit(solution)/shard_map/ppermute | solution.py:61

commit v22 on v12

--- a/solution.py
+++ b/solution.py
@@ -110,7 +110,7 @@
     values = raw.astype(jnp.float32)
     local_sq = jnp.sum(values * values, axis=1)
     if pairwise(ngy):
-        total_sq = fanout_all_reduce(local_sq, "gy", ngy)
+        total_sq = xor_all_reduce(local_sq, "gy", ngy)
     else:
         total_sq = lax.psum(local_sq, "gy")
     inverse = lax.rsqrt(total_sq / features + epsilon)

time: 67.7 us -> 68.4 us (1.010)
  waiting for transfers between devices: 14.3 us -> 15.8 us
    ppermute x8 -> x10, waiting for transfers between devices: 2.52 us -> 5.43 us  [exchange(): return lax.ppermute(x, axis, [(a, a ^ 1 << s) for a in range(n)])]
    ppermute x3 -> x0, starting transfers between devices: 1.91 us -> none  [fanout_all_reduce(): lax.ppermute(x, axis, [(a, a ^ k) for a in range(n)])]
    ppermute x8 -> x10, starting transfers between devices: 6.29 us -> 8.07 us  [exchange(): return lax.ppermute(x, axis, [(a, a ^ 1 << s) for a in range(n)])]
    ppermute x3 -> x0, waiting for transfers between devices: 1.76 us -> none  [fanout_all_reduce(): lax.ppermute(x, axis, [(a, a ^ k) for a in range(n)])]
  transfers between devices with their start and end apart: 17 -> 16, of which waited for: 9 -> 10; matrix products, arithmetic and copies ran while one was open for 5% -> 5% of each run, Pallas kernels for 14% -> 13%
where the time goes in v22:
time: 68.4 us; the launch traced here: 68.1 us
  matrix products  19.2 us (28%)
  starting transfers between devices  17.2 us (25%)
  waiting for transfers between devices  15.8 us (23%)
  Pallas kernels  9.17 us (13%)
  local copies, waits for them, and re-layouts  5.44 us (8%)
  other arithmetic  1.06 us (2%)
    dot_general x2, matrix products, local(): up_part = jnp.dot(piece, w_up[:, cols], preferred_element_type=jnp.float32)  12 us
    pallas_call x2, Pallas kernels, rows_to_vmem(): pl.pallas_call(kernel, out_shape=jax.ShapeDtypeStruct((count, w.shape[1])...  9.17 us
    ppermute x10, starting transfers between devices, exchange(): return lax.ppermute(x, axis, [(a, a ^ 1 << s) for a in range(n)])  8.07 us
    ppermute x3, waiting for transfers between devices, fanout_reduce_scatter(): own = own + lax.ppermute(block, axis, [(a, a ^ k) for a in range(n)])  6.06 us
    ppermute x3, starting transfers between devices, fanout_all_gather(): lax.ppermute(x, axis, [(a, a ^ k) for a in range(n)])  5.62 us
    ppermute x10, waiting for transfers between devices, exchange(): return lax.ppermute(x, axis, [(a, a ^ 1 << s) for a in range(n)])  5.43 us
    ppermute x3, waiting for transfers between devices, fanout_all_gather(): lax.ppermute(x, axis, [(a, a ^ k) for a in range(n)])  4.29 us
    dot_general x2, matrix products, local(): jnp.dot(piece, w_gate[:, cols], preferred_element_type=jnp.float32)  3.66 us
  transfers between devices with their start and end apart: 16, of which 10 were waited for; matrix products, arithmetic and copies ran while one was open for 5% of the time, Pallas kernels for 13%

profile of v22, /device:TPU:0, one launch (start us, length us, event | category | flops | bytes accessed | tf_op | source)
XLA Modules:
  0.0 68.1 jit_solution(9199236223662886835)
XLA Ops:
  0.0 3.0 %collective-permute-start = (bf16[5,2048]{1,0:T(8,128)(2,1)}, bf16[5,2048]{1,0:T(8,128)(2,1)S(1)}, u32[]{:S(2)}, u32[]{:S(2)}) collective-permute-start(bf16[5,2048]{1,0:T(8,128)(2,1)} %param.5), channel_id=1, source_target_pairs={{0,4},{4,0},{8,12},{12,8},{1,5},{5,1},{9,13},{13,9},{2,6},{6,2},{1... | collective-permute-start | bytes 61448 | tf_op jit(solution)/shard_map/ppermute | solution.py:70
  3.0 2.6 %collective-permute-start.1 = (bf16[5,2048]{1,0:T(8,128)(2,1)}, bf16[5,2048]{1,0:T(8,128)(2,1)S(1)}, u32[]{:S(2)}, u32[]{:S(2)}) collective-permute-start(bf16[5,2048]{1,0:T(8,128)(2,1)} %param.5), channel_id=1, source_target_pairs={{0,8},{4,12},{8,0},{12,4},{1,9},{5,13},{9,1},{13,5},{2,10},{6,14},... | collective-permute-start | bytes 61448 | tf_op jit(solution)/shard_map/ppermute | solution.py:70
  5.6 1.0 %dynamic_update_slice.12 = bf16[20,2048]{1,0:T(8,128)(2,1)S(1)} dynamic-update-slice(bf16[20,2048]{1,0:T(8,128)(2,1)S(1)} %broadcast_in_dim.2, bf16[5,2048]{1,0:T(8,128)(2,1)} %param.5, s32[]{:T(128)S(6)} %select_n.66, s32[]{:T(128)} %constant.7.clone.1) | dynamic-update-slice | bytes 40964 | tf_op jit(solution)/shard_map/dynamic_update_slice | solution.py:71
  7.0 1.6 %collective-permute-done.1 = bf16[5,2048]{1,0:T(8,128)(2,1)S(1)} collective-permute-done((bf16[5,2048]{1,0:T(8,128)(2,1)}, bf16[5,2048]{1,0:T(8,128)(2,1)S(1)}, u32[]{:S(2)}, u32[]{:S(2)}) %collective-permute-start.1) | collective-permute-done | bytes 20512 | tf_op jit(solution)/shard_map/ppermute | solution.py:70
  8.9 2.6 %collective-permute-done.2 = bf16[5,2048]{1,0:T(8,128)(2,1)S(1)} collective-permute-done((bf16[5,2048]{1,0:T(8,128)(2,1)}, bf16[5,2048]{1,0:T(8,128)(2,1)S(1)}, u32[]{:S(2)}, u32[]{:S(2)}) %collective-permute-start.2) | collective-permute-done | bytes 20512 | tf_op jit(solution)/shard_map/ppermute | solution.py:70
  12.0 1.1 %collective-permute-done.3 = f32[20]{0:T(128)S(1)} collective-permute-done((f32[20]{0:T(128)S(1)}, f32[20]{0:T(128)S(1)}, u32[]{:S(2)}, u32[]{:S(2)}) %collective-permute-start.3) | collective-permute-done | bytes 112 | tf_op jit(solution)/shard_map/ppermute | solution.py:20
  13.1 1.5 %collective-permute-start.4 = (f32[20]{0:T(128)S(1)}, f32[20]{0:T(128)S(1)}, u32[]{:S(2)}, u32[]{:S(2)}) collective-permute-start(f32[20]{0:T(128)S(1)} %add.116), channel_id=1, source_target_pairs={{0,2},{1,3},{2,0},{3,1},{4,6},{5,7},{6,4},{7,5},{8,10},{9,11},{10,... | collective-permute-start | bytes 248 | tf_op jit(solution)/shard_map/ppermute | solution.py:20
  14.6 2.0 %collective-permute-done.4 = f32[20]{0:T(128)S(1)} collective-permute-done((f32[20]{0:T(128)S(1)}, f32[20]{0:T(128)S(1)}, u32[]{:S(2)}, u32[]{:S(2)}) %collective-permute-start.4) | collective-permute-done | bytes 112 | tf_op jit(solution)/shard_map/ppermute | solution.py:20
  16.7 5.8 %fusion.4 = f32[20,3072]{1,0:T(8,128)S(1)} fusion(bf16[2048,6144]{1,0:T(8,128)(2,1)} %param.8, bf16[20,2048]{1,0:T(8,128)(2,1)S(1)} %dynamic_update_slice.15, f32[2048]{0:T(1024)} %param.6, f32[20]{0:T(128)S(1)} %add_rsqrt_fusion), kind=kOutput, calls=%fused_computation.4 | convolution fusion | flops 251822080 | bytes 12918864 | tf_op jit(solution)/shard_map/dot_general | solution.py:128
  22.4 6.3 %fusion = f32[20,3072]{1,0:T(8,128)S(1)} fusion(bf16[2048,6144]{1,0:T(8,128)(2,1)} %param.8, bf16[20,2048]{1,0:T(8,128)(2,1)S(1)} %dynamic_update_slice.15, f32[2048]{0:T(1024)S(1)} %copy-done.1, f32[20]{0:T(128)S(1)} %add_rsqrt_fusion), kind=kOutput, calls=%fused_computation | convolution fusion | flops 251822080 | bytes 12918864 | tf_op jit(solution)/shard_map/dot_general | solution.py:128
  28.7 3.4 %copy-done = bf16[2048,6144]{1,0:T(8,128)(2,1)S(1)} copy-done((bf16[2048,6144]{1,0:T(8,128)(2,1)S(1)}, bf16[2048,6144]{1,0:T(8,128)(2,1)}, u32[]{:S(2)}) %copy-start) | copy-done | bytes 25165848
  32.1 1.8 %fusion.2 = f32[20,3072]{1,0:T(8,128)S(1)} fusion(bf16[2048,6144]{1,0:T(8,128)(2,1)S(1)} %copy-done, bf16[20,2048]{1,0:T(8,128)(2,1)S(1)} %dynamic_update_slice.15, f32[2048]{0:T(1024)S(1)} %copy-done.1, f32[20]{0:T(128)S(1)} %add_rsqrt_fusion), kind=kOutput, calls=%fused_computation.2 | convolution fusion | flops 251822080 | bytes 12935680 | tf_op jit(solution)/shard_map/dot_general | solution.py:127
  34.0 1.8 %fusion.6 = f32[20,3072]{1,0:T(8,128)S(1)} fusion(bf16[2048,6144]{1,0:T(8,128)(2,1)S(1)} %copy-done, bf16[20,2048]{1,0:T(8,128)(2,1)S(1)} %dynamic_update_slice.15, f32[2048]{0:T(1024)S(1)} %copy-done.1, f32[20]{0:T(128)S(1)} %add_rsqrt_fusion), kind=kOutput, calls=%fused_computation.6 | convolution fusion | flops 251822080 | bytes 12935680 | tf_op jit(solution)/shard_map/dot_general | solution.py:127
  36.5 1.0 %collective-permute-done.9 = f32[2,20,1536]{2,1,0:T(8,128)S(1)} collective-permute-done((f32[2,20,1536]{2,1,0:T(8,128)S(1)}, f32[2,20,1536]{2,1,0:T(8,128)S(1)}, u32[]{:S(2)}, u32[]{:S(2)}) %collective-permute-start.9) | collective-permute-done | bytes 245792 | tf_op jit(solution)/shard_map/ppermute | solution.py:20
  37.6 1.6 %collective-permute-start.10 = (f32[2,20,768]{2,1,0:T(8,128)S(1)}, f32[2,20,768]{2,1,0:T(8,128)S(1)}, u32[]{:S(2)}, u32[]{:S(2)}) collective-permute-start(f32[2,20,768]{2,1,0:T(8,128)S(1)} %pad_maximum_fusion.3), channel_id=1, source_target_pairs={{0,2},{1,3},{2,0},{3,1},{4,6},{5,7},{6,4},{7,5},{8,10},{9,11},{10,... | collective-permute-start | bytes 368648 | tf_op jit(solution)/shard_map/ppermute | solution.py:20
  39.9 4.6 %shard_map.55 = bf16[3072,2048]{1,0:T(8,128)(2,1)S(1)} custom-call(bf16[6144,2048]{1,0:T(8,128)(2,1)} %src.1), custom_call_target="tpu_custom_call" | custom-call | bytes 25165824 | tf_op jit(solution)/shard_map/pallas_call | solution.py:90
  44.5 1.6 %collective-permute-start.11 = (bf16[20,768]{1,0:T(8,128)(2,1)S(1)}, bf16[20,768]{1,0:T(8,128)(2,1)S(1)}, u32[]{:S(2)}, u32[]{:S(2)}) collective-permute-start(bf16[20,768]{1,0:T(8,128)(2,1)S(1)} %fusion.30), channel_id=1, source_target_pairs={{0,2},{1,3},{2,0},{3,1},{4,6},{5,7},{6,4},{7,5},{8,10},{9,11},{10,... | collective-permute-start | bytes 92168 | tf_op jit(solution)/shard_map/ppermute | solution.py:20
  46.8 1.6 %collective-permute-start.7 = (bf16[20,768]{1,0:T(8,128)(2,1)S(1)}, bf16[20,768]{1,0:T(8,128)(2,1)S(1)}, u32[]{:S(2)}, u32[]{:S(2)}) collective-permute-start(bf16[20,768]{1,0:T(8,128)(2,1)S(1)} %fusion.34), channel_id=1, source_target_pairs={{0,2},{1,3},{2,0},{3,1},{4,6},{5,7},{6,4},{7,5},{8,10},{9,11},{10,... | collective-permute-start | bytes 92168 | tf_op jit(solution)/shard_map/ppermute | solution.py:20
  48.3 4.6 %shard_map.56 = bf16[3072,2048]{1,0:T(8,128)(2,1)S(1)} custom-call(bf16[6144,2048]{1,0:T(8,128)(2,1)} %src.1), custom_call_target="tpu_custom_call" | custom-call | bytes 25165824 | tf_op jit(solution)/shard_map/pallas_call | solution.py:90
  54.3 1.7 %fusion.20 = f32[20,2048]{1,0:T(8,128)S(1)} fusion(bf16[3072,2048]{1,0:T(8,128)(2,1)S(1)} %shard_map.56, bf16[20,1536]{1,0:T(8,128)(2,1)S(1)} %collective-permute-done.12, bf16[20,1536]{1,0:T(8,128)(2,1)S(1)} %maximum_select_fusion.5, pred[]{:T(512)S(6)} %eq.8), kind=kOutput, calls=%fused_computation.33 | convolution fusion | flops 252211200 | bytes 12869633 | tf_op jit(solution)/shard_map/dot_general | solution.py:148
  56.0 1.8 %convolution_add_fusion = f32[20,2048]{1,0:T(8,128)S(1)} fusion(f32[20,2048]{1,0:T(8,128)S(1)} %fusion.20, bf16[3072,2048]{1,0:T(8,128)(2,1)S(1)} %shard_map.55, bf16[20,1536]{1,0:T(8,128)(2,1)S(1)} %collective-permute-done.8, bf16[20,1536]{1,0:T(8,128)(2,1)S(1)} %maximum_select_fusion.4, pred[]{:T(512)S(6)} %eq.8), kind=kOutput, calls=%fused_computation.8 | convolution fusion | flops 252252160 | bytes 13033473 | tf_op jit(solution)/shard_map/dot_general | solution.py:148
  58.8 2.6 %collective-permute-start.14 = (f32[5,2048]{1,0:T(8,128)S(1)}, f32[5,2048]{1,0:T(8,128)S(1)}, u32[]{:S(2)}, u32[]{:S(2)}) collective-permute-start(f32[5,2048]{1,0:T(8,128)S(1)} %get-tuple-element.17), channel_id=1, source_target_pairs={{0,8},{4,12},{8,0},{12,4},{1,9},{5,13},{9,1},{13,5},{2,10},{6,14},... | collective-permute-start | bytes 122888 | tf_op jit(solution)/shard_map/ppermute | solution.py:61
  62.2 2.6 %collective-permute-done.15 = f32[5,2048]{1,0:T(8,128)S(1)} collective-permute-done((f32[5,2048]{1,0:T(8,128)S(1)}, f32[5,2048]{1,0:T(8,128)S(1)}, u32[]{:S(2)}, u32[]{:S(2)}) %collective-permute-start.15) | collective-permute-done | bytes 40992 | tf_op jit(solution)/shard_map/ppermute | solution.py:61
  64.7 2.7 %collective-permute-done.14 = f32[5,2048]{1,0:T(8,128)S(1)} collective-permute-done((f32[5,2048]{1,0:T(8,128)S(1)}, f32[5,2048]{1,0:T(8,128)S(1)}, u32[]{:S(2)}, u32[]{:S(2)}) %collective-permute-start.14) | collective-permute-done | bytes 40992 | tf_op jit(solution)/shard_map/ppermute | solution.py:61
  (46 shorter events, 7.0 us)
Async XLA Ops:
  0.0 22.4 %copy-start.1 = (f32[2048]{0:T(1024)S(1)}, f32[2048]{0:T(1024)}, u32[]{:S(2)}) copy-start(f32[2048]{0:T(1024)} %param.6) | copy-start | bytes 24580
  0.0 6.7 %collective-permute-start = (bf16[5,2048]{1,0:T(8,128)(2,1)}, bf16[5,2048]{1,0:T(8,128)(2,1)S(1)}, u32[]{:S(2)}, u32[]{:S(2)}) collective-permute-start(bf16[5,2048]{1,0:T(8,128)(2,1)} %param.5), channel_id=1, source_target_pairs={{0,4},{4,0},{8,12},{12,8},{1,5},{5,1},{9,13},{13,9},{2,6},{6,2},{1... | collective-permute-start | bytes 61448 | tf_op jit(solution)/shard_map/ppermute | solution.py:70
  3.0 5.6 %collective-permute-start.1 = (bf16[5,2048]{1,0:T(8,128)(2,1)}, bf16[5,2048]{1,0:T(8,128)(2,1)S(1)}, u32[]{:S(2)}, u32[]{:S(2)}) collective-permute-start(bf16[5,2048]{1,0:T(8,128)(2,1)} %param.5), channel_id=1, source_target_pairs={{0,8},{4,12},{8,0},{12,4},{1,9},{5,13},{9,1},{13,5},{2,10},{6,14},... | collective-permute-start | bytes 61448 | tf_op jit(solution)/shard_map/ppermute | solution.py:70
  5.6 5.9 %collective-permute-start.2 = (bf16[5,2048]{1,0:T(8,128)(2,1)}, bf16[5,2048]{1,0:T(8,128)(2,1)S(1)}, u32[]{:S(2)}, u32[]{:S(2)}) collective-permute-start(bf16[5,2048]{1,0:T(8,128)(2,1)} %param.5), channel_id=1, source_target_pairs={{0,12},{4,8},{8,4},{12,0},{1,13},{5,9},{9,5},{13,1},{2,14},{6,10},... | collective-permute-start | bytes 61448 | tf_op jit(solution)/shard_map/ppermute | solution.py:70
  11.9 1.2 %collective-permute-start.3 = (f32[20]{0:T(128)S(1)}, f32[20]{0:T(128)S(1)}, u32[]{:S(2)}, u32[]{:S(2)}) collective-permute-start(f32[20]{0:T(128)S(1)} %fusion.8), channel_id=1, source_target_pairs={{0,1},{1,0},{2,3},{3,2},{4,5},{5,4},{6,7},{7,6},{8,9},{9,8},{10,11... | collective-permute-start | bytes 248 | tf_op jit(solution)/shard_map/ppermute | solution.py:20
  13.1 3.5 %collective-permute-start.4 = (f32[20]{0:T(128)S(1)}, f32[20]{0:T(128)S(1)}, u32[]{:S(2)}, u32[]{:S(2)}) collective-permute-start(f32[20]{0:T(128)S(1)} %add.116), channel_id=1, source_target_pairs={{0,2},{1,3},{2,0},{3,1},{4,6},{5,7},{6,4},{7,5},{8,10},{9,11},{10,... | collective-permute-start | bytes 248 | tf_op jit(solution)/shard_map/ppermute | solution.py:20
  16.7 15.5 %copy-start = (bf16[2048,6144]{1,0:T(8,128)(2,1)S(1)}, bf16[2048,6144]{1,0:T(8,128)(2,1)}, u32[]{:S(2)}) copy-start(bf16[2048,6144]{1,0:T(8,128)(2,1)} %param.7) | copy-start | bytes 75497472
  35.9 1.6 %collective-permute-start.9 = (f32[2,20,1536]{2,1,0:T(8,128)S(1)}, f32[2,20,1536]{2,1,0:T(8,128)S(1)}, u32[]{:S(2)}, u32[]{:S(2)}) collective-permute-start(f32[2,20,1536]{2,1,0:T(8,128)S(1)} %pad_maximum_fusion.1), channel_id=1, source_target_pairs={{0,1},{1,0},{2,3},{3,2},{4,5},{5,4},{6,7},{7,6},{8,9},{9,8},{10,11... | collective-permute-start | bytes 737288 | tf_op jit(solution)/shard_map/ppermute | solution.py:20
  36.0 3.2 %collective-permute-start.5 = (f32[2,20,1536]{2,1,0:T(8,128)S(1)}, f32[2,20,1536]{2,1,0:T(8,128)S(1)}, u32[]{:S(2)}, u32[]{:S(2)}) collective-permute-start(f32[2,20,1536]{2,1,0:T(8,128)S(1)} %pad_maximum_fusion), channel_id=1, source_target_pairs={{0,1},{1,0},{2,3},{3,2},{4,5},{5,4},{6,7},{7,6},{8,9},{9,8},{10,11... | collective-permute-start | bytes 737288 | tf_op jit(solution)/shard_map/ppermute | solution.py:20
  37.6 6.9 %collective-permute-start.10 = (f32[2,20,768]{2,1,0:T(8,128)S(1)}, f32[2,20,768]{2,1,0:T(8,128)S(1)}, u32[]{:S(2)}, u32[]{:S(2)}) collective-permute-start(f32[2,20,768]{2,1,0:T(8,128)S(1)} %pad_maximum_fusion.3), channel_id=1, source_target_pairs={{0,2},{1,3},{2,0},{3,1},{4,6},{5,7},{6,4},{7,5},{8,10},{9,11},{10,... | collective-permute-start | bytes 368648 | tf_op jit(solution)/shard_map/ppermute | solution.py:20
  39.3 7.5 %collective-permute-start.6 = (f32[2,20,768]{2,1,0:T(8,128)S(1)}, f32[2,20,768]{2,1,0:T(8,128)S(1)}, u32[]{:S(2)}, u32[]{:S(2)}) collective-permute-start(f32[2,20,768]{2,1,0:T(8,128)S(1)} %pad_maximum_fusion.2), channel_id=1, source_target_pairs={{0,2},{1,3},{2,0},{3,1},{4,6},{5,7},{6,4},{7,5},{8,10},{9,11},{10,... | collective-permute-start | bytes 368648 | tf_op jit(solution)/shard_map/ppermute | solution.py:20
  44.5 8.4 %collective-permute-start.11 = (bf16[20,768]{1,0:T(8,128)(2,1)S(1)}, bf16[20,768]{1,0:T(8,128)(2,1)S(1)}, u32[]{:S(2)}, u32[]{:S(2)}) collective-permute-start(bf16[20,768]{1,0:T(8,128)(2,1)S(1)} %fusion.30), channel_id=1, source_target_pairs={{0,2},{1,3},{2,0},{3,1},{4,6},{5,7},{6,4},{7,5},{8,10},{9,11},{10,... | collective-permute-start | bytes 92168 | tf_op jit(solution)/shard_map/ppermute | solution.py:20
  46.8 6.3 %collective-permute-start.7 = (bf16[20,768]{1,0:T(8,128)(2,1)S(1)}, bf16[20,768]{1,0:T(8,128)(2,1)S(1)}, u32[]{:S(2)}, u32[]{:S(2)}) collective-permute-start(bf16[20,768]{1,0:T(8,128)(2,1)S(1)} %fusion.34), channel_id=1, source_target_pairs={{0,2},{1,3},{2,0},{3,1},{4,6},{5,7},{6,4},{7,5},{8,10},{9,11},{10,... | collective-permute-start | bytes 92168 | tf_op jit(solution)/shard_map/ppermute | solution.py:20
  52.9 1.3 %collective-permute-start.12 = (bf16[20,1536]{1,0:T(8,128)(2,1)S(1)}, bf16[20,1536]{1,0:T(8,128)(2,1)S(1)}, u32[]{:S(2)}, u32[]{:S(2)}) collective-permute-start(bf16[20,1536]{1,0:T(8,128)(2,1)S(1)} %maximum_select_fusion.5), channel_id=1, source_target_pairs={{0,1},{1,0},{2,3},{3,2},{4,5},{5,4},{6,7},{7,6},{8,9},{9,8},{10,11... | collective-permute-start | bytes 184328 | tf_op jit(solution)/shard_map/ppermute | solution.py:20
  53.1 3.0 %collective-permute-start.8 = (bf16[20,1536]{1,0:T(8,128)(2,1)S(1)}, bf16[20,1536]{1,0:T(8,128)(2,1)S(1)}, u32[]{:S(2)}, u32[]{:S(2)}) collective-permute-start(bf16[20,1536]{1,0:T(8,128)(2,1)S(1)} %maximum_select_fusion.4), channel_id=1, source_target_pairs={{0,1},{1,0},{2,3},{3,2},{4,5},{5,4},{6,7},{7,6},{8,9},{9,8},{10,11... | collective-permute-start | bytes 184328 | tf_op jit(solution)/shard_map/ppermute | solution.py:20
  57.8 4.3 %collective-permute-start.13 = (f32[5,2048]{1,0:T(8,128)S(1)}, f32[5,2048]{1,0:T(8,128)S(1)}, u32[]{:S(2)}, u32[]{:S(2)}) collective-permute-start(f32[5,2048]{1,0:T(8,128)S(1)} %get-tuple-element.15), channel_id=1, source_target_pairs={{0,4},{4,0},{8,12},{12,8},{1,5},{5,1},{9,13},{13,9},{2,6},{6,2},{1... | collective-permute-start | bytes 122888 | tf_op jit(solution)/shard_map/ppermute | solution.py:61
  57.9 6.8 %collective-permute-start.15 = (f32[5,2048]{1,0:T(8,128)S(1)}, f32[5,2048]{1,0:T(8,128)S(1)}, u32[]{:S(2)}, u32[]{:S(2)}) collective-permute-start(f32[5,2048]{1,0:T(8,128)S(1)} %get-tuple-element.16), channel_id=1, source_target_pairs={{0,12},{4,8},{8,4},{12,0},{1,13},{5,9},{9,5},{13,1},{2,14},{6,10},... | collective-permute-start | bytes 122888 | tf_op jit(solution)/shard_map/ppermute | solution.py:61
  58.8 8.7 %collective-permute-start.14 = (f32[5,2048]{1,0:T(8,128)S(1)}, f32[5,2048]{1,0:T(8,128)S(1)}, u32[]{:S(2)}, u32[]{:S(2)}) collective-permute-start(f32[5,2048]{1,0:T(8,128)S(1)} %get-tuple-element.17), channel_id=1, source_target_pairs={{0,8},{4,12},{8,0},{12,4},{1,9},{5,13},{9,1},{13,5},{2,10},{6,14},... | collective-permute-start | bytes 122888 | tf_op jit(solution)/shard_map/ppermute | solution.py:61

commit v23 on v12

--- a/solution.py
+++ b/solution.py
@@ -73,10 +73,10 @@
 
 
 def fanout_all_reduce(x, axis, n):
-    me = lax.axis_index(axis)
-    got = jnp.stack([x] + [lax.ppermute(x, axis, [(a, a ^ k) for a in range(n)]) for k in range(1, n)])
-    ordered = jnp.take(got, jnp.arange(n) ^ me, axis=0)
-    return jnp.sum(ordered, axis=0)
+    total = x
+    for k in range(1, n):
+        total = total + lax.ppermute(x, axis, [(a, a ^ k) for a in range(n)])
+    return total
 
 
 def rows_to_vmem(w, start, count):

time: 67.7 us -> 67.3 us (level)
  transfers between devices with their start and end apart: 17 -> 17, of which waited for: 9 -> 10; matrix products, arithmetic and copies ran while one was open for 5% -> 5% of each run, Pallas kernels for 14% -> 14%
where the time goes in v23:
time: 67.3 us; the launch traced here: 67 us
  matrix products  19.2 us (29%)
  starting transfers between devices  17.4 us (26%)
  waiting for transfers between devices  14.6 us (22%)
  Pallas kernels  9.17 us (14%)
  local copies, waits for them, and re-layouts  5.42 us (8%)
  other arithmetic  1.06 us (2%)
    dot_general x2, matrix products, local(): up_part = jnp.dot(piece, w_up[:, cols], preferred_element_type=jnp.float32)  12 us
    pallas_call x2, Pallas kernels, rows_to_vmem(): pl.pallas_call(kernel, out_shape=jax.ShapeDtypeStruct((count, w.shape[1])...  9.17 us
    ppermute x8, starting transfers between devices, exchange(): return lax.ppermute(x, axis, [(a, a ^ 1 << s) for a in range(n)])  6.29 us
    ppermute x3, waiting for transfers between devices, fanout_reduce_scatter(): own = own + lax.ppermute(block, axis, [(a, a ^ k) for a in range(n)])  6.06 us
    ppermute x3, starting transfers between devices, fanout_all_gather(): lax.ppermute(x, axis, [(a, a ^ k) for a in range(n)])  5.62 us
    ppermute x3, waiting for transfers between devices, fanout_all_gather(): lax.ppermute(x, axis, [(a, a ^ k) for a in range(n)])  4.29 us
    dot_general x2, matrix products, local(): jnp.dot(piece, w_gate[:, cols], preferred_element_type=jnp.float32)  3.64 us
    ppermute x3, starting transfers between devices, fanout_reduce_scatter(): own = own + lax.ppermute(block, axis, [(a, a ^ k) for a in range(n)])  3.55 us
  transfers between devices with their start and end apart: 17, of which 10 were waited for; matrix products, arithmetic and copies ran while one was open for 5% of the time, Pallas kernels for 14%

profile of v23, /device:TPU:0, one launch (start us, length us, event | category | flops | bytes accessed | tf_op | source)
XLA Modules:
  0.0 67.0 jit_solution(1325835289361148742)
XLA Ops:
  0.0 3.0 %collective-permute-start = (bf16[5,2048]{1,0:T(8,128)(2,1)}, bf16[5,2048]{1,0:T(8,128)(2,1)S(1)}, u32[]{:S(2)}, u32[]{:S(2)}) collective-permute-start(bf16[5,2048]{1,0:T(8,128)(2,1)} %param.5), channel_id=1, source_target_pairs={{0,4},{4,0},{8,12},{12,8},{1,5},{5,1},{9,13},{13,9},{2,6},{6,2},{1... | collective-permute-start | bytes 61448 | tf_op jit(solution)/shard_map/ppermute | solution.py:70
  3.0 2.6 %collective-permute-start.1 = (bf16[5,2048]{1,0:T(8,128)(2,1)}, bf16[5,2048]{1,0:T(8,128)(2,1)S(1)}, u32[]{:S(2)}, u32[]{:S(2)}) collective-permute-start(bf16[5,2048]{1,0:T(8,128)(2,1)} %param.5), channel_id=1, source_target_pairs={{0,8},{4,12},{8,0},{12,4},{1,9},{5,13},{9,1},{13,5},{2,10},{6,14},... | collective-permute-start | bytes 61448 | tf_op jit(solution)/shard_map/ppermute | solution.py:70
  5.6 1.0 %dynamic_update_slice.12 = bf16[20,2048]{1,0:T(8,128)(2,1)S(1)} dynamic-update-slice(bf16[20,2048]{1,0:T(8,128)(2,1)S(1)} %broadcast_in_dim.2, bf16[5,2048]{1,0:T(8,128)(2,1)} %param.5, s32[]{:T(128)S(6)} %select_n.66, s32[]{:T(128)} %constant.7.clone.1) | dynamic-update-slice | bytes 40964 | tf_op jit(solution)/shard_map/dynamic_update_slice | solution.py:71
  7.0 1.6 %collective-permute-done.1 = bf16[5,2048]{1,0:T(8,128)(2,1)S(1)} collective-permute-done((bf16[5,2048]{1,0:T(8,128)(2,1)}, bf16[5,2048]{1,0:T(8,128)(2,1)S(1)}, u32[]{:S(2)}, u32[]{:S(2)}) %collective-permute-start.1) | collective-permute-done | bytes 20512 | tf_op jit(solution)/shard_map/ppermute | solution.py:70
  8.9 2.6 %collective-permute-done.2 = bf16[5,2048]{1,0:T(8,128)(2,1)S(1)} collective-permute-done((bf16[5,2048]{1,0:T(8,128)(2,1)}, bf16[5,2048]{1,0:T(8,128)(2,1)S(1)}, u32[]{:S(2)}, u32[]{:S(2)}) %collective-permute-start.2) | collective-permute-done | bytes 20512 | tf_op jit(solution)/shard_map/ppermute | solution.py:70
  12.0 1.6 %collective-permute-start.4 = (f32[20]{0:T(128)S(1)}, f32[20]{0:T(128)S(1)}, u32[]{:S(2)}, u32[]{:S(2)}) collective-permute-start(f32[20]{0:T(128)S(1)} %fusion.8), channel_id=1, source_target_pairs={{0,2},{1,3},{2,0},{3,1},{4,6},{5,7},{6,4},{7,5},{8,10},{9,11},{10,... | collective-permute-start | bytes 248 | tf_op jit(solution)/shard_map/ppermute | solution.py:78
  13.9 1.1 %collective-permute-done.5 = f32[20]{0:T(128)S(1)} collective-permute-done((f32[20]{0:T(128)S(1)}, f32[20]{0:T(128)S(1)}, u32[]{:S(2)}, u32[]{:S(2)}) %collective-permute-start.5) | collective-permute-done | bytes 112 | tf_op jit(solution)/shard_map/ppermute | solution.py:78
  15.6 5.8 %fusion.4 = f32[20,3072]{1,0:T(8,128)S(1)} fusion(bf16[2048,6144]{1,0:T(8,128)(2,1)} %param.8, bf16[20,2048]{1,0:T(8,128)(2,1)S(1)} %dynamic_update_slice.15, f32[2048]{0:T(1024)} %param.6, f32[20]{0:T(128)S(1)} %add_rsqrt_fusion), kind=kOutput, calls=%fused_computation.4 | convolution fusion | flops 251822080 | bytes 12918864 | tf_op jit(solution)/shard_map/dot_general | solution.py:128
  21.4 6.3 %fusion = f32[20,3072]{1,0:T(8,128)S(1)} fusion(bf16[2048,6144]{1,0:T(8,128)(2,1)} %param.8, bf16[20,2048]{1,0:T(8,128)(2,1)S(1)} %dynamic_update_slice.15, f32[2048]{0:T(1024)S(1)} %copy-done.1, f32[20]{0:T(128)S(1)} %add_rsqrt_fusion), kind=kOutput, calls=%fused_computation | convolution fusion | flops 251822080 | bytes 12918864 | tf_op jit(solution)/shard_map/dot_general | solution.py:128
  27.7 3.4 %copy-done = bf16[2048,6144]{1,0:T(8,128)(2,1)S(1)} copy-done((bf16[2048,6144]{1,0:T(8,128)(2,1)S(1)}, bf16[2048,6144]{1,0:T(8,128)(2,1)}, u32[]{:S(2)}) %copy-start) | copy-done | bytes 25165848
  31.1 1.8 %fusion.2 = f32[20,3072]{1,0:T(8,128)S(1)} fusion(bf16[2048,6144]{1,0:T(8,128)(2,1)S(1)} %copy-done, bf16[20,2048]{1,0:T(8,128)(2,1)S(1)} %dynamic_update_slice.15, f32[2048]{0:T(1024)S(1)} %copy-done.1, f32[20]{0:T(128)S(1)} %add_rsqrt_fusion), kind=kOutput, calls=%fused_computation.2 | convolution fusion | flops 251822080 | bytes 12935680 | tf_op jit(solution)/shard_map/dot_general | solution.py:127
  32.9 1.8 %fusion.6 = f32[20,3072]{1,0:T(8,128)S(1)} fusion(bf16[2048,6144]{1,0:T(8,128)(2,1)S(1)} %copy-done, bf16[20,2048]{1,0:T(8,128)(2,1)S(1)} %dynamic_update_slice.15, f32[2048]{0:T(1024)S(1)} %copy-done.1, f32[20]{0:T(128)S(1)} %add_rsqrt_fusion), kind=kOutput, calls=%fused_computation.6 | convolution fusion | flops 251822080 | bytes 12935680 | tf_op jit(solution)/shard_map/dot_general | solution.py:127
  35.5 1.0 %collective-permute-done.10 = f32[2,20,1536]{2,1,0:T(8,128)S(1)} collective-permute-done((f32[2,20,1536]{2,1,0:T(8,128)S(1)}, f32[2,20,1536]{2,1,0:T(8,128)S(1)}, u32[]{:S(2)}, u32[]{:S(2)}) %collective-permute-start.10) | collective-permute-done | bytes 245792 | tf_op jit(solution)/shard_map/ppermute | solution.py:20
  36.6 1.6 %collective-permute-start.11 = (f32[2,20,768]{2,1,0:T(8,128)S(1)}, f32[2,20,768]{2,1,0:T(8,128)S(1)}, u32[]{:S(2)}, u32[]{:S(2)}) collective-permute-start(f32[2,20,768]{2,1,0:T(8,128)S(1)} %pad_maximum_fusion.3), channel_id=1, source_target_pairs={{0,2},{1,3},{2,0},{3,1},{4,6},{5,7},{6,4},{7,5},{8,10},{9,11},{10,... | collective-permute-start | bytes 368648 | tf_op jit(solution)/shard_map/ppermute | solution.py:20
  38.8 4.6 %shard_map.55 = bf16[3072,2048]{1,0:T(8,128)(2,1)S(1)} custom-call(bf16[6144,2048]{1,0:T(8,128)(2,1)} %src.1), custom_call_target="tpu_custom_call" | custom-call | bytes 25165824 | tf_op jit(solution)/shard_map/pallas_call | solution.py:90
  43.5 1.5 %collective-permute-start.12 = (bf16[20,768]{1,0:T(8,128)(2,1)S(1)}, bf16[20,768]{1,0:T(8,128)(2,1)S(1)}, u32[]{:S(2)}, u32[]{:S(2)}) collective-permute-start(bf16[20,768]{1,0:T(8,128)(2,1)S(1)} %fusion.30), channel_id=1, source_target_pairs={{0,2},{1,3},{2,0},{3,1},{4,6},{5,7},{6,4},{7,5},{8,10},{9,11},{10,... | collective-permute-start | bytes 92168 | tf_op jit(solution)/shard_map/ppermute | solution.py:20
  45.0 0.9 %collective-permute-done.7 = f32[2,20,768]{2,1,0:T(8,128)S(1)} collective-permute-done((f32[2,20,768]{2,1,0:T(8,128)S(1)}, f32[2,20,768]{2,1,0:T(8,128)S(1)}, u32[]{:S(2)}, u32[]{:S(2)}) %collective-permute-start.7) | collective-permute-done | bytes 122912 | tf_op jit(solution)/shard_map/ppermute | solution.py:20
  45.9 1.3 %collective-permute-start.8 = (bf16[20,768]{1,0:T(8,128)(2,1)S(1)}, bf16[20,768]{1,0:T(8,128)(2,1)S(1)}, u32[]{:S(2)}, u32[]{:S(2)}) collective-permute-start(bf16[20,768]{1,0:T(8,128)(2,1)S(1)} %fusion.34), channel_id=1, source_target_pairs={{0,2},{1,3},{2,0},{3,1},{4,6},{5,7},{6,4},{7,5},{8,10},{9,11},{10,... | collective-permute-start | bytes 92168 | tf_op jit(solution)/shard_map/ppermute | solution.py:20
  47.3 4.6 %shard_map.56 = bf16[3072,2048]{1,0:T(8,128)(2,1)S(1)} custom-call(bf16[6144,2048]{1,0:T(8,128)(2,1)} %src.1), custom_call_target="tpu_custom_call" | custom-call | bytes 25165824 | tf_op jit(solution)/shard_map/pallas_call | solution.py:90
  53.2 1.7 %fusion.20 = f32[20,2048]{1,0:T(8,128)S(1)} fusion(bf16[3072,2048]{1,0:T(8,128)(2,1)S(1)} %shard_map.56, bf16[20,1536]{1,0:T(8,128)(2,1)S(1)} %collective-permute-done.13, bf16[20,1536]{1,0:T(8,128)(2,1)S(1)} %maximum_select_fusion.5, pred[]{:T(512)S(6)} %eq.8), kind=kOutput, calls=%fused_computation.33 | convolution fusion | flops 252211200 | bytes 12869633 | tf_op jit(solution)/shard_map/dot_general | solution.py:148
  55.0 1.8 %convolution_add_fusion = f32[20,2048]{1,0:T(8,128)S(1)} fusion(f32[20,2048]{1,0:T(8,128)S(1)} %fusion.20, bf16[3072,2048]{1,0:T(8,128)(2,1)S(1)} %shard_map.55, bf16[20,1536]{1,0:T(8,128)(2,1)S(1)} %collective-permute-done.9, bf16[20,1536]{1,0:T(8,128)(2,1)S(1)} %maximum_select_fusion.4, pred[]{:T(512)S(6)} %eq.8), kind=kOutput, calls=%fused_computation.8 | convolution fusion | flops 252252160 | bytes 13033473 | tf_op jit(solution)/shard_map/dot_general | solution.py:148
  57.7 2.6 %collective-permute-start.15 = (f32[5,2048]{1,0:T(8,128)S(1)}, f32[5,2048]{1,0:T(8,128)S(1)}, u32[]{:S(2)}, u32[]{:S(2)}) collective-permute-start(f32[5,2048]{1,0:T(8,128)S(1)} %get-tuple-element.17), channel_id=1, source_target_pairs={{0,8},{4,12},{8,0},{12,4},{1,9},{5,13},{9,1},{13,5},{2,10},{6,14},... | collective-permute-start | bytes 122888 | tf_op jit(solution)/shard_map/ppermute | solution.py:61
  61.1 2.6 %collective-permute-done.16 = f32[5,2048]{1,0:T(8,128)S(1)} collective-permute-done((f32[5,2048]{1,0:T(8,128)S(1)}, f32[5,2048]{1,0:T(8,128)S(1)}, u32[]{:S(2)}, u32[]{:S(2)}) %collective-permute-start.16) | collective-permute-done | bytes 40992 | tf_op jit(solution)/shard_map/ppermute | solution.py:61
  63.7 2.7 %collective-permute-done.15 = f32[5,2048]{1,0:T(8,128)S(1)} collective-permute-done((f32[5,2048]{1,0:T(8,128)S(1)}, f32[5,2048]{1,0:T(8,128)S(1)}, u32[]{:S(2)}, u32[]{:S(2)}) %collective-permute-start.15) | collective-permute-done | bytes 40992 | tf_op jit(solution)/shard_map/ppermute | solution.py:61
  (47 shorter events, 7.3 us)
Async XLA Ops:
  0.0 21.4 %copy-start.1 = (f32[2048]{0:T(1024)S(1)}, f32[2048]{0:T(1024)}, u32[]{:S(2)}) copy-start(f32[2048]{0:T(1024)} %param.6) | copy-start | bytes 24580
  0.0 6.7 %collective-permute-start = (bf16[5,2048]{1,0:T(8,128)(2,1)}, bf16[5,2048]{1,0:T(8,128)(2,1)S(1)}, u32[]{:S(2)}, u32[]{:S(2)}) collective-permute-start(bf16[5,2048]{1,0:T(8,128)(2,1)} %param.5), channel_id=1, source_target_pairs={{0,4},{4,0},{8,12},{12,8},{1,5},{5,1},{9,13},{13,9},{2,6},{6,2},{1... | collective-permute-start | bytes 61448 | tf_op jit(solution)/shard_map/ppermute | solution.py:70
  3.0 5.6 %collective-permute-start.1 = (bf16[5,2048]{1,0:T(8,128)(2,1)}, bf16[5,2048]{1,0:T(8,128)(2,1)S(1)}, u32[]{:S(2)}, u32[]{:S(2)}) collective-permute-start(bf16[5,2048]{1,0:T(8,128)(2,1)} %param.5), channel_id=1, source_target_pairs={{0,8},{4,12},{8,0},{12,4},{1,9},{5,13},{9,1},{13,5},{2,10},{6,14},... | collective-permute-start | bytes 61448 | tf_op jit(solution)/shard_map/ppermute | solution.py:70
  5.6 5.9 %collective-permute-start.2 = (bf16[5,2048]{1,0:T(8,128)(2,1)}, bf16[5,2048]{1,0:T(8,128)(2,1)S(1)}, u32[]{:S(2)}, u32[]{:S(2)}) collective-permute-start(bf16[5,2048]{1,0:T(8,128)(2,1)} %param.5), channel_id=1, source_target_pairs={{0,12},{4,8},{8,4},{12,0},{1,13},{5,9},{9,5},{13,1},{2,14},{6,10},... | collective-permute-start | bytes 61448 | tf_op jit(solution)/shard_map/ppermute | solution.py:70
  11.9 3.0 %collective-permute-start.5 = (f32[20]{0:T(128)S(1)}, f32[20]{0:T(128)S(1)}, u32[]{:S(2)}, u32[]{:S(2)}) collective-permute-start(f32[20]{0:T(128)S(1)} %fusion.8), channel_id=1, source_target_pairs={{0,3},{1,2},{2,1},{3,0},{4,7},{5,6},{6,5},{7,4},{8,11},{9,10},{10,... | collective-permute-start | bytes 248 | tf_op jit(solution)/shard_map/ppermute | solution.py:78
  12.0 3.6 %collective-permute-start.4 = (f32[20]{0:T(128)S(1)}, f32[20]{0:T(128)S(1)}, u32[]{:S(2)}, u32[]{:S(2)}) collective-permute-start(f32[20]{0:T(128)S(1)} %fusion.8), channel_id=1, source_target_pairs={{0,2},{1,3},{2,0},{3,1},{4,6},{5,7},{6,4},{7,5},{8,10},{9,11},{10,... | collective-permute-start | bytes 248 | tf_op jit(solution)/shard_map/ppermute | solution.py:78
  13.6 2.1 %collective-permute-start.3 = (f32[20]{0:T(128)S(1)}, f32[20]{0:T(128)S(1)}, u32[]{:S(2)}, u32[]{:S(2)}) collective-permute-start(f32[20]{0:T(128)S(1)} %fusion.8), channel_id=1, source_target_pairs={{0,1},{1,0},{2,3},{3,2},{4,5},{5,4},{6,7},{7,6},{8,9},{9,8},{10,11... | collective-permute-start | bytes 248 | tf_op jit(solution)/shard_map/ppermute | solution.py:78
  15.6 15.5 %copy-start = (bf16[2048,6144]{1,0:T(8,128)(2,1)S(1)}, bf16[2048,6144]{1,0:T(8,128)(2,1)}, u32[]{:S(2)}) copy-start(bf16[2048,6144]{1,0:T(8,128)(2,1)} %param.7) | copy-start | bytes 75497472
  34.8 1.7 %collective-permute-start.10 = (f32[2,20,1536]{2,1,0:T(8,128)S(1)}, f32[2,20,1536]{2,1,0:T(8,128)S(1)}, u32[]{:S(2)}, u32[]{:S(2)}) collective-permute-start(f32[2,20,1536]{2,1,0:T(8,128)S(1)} %pad_maximum_fusion.1), channel_id=1, source_target_pairs={{0,1},{1,0},{2,3},{3,2},{4,5},{5,4},{6,7},{7,6},{8,9},{9,8},{10,11... | collective-permute-start | bytes 737288 | tf_op jit(solution)/shard_map/ppermute | solution.py:20
  35.3 2.8 %collective-permute-start.6 = (f32[2,20,1536]{2,1,0:T(8,128)S(1)}, f32[2,20,1536]{2,1,0:T(8,128)S(1)}, u32[]{:S(2)}, u32[]{:S(2)}) collective-permute-start(f32[2,20,1536]{2,1,0:T(8,128)S(1)} %pad_maximum_fusion), channel_id=1, source_target_pairs={{0,1},{1,0},{2,3},{3,2},{4,5},{5,4},{6,7},{7,6},{8,9},{9,8},{10,11... | collective-permute-start | bytes 737288 | tf_op jit(solution)/shard_map/ppermute | solution.py:20
  36.6 6.9 %collective-permute-start.11 = (f32[2,20,768]{2,1,0:T(8,128)S(1)}, f32[2,20,768]{2,1,0:T(8,128)S(1)}, u32[]{:S(2)}, u32[]{:S(2)}) collective-permute-start(f32[2,20,768]{2,1,0:T(8,128)S(1)} %pad_maximum_fusion.3), channel_id=1, source_target_pairs={{0,2},{1,3},{2,0},{3,1},{4,6},{5,7},{6,4},{7,5},{8,10},{9,11},{10,... | collective-permute-start | bytes 368648 | tf_op jit(solution)/shard_map/ppermute | solution.py:20
  38.2 7.7 %collective-permute-start.7 = (f32[2,20,768]{2,1,0:T(8,128)S(1)}, f32[2,20,768]{2,1,0:T(8,128)S(1)}, u32[]{:S(2)}, u32[]{:S(2)}) collective-permute-start(f32[2,20,768]{2,1,0:T(8,128)S(1)} %pad_maximum_fusion.2), channel_id=1, source_target_pairs={{0,2},{1,3},{2,0},{3,1},{4,6},{5,7},{6,4},{7,5},{8,10},{9,11},{10,... | collective-permute-start | bytes 368648 | tf_op jit(solution)/shard_map/ppermute | solution.py:20
  43.5 8.4 %collective-permute-start.12 = (bf16[20,768]{1,0:T(8,128)(2,1)S(1)}, bf16[20,768]{1,0:T(8,128)(2,1)S(1)}, u32[]{:S(2)}, u32[]{:S(2)}) collective-permute-start(bf16[20,768]{1,0:T(8,128)(2,1)S(1)} %fusion.30), channel_id=1, source_target_pairs={{0,2},{1,3},{2,0},{3,1},{4,6},{5,7},{6,4},{7,5},{8,10},{9,11},{10,... | collective-permute-start | bytes 92168 | tf_op jit(solution)/shard_map/ppermute | solution.py:20
  45.9 6.0 %collective-permute-start.8 = (bf16[20,768]{1,0:T(8,128)(2,1)S(1)}, bf16[20,768]{1,0:T(8,128)(2,1)S(1)}, u32[]{:S(2)}, u32[]{:S(2)}) collective-permute-start(bf16[20,768]{1,0:T(8,128)(2,1)S(1)} %fusion.34), channel_id=1, source_target_pairs={{0,2},{1,3},{2,0},{3,1},{4,6},{5,7},{6,4},{7,5},{8,10},{9,11},{10,... | collective-permute-start | bytes 92168 | tf_op jit(solution)/shard_map/ppermute | solution.py:20
  51.9 1.3 %collective-permute-start.13 = (bf16[20,1536]{1,0:T(8,128)(2,1)S(1)}, bf16[20,1536]{1,0:T(8,128)(2,1)S(1)}, u32[]{:S(2)}, u32[]{:S(2)}) collective-permute-start(bf16[20,1536]{1,0:T(8,128)(2,1)S(1)} %maximum_select_fusion.5), channel_id=1, source_target_pairs={{0,1},{1,0},{2,3},{3,2},{4,5},{5,4},{6,7},{7,6},{8,9},{9,8},{10,11... | collective-permute-start | bytes 184328 | tf_op jit(solution)/shard_map/ppermute | solution.py:20
  52.0 3.0 %collective-permute-start.9 = (bf16[20,1536]{1,0:T(8,128)(2,1)S(1)}, bf16[20,1536]{1,0:T(8,128)(2,1)S(1)}, u32[]{:S(2)}, u32[]{:S(2)}) collective-permute-start(bf16[20,1536]{1,0:T(8,128)(2,1)S(1)} %maximum_select_fusion.4), channel_id=1, source_target_pairs={{0,1},{1,0},{2,3},{3,2},{4,5},{5,4},{6,7},{7,6},{8,9},{9,8},{10,11... | collective-permute-start | bytes 184328 | tf_op jit(solution)/shard_map/ppermute | solution.py:20
  56.8 4.3 %collective-permute-start.14 = (f32[5,2048]{1,0:T(8,128)S(1)}, f32[5,2048]{1,0:T(8,128)S(1)}, u32[]{:S(2)}, u32[]{:S(2)}) collective-permute-start(f32[5,2048]{1,0:T(8,128)S(1)} %get-tuple-element.15), channel_id=1, source_target_pairs={{0,4},{4,0},{8,12},{12,8},{1,5},{5,1},{9,13},{13,9},{2,6},{6,2},{1... | collective-permute-start | bytes 122888 | tf_op jit(solution)/shard_map/ppermute | solution.py:61
  56.9 6.8 %collective-permute-start.16 = (f32[5,2048]{1,0:T(8,128)S(1)}, f32[5,2048]{1,0:T(8,128)S(1)}, u32[]{:S(2)}, u32[]{:S(2)}) collective-permute-start(f32[5,2048]{1,0:T(8,128)S(1)} %get-tuple-element.16), channel_id=1, source_target_pairs={{0,12},{4,8},{8,4},{12,0},{1,13},{5,9},{9,5},{13,1},{2,14},{6,10},... | collective-permute-start | bytes 122888 | tf_op jit(solution)/shard_map/ppermute | solution.py:61
  57.7 8.7 %collective-permute-start.15 = (f32[5,2048]{1,0:T(8,128)S(1)}, f32[5,2048]{1,0:T(8,128)S(1)}, u32[]{:S(2)}, u32[]{:S(2)}) collective-permute-start(f32[5,2048]{1,0:T(8,128)S(1)} %get-tuple-element.17), channel_id=1, source_target_pairs={{0,8},{4,12},{8,0},{12,4},{1,9},{5,13},{9,1},{13,5},{2,10},{6,14},... | collective-permute-start | bytes 122888 | tf_op jit(solution)/shard_map/ppermute | solution.py:61

commit v24 on v12

--- a/solution.py
+++ b/solution.py
@@ -56,7 +56,7 @@
     me = lax.axis_index(axis)
     rows = x.shape[0] // n
     own = lax.dynamic_slice_in_dim(x, gathered_position(me, bits) * rows, rows, axis=0)
-    for k in range(1, n):
+    for k in range(n - 1, 0, -1):
         block = lax.dynamic_slice_in_dim(x, gathered_position(me ^ k, bits) * rows, rows, axis=0)
         own = own + lax.ppermute(block, axis, [(a, a ^ k) for a in range(n)])
     return own
@@ -66,7 +66,7 @@
     me = lax.axis_index(axis)
     rows = x.shape[0]
     out = jnp.zeros((n * rows,) + x.shape[1:], x.dtype)
-    for k in range(n):
+    for k in [0] + list(range(n - 1, 0, -1)):
         block = x if k == 0 else lax.ppermute(x, axis, [(a, a ^ k) for a in range(n)])
         out = lax.dynamic_update_slice_in_dim(out, block, gathered_position(me ^ k, bits) * rows, axis=0)
     return out

time: 67.7 us -> 67.1 us (level)
  waiting for transfers between devices: 14.3 us -> 12.8 us
  starting transfers between devices: 17.4 us -> 18.3 us
    ppermute x3, starting transfers between devices: 3.55 us -> 4.45 us  [fanout_reduce_scatter(): own = own + lax.ppermute(block, axis, [(a, a ^ k) for a in range(n)])]
    ppermute x3, waiting for transfers between devices: 6.12 us -> 5.32 us  [fanout_reduce_scatter(): own = own + lax.ppermute(block, axis, [(a, a ^ k) for a in range(n)])]
    ppermute x3, waiting for transfers between devices: 3.86 us -> 3.17 us  [fanout_all_gather(): lax.ppermute(x, axis, [(a, a ^ k) for a in range(n)])]
  transfers between devices with their start and end apart: 17 -> 17, of which waited for: 9 -> 10; matrix products, arithmetic and copies ran while one was open for 5% -> 5% of each run, Pallas kernels for 14% -> 14%
where the time goes in v24:
time: 67.1 us; the launch traced here: 66.8 us
  matrix products  19.2 us (29%)
  starting transfers between devices  18.3 us (27%)
  waiting for transfers between devices  12.8 us (19%)
  Pallas kernels  9.17 us (14%)
  local copies, waits for them, and re-layouts  5.95 us (9%)
  other arithmetic  1.18 us (2%)
    dot_general x2, matrix products, local(): up_part = jnp.dot(piece, w_up[:, cols], preferred_element_type=jnp.float32)  12 us
    pallas_call x2, Pallas kernels, rows_to_vmem(): pl.pallas_call(kernel, out_shape=jax.ShapeDtypeStruct((count, w.shape[1])...  9.17 us
    ppermute x8, starting transfers between devices, exchange(): return lax.ppermute(x, axis, [(a, a ^ 1 << s) for a in range(n)])  6.29 us
    ppermute x3, starting transfers between devices, fanout_all_gather(): lax.ppermute(x, axis, [(a, a ^ k) for a in range(n)])  5.68 us
    ppermute x3, waiting for transfers between devices, fanout_reduce_scatter(): own = own + lax.ppermute(block, axis, [(a, a ^ k) for a in range(n)])  5.32 us
    ppermute x3, starting transfers between devices, fanout_reduce_scatter(): own = own + lax.ppermute(block, axis, [(a, a ^ k) for a in range(n)])  4.45 us
    dot_general x2, matrix products, local(): jnp.dot(piece, w_gate[:, cols], preferred_element_type=jnp.float32)  3.61 us
    dot_general x2, matrix products, local(): term = jnp.dot(hidden_all, down, preferred_element_type=jnp.float32)  3.53 us
  transfers between devices with their start and end apart: 17, of which 10 were waited for; matrix products, arithmetic and copies ran while one was open for 5% of the time, Pallas kernels for 14%

profile of v24, /device:TPU:0, one launch (start us, length us, event | category | flops | bytes accessed | tf_op | source)
XLA Modules:
  0.0 66.8 jit_solution(2062834330622092043)
XLA Ops:
  0.0 5.0 %collective-permute-start = (bf16[5,2048]{1,0:T(8,128)(2,1)}, bf16[5,2048]{1,0:T(8,128)(2,1)S(1)}, u32[]{:S(2)}, u32[]{:S(2)}) collective-permute-start(bf16[5,2048]{1,0:T(8,128)(2,1)} %param.5), channel_id=1, source_target_pairs={{0,12},{4,8},{8,4},{12,0},{1,13},{5,9},{9,5},{13,1},{2,14},{6,10},... | collective-permute-start | bytes 61448 | tf_op jit(solution)/shard_map/ppermute | solution.py:70
  5.8 1.0 %dynamic_update_slice.12 = bf16[20,2048]{1,0:T(8,128)(2,1)S(1)} dynamic-update-slice(bf16[20,2048]{1,0:T(8,128)(2,1)S(1)} %broadcast_in_dim.15, bf16[5,2048]{1,0:T(8,128)(2,1)} %param.5, s32[]{:T(128)S(6)} %select_n.86, s32[]{:T(128)} %constant.19.clone.1) | dynamic-update-slice | bytes 40964 | tf_op jit(solution)/shard_map/dynamic_update_slice | solution.py:71
  7.4 2.8 %collective-permute-done.1 = bf16[5,2048]{1,0:T(8,128)(2,1)S(1)} collective-permute-done((bf16[5,2048]{1,0:T(8,128)(2,1)}, bf16[5,2048]{1,0:T(8,128)(2,1)S(1)}, u32[]{:S(2)}, u32[]{:S(2)}) %collective-permute-start.1) | collective-permute-done | bytes 20512 | tf_op jit(solution)/shard_map/ppermute | solution.py:70
  11.0 1.6 %collective-permute-start.4 = (f32[20]{0:T(128)S(1)}, f32[20]{0:T(128)S(1)}, u32[]{:S(2)}, u32[]{:S(2)}) collective-permute-start(f32[20]{0:T(128)S(1)} %fusion.8), channel_id=1, source_target_pairs={{0,2},{1,3},{2,0},{3,1},{4,6},{5,7},{6,4},{7,5},{8,10},{9,11},{10,... | collective-permute-start | bytes 248 | tf_op jit(solution)/shard_map/ppermute | solution.py:77
  12.8 1.1 %collective-permute-done.5 = f32[20]{0:T(128)S(1)} collective-permute-done((f32[20]{0:T(128)S(1)}, f32[20]{0:T(128)S(1)}, u32[]{:S(2)}, u32[]{:S(2)}) %collective-permute-start.5) | collective-permute-done | bytes 112 | tf_op jit(solution)/shard_map/ppermute | solution.py:77
  15.3 5.8 %fusion.4 = f32[20,3072]{1,0:T(8,128)S(1)} fusion(bf16[2048,6144]{1,0:T(8,128)(2,1)} %param.8, bf16[20,2048]{1,0:T(8,128)(2,1)S(1)} %dynamic_update_slice.15, f32[2048]{0:T(1024)} %param.6, f32[20]{0:T(128)S(1)} %add_rsqrt_fusion), kind=kOutput, calls=%fused_computation.5 | convolution fusion | flops 251822080 | bytes 12918864 | tf_op jit(solution)/shard_map/dot_general | solution.py:128
  21.1 6.3 %fusion = f32[20,3072]{1,0:T(8,128)S(1)} fusion(bf16[2048,6144]{1,0:T(8,128)(2,1)} %param.8, bf16[20,2048]{1,0:T(8,128)(2,1)S(1)} %dynamic_update_slice.15, f32[2048]{0:T(1024)S(1)} %copy-done.1, f32[20]{0:T(128)S(1)} %add_rsqrt_fusion), kind=kOutput, calls=%fused_computation.1 | convolution fusion | flops 251822080 | bytes 12918864 | tf_op jit(solution)/shard_map/dot_general | solution.py:128
  27.3 3.4 %copy-done = bf16[2048,6144]{1,0:T(8,128)(2,1)S(1)} copy-done((bf16[2048,6144]{1,0:T(8,128)(2,1)S(1)}, bf16[2048,6144]{1,0:T(8,128)(2,1)}, u32[]{:S(2)}) %copy-start) | copy-done | bytes 25165848
  30.7 1.8 %fusion.2 = f32[20,3072]{1,0:T(8,128)S(1)} fusion(bf16[2048,6144]{1,0:T(8,128)(2,1)S(1)} %copy-done, bf16[20,2048]{1,0:T(8,128)(2,1)S(1)} %dynamic_update_slice.15, f32[2048]{0:T(1024)S(1)} %copy-done.1, f32[20]{0:T(128)S(1)} %add_rsqrt_fusion), kind=kOutput, calls=%fused_computation.3 | convolution fusion | flops 251822080 | bytes 12935680 | tf_op jit(solution)/shard_map/dot_general | solution.py:127
  32.5 1.8 %fusion.6 = f32[20,3072]{1,0:T(8,128)S(1)} fusion(bf16[2048,6144]{1,0:T(8,128)(2,1)S(1)} %copy-done, bf16[20,2048]{1,0:T(8,128)(2,1)S(1)} %dynamic_update_slice.15, f32[2048]{0:T(1024)S(1)} %copy-done.1, f32[20]{0:T(128)S(1)} %add_rsqrt_fusion), kind=kOutput, calls=%fused_computation.7 | convolution fusion | flops 251822080 | bytes 12935680 | tf_op jit(solution)/shard_map/dot_general | solution.py:127
  35.1 1.0 %collective-permute-done.10 = f32[2,20,1536]{2,1,0:T(8,128)S(1)} collective-permute-done((f32[2,20,1536]{2,1,0:T(8,128)S(1)}, f32[2,20,1536]{2,1,0:T(8,128)S(1)}, u32[]{:S(2)}, u32[]{:S(2)}) %collective-permute-start.10) | collective-permute-done | bytes 245792 | tf_op jit(solution)/shard_map/ppermute | solution.py:20
  36.2 1.6 %collective-permute-start.11 = (f32[2,20,768]{2,1,0:T(8,128)S(1)}, f32[2,20,768]{2,1,0:T(8,128)S(1)}, u32[]{:S(2)}, u32[]{:S(2)}) collective-permute-start(f32[2,20,768]{2,1,0:T(8,128)S(1)} %pad_maximum_fusion.3), channel_id=1, source_target_pairs={{0,2},{1,3},{2,0},{3,1},{4,6},{5,7},{6,4},{7,5},{8,10},{9,11},{10,... | collective-permute-start | bytes 368648 | tf_op jit(solution)/shard_map/ppermute | solution.py:20
  38.4 4.6 %shard_map.55 = bf16[3072,2048]{1,0:T(8,128)(2,1)S(1)} custom-call(bf16[6144,2048]{1,0:T(8,128)(2,1)} %src.1), custom_call_target="tpu_custom_call" | custom-call | bytes 25165824 | tf_op jit(solution)/shard_map/pallas_call | solution.py:90
  43.1 1.5 %collective-permute-start.12 = (bf16[20,768]{1,0:T(8,128)(2,1)S(1)}, bf16[20,768]{1,0:T(8,128)(2,1)S(1)}, u32[]{:S(2)}, u32[]{:S(2)}) collective-permute-start(bf16[20,768]{1,0:T(8,128)(2,1)S(1)} %fusion.30), channel_id=1, source_target_pairs={{0,2},{1,3},{2,0},{3,1},{4,6},{5,7},{6,4},{7,5},{8,10},{9,11},{10,... | collective-permute-start | bytes 92168 | tf_op jit(solution)/shard_map/ppermute | solution.py:20
  44.6 0.9 %collective-permute-done.7 = f32[2,20,768]{2,1,0:T(8,128)S(1)} collective-permute-done((f32[2,20,768]{2,1,0:T(8,128)S(1)}, f32[2,20,768]{2,1,0:T(8,128)S(1)}, u32[]{:S(2)}, u32[]{:S(2)}) %collective-permute-start.7) | collective-permute-done | bytes 122912 | tf_op jit(solution)/shard_map/ppermute | solution.py:20
  45.6 1.3 %collective-permute-start.8 = (bf16[20,768]{1,0:T(8,128)(2,1)S(1)}, bf16[20,768]{1,0:T(8,128)(2,1)S(1)}, u32[]{:S(2)}, u32[]{:S(2)}) collective-permute-start(bf16[20,768]{1,0:T(8,128)(2,1)S(1)} %fusion.34), channel_id=1, source_target_pairs={{0,2},{1,3},{2,0},{3,1},{4,6},{5,7},{6,4},{7,5},{8,10},{9,11},{10,... | collective-permute-start | bytes 92168 | tf_op jit(solution)/shard_map/ppermute | solution.py:20
  46.9 4.6 %shard_map.56 = bf16[3072,2048]{1,0:T(8,128)(2,1)S(1)} custom-call(bf16[6144,2048]{1,0:T(8,128)(2,1)} %src.1), custom_call_target="tpu_custom_call" | custom-call | bytes 25165824 | tf_op jit(solution)/shard_map/pallas_call | solution.py:90
  52.2 0.7 collective-permute-done.13
  52.8 1.8 %fusion.20 = f32[20,2048]{1,0:T(8,128)S(1)} fusion(bf16[3072,2048]{1,0:T(8,128)(2,1)S(1)} %shard_map.56, bf16[20,1536]{1,0:T(8,128)(2,1)S(1)} %collective-permute-done.13, bf16[20,1536]{1,0:T(8,128)(2,1)S(1)} %maximum_select_fusion.5, pred[]{:T(512)S(6)} %eq.8), kind=kOutput, calls=%fused_computation.34 | convolution fusion | flops 252211200 | bytes 12869633 | tf_op jit(solution)/shard_map/dot_general | solution.py:148
  54.6 1.8 %convolution_add_fusion = f32[20,2048]{1,0:T(8,128)S(1)} fusion(f32[20,2048]{1,0:T(8,128)S(1)} %fusion.20, bf16[3072,2048]{1,0:T(8,128)(2,1)S(1)} %shard_map.55, bf16[20,1536]{1,0:T(8,128)(2,1)S(1)} %collective-permute-done.9, bf16[20,1536]{1,0:T(8,128)(2,1)S(1)} %maximum_select_fusion.4, pred[]{:T(512)S(6)} %eq.8), kind=kOutput, calls=%fused_computation.9 | convolution fusion | flops 252252160 | bytes 13033473 | tf_op jit(solution)/shard_map/dot_general | solution.py:148
  56.4 1.8 %collective-permute-start.14 = (f32[5,2048]{1,0:T(8,128)S(1)}, f32[5,2048]{1,0:T(8,128)S(1)}, u32[]{:S(2)}, u32[]{:S(2)}) collective-permute-start(f32[5,2048]{1,0:T(8,128)S(1)} %get-tuple-element.15), channel_id=1, source_target_pairs={{0,12},{4,8},{8,4},{12,0},{1,13},{5,9},{9,5},{13,1},{2,14},{6,10},... | collective-permute-start | bytes 122888 | tf_op jit(solution)/shard_map/ppermute | solution.py:61
  58.5 2.4 %collective-permute-start.15 = (f32[5,2048]{1,0:T(8,128)S(1)}, f32[5,2048]{1,0:T(8,128)S(1)}, u32[]{:S(2)}, u32[]{:S(2)}) collective-permute-start(f32[5,2048]{1,0:T(8,128)S(1)} %get-tuple-element.17), channel_id=1, source_target_pairs={{0,8},{4,12},{8,0},{12,4},{1,9},{5,13},{9,1},{13,5},{2,10},{6,14},... | collective-permute-start | bytes 122888 | tf_op jit(solution)/shard_map/ppermute | solution.py:61
  60.9 2.4 %collective-permute-done.14 = f32[5,2048]{1,0:T(8,128)S(1)} collective-permute-done((f32[5,2048]{1,0:T(8,128)S(1)}, f32[5,2048]{1,0:T(8,128)S(1)}, u32[]{:S(2)}, u32[]{:S(2)}) %collective-permute-start.14) | collective-permute-done | bytes 40992 | tf_op jit(solution)/shard_map/ppermute | solution.py:61
  63.8 2.4 %collective-permute-done.15 = f32[5,2048]{1,0:T(8,128)S(1)} collective-permute-done((f32[5,2048]{1,0:T(8,128)S(1)}, f32[5,2048]{1,0:T(8,128)S(1)}, u32[]{:S(2)}, u32[]{:S(2)}) %collective-permute-start.15) | collective-permute-done | bytes 40992 | tf_op jit(solution)/shard_map/ppermute | solution.py:61
  (53 shorter events, 7.4 us)
Async XLA Ops:
  0.0 21.1 %copy-start.1 = (f32[2048]{0:T(1024)S(1)}, f32[2048]{0:T(1024)}, u32[]{:S(2)}) copy-start(f32[2048]{0:T(1024)} %param.6) | copy-start | bytes 24580
  0.0 7.2 %collective-permute-start = (bf16[5,2048]{1,0:T(8,128)(2,1)}, bf16[5,2048]{1,0:T(8,128)(2,1)S(1)}, u32[]{:S(2)}, u32[]{:S(2)}) collective-permute-start(bf16[5,2048]{1,0:T(8,128)(2,1)} %param.5), channel_id=1, source_target_pairs={{0,12},{4,8},{8,4},{12,0},{1,13},{5,9},{9,5},{13,1},{2,14},{6,10},... | collective-permute-start | bytes 61448 | tf_op jit(solution)/shard_map/ppermute | solution.py:70
  5.1 5.4 %collective-permute-start.2 = (bf16[5,2048]{1,0:T(8,128)(2,1)}, bf16[5,2048]{1,0:T(8,128)(2,1)S(1)}, u32[]{:S(2)}, u32[]{:S(2)}) collective-permute-start(bf16[5,2048]{1,0:T(8,128)(2,1)} %param.5), channel_id=1, source_target_pairs={{0,4},{4,0},{8,12},{12,8},{1,5},{5,1},{9,13},{13,9},{2,6},{6,2},{1... | collective-permute-start | bytes 61448 | tf_op jit(solution)/shard_map/ppermute | solution.py:70
  5.1 5.1 %collective-permute-start.1 = (bf16[5,2048]{1,0:T(8,128)(2,1)}, bf16[5,2048]{1,0:T(8,128)(2,1)S(1)}, u32[]{:S(2)}, u32[]{:S(2)}) collective-permute-start(bf16[5,2048]{1,0:T(8,128)(2,1)} %param.5), channel_id=1, source_target_pairs={{0,8},{4,12},{8,0},{12,4},{1,9},{5,13},{9,1},{13,5},{2,10},{6,14},... | collective-permute-start | bytes 61448 | tf_op jit(solution)/shard_map/ppermute | solution.py:70
  10.9 3.0 %collective-permute-start.5 = (f32[20]{0:T(128)S(1)}, f32[20]{0:T(128)S(1)}, u32[]{:S(2)}, u32[]{:S(2)}) collective-permute-start(f32[20]{0:T(128)S(1)} %fusion.8), channel_id=1, source_target_pairs={{0,3},{1,2},{2,1},{3,0},{4,7},{5,6},{6,5},{7,4},{8,11},{9,10},{10,... | collective-permute-start | bytes 248 | tf_op jit(solution)/shard_map/ppermute | solution.py:77
  11.0 3.6 %collective-permute-start.4 = (f32[20]{0:T(128)S(1)}, f32[20]{0:T(128)S(1)}, u32[]{:S(2)}, u32[]{:S(2)}) collective-permute-start(f32[20]{0:T(128)S(1)} %fusion.8), channel_id=1, source_target_pairs={{0,2},{1,3},{2,0},{3,1},{4,6},{5,7},{6,4},{7,5},{8,10},{9,11},{10,... | collective-permute-start | bytes 248 | tf_op jit(solution)/shard_map/ppermute | solution.py:77
  12.6 2.1 %collective-permute-start.3 = (f32[20]{0:T(128)S(1)}, f32[20]{0:T(128)S(1)}, u32[]{:S(2)}, u32[]{:S(2)}) collective-permute-start(f32[20]{0:T(128)S(1)} %fusion.8), channel_id=1, source_target_pairs={{0,1},{1,0},{2,3},{3,2},{4,5},{5,4},{6,7},{7,6},{8,9},{9,8},{10,11... | collective-permute-start | bytes 248 | tf_op jit(solution)/shard_map/ppermute | solution.py:77
  15.3 15.5 %copy-start = (bf16[2048,6144]{1,0:T(8,128)(2,1)S(1)}, bf16[2048,6144]{1,0:T(8,128)(2,1)}, u32[]{:S(2)}) copy-start(bf16[2048,6144]{1,0:T(8,128)(2,1)} %param.7) | copy-start | bytes 75497472
  34.4 1.7 %collective-permute-start.10 = (f32[2,20,1536]{2,1,0:T(8,128)S(1)}, f32[2,20,1536]{2,1,0:T(8,128)S(1)}, u32[]{:S(2)}, u32[]{:S(2)}) collective-permute-start(f32[2,20,1536]{2,1,0:T(8,128)S(1)} %pad_maximum_fusion.1), channel_id=1, source_target_pairs={{0,1},{1,0},{2,3},{3,2},{4,5},{5,4},{6,7},{7,6},{8,9},{9,8},{10,11... | collective-permute-start | bytes 737288 | tf_op jit(solution)/shard_map/ppermute | solution.py:20
  34.9 2.8 %collective-permute-start.6 = (f32[2,20,1536]{2,1,0:T(8,128)S(1)}, f32[2,20,1536]{2,1,0:T(8,128)S(1)}, u32[]{:S(2)}, u32[]{:S(2)}) collective-permute-start(f32[2,20,1536]{2,1,0:T(8,128)S(1)} %pad_maximum_fusion), channel_id=1, source_target_pairs={{0,1},{1,0},{2,3},{3,2},{4,5},{5,4},{6,7},{7,6},{8,9},{9,8},{10,11... | collective-permute-start | bytes 737288 | tf_op jit(solution)/shard_map/ppermute | solution.py:20
  36.2 6.9 %collective-permute-start.11 = (f32[2,20,768]{2,1,0:T(8,128)S(1)}, f32[2,20,768]{2,1,0:T(8,128)S(1)}, u32[]{:S(2)}, u32[]{:S(2)}) collective-permute-start(f32[2,20,768]{2,1,0:T(8,128)S(1)} %pad_maximum_fusion.3), channel_id=1, source_target_pairs={{0,2},{1,3},{2,0},{3,1},{4,6},{5,7},{6,4},{7,5},{8,10},{9,11},{10,... | collective-permute-start | bytes 368648 | tf_op jit(solution)/shard_map/ppermute | solution.py:20
  37.8 7.7 %collective-permute-start.7 = (f32[2,20,768]{2,1,0:T(8,128)S(1)}, f32[2,20,768]{2,1,0:T(8,128)S(1)}, u32[]{:S(2)}, u32[]{:S(2)}) collective-permute-start(f32[2,20,768]{2,1,0:T(8,128)S(1)} %pad_maximum_fusion.2), channel_id=1, source_target_pairs={{0,2},{1,3},{2,0},{3,1},{4,6},{5,7},{6,4},{7,5},{8,10},{9,11},{10,... | collective-permute-start | bytes 368648 | tf_op jit(solution)/shard_map/ppermute | solution.py:20
  43.1 8.4 %collective-permute-start.12 = (bf16[20,768]{1,0:T(8,128)(2,1)S(1)}, bf16[20,768]{1,0:T(8,128)(2,1)S(1)}, u32[]{:S(2)}, u32[]{:S(2)}) collective-permute-start(bf16[20,768]{1,0:T(8,128)(2,1)S(1)} %fusion.30), channel_id=1, source_target_pairs={{0,2},{1,3},{2,0},{3,1},{4,6},{5,7},{6,4},{7,5},{8,10},{9,11},{10,... | collective-permute-start | bytes 92168 | tf_op jit(solution)/shard_map/ppermute | solution.py:20
  45.6 6.0 %collective-permute-start.8 = (bf16[20,768]{1,0:T(8,128)(2,1)S(1)}, bf16[20,768]{1,0:T(8,128)(2,1)S(1)}, u32[]{:S(2)}, u32[]{:S(2)}) collective-permute-start(bf16[20,768]{1,0:T(8,128)(2,1)S(1)} %fusion.34), channel_id=1, source_target_pairs={{0,2},{1,3},{2,0},{3,1},{4,6},{5,7},{6,4},{7,5},{8,10},{9,11},{10,... | collective-permute-start | bytes 92168 | tf_op jit(solution)/shard_map/ppermute | solution.py:20
  51.5 1.3 %collective-permute-start.13 = (bf16[20,1536]{1,0:T(8,128)(2,1)S(1)}, bf16[20,1536]{1,0:T(8,128)(2,1)S(1)}, u32[]{:S(2)}, u32[]{:S(2)}) collective-permute-start(bf16[20,1536]{1,0:T(8,128)(2,1)S(1)} %maximum_select_fusion.5), channel_id=1, source_target_pairs={{0,1},{1,0},{2,3},{3,2},{4,5},{5,4},{6,7},{7,6},{8,9},{9,8},{10,11... | collective-permute-start | bytes 184328 | tf_op jit(solution)/shard_map/ppermute | solution.py:20
  51.6 3.0 %collective-permute-start.9 = (bf16[20,1536]{1,0:T(8,128)(2,1)S(1)}, bf16[20,1536]{1,0:T(8,128)(2,1)S(1)}, u32[]{:S(2)}, u32[]{:S(2)}) collective-permute-start(bf16[20,1536]{1,0:T(8,128)(2,1)S(1)} %maximum_select_fusion.4), channel_id=1, source_target_pairs={{0,1},{1,0},{2,3},{3,2},{4,5},{5,4},{6,7},{7,6},{8,9},{9,8},{10,11... | collective-permute-start | bytes 184328 | tf_op jit(solution)/shard_map/ppermute | solution.py:20
  56.4 6.8 %collective-permute-start.14 = (f32[5,2048]{1,0:T(8,128)S(1)}, f32[5,2048]{1,0:T(8,128)S(1)}, u32[]{:S(2)}, u32[]{:S(2)}) collective-permute-start(f32[5,2048]{1,0:T(8,128)S(1)} %get-tuple-element.15), channel_id=1, source_target_pairs={{0,12},{4,8},{8,4},{12,0},{1,13},{5,9},{9,5},{13,1},{2,14},{6,10},... | collective-permute-start | bytes 122888 | tf_op jit(solution)/shard_map/ppermute | solution.py:61
  58.2 5.6 %collective-permute-start.16 = (f32[5,2048]{1,0:T(8,128)S(1)}, f32[5,2048]{1,0:T(8,128)S(1)}, u32[]{:S(2)}, u32[]{:S(2)}) collective-permute-start(f32[5,2048]{1,0:T(8,128)S(1)} %get-tuple-element.16), channel_id=1, source_target_pairs={{0,4},{4,0},{8,12},{12,8},{1,5},{5,1},{9,13},{13,9},{2,6},{6,2},{1... | collective-permute-start | bytes 122888 | tf_op jit(solution)/shard_map/ppermute | solution.py:61
  58.5 7.7 %collective-permute-start.15 = (f32[5,2048]{1,0:T(8,128)S(1)}, f32[5,2048]{1,0:T(8,128)S(1)}, u32[]{:S(2)}, u32[]{:S(2)}) collective-permute-start(f32[5,2048]{1,0:T(8,128)S(1)} %get-tuple-element.17), channel_id=1, source_target_pairs={{0,8},{4,12},{8,0},{12,4},{1,9},{5,13},{9,1},{13,5},{2,10},{6,14},... | collective-permute-start | bytes 122888 | tf_op jit(solution)/shard_map/ppermute | solution.py:61

commit v25 on v24

--- a/solution.py
+++ b/solution.py
@@ -74,7 +74,8 @@
 
 def fanout_all_reduce(x, axis, n):
     me = lax.axis_index(axis)
-    got = jnp.stack([x] + [lax.ppermute(x, axis, [(a, a ^ k) for a in range(n)]) for k in range(1, n)])
+    recv = {k: lax.ppermute(x, axis, [(a, a ^ k) for a in range(n)]) for k in range(n - 1, 0, -1)}
+    got = jnp.stack([x] + [recv[k] for k in range(1, n)])
     ordered = jnp.take(got, jnp.arange(n) ^ me, axis=0)
     return jnp.sum(ordered, axis=0)
 

time: 67.1 us -> 67.1 us (level)
  no operation moved by 1% of the time
where the time goes in v25:
time: 67.1 us; the launch traced here: 66.8 us
  matrix products  19.2 us (29%)
  starting transfers between devices  18.3 us (27%)
  waiting for transfers between devices  12.8 us (19%)
  Pallas kernels  9.17 us (14%)
  local copies, waits for them, and re-layouts  5.95 us (9%)
  other arithmetic  1.18 us (2%)
    dot_general x2, matrix products, local(): up_part = jnp.dot(piece, w_up[:, cols], preferred_element_type=jnp.float32)  12 us
    pallas_call x2, Pallas kernels, rows_to_vmem(): pl.pallas_call(kernel, out_shape=jax.ShapeDtypeStruct((count, w.shape[1])...  9.17 us
    ppermute x8, starting transfers between devices, exchange(): return lax.ppermute(x, axis, [(a, a ^ 1 << s) for a in range(n)])  6.29 us
    ppermute x3, starting transfers between devices, fanout_all_gather(): lax.ppermute(x, axis, [(a, a ^ k) for a in range(n)])  5.68 us
    ppermute x3, waiting for transfers between devices, fanout_reduce_scatter(): own = own + lax.ppermute(block, axis, [(a, a ^ k) for a in range(n)])  5.32 us
    ppermute x3, starting transfers between devices, fanout_reduce_scatter(): own = own + lax.ppermute(block, axis, [(a, a ^ k) for a in range(n)])  4.45 us
    dot_general x2, matrix products, local(): jnp.dot(piece, w_gate[:, cols], preferred_element_type=jnp.float32)  3.61 us
    dot_general x2, matrix products, local(): term = jnp.dot(hidden_all, down, preferred_element_type=jnp.float32)  3.53 us
  transfers between devices with their start and end apart: 17, of which 10 were waited for; matrix products, arithmetic and copies ran while one was open for 5% of the time, Pallas kernels for 14%

profile of v25, /device:TPU:0, one launch (start us, length us, event | category | flops | bytes accessed | tf_op | source)
XLA Modules:
  0.0 66.8 jit_solution(2062834330622092043)
XLA Ops:
  0.0 5.0 %collective-permute-start = (bf16[5,2048]{1,0:T(8,128)(2,1)}, bf16[5,2048]{1,0:T(8,128)(2,1)S(1)}, u32[]{:S(2)}, u32[]{:S(2)}) collective-permute-start(bf16[5,2048]{1,0:T(8,128)(2,1)} %param.5), channel_id=1, source_target_pairs={{0,12},{4,8},{8,4},{12,0},{1,13},{5,9},{9,5},{13,1},{2,14},{6,10},... | collective-permute-start | bytes 61448 | tf_op jit(solution)/shard_map/ppermute | solution.py:70
  5.8 1.0 %dynamic_update_slice.12 = bf16[20,2048]{1,0:T(8,128)(2,1)S(1)} dynamic-update-slice(bf16[20,2048]{1,0:T(8,128)(2,1)S(1)} %broadcast_in_dim.15, bf16[5,2048]{1,0:T(8,128)(2,1)} %param.5, s32[]{:T(128)S(6)} %select_n.86, s32[]{:T(128)} %constant.19.clone.1) | dynamic-update-slice | bytes 40964 | tf_op jit(solution)/shard_map/dynamic_update_slice | solution.py:71
  7.4 2.8 %collective-permute-done.1 = bf16[5,2048]{1,0:T(8,128)(2,1)S(1)} collective-permute-done((bf16[5,2048]{1,0:T(8,128)(2,1)}, bf16[5,2048]{1,0:T(8,128)(2,1)S(1)}, u32[]{:S(2)}, u32[]{:S(2)}) %collective-permute-start.1) | collective-permute-done | bytes 20512 | tf_op jit(solution)/shard_map/ppermute | solution.py:70
  11.0 1.6 %collective-permute-start.4 = (f32[20]{0:T(128)S(1)}, f32[20]{0:T(128)S(1)}, u32[]{:S(2)}, u32[]{:S(2)}) collective-permute-start(f32[20]{0:T(128)S(1)} %fusion.8), channel_id=1, source_target_pairs={{0,2},{1,3},{2,0},{3,1},{4,6},{5,7},{6,4},{7,5},{8,10},{9,11},{10,... | collective-permute-start | bytes 248 | tf_op jit(solution)/shard_map/ppermute | solution.py:77
  12.8 1.1 %collective-permute-done.5 = f32[20]{0:T(128)S(1)} collective-permute-done((f32[20]{0:T(128)S(1)}, f32[20]{0:T(128)S(1)}, u32[]{:S(2)}, u32[]{:S(2)}) %collective-permute-start.5) | collective-permute-done | bytes 112 | tf_op jit(solution)/shard_map/ppermute | solution.py:77
  15.3 5.8 %fusion.4 = f32[20,3072]{1,0:T(8,128)S(1)} fusion(bf16[2048,6144]{1,0:T(8,128)(2,1)} %param.8, bf16[20,2048]{1,0:T(8,128)(2,1)S(1)} %dynamic_update_slice.15, f32[2048]{0:T(1024)} %param.6, f32[20]{0:T(128)S(1)} %add_rsqrt_fusion), kind=kOutput, calls=%fused_computation.5 | convolution fusion | flops 251822080 | bytes 12918864 | tf_op jit(solution)/shard_map/dot_general | solution.py:129
  21.1 6.3 %fusion = f32[20,3072]{1,0:T(8,128)S(1)} fusion(bf16[2048,6144]{1,0:T(8,128)(2,1)} %param.8, bf16[20,2048]{1,0:T(8,128)(2,1)S(1)} %dynamic_update_slice.15, f32[2048]{0:T(1024)S(1)} %copy-done.1, f32[20]{0:T(128)S(1)} %add_rsqrt_fusion), kind=kOutput, calls=%fused_computation.1 | convolution fusion | flops 251822080 | bytes 12918864 | tf_op jit(solution)/shard_map/dot_general | solution.py:129
  27.3 3.4 %copy-done = bf16[2048,6144]{1,0:T(8,128)(2,1)S(1)} copy-done((bf16[2048,6144]{1,0:T(8,128)(2,1)S(1)}, bf16[2048,6144]{1,0:T(8,128)(2,1)}, u32[]{:S(2)}) %copy-start) | copy-done | bytes 25165848
  30.7 1.8 %fusion.2 = f32[20,3072]{1,0:T(8,128)S(1)} fusion(bf16[2048,6144]{1,0:T(8,128)(2,1)S(1)} %copy-done, bf16[20,2048]{1,0:T(8,128)(2,1)S(1)} %dynamic_update_slice.15, f32[2048]{0:T(1024)S(1)} %copy-done.1, f32[20]{0:T(128)S(1)} %add_rsqrt_fusion), kind=kOutput, calls=%fused_computation.3 | convolution fusion | flops 251822080 | bytes 12935680 | tf_op jit(solution)/shard_map/dot_general | solution.py:128
  32.5 1.8 %fusion.6 = f32[20,3072]{1,0:T(8,128)S(1)} fusion(bf16[2048,6144]{1,0:T(8,128)(2,1)S(1)} %copy-done, bf16[20,2048]{1,0:T(8,128)(2,1)S(1)} %dynamic_update_slice.15, f32[2048]{0:T(1024)S(1)} %copy-done.1, f32[20]{0:T(128)S(1)} %add_rsqrt_fusion), kind=kOutput, calls=%fused_computation.7 | convolution fusion | flops 251822080 | bytes 12935680 | tf_op jit(solution)/shard_map/dot_general | solution.py:128
  35.1 1.0 %collective-permute-done.10 = f32[2,20,1536]{2,1,0:T(8,128)S(1)} collective-permute-done((f32[2,20,1536]{2,1,0:T(8,128)S(1)}, f32[2,20,1536]{2,1,0:T(8,128)S(1)}, u32[]{:S(2)}, u32[]{:S(2)}) %collective-permute-start.10) | collective-permute-done | bytes 245792 | tf_op jit(solution)/shard_map/ppermute | solution.py:20
  36.2 1.6 %collective-permute-start.11 = (f32[2,20,768]{2,1,0:T(8,128)S(1)}, f32[2,20,768]{2,1,0:T(8,128)S(1)}, u32[]{:S(2)}, u32[]{:S(2)}) collective-permute-start(f32[2,20,768]{2,1,0:T(8,128)S(1)} %pad_maximum_fusion.3), channel_id=1, source_target_pairs={{0,2},{1,3},{2,0},{3,1},{4,6},{5,7},{6,4},{7,5},{8,10},{9,11},{10,... | collective-permute-start | bytes 368648 | tf_op jit(solution)/shard_map/ppermute | solution.py:20
  38.4 4.6 %shard_map.55 = bf16[3072,2048]{1,0:T(8,128)(2,1)S(1)} custom-call(bf16[6144,2048]{1,0:T(8,128)(2,1)} %src.1), custom_call_target="tpu_custom_call" | custom-call | bytes 25165824 | tf_op jit(solution)/shard_map/pallas_call | solution.py:91
  43.1 1.5 %collective-permute-start.12 = (bf16[20,768]{1,0:T(8,128)(2,1)S(1)}, bf16[20,768]{1,0:T(8,128)(2,1)S(1)}, u32[]{:S(2)}, u32[]{:S(2)}) collective-permute-start(bf16[20,768]{1,0:T(8,128)(2,1)S(1)} %fusion.30), channel_id=1, source_target_pairs={{0,2},{1,3},{2,0},{3,1},{4,6},{5,7},{6,4},{7,5},{8,10},{9,11},{10,... | collective-permute-start | bytes 92168 | tf_op jit(solution)/shard_map/ppermute | solution.py:20
  44.6 0.9 %collective-permute-done.7 = f32[2,20,768]{2,1,0:T(8,128)S(1)} collective-permute-done((f32[2,20,768]{2,1,0:T(8,128)S(1)}, f32[2,20,768]{2,1,0:T(8,128)S(1)}, u32[]{:S(2)}, u32[]{:S(2)}) %collective-permute-start.7) | collective-permute-done | bytes 122912 | tf_op jit(solution)/shard_map/ppermute | solution.py:20
  45.6 1.3 %collective-permute-start.8 = (bf16[20,768]{1,0:T(8,128)(2,1)S(1)}, bf16[20,768]{1,0:T(8,128)(2,1)S(1)}, u32[]{:S(2)}, u32[]{:S(2)}) collective-permute-start(bf16[20,768]{1,0:T(8,128)(2,1)S(1)} %fusion.34), channel_id=1, source_target_pairs={{0,2},{1,3},{2,0},{3,1},{4,6},{5,7},{6,4},{7,5},{8,10},{9,11},{10,... | collective-permute-start | bytes 92168 | tf_op jit(solution)/shard_map/ppermute | solution.py:20
  46.9 4.6 %shard_map.56 = bf16[3072,2048]{1,0:T(8,128)(2,1)S(1)} custom-call(bf16[6144,2048]{1,0:T(8,128)(2,1)} %src.1), custom_call_target="tpu_custom_call" | custom-call | bytes 25165824 | tf_op jit(solution)/shard_map/pallas_call | solution.py:91
  52.2 0.7 collective-permute-done.13
  52.8 1.8 %fusion.20 = f32[20,2048]{1,0:T(8,128)S(1)} fusion(bf16[3072,2048]{1,0:T(8,128)(2,1)S(1)} %shard_map.56, bf16[20,1536]{1,0:T(8,128)(2,1)S(1)} %collective-permute-done.13, bf16[20,1536]{1,0:T(8,128)(2,1)S(1)} %maximum_select_fusion.5, pred[]{:T(512)S(6)} %eq.8), kind=kOutput, calls=%fused_computation.34 | convolution fusion | flops 252211200 | bytes 12869633 | tf_op jit(solution)/shard_map/dot_general | solution.py:149
  54.6 1.8 %convolution_add_fusion = f32[20,2048]{1,0:T(8,128)S(1)} fusion(f32[20,2048]{1,0:T(8,128)S(1)} %fusion.20, bf16[3072,2048]{1,0:T(8,128)(2,1)S(1)} %shard_map.55, bf16[20,1536]{1,0:T(8,128)(2,1)S(1)} %collective-permute-done.9, bf16[20,1536]{1,0:T(8,128)(2,1)S(1)} %maximum_select_fusion.4, pred[]{:T(512)S(6)} %eq.8), kind=kOutput, calls=%fused_computation.9 | convolution fusion | flops 252252160 | bytes 13033473 | tf_op jit(solution)/shard_map/dot_general | solution.py:149
  56.4 1.8 %collective-permute-start.14 = (f32[5,2048]{1,0:T(8,128)S(1)}, f32[5,2048]{1,0:T(8,128)S(1)}, u32[]{:S(2)}, u32[]{:S(2)}) collective-permute-start(f32[5,2048]{1,0:T(8,128)S(1)} %get-tuple-element.15), channel_id=1, source_target_pairs={{0,12},{4,8},{8,4},{12,0},{1,13},{5,9},{9,5},{13,1},{2,14},{6,10},... | collective-permute-start | bytes 122888 | tf_op jit(solution)/shard_map/ppermute | solution.py:61
  58.5 2.4 %collective-permute-start.15 = (f32[5,2048]{1,0:T(8,128)S(1)}, f32[5,2048]{1,0:T(8,128)S(1)}, u32[]{:S(2)}, u32[]{:S(2)}) collective-permute-start(f32[5,2048]{1,0:T(8,128)S(1)} %get-tuple-element.17), channel_id=1, source_target_pairs={{0,8},{4,12},{8,0},{12,4},{1,9},{5,13},{9,1},{13,5},{2,10},{6,14},... | collective-permute-start | bytes 122888 | tf_op jit(solution)/shard_map/ppermute | solution.py:61
  60.9 2.4 %collective-permute-done.14 = f32[5,2048]{1,0:T(8,128)S(1)} collective-permute-done((f32[5,2048]{1,0:T(8,128)S(1)}, f32[5,2048]{1,0:T(8,128)S(1)}, u32[]{:S(2)}, u32[]{:S(2)}) %collective-permute-start.14) | collective-permute-done | bytes 40992 | tf_op jit(solution)/shard_map/ppermute | solution.py:61
  63.8 2.4 %collective-permute-done.15 = f32[5,2048]{1,0:T(8,128)S(1)} collective-permute-done((f32[5,2048]{1,0:T(8,128)S(1)}, f32[5,2048]{1,0:T(8,128)S(1)}, u32[]{:S(2)}, u32[]{:S(2)}) %collective-permute-start.15) | collective-permute-done | bytes 40992 | tf_op jit(solution)/shard_map/ppermute | solution.py:61
  (53 shorter events, 7.4 us)
Async XLA Ops:
  0.0 21.1 %copy-start.1 = (f32[2048]{0:T(1024)S(1)}, f32[2048]{0:T(1024)}, u32[]{:S(2)}) copy-start(f32[2048]{0:T(1024)} %param.6) | copy-start | bytes 24580
  0.0 7.2 %collective-permute-start = (bf16[5,2048]{1,0:T(8,128)(2,1)}, bf16[5,2048]{1,0:T(8,128)(2,1)S(1)}, u32[]{:S(2)}, u32[]{:S(2)}) collective-permute-start(bf16[5,2048]{1,0:T(8,128)(2,1)} %param.5), channel_id=1, source_target_pairs={{0,12},{4,8},{8,4},{12,0},{1,13},{5,9},{9,5},{13,1},{2,14},{6,10},... | collective-permute-start | bytes 61448 | tf_op jit(solution)/shard_map/ppermute | solution.py:70
  5.1 5.4 %collective-permute-start.2 = (bf16[5,2048]{1,0:T(8,128)(2,1)}, bf16[5,2048]{1,0:T(8,128)(2,1)S(1)}, u32[]{:S(2)}, u32[]{:S(2)}) collective-permute-start(bf16[5,2048]{1,0:T(8,128)(2,1)} %param.5), channel_id=1, source_target_pairs={{0,4},{4,0},{8,12},{12,8},{1,5},{5,1},{9,13},{13,9},{2,6},{6,2},{1... | collective-permute-start | bytes 61448 | tf_op jit(solution)/shard_map/ppermute | solution.py:70
  5.1 5.1 %collective-permute-start.1 = (bf16[5,2048]{1,0:T(8,128)(2,1)}, bf16[5,2048]{1,0:T(8,128)(2,1)S(1)}, u32[]{:S(2)}, u32[]{:S(2)}) collective-permute-start(bf16[5,2048]{1,0:T(8,128)(2,1)} %param.5), channel_id=1, source_target_pairs={{0,8},{4,12},{8,0},{12,4},{1,9},{5,13},{9,1},{13,5},{2,10},{6,14},... | collective-permute-start | bytes 61448 | tf_op jit(solution)/shard_map/ppermute | solution.py:70
  10.9 3.0 %collective-permute-start.5 = (f32[20]{0:T(128)S(1)}, f32[20]{0:T(128)S(1)}, u32[]{:S(2)}, u32[]{:S(2)}) collective-permute-start(f32[20]{0:T(128)S(1)} %fusion.8), channel_id=1, source_target_pairs={{0,3},{1,2},{2,1},{3,0},{4,7},{5,6},{6,5},{7,4},{8,11},{9,10},{10,... | collective-permute-start | bytes 248 | tf_op jit(solution)/shard_map/ppermute | solution.py:77
  11.0 3.6 %collective-permute-start.4 = (f32[20]{0:T(128)S(1)}, f32[20]{0:T(128)S(1)}, u32[]{:S(2)}, u32[]{:S(2)}) collective-permute-start(f32[20]{0:T(128)S(1)} %fusion.8), channel_id=1, source_target_pairs={{0,2},{1,3},{2,0},{3,1},{4,6},{5,7},{6,4},{7,5},{8,10},{9,11},{10,... | collective-permute-start | bytes 248 | tf_op jit(solution)/shard_map/ppermute | solution.py:77
  12.6 2.1 %collective-permute-start.3 = (f32[20]{0:T(128)S(1)}, f32[20]{0:T(128)S(1)}, u32[]{:S(2)}, u32[]{:S(2)}) collective-permute-start(f32[20]{0:T(128)S(1)} %fusion.8), channel_id=1, source_target_pairs={{0,1},{1,0},{2,3},{3,2},{4,5},{5,4},{6,7},{7,6},{8,9},{9,8},{10,11... | collective-permute-start | bytes 248 | tf_op jit(solution)/shard_map/ppermute | solution.py:77
  15.3 15.5 %copy-start = (bf16[2048,6144]{1,0:T(8,128)(2,1)S(1)}, bf16[2048,6144]{1,0:T(8,128)(2,1)}, u32[]{:S(2)}) copy-start(bf16[2048,6144]{1,0:T(8,128)(2,1)} %param.7) | copy-start | bytes 75497472
  34.4 1.7 %collective-permute-start.10 = (f32[2,20,1536]{2,1,0:T(8,128)S(1)}, f32[2,20,1536]{2,1,0:T(8,128)S(1)}, u32[]{:S(2)}, u32[]{:S(2)}) collective-permute-start(f32[2,20,1536]{2,1,0:T(8,128)S(1)} %pad_maximum_fusion.1), channel_id=1, source_target_pairs={{0,1},{1,0},{2,3},{3,2},{4,5},{5,4},{6,7},{7,6},{8,9},{9,8},{10,11... | collective-permute-start | bytes 737288 | tf_op jit(solution)/shard_map/ppermute | solution.py:20
  34.9 2.8 %collective-permute-start.6 = (f32[2,20,1536]{2,1,0:T(8,128)S(1)}, f32[2,20,1536]{2,1,0:T(8,128)S(1)}, u32[]{:S(2)}, u32[]{:S(2)}) collective-permute-start(f32[2,20,1536]{2,1,0:T(8,128)S(1)} %pad_maximum_fusion), channel_id=1, source_target_pairs={{0,1},{1,0},{2,3},{3,2},{4,5},{5,4},{6,7},{7,6},{8,9},{9,8},{10,11... | collective-permute-start | bytes 737288 | tf_op jit(solution)/shard_map/ppermute | solution.py:20
  36.2 6.9 %collective-permute-start.11 = (f32[2,20,768]{2,1,0:T(8,128)S(1)}, f32[2,20,768]{2,1,0:T(8,128)S(1)}, u32[]{:S(2)}, u32[]{:S(2)}) collective-permute-start(f32[2,20,768]{2,1,0:T(8,128)S(1)} %pad_maximum_fusion.3), channel_id=1, source_target_pairs={{0,2},{1,3},{2,0},{3,1},{4,6},{5,7},{6,4},{7,5},{8,10},{9,11},{10,... | collective-permute-start | bytes 368648 | tf_op jit(solution)/shard_map/ppermute | solution.py:20
  37.8 7.7 %collective-permute-start.7 = (f32[2,20,768]{2,1,0:T(8,128)S(1)}, f32[2,20,768]{2,1,0:T(8,128)S(1)}, u32[]{:S(2)}, u32[]{:S(2)}) collective-permute-start(f32[2,20,768]{2,1,0:T(8,128)S(1)} %pad_maximum_fusion.2), channel_id=1, source_target_pairs={{0,2},{1,3},{2,0},{3,1},{4,6},{5,7},{6,4},{7,5},{8,10},{9,11},{10,... | collective-permute-start | bytes 368648 | tf_op jit(solution)/shard_map/ppermute | solution.py:20
  43.1 8.4 %collective-permute-start.12 = (bf16[20,768]{1,0:T(8,128)(2,1)S(1)}, bf16[20,768]{1,0:T(8,128)(2,1)S(1)}, u32[]{:S(2)}, u32[]{:S(2)}) collective-permute-start(bf16[20,768]{1,0:T(8,128)(2,1)S(1)} %fusion.30), channel_id=1, source_target_pairs={{0,2},{1,3},{2,0},{3,1},{4,6},{5,7},{6,4},{7,5},{8,10},{9,11},{10,... | collective-permute-start | bytes 92168 | tf_op jit(solution)/shard_map/ppermute | solution.py:20
  45.6 6.0 %collective-permute-start.8 = (bf16[20,768]{1,0:T(8,128)(2,1)S(1)}, bf16[20,768]{1,0:T(8,128)(2,1)S(1)}, u32[]{:S(2)}, u32[]{:S(2)}) collective-permute-start(bf16[20,768]{1,0:T(8,128)(2,1)S(1)} %fusion.34), channel_id=1, source_target_pairs={{0,2},{1,3},{2,0},{3,1},{4,6},{5,7},{6,4},{7,5},{8,10},{9,11},{10,... | collective-permute-start | bytes 92168 | tf_op jit(solution)/shard_map/ppermute | solution.py:20
  51.5 1.3 %collective-permute-start.13 = (bf16[20,1536]{1,0:T(8,128)(2,1)S(1)}, bf16[20,1536]{1,0:T(8,128)(2,1)S(1)}, u32[]{:S(2)}, u32[]{:S(2)}) collective-permute-start(bf16[20,1536]{1,0:T(8,128)(2,1)S(1)} %maximum_select_fusion.5), channel_id=1, source_target_pairs={{0,1},{1,0},{2,3},{3,2},{4,5},{5,4},{6,7},{7,6},{8,9},{9,8},{10,11... | collective-permute-start | bytes 184328 | tf_op jit(solution)/shard_map/ppermute | solution.py:20
  51.6 3.0 %collective-permute-start.9 = (bf16[20,1536]{1,0:T(8,128)(2,1)S(1)}, bf16[20,1536]{1,0:T(8,128)(2,1)S(1)}, u32[]{:S(2)}, u32[]{:S(2)}) collective-permute-start(bf16[20,1536]{1,0:T(8,128)(2,1)S(1)} %maximum_select_fusion.4), channel_id=1, source_target_pairs={{0,1},{1,0},{2,3},{3,2},{4,5},{5,4},{6,7},{7,6},{8,9},{9,8},{10,11... | collective-permute-start | bytes 184328 | tf_op jit(solution)/shard_map/ppermute | solution.py:20
  56.4 6.8 %collective-permute-start.14 = (f32[5,2048]{1,0:T(8,128)S(1)}, f32[5,2048]{1,0:T(8,128)S(1)}, u32[]{:S(2)}, u32[]{:S(2)}) collective-permute-start(f32[5,2048]{1,0:T(8,128)S(1)} %get-tuple-element.15), channel_id=1, source_target_pairs={{0,12},{4,8},{8,4},{12,0},{1,13},{5,9},{9,5},{13,1},{2,14},{6,10},... | collective-permute-start | bytes 122888 | tf_op jit(solution)/shard_map/ppermute | solution.py:61
  58.2 5.6 %collective-permute-start.16 = (f32[5,2048]{1,0:T(8,128)S(1)}, f32[5,2048]{1,0:T(8,128)S(1)}, u32[]{:S(2)}, u32[]{:S(2)}) collective-permute-start(f32[5,2048]{1,0:T(8,128)S(1)} %get-tuple-element.16), channel_id=1, source_target_pairs={{0,4},{4,0},{8,12},{12,8},{1,5},{5,1},{9,13},{13,9},{2,6},{6,2},{1... | collective-permute-start | bytes 122888 | tf_op jit(solution)/shard_map/ppermute | solution.py:61
  58.5 7.7 %collective-permute-start.15 = (f32[5,2048]{1,0:T(8,128)S(1)}, f32[5,2048]{1,0:T(8,128)S(1)}, u32[]{:S(2)}, u32[]{:S(2)}) collective-permute-start(f32[5,2048]{1,0:T(8,128)S(1)} %get-tuple-element.17), channel_id=1, source_target_pairs={{0,8},{4,12},{8,0},{12,4},{1,9},{5,13},{9,1},{13,5},{2,10},{6,14},... | collective-permute-start | bytes 122888 | tf_op jit(solution)/shard_map/ppermute | solution.py:61
